TPU v7x, 32 devices: a whole 2x2x4 slice. The times are simulated.
32 devices in a mesh: gx: 4 (over y, x), gy: 4 (over z), gz: 2 (over core).
Axes of the slice: x: 2, y: 2, z: 4, core: 2. Of those that a mesh axis runs over, the one named last changes fastest.
Arguments:
- heart_state: float32 [19, 32, 128, 256], P(None, 'gx', 'gy', 'gz'), may hold values from -4 to 4, as said below
- cell_type: int32 [32, 128, 256], P('gx', 'gy', 'gz'), may hold values from 0 to 2
- gate_half: float32 [18], replicated, may hold values from -1 to 1
- gate_slope: float32 [18], replicated, may hold values from 0.15 to 0.6
- gate_tau: float32 [18], replicated, may hold values from 0.03 to 1.5
- conduct: float32 [3, 9], replicated, may hold values from 0.1 to 1.5
- reversal: float32 [9], replicated, may hold values from -2 to 2
- block_device: int32 [32, 128, 2], P('gx', 'gy', 'gz'), may hold values from 0 to 31, as said below
- block_row: int32 [32, 128, 2], P('gx', 'gy', 'gz'), may hold values from 0 to 2047, as said below
- tissue: int32 [128, 256, 256], P('gx', 'gy', 'gz'), may hold values from 0 to 3
- tissue_sigma: float32 [4, 3], replicated, may hold values from 0.2 to 2
Outputs:
- heart_next: float32 [19, 32, 128, 256], P(None, 'gx', 'gy', 'gz')
- potential: float32 [128, 256, 4, 256], P('gx', 'gy', None, 'gz')
Inputs may be any that keep to these rules, and one draw needn't show every extreme that they name: `heart_state`: row 0 (the voltage) lies within -4 to 4, rows 1 to 18 (gates) within 0 to 1. `block_device`: in every aligned group of four devices, one device is named exactly 24 times by the blocks of every device, one exactly 24 // 3 times by the blocks of every device, and the other two by none; which ones, and the order of the blocks, vary. `block_row`: blocks sent to the same device cover different rows; a device receives at most 768 blocks, and a quarter of the devices receive exactly that many.
All inputs are finite; a program needn't handle non-finite values.
Results may differ from a plain program's by a relative error of at most 0.0001.
Values sent between devices are 32-bit elements; how exact they have to be, the bound alone decides.
No kernel may reach another device: no remote copies, remote signals or barrier semaphores. Data moves between devices by JAX's collectives and lax.ppermute only.
A program may use at most 256 MiB of HBM per device.

v0:
```python
import jax
import jax.numpy as jnp
from jax import lax
from jax.sharding import PartitionSpec as P
from jax.experimental import pallas as pl
from jax.experimental.pallas import tpu as pltpu
import functools

STEPS = 4
SWEEPS = 4


DT_HEART = 0.05
SIGMA_HEART = 1.0
SCREEN = 0.05
LOW_EDGE = 0.1
HIGH_EDGE = 1.9


def chebyshev_weights(sweep_count):
    spectrum_mid = 0.5 * (HIGH_EDGE + LOW_EDGE)
    half_width = 0.5 * (HIGH_EDGE - LOW_EDGE)
    half_ratio = spectrum_mid / half_width
    rho_old = 1.0 / half_ratio
    first_coef = []
    second_coef = []
    for sweep in range(1, sweep_count):
        rho_new = 1.0 / (2.0 * half_ratio - rho_old)
        first_coef.append(rho_new * rho_old)
        second_coef.append(2.0 * rho_new / half_width)
        rho_old = rho_new
    return (spectrum_mid, first_coef, second_coef)


def face_halos(block, axis, dim):
    top = lax.index_in_dim(block, block.shape[dim] - 1, axis=dim, keepdims=False)
    bottom = lax.index_in_dim(block, 0, axis=dim, keepdims=False)
    return exchange(top, bottom, axis)


def shifted(block, low, high, dim):
    n = block.shape[dim]
    low = jnp.expand_dims(low, dim)
    high = jnp.expand_dims(high, dim)
    minus = jnp.concatenate([low, lax.slice_in_dim(block, 0, n - 1, axis=dim)], axis=dim)
    plus = jnp.concatenate([lax.slice_in_dim(block, 1, n, axis=dim), high], axis=dim)
    return minus, plus


def membrane(voltage, gate_state, cell_type, gate_half, gate_slope, gate_tau, conduct, reversal):
    gate_count = gate_half.shape[0]
    lead_shape = (-1,) + (1,) * voltage.ndim
    gate_sign = jnp.where(jnp.arange(gate_count) % 2 == 0, 1.0, -1.0).astype(jnp.float32)
    exponent = (gate_sign / gate_slope).reshape(lead_shape) * (
        voltage[None] - gate_half.reshape(lead_shape)
    )
    steady = jax.nn.sigmoid(exponent)
    time_const = gate_tau.reshape(lead_shape) * (0.5 + steady)
    gate_state = steady + (gate_state - steady) * jnp.exp(-DT_HEART / time_const)
    weight = jnp.zeros(gate_state[0::2].shape, jnp.float32)
    for cell_kind in range(conduct.shape[0]):
        weight = weight + jnp.where(
            cell_type[None] == cell_kind, conduct[cell_kind].reshape(lead_shape), 0.0
        )
    ion_current = jnp.sum(
        weight
        * gate_state[0::2]
        * gate_state[1::2]
        * (voltage[None] - reversal.reshape(lead_shape)),
        axis=0,
    )
    return (gate_state, ion_current)


def heart_laplace(voltage):
    parts = []
    for axis, dim in (("gx", 0), ("gy", 1), ("gz", 2)):
        low, high = face_halos(voltage, axis, dim)
        minus, plus = shifted(voltage, low, high, dim)
        parts.append((plus, minus))
    total = parts[0][0] + parts[0][1]
    total = total + parts[1][0] + parts[1][1]
    total = total + parts[2][0] + parts[2][1]
    return total - 6.0 * voltage


def exchange(top, bottom, axis):
    count = lax.axis_size(axis)
    if count == 2:
        index = lax.axis_index(axis)
        got = lax.ppermute(jnp.where(index == 0, top, bottom), axis, [(0, 1), (1, 0)])
        zero = jnp.zeros_like(got)
        return jnp.where(index == 1, got, zero), jnp.where(index == 0, got, zero)
    forward = [(i, i + 1) for i in range(count - 1)]
    backward = [(i + 1, i) for i in range(count - 1)]
    return lax.ppermute(top, axis, forward), lax.ppermute(bottom, axis, backward)


def write_faces(x, value, xf_lo, xf_hi, yf_lo, yf_hi, zf_lo, zf_hi):
    nx = yf_lo.shape[1]
    ny, nz = value.shape

    @pl.when(x == 0)
    def _():
        xf_lo[0] = value

    @pl.when(x == nx - 1)
    def _():
        xf_hi[0] = value

    yf_lo[0, x] = value[0:1, :]
    yf_hi[0, x] = value[ny - 1:ny, :]
    flipped = value.T
    zf_lo[0, pl.ds(x, 1), :] = flipped[0:1, :]
    zf_hi[0, pl.ds(x, 1), :] = flipped[nz - 1:nz, :]


def sweep_kernel(first, second, d_ref, r_ref, p_ref, fxp, fxm, fyp, fym, fzp, fzm, dg_ref,
                 xlo, xhi, ylo, yhi, zedge, r_out, d_out, p_out, *face_out):
    nx, ny, nz = d_ref.shape[1], d_ref.shape[2], d_ref.shape[3]
    row = lax.broadcasted_iota(jnp.int32, (ny, nz), 0)
    lane = lax.broadcasted_iota(jnp.int32, (ny, nz), 1)

    def body(x, carry):
        centre = d_ref[0, x]
        below = d_ref[0, jnp.maximum(x - 1, 0)]
        above = d_ref[0, jnp.minimum(x + 1, nx - 1)]
        x_minus = jnp.where(x == 0, xlo[0], below)
        x_plus = jnp.where(x == nx - 1, xhi[0], above)
        y_minus = jnp.where(row == 0, ylo[0, x], pltpu.roll(centre, 1, 0))
        y_plus = jnp.where(row == ny - 1, yhi[0, x], pltpu.roll(centre, ny - 1, 0))
        edge = zedge[0, x]
        z_minus = jnp.where(lane == 0, edge, pltpu.roll(centre, 1, 1))
        z_plus = jnp.where(lane == nz - 1, edge, pltpu.roll(centre, nz - 1, 1))
        beside = fxp[x] * x_plus + fxm[x] * x_minus
        beside = beside + fyp[x] * y_plus + fym[x] * y_minus
        beside = beside + fzp[x] * z_plus + fzm[x] * z_minus
        diag = dg_ref[x]
        residual = r_ref[0, x] - (diag * centre - beside)
        step_dir = first * centre + second * (residual / diag)
        r_out[0, x] = residual
        d_out[0, x] = step_dir
        p_out[0, x] = p_ref[0, x] + step_dir
        write_faces(x, step_dir, *face_out)
        return carry

    lax.fori_loop(0, nx, body, 0)


def initial_kernel(mid, r_ref, dg_ref, d_out, *face_out):
    nx = r_ref.shape[1]

    def body(x, carry):
        step_dir = r_ref[0, x] / dg_ref[x] / mid
        d_out[0, x] = step_dir
        write_faces(x, step_dir, *face_out)
        return carry

    lax.fori_loop(0, nx, body, 0)


def specs(shape):
    steps, nx, ny, nz = shape
    full = pl.BlockSpec((1, nx, ny, nz), lambda s: (s, 0, 0, 0))
    fixed = pl.BlockSpec((nx, ny, nz), lambda s: (0, 0, 0))
    x_face = pl.BlockSpec((1, ny, nz), lambda s: (s, 0, 0))
    y_face = pl.BlockSpec((1, nx, 1, nz), lambda s: (s, 0, 0, 0))
    z_face = pl.BlockSpec((1, nx, ny), lambda s: (s, 0, 0))
    face_specs = [x_face, x_face, y_face, y_face, z_face, z_face]
    face_shapes = [
        jax.ShapeDtypeStruct((steps, ny, nz), jnp.float32),
        jax.ShapeDtypeStruct((steps, ny, nz), jnp.float32),
        jax.ShapeDtypeStruct((steps, nx, 1, nz), jnp.float32),
        jax.ShapeDtypeStruct((steps, nx, 1, nz), jnp.float32),
        jax.ShapeDtypeStruct((steps, nx, ny), jnp.float32),
        jax.ShapeDtypeStruct((steps, nx, ny), jnp.float32),
    ]
    return full, fixed, face_specs, face_shapes


def run_initial(mid, source, diagonal):
    full, fixed, face_specs, face_shapes = specs(source.shape)
    shape = jax.ShapeDtypeStruct(source.shape, jnp.float32)
    size = source.size
    outs = pl.pallas_call(
        functools.partial(initial_kernel, mid),
        grid=(source.shape[0],),
        in_specs=[full, fixed],
        out_specs=[full] + face_specs,
        out_shape=[shape] + face_shapes,
        cost_estimate=pl.CostEstimate(flops=2 * size, transcendentals=0, bytes_accessed=8 * size + 4 * size // source.shape[0]),
        name="chebyshev_start",
    )(source, diagonal)
    return outs[0], outs[1:]


def run_sweep(first, second, step_dir, residual, potential, faces, diagonal, halos):
    full, fixed, face_specs, face_shapes = specs(step_dir.shape)
    steps, nx, ny, nz = step_dir.shape
    x_face, y_face = face_specs[0], face_specs[2]
    shape = jax.ShapeDtypeStruct(step_dir.shape, jnp.float32)
    size = step_dir.size
    outs = pl.pallas_call(
        functools.partial(sweep_kernel, first, second),
        grid=(steps,),
        in_specs=[full, full, full] + [fixed] * 7 + [x_face, x_face, y_face, y_face, full],
        out_specs=[full, full, full] + face_specs,
        out_shape=[shape, shape, shape] + face_shapes,
        cost_estimate=pl.CostEstimate(flops=30 * size, transcendentals=0, bytes_accessed=4 * 7 * size + 4 * 7 * size // steps),
        name="chebyshev_sweep",
    )(step_dir, residual, potential, *faces, diagonal, *halos)
    return outs[0], outs[1], outs[2], outs[3:]


def local(
    heart_state,
    cell_type,
    gate_half,
    gate_slope,
    gate_tau,
    conduct,
    reversal,
    block_device,
    block_row,
    tissue,
    tissue_sigma,
):
    voltage = heart_state[0]
    gate_state = heart_state[1:]
    heart_x, heart_y, row_len = voltage.shape
    blocks = heart_x * heart_y
    devices = lax.axis_size("gx") * lax.axis_size("gy") * lax.axis_size("gz")
    capacity = 3 * blocks // devices
    slots = devices * capacity
    torso_x, torso_y, torso_z = tissue.shape
    torso_rows = torso_x * torso_y

    dest_dev = block_device.reshape(blocks)
    dest_row = block_row.reshape(blocks)
    one_hot = (dest_dev[:, None] == jnp.arange(devices, dtype=jnp.int32)[None, :]).astype(jnp.int32)
    running = jnp.cumsum(one_hot, axis=0) - 1
    slot_rank = jnp.sum(running * one_hot, axis=1)
    slot_index = dest_dev * capacity + slot_rank
    slot_match = slot_index[None, :] == jnp.arange(slots, dtype=jnp.int32)[:, None]
    slot_used = jnp.any(slot_match, axis=1)
    slot_block = jnp.argmax(slot_match, axis=1).astype(jnp.int32)
    send_rows = jnp.where(slot_used, dest_row[slot_block], torso_rows)
    recv_rows = lax.all_to_all(
        send_rows.reshape(devices, capacity), ("gx", "gy", "gz"), 0, 0, tiled=True
    ).reshape(slots)
    row_match = recv_rows[None, :] == jnp.arange(torso_rows, dtype=jnp.int32)[:, None]
    row_used = jnp.any(row_match, axis=1)
    row_slot = jnp.argmax(row_match, axis=1).astype(jnp.int32)

    currents = []
    for time_step in range(STEPS):
        gate_state, ion_current = membrane(
            voltage, gate_state, cell_type, gate_half, gate_slope, gate_tau, conduct, reversal
        )
        current = SIGMA_HEART * heart_laplace(voltage)
        currents.append(current)
        voltage = voltage + DT_HEART * (current - ion_current)
    heart_next = jnp.concatenate([voltage[None], gate_state], axis=0)

    payload = jnp.stack([item.reshape(blocks, row_len) for item in currents], axis=0)
    send_values = jnp.where(slot_used[None, :, None], jnp.take(payload, slot_block, axis=1), 0.0)
    received = lax.all_to_all(
        send_values.reshape(STEPS, devices, capacity, row_len),
        ("gx", "gy", "gz"),
        1,
        1,
        tiled=True,
    ).reshape(STEPS, slots, row_len)
    source = jnp.where(row_used[None, :, None], jnp.take(received, row_slot, axis=1), 0.0)
    source = source.reshape(STEPS, torso_x, torso_y, torso_z)

    sigma = []
    for dim_index in range(3):
        value = jnp.zeros(tissue.shape, jnp.float32)
        for tissue_kind in range(tissue_sigma.shape[0]):
            value = value + jnp.where(tissue == tissue_kind, tissue_sigma[tissue_kind, dim_index], 0.0)
        sigma.append(value)
    faces = []
    for dim_index, axis in enumerate(("gx", "gy", "gz")):
        low, high = face_halos(sigma[dim_index], axis, dim_index)
        minus, plus = shifted(sigma[dim_index], low, high, dim_index)
        faces.append(0.5 * (sigma[dim_index] + plus))
        faces.append(0.5 * (sigma[dim_index] + minus))
    diagonal = SCREEN + faces[0] + faces[1] + faces[2] + faces[3] + faces[4] + faces[5]

    spectrum_mid, first_coef, second_coef = chebyshev_weights(SWEEPS)
    residual = source
    step_dir, dir_faces = run_initial(spectrum_mid, residual, diagonal)
    potential = step_dir
    lane = lax.broadcasted_iota(jnp.int32, step_dir.shape, 3)
    for sweep in range(1, SWEEPS):
        x_low, x_high = exchange(dir_faces[1], dir_faces[0], "gx")
        y_low, y_high = exchange(dir_faces[3], dir_faces[2], "gy")
        z_low, z_high = exchange(dir_faces[5], dir_faces[4], "gz")
        zedge = jnp.where(lane == 0, z_low[..., None], jnp.where(lane == torso_z - 1, z_high[..., None], 0.0))
        halos = (x_low, x_high, y_low, y_high, zedge)
        residual, step_dir, potential, dir_faces = run_sweep(
            first_coef[sweep - 1], second_coef[sweep - 1], step_dir, residual, potential, faces, diagonal, halos
        )
    return (heart_next, jnp.transpose(potential, (1, 2, 0, 3)))


def solution(mesh):
    in_specs = (
        P(None, "gx", "gy", "gz"),
        P("gx", "gy", "gz"),
        P(),
        P(),
        P(),
        P(),
        P(),
        P("gx", "gy", "gz"),
        P("gx", "gy", "gz"),
        P("gx", "gy", "gz"),
        P(),
    )
    out_specs = (P(None, "gx", "gy", "gz"), P("gx", "gy", None, "gz"))
    return jax.shard_map(local, mesh=mesh, in_specs=in_specs, out_specs=out_specs, check_vma=False)
```

profile of v0, /device:TPU:0, one launch (start us, length us, event | category | flops | bytes accessed | tf_op | source)
XLA Modules:
  0.0 392.5 jit_solution(15259323434130598180)
XLA Ops:
  0.6 1.8 fusion.120
  2.4 4.5 %select_add_fusion.3 = (f32[32,64,128]{2,1,0:T(8,128)S(1)}, pred[32,64,128]{2,1,0:T(8,128)(4,1)S(1)}, pred[32,64,128]{2,1,0:T(8,128)(4,1)S(1)}, pred[32,64,128]{2,1,0:T(8,128)(4,1)S(1)}, pred[32,64,128]{2,1,0:T(8,128)(4,1)S(1)}) fusion(f32[]{:T(128)} %bitcast.137, f32[]{:T(128)} %bitcast.136, f32[]{:T(128)} %bitcast.135, f32[]{:T(128)} %bitcast.134, ...), kind=kLoop, calls=%fused_computation.38 | loop fusion | flops 2883584 | bytes 3145744 | tf_op jit(solution)/shard_map/add | solution.py:281
  7.0 5.9 %select_add_fusion.1 = (f32[32,64,128]{2,1,0:T(8,128)S(1)}, f32[32,64,128]{2,1,0:T(8,128)S(1)}) fusion(pred[32,64,128]{2,1,0:T(8,128)(4,1)S(1)} %get-tuple-element.115, pred[32,64,128]{2,1,0:T(8,128)(4,1)S(1)} %get-tuple-element.114, pred[32,64,128]{2,1,0:T(8,128)(4,1)S(1)} %get-tuple-element.113, pred[32,64,128]{2,1,0:T(8,128)(4,1)S(1)} %get-tuple-element.112, ...), kind=kLoop, calls=%fused_computation.36 | loop fusion | flops 3670016 | bytes 3145760 | tf_op jit(solution)/shard_map/add | solution.py:281
  16.0 1.6 fusion.100
  17.9 5.6 %collective-permute-start.3 = (f32[8,128]{1,0:T(8,128)S(1)}, f32[8,128]{1,0:T(8,128)S(1)}, u32[]{:S(2)}, u32[]{:S(2)}) collective-permute-start(f32[8,128]{1,0:T(8,128)S(1)} %bitcast.364), channel_id=1, source_target_pairs={{0,2},{2,4},{4,6},{1,3},{3,5},{5,7},{8,10},{10,12},{12,14},{9,11},... | collective-permute-start | bytes 12296 | tf_op jit(solution)/shard_map/ppermute | solution.py:96
  28.7 5.0 %gather_fusion = s32[768]{0:T(1024)S(1)} fusion(s32[256]{0:T(256)S(1)} %reshape.1762, s32[1024]{0:T(1024)S(1)} %pad_clamp_fusion), kind=kCustom, calls=%fused_computation | custom fusion | bytes 9216 | tf_op jit(solution)/shard_map/gather | solution.py:247
  34.4 7.7 %all-to-all-start = ((s32[32,1,24]{2,1,0:T(1,128)}), s32[32,1,24]{2,1,0:T(1,128)S(1)}, u32[]{:S(2)}, u32[]{:S(2)}) async-start(s32[32,1,24]{2,1,0:T(1,128)} %bitcast.106), calls=%async_computation | async-start | bytes 32768 | tf_op jit(solution)/shard_map/all_to_all | solution.py:248
  42.0 1.7 fusion.101
  43.8 1.5 fusion.103
  45.2 1.5 fusion.104
  49.9 1.5 multiply_add_fusion.3
  56.8 2.6 iota_reduce_fusion
  62.1 4.7 %collective-permute-start.1 = (f32[32,128]{1,0:T(8,128)S(1)}, f32[32,128]{1,0:T(8,128)S(1)}, u32[]{:S(2)}, u32[]{:S(2)}) collective-permute-start(f32[32,128]{1,0:T(8,128)S(1)} %get-tuple-element.133), channel_id=1, source_target_pairs={{0,8},{8,16},{16,24},{1,9},{9,17},{17,25},{2,10},{10,18},{18,26},{... | collective-permute-start | bytes 49160 | tf_op jit(solution)/shard_map/ppermute | solution.py:96
  68.2 1.4 copy.2291
  73.9 2.8 multiply_add_fusion.2
  78.6 5.2 %collective-permute-start.6 = (f32[32,128]{1,0:T(8,128)S(1)}, f32[32,128]{1,0:T(8,128)S(1)}, u32[]{:S(2)}, u32[]{:S(2)}) collective-permute-start(f32[32,128]{1,0:T(8,128)S(1)} %get-tuple-element.193), channel_id=1, source_target_pairs={{0,8},{8,16},{16,24},{1,9},{9,17},{17,25},{2,10},{10,18},{18,26},{... | collective-permute-start | bytes 49160 | tf_op jit(solution)/shard_map/ppermute | solution.py:96
  85.2 4.5 %collective-permute-start.8 = (f32[8,128]{1,0:T(8,128)S(1)}, f32[8,128]{1,0:T(8,128)S(1)}, u32[]{:S(2)}, u32[]{:S(2)}) collective-permute-start(f32[8,128]{1,0:T(8,128)S(1)} %bitcast.365), channel_id=1, source_target_pairs={{0,2},{2,4},{4,6},{1,3},{3,5},{5,7},{8,10},{10,12},{12,14},{9,11},... | collective-permute-start | bytes 12296 | tf_op jit(solution)/shard_map/ppermute | solution.py:96
  98.6 4.2 %multiply_add_fusion.1 = f32[18,8,32,128]{3,2,1,0:T(8,128)S(1)} fusion(f32[8,32,128]{2,1,0:T(8,128)S(1)} %bitcast.305, f32[18]{0:T(128)S(1)} %copy-done.83, f32[18]{0:T(128)S(1)} %copy-done.86, f32[18]{0:T(128)S(1)} %copy-done.89, f32[8,32,128]{2,1,0:T(8,128)S(1)} %bitcast.297, f32[19,8,32,128]{3,2,1,0:T(8,128)S(1)} %copy-done.4, ...), kind=kLoop, calls=%fused_computation.12 | loop fusion | flops 19464192 | bytes 5112024 | tf_op jit(solution)/shard_map/add | solution.py:59
  103.4 4.8 %collective-permute-start.11 = (f32[32,128]{1,0:T(8,128)S(1)}, f32[32,128]{1,0:T(8,128)S(1)}, u32[]{:S(2)}, u32[]{:S(2)}) collective-permute-start(f32[32,128]{1,0:T(8,128)S(1)} %get-tuple-element.177), channel_id=1, source_target_pairs={{0,8},{8,16},{16,24},{1,9},{9,17},{17,25},{2,10},{10,18},{18,26},{... | collective-permute-start | bytes 49160 | tf_op jit(solution)/shard_map/ppermute | solution.py:96
  111.8 4.5 %collective-permute-start.13 = (f32[8,128]{1,0:T(8,128)S(1)}, f32[8,128]{1,0:T(8,128)S(1)}, u32[]{:S(2)}, u32[]{:S(2)}) collective-permute-start(f32[8,128]{1,0:T(8,128)S(1)} %bitcast.368), channel_id=1, source_target_pairs={{0,2},{2,4},{4,6},{1,3},{3,5},{5,7},{8,10},{10,12},{12,14},{9,11},... | collective-permute-start | bytes 12296 | tf_op jit(solution)/shard_map/ppermute | solution.py:96
  122.8 5.2 %collective-permute-start.16 = (f32[32,128]{1,0:T(8,128)S(1)}, f32[32,128]{1,0:T(8,128)S(1)}, u32[]{:S(2)}, u32[]{:S(2)}) collective-permute-start(f32[32,128]{1,0:T(8,128)S(1)} %get-tuple-element.161), channel_id=1, source_target_pairs={{0,8},{8,16},{16,24},{1,9},{9,17},{17,25},{2,10},{10,18},{18,26},{... | collective-permute-start | bytes 49160 | tf_op jit(solution)/shard_map/ppermute | solution.py:96
  129.3 4.8 %collective-permute-start.18 = (f32[8,128]{1,0:T(8,128)S(1)}, f32[8,128]{1,0:T(8,128)S(1)}, u32[]{:S(2)}, u32[]{:S(2)}) collective-permute-start(f32[8,128]{1,0:T(8,128)S(1)} %bitcast.366), channel_id=1, source_target_pairs={{0,2},{2,4},{4,6},{1,3},{3,5},{5,7},{8,10},{10,12},{12,14},{9,11},... | collective-permute-start | bytes 12296 | tf_op jit(solution)/shard_map/ppermute | solution.py:96
  134.5 4.5 %collective-permute-start.23 = (f32[32,128]{1,0:T(8,128)}, f32[32,128]{1,0:T(8,128)}, u32[]{:S(2)}, u32[]{:S(2)}) collective-permute-start(f32[32,128]{1,0:T(8,128)} %bitcast.148), channel_id=1, source_target_pairs={{0,2},{2,4},{4,6},{1,3},{3,5},{5,7},{8,10},{10,12},{12,14},{9,11},... | collective-permute-start | bytes 49160 | tf_op jit(solution)/shard_map/ppermute | solution.py:96
  140.3 6.1 %collective-permute-start.21 = (f32[64,128]{1,0:T(8,128)}, f32[64,128]{1,0:T(8,128)}, u32[]{:S(2)}, u32[]{:S(2)}) collective-permute-start(f32[64,128]{1,0:T(8,128)} %get-tuple-element.143), channel_id=1, source_target_pairs={{0,8},{8,16},{16,24},{1,9},{9,17},{17,25},{2,10},{10,18},{18,26},{... | collective-permute-start | bytes 98312 | tf_op jit(solution)/shard_map/ppermute | solution.py:96
  148.6 3.0 gather_fusion.1
  151.5 4.9 %select_select_fusion.4 = f32[4,32,24,128]{3,0,2,1:T(4,128)} fusion(f32[4,32,24,128]{3,0,2,1:T(4,128)S(1)} %bitcast.290, pred[32,24]{1,0:T(8,128)(4,1)} %broadcast_in_dim.436, pred[32,24]{1,0:T(8,128)(4,1)} %broadcast_in_dim.434), kind=kLoop, calls=%fused_computation.15 | loop fusion | flops 786432 | bytes 3147264 | tf_op jit(solution)/shard_map/jit(_where)/select_n | solution.py:266
  156.4 3.4 all-to-all-start.1
  159.9 8.9 %add_add_fusion = (f32[32,64,128]{2,1,0:T(8,128)}, f32[32,64,128]{2,1,0:T(8,128)}, f32[32,64,128]{2,1,0:T(8,128)}, f32[32,64,128]{2,1,0:T(8,128)}, f32[32,64,128...) fusion(f32[32,64,128]{2,1,0:T(8,128)} %copy-done.1, f32[1,64,128]{2,1,0:T(8,128)} %bitcast.139, ...), kind=kLoop, calls=%fused_computation.35 | loop fusion | flops 6291456 | bytes 16777216 | tf_op jit(solution)/shard_map/add | solution.py:289
  171.1 7.5 %multiply_add_fusion = f32[18,8,32,128]{3,2,1,0:T(8,128)} fusion(f32[8,32,128]{2,1,0:T(8,128)S(1)} %bitcast.308, f32[18]{0:T(128)} %param.15, f32[18]{0:T(128)} %param.13, f32[18]{0:T(128)} %copy-done.87, f32[8,32,128]{2,1,0:T(8,128)S(1)} %bitcast.307, f32[8,32,128]{2,1,0:T(8,128)S(1)} %bitcast.298, f32[19,8,32,128]{3,2,1,0:T(8,128)} %param.11, ...), kind=kLoop, calls=%fused_computation.11 | loop fusion | flops 25952256 | bytes 5243096 | tf_op jit(solution)/shard_map/add | solution.py:59
  178.6 19.9 %all-to-all-done.1 = f32[4,32,24,128]{3,0,2,1:T(4,128)S(1)} async-done(((f32[4,32,24,128]{3,0,2,1:T(4,128)}), f32[4,32,24,128]{3,0,2,1:T(4,128)S(1)}, u32[]{:S(2)}, u32[]{:S(2)}) %all-to-all-start.1) | async-done | bytes 1572896 | tf_op jit(solution)/shard_map/all_to_all | solution.py:267
  198.5 15.2 %gather_fusion.2 = f32[2048,4,128]{2,1,0:T(4,128)} fusion(f32[4,768,128]{2,0,1:T(4,128)S(1)} %bitcast.287, s32[2048]{0:T(1024)S(1)} %copy-done.56), kind=kCustom, calls=%fused_computation.2 | custom fusion | bytes 8396800 | tf_op jit(solution)/shard_map/jit(_take)/gather | solution.py:274
  213.8 2.5 copy.2287
  216.3 2.8 select_select_fusion.3.r_ref
  219.1 17.1 %chebyshev_start.1 = (f32[4,32,64,128]{3,2,1,0:T(8,128)}, f32[4,64,128]{2,1,0:T(8,128)}, f32[4,64,128]{2,1,0:T(8,128)}, f32[4,32,1,128]{3,2,1,0:T(1,128)}, f32[4...) custom-call(f32[4,32,64,128]{3,2,1,0:T(8,128)} %select_select_fusion.3.r_ref, ...), custom_call_target="tpu_custom_call" | custom-call | flops 2097152 | bytes 9437184 | tf_op jit(solution)/shard_map/chebyshev_start/pallas_call | solution.py:185
  238.0 2.7 collective-permute-start.25
  244.7 3.8 select_select_fusion.2.zedge
  250.4 32.0 %chebyshev_sweep.3 = (f32[4,32,64,128]{3,2,1,0:T(8,128)}, f32[4,32,64,128]{3,2,1,0:T(8,128)}, f32[4,32,64,128]{3,2,1,0:T(8,128)}, f32[4,64,128]{2,1,0:T(8,128)},...) custom-call(f32[4,32,64,128]{3,2,1,0:T(8,128)} %get-tuple-element.32, ...), custom_call_target="tpu_custom_call" | custom-call | flops 31457280 | bytes 36700160 | tf_op jit(solution)/shard_map/chebyshev_sweep/pallas_call | solution.py:203
  284.6 4.6 %collective-permute-start.30 = (f32[4,64,128]{2,1,0:T(8,128)}, f32[4,64,128]{2,1,0:T(8,128)S(1)}, u32[]{:S(2)}, u32[]{:S(2)}) collective-permute-start(f32[4,64,128]{2,1,0:T(8,128)} %get-tuple-element.42), channel_id=1, source_target_pairs={{0,8},{8,16},{16,24},{1,9},{9,17},{17,25},{2,10},{10,18},{18,26},{... | collective-permute-start | bytes 393224 | tf_op jit(solution)/shard_map/ppermute | solution.py:96
  290.5 3.4 collective-permute-start.32
  295.2 4.5 %select_select_fusion.1.zedge = f32[4,32,64,128]{3,2,1,0:T(8,128)} fusion(f32[4,32,64]{2,1,0:T(8,128)S(1)} %get-tuple-element.211, f32[4,32,64]{2,1,0:T(8,128)S(1)} %get-tuple-element.210, pred[128]{0:T(512)(128)(4,1)} %get-tuple-element.239, pred[128]{0:T(512)(128)(4,1)} %get-tuple-element.240), kind=kLoop, calls=%fused_computation.7 | loop fusion | flops 2097152 | bytes 4260096 | tf_op jit(solution)/shard_map/jit(_where)/select_n | solution.py:300
  300.9 32.0 %chebyshev_sweep.4 = (f32[4,32,64,128]{3,2,1,0:T(8,128)}, f32[4,32,64,128]{3,2,1,0:T(8,128)}, f32[4,32,64,128]{3,2,1,0:T(8,128)}, f32[4,64,128]{2,1,0:T(8,128)},...) custom-call(f32[4,32,64,128]{3,2,1,0:T(8,128)} %get-tuple-element.39, ...), custom_call_target="tpu_custom_call" | custom-call | flops 31457280 | bytes 36700160 | tf_op jit(solution)/shard_map/chebyshev_sweep/pallas_call | solution.py:203
  333.9 1.8 pad_maximum_fusion
  335.7 4.9 %collective-permute-start.35 = (f32[4,64,128]{2,1,0:T(8,128)S(1)}, f32[4,64,128]{2,1,0:T(8,128)S(1)}, u32[]{:S(2)}, u32[]{:S(2)}) collective-permute-start(f32[4,64,128]{2,1,0:T(8,128)S(1)} %copy-done.92), channel_id=1, source_target_pairs={{0,8},{8,16},{16,24},{1,9},{9,17},{17,25},{2,10},{10,18},{18,26},{... | collective-permute-start | bytes 393224 | tf_op jit(solution)/shard_map/ppermute | solution.py:96
  341.9 4.0 %collective-permute-start.37 = (f32[4,32,1,128]{3,2,1,0:T(1,128)S(1)}, f32[4,32,1,128]{3,2,1,0:T(1,128)S(1)}, u32[]{:S(2)}, u32[]{:S(2)}) collective-permute-start(f32[4,32,1,128]{3,2,1,0:T(1,128)S(1)} %copy-done.94), channel_id=1, source_target_pairs={{0,2},{2,4},{4,6},{1,3},{3,5},{5,7},{8,10},{10,12},{12,14},{9,11},... | collective-permute-start | bytes 196616 | tf_op jit(solution)/shard_map/ppermute | solution.py:96
  345.9 1.6 collective-permute-start.38
  347.5 3.8 select_select_fusion.zedge
  352.8 31.9 %chebyshev_sweep.5 = (f32[4,32,64,128]{3,2,1,0:T(8,128)}, f32[4,32,64,128]{3,2,1,0:T(8,128)}, f32[4,32,64,128]{3,2,1,0:T(8,128)}, f32[4,64,128]{2,1,0:T(8,128)},...) custom-call(f32[4,32,64,128]{3,2,1,0:T(8,128)} %get-tuple-element.48, ...), custom_call_target="tpu_custom_call" | custom-call | flops 31457280 | bytes 36700160 | tf_op jit(solution)/shard_map/chebyshev_sweep/pallas_call | solution.py:203
  384.7 7.8 %copy.2292 = f32[32,64,4,128]{3,2,1,0:T(4,128)} copy(f32[32,64,4,128]{3,1,0,2:T(8,128)} %bitcast.291) | data formatting | bytes 8388608
  (367 shorter events, 72.4 us)
Async XLA Ops:
  7.0 39.8 %copy-start.1 = (f32[32,64,128]{2,1,0:T(8,128)}, f32[32,64,128]{2,1,0:T(8,128)S(1)}, u32[]{:S(2)}) copy-start(f32[32,64,128]{2,1,0:T(8,128)S(1)} %get-tuple-element.111) | copy-start | bytes 3145732
  13.5 48.6 %collective-permute-start.24 = (f32[32,64]{1,0:T(8,128)S(1)}, f32[32,64]{1,0:T(8,128)S(1)}, u32[]{:S(2)}, u32[]{:S(2)}) collective-permute-start(f32[32,64]{1,0:T(8,128)S(1)} %fusion.1), channel_id=1, source_target_pairs={{0,1},{1,0},{2,3},{3,2},{4,5},{5,4},{6,7},{7,6},{8,9},{9,8},{10,11... | collective-permute-start | bytes 24584 | tf_op jit(solution)/shard_map/ppermute | solution.py:91
  14.7 145.2 %collective-permute-start.22 = (f32[32,128]{1,0:T(8,128)}, f32[32,128]{1,0:T(8,128)}, u32[]{:S(2)}, u32[]{:S(2)}) collective-permute-start(f32[32,128]{1,0:T(8,128)} %bitcast.146), channel_id=1, source_target_pairs={{2,0},{4,2},{6,4},{3,1},{5,3},{7,5},{10,8},{12,10},{14,12},{11,9},... | collective-permute-start | bytes 49160 | tf_op jit(solution)/shard_map/ppermute | solution.py:96
  17.7 36.2 %collective-permute-start.4 = (f32[8,32]{1,0:T(8,128)S(1)}, f32[8,32]{1,0:T(8,128)S(1)}, u32[]{:S(2)}, u32[]{:S(2)}) collective-permute-start(f32[8,32]{1,0:T(8,128)S(1)} %fusion.12), channel_id=1, source_target_pairs={{0,1},{1,0},{2,3},{3,2},{4,5},{5,4},{6,7},{7,6},{8,9},{9,8},{10,11... | collective-permute-start | bytes 3080 | tf_op jit(solution)/shard_map/ppermute | solution.py:91
  17.9 51.9 %collective-permute-start.3 = (f32[8,128]{1,0:T(8,128)S(1)}, f32[8,128]{1,0:T(8,128)S(1)}, u32[]{:S(2)}, u32[]{:S(2)}) collective-permute-start(f32[8,128]{1,0:T(8,128)S(1)} %bitcast.364), channel_id=1, source_target_pairs={{0,2},{2,4},{4,6},{1,3},{3,5},{5,7},{8,10},{10,12},{12,14},{9,11},... | collective-permute-start | bytes 12296 | tf_op jit(solution)/shard_map/ppermute | solution.py:96
  23.4 46.3 %collective-permute-start.2 = (f32[8,128]{1,0:T(8,128)S(1)}, f32[8,128]{1,0:T(8,128)S(1)}, u32[]{:S(2)}, u32[]{:S(2)}) collective-permute-start(f32[8,128]{1,0:T(8,128)S(1)} %bitcast.363), channel_id=1, source_target_pairs={{2,0},{4,2},{6,4},{3,1},{5,3},{7,5},{10,8},{12,10},{14,12},{11,9},... | collective-permute-start | bytes 12296 | tf_op jit(solution)/shard_map/ppermute | solution.py:96
  34.4 21.7 %all-to-all-start = ((s32[32,1,24]{2,1,0:T(1,128)}), s32[32,1,24]{2,1,0:T(1,128)S(1)}, u32[]{:S(2)}, u32[]{:S(2)}) async-start(s32[32,1,24]{2,1,0:T(1,128)} %bitcast.106), calls=%async_computation | async-start | bytes 32768 | tf_op jit(solution)/shard_map/all_to_all | solution.py:248
  49.8 52.9 %copy-start.8 = (pred[8,32,128]{2,1,0:T(8,128)(4,1)}, pred[8,32,128]{2,1,0:T(8,128)(4,1)S(1)}, u32[]{:S(2)}) copy-start(pred[8,32,128]{2,1,0:T(8,128)(4,1)S(1)} %get-tuple-element.203) | copy-start | bytes 98308
  49.8 52.9 %copy-start.10 = (pred[8,32,128]{2,1,0:T(8,128)(4,1)}, pred[8,32,128]{2,1,0:T(8,128)(4,1)S(1)}, u32[]{:S(2)}) copy-start(pred[8,32,128]{2,1,0:T(8,128)(4,1)S(1)} %get-tuple-element.204) | copy-start | bytes 98308
  49.8 52.9 %copy-start.12 = (pred[8,32,128]{2,1,0:T(8,128)(4,1)}, pred[8,32,128]{2,1,0:T(8,128)(4,1)S(1)}, u32[]{:S(2)}) copy-start(pred[8,32,128]{2,1,0:T(8,128)(4,1)S(1)} %get-tuple-element.205) | copy-start | bytes 98308
  49.9 52.9 %copy-start.64 = (f32[9]{0:T(128)}, f32[9]{0:T(128)S(1)}, u32[]{:S(2)}) copy-start(f32[9]{0:T(128)S(1)} %get-tuple-element.236) | copy-start | bytes 112
  49.9 52.9 %copy-start.66 = (f32[9]{0:T(128)}, f32[9]{0:T(128)S(1)}, u32[]{:S(2)}) copy-start(f32[9]{0:T(128)S(1)} %get-tuple-element.237) | copy-start | bytes 112
  53.9 15.8 %collective-permute-start = (f32[32,128]{1,0:T(8,128)S(1)}, f32[32,128]{1,0:T(8,128)S(1)}, u32[]{:S(2)}, u32[]{:S(2)}) collective-permute-start(f32[32,128]{1,0:T(8,128)S(1)} %get-tuple-element.134), channel_id=1, source_target_pairs={{8,0},{16,8},{24,16},{9,1},{17,9},{25,17},{10,2},{18,10},{26,18},{... | collective-permute-start | bytes 49160 | tf_op jit(solution)/shard_map/ppermute | solution.py:96
  62.1 7.7 %collective-permute-start.1 = (f32[32,128]{1,0:T(8,128)S(1)}, f32[32,128]{1,0:T(8,128)S(1)}, u32[]{:S(2)}, u32[]{:S(2)}) collective-permute-start(f32[32,128]{1,0:T(8,128)S(1)} %get-tuple-element.133), channel_id=1, source_target_pairs={{0,8},{8,16},{16,24},{1,9},{9,17},{17,25},{2,10},{10,18},{18,26},{... | collective-permute-start | bytes 49160 | tf_op jit(solution)/shard_map/ppermute | solution.py:96
  77.3 7.9 %collective-permute-start.9 = (f32[8,32]{1,0:T(8,128)S(1)}, f32[8,32]{1,0:T(8,128)S(1)}, u32[]{:S(2)}, u32[]{:S(2)}) collective-permute-start(f32[8,32]{1,0:T(8,128)S(1)} %fusion.11), channel_id=1, source_target_pairs={{0,1},{1,0},{2,3},{3,2},{4,5},{5,4},{6,7},{7,6},{8,9},{9,8},{10,11... | collective-permute-start | bytes 3080 | tf_op jit(solution)/shard_map/ppermute | solution.py:91
  77.3 15.8 %collective-permute-start.5 = (f32[32,128]{1,0:T(8,128)S(1)}, f32[32,128]{1,0:T(8,128)S(1)}, u32[]{:S(2)}, u32[]{:S(2)}) collective-permute-start(f32[32,128]{1,0:T(8,128)S(1)} %get-tuple-element.194), channel_id=1, source_target_pairs={{8,0},{16,8},{24,16},{9,1},{17,9},{25,17},{10,2},{18,10},{26,18},{... | collective-permute-start | bytes 49160 | tf_op jit(solution)/shard_map/ppermute | solution.py:96
  78.6 14.5 %collective-permute-start.6 = (f32[32,128]{1,0:T(8,128)S(1)}, f32[32,128]{1,0:T(8,128)S(1)}, u32[]{:S(2)}, u32[]{:S(2)}) collective-permute-start(f32[32,128]{1,0:T(8,128)S(1)} %get-tuple-element.193), channel_id=1, source_target_pairs={{0,8},{8,16},{16,24},{1,9},{9,17},{17,25},{2,10},{10,18},{18,26},{... | collective-permute-start | bytes 49160 | tf_op jit(solution)/shard_map/ppermute | solution.py:96
  83.9 9.3 %collective-permute-start.7 = (f32[8,128]{1,0:T(8,128)S(1)}, f32[8,128]{1,0:T(8,128)S(1)}, u32[]{:S(2)}, u32[]{:S(2)}) collective-permute-start(f32[8,128]{1,0:T(8,128)S(1)} %bitcast.367), channel_id=1, source_target_pairs={{2,0},{4,2},{6,4},{3,1},{5,3},{7,5},{10,8},{12,10},{14,12},{11,9},... | collective-permute-start | bytes 12296 | tf_op jit(solution)/shard_map/ppermute | solution.py:96
  85.2 8.0 %collective-permute-start.8 = (f32[8,128]{1,0:T(8,128)S(1)}, f32[8,128]{1,0:T(8,128)S(1)}, u32[]{:S(2)}, u32[]{:S(2)}) collective-permute-start(f32[8,128]{1,0:T(8,128)S(1)} %bitcast.365), channel_id=1, source_target_pairs={{0,2},{2,4},{4,6},{1,3},{3,5},{5,7},{8,10},{10,12},{12,14},{9,11},... | collective-permute-start | bytes 12296 | tf_op jit(solution)/shard_map/ppermute | solution.py:96
  103.3 8.4 %collective-permute-start.14 = (f32[8,32]{1,0:T(8,128)S(1)}, f32[8,32]{1,0:T(8,128)S(1)}, u32[]{:S(2)}, u32[]{:S(2)}) collective-permute-start(f32[8,32]{1,0:T(8,128)S(1)} %fusion.10), channel_id=1, source_target_pairs={{0,1},{1,0},{2,3},{3,2},{4,5},{5,4},{6,7},{7,6},{8,9},{9,8},{10,11... | collective-permute-start | bytes 3080 | tf_op jit(solution)/shard_map/ppermute | solution.py:91
  103.4 14.2 %collective-permute-start.11 = (f32[32,128]{1,0:T(8,128)S(1)}, f32[32,128]{1,0:T(8,128)S(1)}, u32[]{:S(2)}, u32[]{:S(2)}) collective-permute-start(f32[32,128]{1,0:T(8,128)S(1)} %get-tuple-element.177), channel_id=1, source_target_pairs={{0,8},{8,16},{16,24},{1,9},{9,17},{17,25},{2,10},{10,18},{18,26},{... | collective-permute-start | bytes 49160 | tf_op jit(solution)/shard_map/ppermute | solution.py:96
  109.2 8.5 %collective-permute-start.10 = (f32[32,128]{1,0:T(8,128)S(1)}, f32[32,128]{1,0:T(8,128)S(1)}, u32[]{:S(2)}, u32[]{:S(2)}) collective-permute-start(f32[32,128]{1,0:T(8,128)S(1)} %get-tuple-element.178), channel_id=1, source_target_pairs={{8,0},{16,8},{24,16},{9,1},{17,9},{25,17},{10,2},{18,10},{26,18},{... | collective-permute-start | bytes 49160 | tf_op jit(solution)/shard_map/ppermute | solution.py:96
  110.5 6.4 %collective-permute-start.12 = (f32[8,128]{1,0:T(8,128)S(1)}, f32[8,128]{1,0:T(8,128)S(1)}, u32[]{:S(2)}, u32[]{:S(2)}) collective-permute-start(f32[8,128]{1,0:T(8,128)S(1)} %bitcast.370), channel_id=1, source_target_pairs={{2,0},{4,2},{6,4},{3,1},{5,3},{7,5},{10,8},{12,10},{14,12},{11,9},... | collective-permute-start | bytes 12296 | tf_op jit(solution)/shard_map/ppermute | solution.py:96
  111.8 5.9 %collective-permute-start.13 = (f32[8,128]{1,0:T(8,128)S(1)}, f32[8,128]{1,0:T(8,128)S(1)}, u32[]{:S(2)}, u32[]{:S(2)}) collective-permute-start(f32[8,128]{1,0:T(8,128)S(1)} %bitcast.368), channel_id=1, source_target_pairs={{0,2},{2,4},{4,6},{1,3},{3,5},{5,7},{8,10},{10,12},{12,14},{9,11},... | collective-permute-start | bytes 12296 | tf_op jit(solution)/shard_map/ppermute | solution.py:96
  121.4 7.9 %collective-permute-start.19 = (f32[8,32]{1,0:T(8,128)S(1)}, f32[8,32]{1,0:T(8,128)S(1)}, u32[]{:S(2)}, u32[]{:S(2)}) collective-permute-start(f32[8,32]{1,0:T(8,128)S(1)} %fusion.9), channel_id=1, source_target_pairs={{0,1},{1,0},{2,3},{3,2},{4,5},{5,4},{6,7},{7,6},{8,9},{9,8},{10,11... | collective-permute-start | bytes 3080 | tf_op jit(solution)/shard_map/ppermute | solution.py:91
  121.5 18.8 %collective-permute-start.15 = (f32[32,128]{1,0:T(8,128)S(1)}, f32[32,128]{1,0:T(8,128)S(1)}, u32[]{:S(2)}, u32[]{:S(2)}) collective-permute-start(f32[32,128]{1,0:T(8,128)S(1)} %get-tuple-element.162), channel_id=1, source_target_pairs={{8,0},{16,8},{24,16},{9,1},{17,9},{25,17},{10,2},{18,10},{26,18},{... | collective-permute-start | bytes 49160 | tf_op jit(solution)/shard_map/ppermute | solution.py:96
  122.8 23.5 %collective-permute-start.16 = (f32[32,128]{1,0:T(8,128)S(1)}, f32[32,128]{1,0:T(8,128)S(1)}, u32[]{:S(2)}, u32[]{:S(2)}) collective-permute-start(f32[32,128]{1,0:T(8,128)S(1)} %get-tuple-element.161), channel_id=1, source_target_pairs={{0,8},{8,16},{16,24},{1,9},{9,17},{17,25},{2,10},{10,18},{18,26},{... | collective-permute-start | bytes 49160 | tf_op jit(solution)/shard_map/ppermute | solution.py:96
  128.0 6.4 %collective-permute-start.17 = (f32[8,128]{1,0:T(8,128)S(1)}, f32[8,128]{1,0:T(8,128)S(1)}, u32[]{:S(2)}, u32[]{:S(2)}) collective-permute-start(f32[8,128]{1,0:T(8,128)S(1)} %bitcast.369), channel_id=1, source_target_pairs={{2,0},{4,2},{6,4},{3,1},{5,3},{7,5},{10,8},{12,10},{14,12},{11,9},... | collective-permute-start | bytes 12296 | tf_op jit(solution)/shard_map/ppermute | solution.py:96
  129.3 9.7 %collective-permute-start.18 = (f32[8,128]{1,0:T(8,128)S(1)}, f32[8,128]{1,0:T(8,128)S(1)}, u32[]{:S(2)}, u32[]{:S(2)}) collective-permute-start(f32[8,128]{1,0:T(8,128)S(1)} %bitcast.366), channel_id=1, source_target_pairs={{0,2},{2,4},{4,6},{1,3},{3,5},{5,7},{8,10},{10,12},{12,14},{9,11},... | collective-permute-start | bytes 12296 | tf_op jit(solution)/shard_map/ppermute | solution.py:96
  134.5 25.4 %collective-permute-start.23 = (f32[32,128]{1,0:T(8,128)}, f32[32,128]{1,0:T(8,128)}, u32[]{:S(2)}, u32[]{:S(2)}) collective-permute-start(f32[32,128]{1,0:T(8,128)} %bitcast.148), channel_id=1, source_target_pairs={{0,2},{2,4},{4,6},{1,3},{3,5},{5,7},{8,10},{10,12},{12,14},{9,11},... | collective-permute-start | bytes 49160 | tf_op jit(solution)/shard_map/ppermute | solution.py:96
  139.0 20.9 %collective-permute-start.20 = (f32[64,128]{1,0:T(8,128)}, f32[64,128]{1,0:T(8,128)}, u32[]{:S(2)}, u32[]{:S(2)}) collective-permute-start(f32[64,128]{1,0:T(8,128)} %get-tuple-element.144), channel_id=1, source_target_pairs={{8,0},{16,8},{24,16},{9,1},{17,9},{25,17},{10,2},{18,10},{26,18},{... | collective-permute-start | bytes 98312 | tf_op jit(solution)/shard_map/ppermute | solution.py:96
  140.3 19.6 %collective-permute-start.21 = (f32[64,128]{1,0:T(8,128)}, f32[64,128]{1,0:T(8,128)}, u32[]{:S(2)}, u32[]{:S(2)}) collective-permute-start(f32[64,128]{1,0:T(8,128)} %get-tuple-element.143), channel_id=1, source_target_pairs={{0,8},{8,16},{16,24},{1,9},{9,17},{17,25},{2,10},{10,18},{18,26},{... | collective-permute-start | bytes 98312 | tf_op jit(solution)/shard_map/ppermute | solution.py:96
  156.4 42.1 %all-to-all-start.1 = ((f32[4,32,24,128]{3,0,2,1:T(4,128)}), f32[4,32,24,128]{3,0,2,1:T(4,128)S(1)}, u32[]{:S(2)}, u32[]{:S(2)}) async-start(f32[4,32,24,128]{3,0,2,1:T(4,128)} %select_select_fusion.4), calls=%async_computation.1 | async-start | bytes 3145728 | tf_op jit(solution)/shard_map/all_to_all | solution.py:267
  237.1 7.5 %collective-permute-start.29 = (f32[4,32,64]{2,1,0:T(8,128)S(1)}, f32[4,32,64]{2,1,0:T(8,128)S(1)}, u32[]{:S(2)}, u32[]{:S(2)}) collective-permute-start(f32[4,32,64]{2,1,0:T(8,128)S(1)} %broadcast_select_fusion.8), channel_id=1, source_target_pairs={{0,1},{1,0},{2,3},{3,2},{4,5},{5,4},{6,7},{7,6},{8,9},{9,8},{10,11... | collective-permute-start | bytes 98312 | tf_op jit(solution)/shard_map/ppermute | solution.py:91
  238.0 11.7 %collective-permute-start.25 = (f32[4,64,128]{2,1,0:T(8,128)}, f32[4,64,128]{2,1,0:T(8,128)S(1)}, u32[]{:S(2)}, u32[]{:S(2)}) collective-permute-start(f32[4,64,128]{2,1,0:T(8,128)} %get-tuple-element.33), channel_id=1, source_target_pairs={{0,8},{8,16},{16,24},{1,9},{9,17},{17,25},{2,10},{10,18},{18,26},{... | collective-permute-start | bytes 393224 | tf_op jit(solution)/shard_map/ppermute | solution.py:96
  240.7 9.0 %collective-permute-start.26 = (f32[4,64,128]{2,1,0:T(8,128)}, f32[4,64,128]{2,1,0:T(8,128)S(1)}, u32[]{:S(2)}, u32[]{:S(2)}) collective-permute-start(f32[4,64,128]{2,1,0:T(8,128)} %get-tuple-element.34), channel_id=1, source_target_pairs={{8,0},{16,8},{24,16},{9,1},{17,9},{25,17},{10,2},{18,10},{26,18},{... | collective-permute-start | bytes 393224 | tf_op jit(solution)/shard_map/ppermute | solution.py:96
  242.0 6.5 %collective-permute-start.27 = (f32[4,32,1,128]{3,2,1,0:T(1,128)}, f32[4,32,1,128]{3,2,1,0:T(1,128)S(1)}, u32[]{:S(2)}, u32[]{:S(2)}) collective-permute-start(f32[4,32,1,128]{3,2,1,0:T(1,128)} %get-tuple-element.35), channel_id=1, source_target_pairs={{0,2},{2,4},{4,6},{1,3},{3,5},{5,7},{8,10},{10,12},{12,14},{9,11},... | collective-permute-start | bytes 196616 | tf_op jit(solution)/shard_map/ppermute | solution.py:96
  243.3 6.4 %collective-permute-start.28 = (f32[4,32,1,128]{3,2,1,0:T(1,128)}, f32[4,32,1,128]{3,2,1,0:T(1,128)S(1)}, u32[]{:S(2)}, u32[]{:S(2)}) collective-permute-start(f32[4,32,1,128]{3,2,1,0:T(1,128)} %get-tuple-element.36), channel_id=1, source_target_pairs={{2,0},{4,2},{6,4},{3,1},{5,3},{7,5},{10,8},{12,10},{14,12},{11,9},... | collective-permute-start | bytes 196616 | tf_op jit(solution)/shard_map/ppermute | solution.py:96
  283.4 11.8 %collective-permute-start.34 = (f32[4,32,64]{2,1,0:T(8,128)S(1)}, f32[4,32,64]{2,1,0:T(8,128)S(1)}, u32[]{:S(2)}, u32[]{:S(2)}) collective-permute-start(f32[4,32,64]{2,1,0:T(8,128)S(1)} %broadcast_select_fusion.7), channel_id=1, source_target_pairs={{0,1},{1,0},{2,3},{3,2},{4,5},{5,4},{6,7},{7,6},{8,9},{9,8},{10,11... | collective-permute-start | bytes 98312 | tf_op jit(solution)/shard_map/ppermute | solution.py:91
  284.6 15.6 %collective-permute-start.30 = (f32[4,64,128]{2,1,0:T(8,128)}, f32[4,64,128]{2,1,0:T(8,128)S(1)}, u32[]{:S(2)}, u32[]{:S(2)}) collective-permute-start(f32[4,64,128]{2,1,0:T(8,128)} %get-tuple-element.42), channel_id=1, source_target_pairs={{0,8},{8,16},{16,24},{1,9},{9,17},{17,25},{2,10},{10,18},{18,26},{... | collective-permute-start | bytes 393224 | tf_op jit(solution)/shard_map/ppermute | solution.py:96
  289.2 11.0 %collective-permute-start.31 = (f32[4,64,128]{2,1,0:T(8,128)}, f32[4,64,128]{2,1,0:T(8,128)S(1)}, u32[]{:S(2)}, u32[]{:S(2)}) collective-permute-start(f32[4,64,128]{2,1,0:T(8,128)} %get-tuple-element.43), channel_id=1, source_target_pairs={{8,0},{16,8},{24,16},{9,1},{17,9},{25,17},{10,2},{18,10},{26,18},{... | collective-permute-start | bytes 393224 | tf_op jit(solution)/shard_map/ppermute | solution.py:96
  290.5 9.2 %collective-permute-start.32 = (f32[4,32,1,128]{3,2,1,0:T(1,128)}, f32[4,32,1,128]{3,2,1,0:T(1,128)S(1)}, u32[]{:S(2)}, u32[]{:S(2)}) collective-permute-start(f32[4,32,1,128]{3,2,1,0:T(1,128)} %get-tuple-element.44), channel_id=1, source_target_pairs={{0,2},{2,4},{4,6},{1,3},{3,5},{5,7},{8,10},{10,12},{12,14},{9,11},... | collective-permute-start | bytes 196616 | tf_op jit(solution)/shard_map/ppermute | solution.py:96
  293.8 6.4 %collective-permute-start.33 = (f32[4,32,1,128]{3,2,1,0:T(1,128)}, f32[4,32,1,128]{3,2,1,0:T(1,128)S(1)}, u32[]{:S(2)}, u32[]{:S(2)}) collective-permute-start(f32[4,32,1,128]{3,2,1,0:T(1,128)} %get-tuple-element.45), channel_id=1, source_target_pairs={{2,0},{4,2},{6,4},{3,1},{5,3},{7,5},{10,8},{12,10},{14,12},{11,9},... | collective-permute-start | bytes 196616 | tf_op jit(solution)/shard_map/ppermute | solution.py:96
  333.8 13.6 %collective-permute-start.39 = (f32[4,32,64]{2,1,0:T(8,128)S(1)}, f32[4,32,64]{2,1,0:T(8,128)S(1)}, u32[]{:S(2)}, u32[]{:S(2)}) collective-permute-start(f32[4,32,64]{2,1,0:T(8,128)S(1)} %broadcast_select_fusion.6), channel_id=1, source_target_pairs={{0,1},{1,0},{2,3},{3,2},{4,5},{5,4},{6,7},{7,6},{8,9},{9,8},{10,11... | collective-permute-start | bytes 98312 | tf_op jit(solution)/shard_map/ppermute | solution.py:91
  335.7 16.4 %collective-permute-start.35 = (f32[4,64,128]{2,1,0:T(8,128)S(1)}, f32[4,64,128]{2,1,0:T(8,128)S(1)}, u32[]{:S(2)}, u32[]{:S(2)}) collective-permute-start(f32[4,64,128]{2,1,0:T(8,128)S(1)} %copy-done.92), channel_id=1, source_target_pairs={{0,8},{8,16},{16,24},{1,9},{9,17},{17,25},{2,10},{10,18},{18,26},{... | collective-permute-start | bytes 393224 | tf_op jit(solution)/shard_map/ppermute | solution.py:96
  340.6 11.5 %collective-permute-start.36 = (f32[4,64,128]{2,1,0:T(8,128)S(1)}, f32[4,64,128]{2,1,0:T(8,128)S(1)}, u32[]{:S(2)}, u32[]{:S(2)}) collective-permute-start(f32[4,64,128]{2,1,0:T(8,128)S(1)} %copy-done.91), channel_id=1, source_target_pairs={{8,0},{16,8},{24,16},{9,1},{17,9},{25,17},{10,2},{18,10},{26,18},{... | collective-permute-start | bytes 393224 | tf_op jit(solution)/shard_map/ppermute | solution.py:96
  341.9 9.4 %collective-permute-start.37 = (f32[4,32,1,128]{3,2,1,0:T(1,128)S(1)}, f32[4,32,1,128]{3,2,1,0:T(1,128)S(1)}, u32[]{:S(2)}, u32[]{:S(2)}) collective-permute-start(f32[4,32,1,128]{3,2,1,0:T(1,128)S(1)} %copy-done.94), channel_id=1, source_target_pairs={{0,2},{2,4},{4,6},{1,3},{3,5},{5,7},{8,10},{10,12},{12,14},{9,11},... | collective-permute-start | bytes 196616 | tf_op jit(solution)/shard_map/ppermute | solution.py:96
  345.9 6.2 %collective-permute-start.38 = (f32[4,32,1,128]{3,2,1,0:T(1,128)S(1)}, f32[4,32,1,128]{3,2,1,0:T(1,128)S(1)}, u32[]{:S(2)}, u32[]{:S(2)}) collective-permute-start(f32[4,32,1,128]{3,2,1,0:T(1,128)S(1)} %copy-done.93), channel_id=1, source_target_pairs={{2,0},{4,2},{6,4},{3,1},{5,3},{7,5},{10,8},{12,10},{14,12},{11,9},... | collective-permute-start | bytes 196616 | tf_op jit(solution)/shard_map/ppermute | solution.py:96
  (90 other events, 777.8 us)
where the time goes:
time: 397 us; the launch traced here: 393 us
  Pallas kernels  113 us (28%)
  starting transfers between devices  104 us (26%)
  other arithmetic  80.6 us (20%)
  local copies, waits for them, and re-layouts  69.1 us (17%)
  waiting for transfers between devices  23.3 us (6%)
    pallas_call x3, Pallas kernels, run_sweep(): pl.pallas_call(functools.partial(sweep_kernel, first, second), grid=(step...  95.9 us
    ppermute x16, starting transfers between devices, exchange(): lax.ppermute(top, axis, forward)  70.8 us
    ppermute x16, starting transfers between devices, exchange(): lax.ppermute(bottom, axis, backward)  20.9 us
    all_to_all x1, waiting for transfers between devices, local(): lax.all_to_all(send_values.reshape(STEPS, devices, capacity, row_len), ('...  19.9 us
    gather x2, local copies, waits for them, and re-layouts, local(): jnp.take(received, row_slot, axis=1)  17.7 us
    pallas_call x1, Pallas kernels, run_initial(): pl.pallas_call(functools.partial(initial_kernel, mid), grid=(source.shape...  17.1 us
    add x4, other arithmetic, membrane(): steady + (gate_state - steady) * jnp.exp(-DT_HEART / time_const)  16.1 us
    select_n x3, other arithmetic, local(): jnp.where(lane == 0, z_low[..., None], jnp.where(lane == torso_z - 1, z_h...  12 us
  transfers between devices with their start and end apart: 42, of which 5 were waited for; matrix products, arithmetic and copies ran while one was open for 26% of the time, Pallas kernels for 0%

commit v1 on v0

--- a/solution.py
+++ b/solution.py
@@ -96,9 +96,11 @@
     return lax.ppermute(top, axis, forward), lax.ppermute(bottom, axis, backward)
 
 
-def write_faces(x, value, xf_lo, xf_hi, yf_lo, yf_hi, zf_lo, zf_hi):
+def write_faces(x, value, columns, xf_lo, xf_hi, yf_lo, yf_hi, zf_lo, zf_hi):
     nx = yf_lo.shape[1]
     ny, nz = value.shape
+    half = nz // 2
+    lane = lax.broadcasted_iota(jnp.int32, (ny, nz), 1)
 
     @pl.when(x == 0)
     def _():
@@ -110,16 +112,28 @@
 
     yf_lo[0, x] = value[0:1, :]
     yf_hi[0, x] = value[ny - 1:ny, :]
-    flipped = value.T
-    zf_lo[0, pl.ds(x, 1), :] = flipped[0:1, :]
-    zf_hi[0, pl.ds(x, 1), :] = flipped[nz - 1:nz, :]
+    columns = jnp.where(lane == x, jnp.broadcast_to(value[:, 0:1], (ny, nz)), columns)
+    columns = jnp.where(lane == half + x, jnp.broadcast_to(value[:, nz - 1:nz], (ny, nz)), columns)
+    return columns
+
+
+def finish_faces(columns, xf_lo, xf_hi, yf_lo, yf_hi, zf_lo, zf_hi):
+    nx = yf_lo.shape[1]
+    half = columns.shape[1] // 2
+    flipped = columns.T
+    zf_lo[0] = flipped[0:nx, :]
+    zf_hi[0] = flipped[half:half + nx, :]
 
 
 def sweep_kernel(first, second, d_ref, r_ref, p_ref, fxp, fxm, fyp, fym, fzp, fzm, dg_ref,
-                 xlo, xhi, ylo, yhi, zedge, r_out, d_out, p_out, *face_out):
+                 xlo, xhi, ylo, yhi, zlo, zhi, r_out, d_out, p_out, *face_out):
     nx, ny, nz = d_ref.shape[1], d_ref.shape[2], d_ref.shape[3]
     row = lax.broadcasted_iota(jnp.int32, (ny, nz), 0)
     lane = lax.broadcasted_iota(jnp.int32, (ny, nz), 1)
+    blank = jnp.zeros((nz - nx, ny), jnp.float32)
+    low_cols = jnp.concatenate([zlo[0], blank], axis=0).T
+    high_rows = zhi[0]
+    high_cols = jnp.concatenate([high_rows[1:nx], blank, high_rows[0:1]], axis=0).T
 
     def body(x, carry):
         centre = d_ref[0, x]
@@ -129,9 +143,9 @@
         x_plus = jnp.where(x == nx - 1, xhi[0], above)
         y_minus = jnp.where(row == 0, ylo[0, x], pltpu.roll(centre, 1, 0))
         y_plus = jnp.where(row == ny - 1, yhi[0, x], pltpu.roll(centre, ny - 1, 0))
-        edge = zedge[0, x]
-        z_minus = jnp.where(lane == 0, edge, pltpu.roll(centre, 1, 1))
-        z_plus = jnp.where(lane == nz - 1, edge, pltpu.roll(centre, nz - 1, 1))
+        turn = lax.rem(nz - x, nz)
+        z_minus = jnp.where(lane == 0, pltpu.roll(low_cols, turn, 1), pltpu.roll(centre, 1, 1))
+        z_plus = jnp.where(lane == nz - 1, pltpu.roll(high_cols, turn, 1), pltpu.roll(centre, nz - 1, 1))
         beside = fxp[x] * x_plus + fxm[x] * x_minus
         beside = beside + fyp[x] * y_plus + fym[x] * y_minus
         beside = beside + fzp[x] * z_plus + fzm[x] * z_minus
@@ -141,22 +155,22 @@
         r_out[0, x] = residual
         d_out[0, x] = step_dir
         p_out[0, x] = p_ref[0, x] + step_dir
-        write_faces(x, step_dir, *face_out)
-        return carry
-
-    lax.fori_loop(0, nx, body, 0)
+        return write_faces(x, step_dir, carry, *face_out)
+
+    columns = lax.fori_loop(0, nx, body, jnp.zeros((ny, nz), jnp.float32))
+    finish_faces(columns, *face_out)
 
 
 def initial_kernel(mid, r_ref, dg_ref, d_out, *face_out):
-    nx = r_ref.shape[1]
+    nx, ny, nz = r_ref.shape[1], r_ref.shape[2], r_ref.shape[3]
 
     def body(x, carry):
         step_dir = r_ref[0, x] / dg_ref[x] / mid
         d_out[0, x] = step_dir
-        write_faces(x, step_dir, *face_out)
-        return carry
-
-    lax.fori_loop(0, nx, body, 0)
+        return write_faces(x, step_dir, carry, *face_out)
+
+    columns = lax.fori_loop(0, nx, body, jnp.zeros((ny, nz), jnp.float32))
+    finish_faces(columns, *face_out)
 
 
 def specs(shape):
@@ -203,7 +217,7 @@
     outs = pl.pallas_call(
         functools.partial(sweep_kernel, first, second),
         grid=(steps,),
-        in_specs=[full, full, full] + [fixed] * 7 + [x_face, x_face, y_face, y_face, full],
+        in_specs=[full, full, full] + [fixed] * 7 + [x_face, x_face, y_face, y_face, face_specs[4], face_specs[4]],
         out_specs=[full, full, full] + face_specs,
         out_shape=[shape, shape, shape] + face_shapes,
         cost_estimate=pl.CostEstimate(flops=30 * size, transcendentals=0, bytes_accessed=4 * 7 * size + 4 * 7 * size // steps),
@@ -292,13 +306,11 @@
     residual = source
     step_dir, dir_faces = run_initial(spectrum_mid, residual, diagonal)
     potential = step_dir
-    lane = lax.broadcasted_iota(jnp.int32, step_dir.shape, 3)
     for sweep in range(1, SWEEPS):
         x_low, x_high = exchange(dir_faces[1], dir_faces[0], "gx")
         y_low, y_high = exchange(dir_faces[3], dir_faces[2], "gy")
         z_low, z_high = exchange(dir_faces[5], dir_faces[4], "gz")
-        zedge = jnp.where(lane == 0, z_low[..., None], jnp.where(lane == torso_z - 1, z_high[..., None], 0.0))
-        halos = (x_low, x_high, y_low, y_high, zedge)
+        halos = (x_low, x_high, y_low, y_high, z_low, z_high)
         residual, step_dir, potential, dir_faces = run_sweep(
             first_coef[sweep - 1], second_coef[sweep - 1], step_dir, residual, potential, faces, diagonal, halos
         )

time: 397 us -> 395 us (level)
  waiting for transfers between devices: 23.3 us -> 34.4 us
  other arithmetic: 80.6 us -> 70.3 us
    select_n x3 -> x0, other arithmetic: 12 us -> none  [local(): jnp.where(lane == 0, z_low[..., None], jnp.where(lane == torso_z - 1, z_h...]
    ppermute x16, waiting for transfers between devices: 2.58 us -> 12.6 us  [exchange(): lax.ppermute(bottom, axis, backward)]
  transfers between devices with their start and end apart: 42 -> 42, of which waited for: 5 -> 7; matrix products, arithmetic and copies ran while one was open for 26% -> 23% of each run, Pallas kernels for 0% -> 0%
where the time goes in v1:
time: 395 us; the launch traced here: 391 us
  Pallas kernels  113 us (29%)
  starting transfers between devices  102 us (26%)
  other arithmetic  70.3 us (18%)
  local copies, waits for them, and re-layouts  68.3 us (17%)
  waiting for transfers between devices  34.4 us (9%)
    pallas_call x3, Pallas kernels, run_sweep(): pl.pallas_call(functools.partial(sweep_kernel, first, second), grid=(step...  97.6 us
    ppermute x16, starting transfers between devices, exchange(): lax.ppermute(top, axis, forward)  69.7 us
    ppermute x16, starting transfers between devices, exchange(): lax.ppermute(bottom, axis, backward)  20.6 us
    all_to_all x1, waiting for transfers between devices, local(): lax.all_to_all(send_values.reshape(STEPS, devices, capacity, row_len), ('...  20.6 us
    gather x2, local copies, waits for them, and re-layouts, local(): jnp.take(received, row_slot, axis=1)  17.7 us
    add x4, other arithmetic, membrane(): steady + (gate_state - steady) * jnp.exp(-DT_HEART / time_const)  16.1 us
    pallas_call x1, Pallas kernels, run_initial(): pl.pallas_call(functools.partial(initial_kernel, mid), grid=(source.shape...  15.6 us
    ppermute x16, waiting for transfers between devices, exchange(): lax.ppermute(bottom, axis, backward)  12.6 us
  transfers between devices with their start and end apart: 42, of which 7 were waited for; matrix products, arithmetic and copies ran while one was open for 23% of the time, Pallas kernels for 0%

profile of v1, /device:TPU:0, one launch (start us, length us, event | category | flops | bytes accessed | tf_op | source)
XLA Modules:
  0.0 391.2 jit_solution(1792591088026510749)
XLA Ops:
  0.6 1.8 fusion.120
  2.4 4.5 %select_add_fusion.3 = (f32[32,64,128]{2,1,0:T(8,128)S(1)}, pred[32,64,128]{2,1,0:T(8,128)(4,1)S(1)}, pred[32,64,128]{2,1,0:T(8,128)(4,1)S(1)}, pred[32,64,128]{2,1,0:T(8,128)(4,1)S(1)}, pred[32,64,128]{2,1,0:T(8,128)(4,1)S(1)}) fusion(f32[]{:T(128)} %bitcast.137, f32[]{:T(128)} %bitcast.136, f32[]{:T(128)} %bitcast.135, f32[]{:T(128)} %bitcast.134, ...), kind=kLoop, calls=%fused_computation.35 | loop fusion | flops 2883584 | bytes 3145744 | tf_op jit(solution)/shard_map/add | solution.py:295
  7.0 5.9 %select_add_fusion.1 = (f32[32,64,128]{2,1,0:T(8,128)S(1)}, f32[32,64,128]{2,1,0:T(8,128)S(1)}) fusion(pred[32,64,128]{2,1,0:T(8,128)(4,1)S(1)} %get-tuple-element.115, pred[32,64,128]{2,1,0:T(8,128)(4,1)S(1)} %get-tuple-element.114, pred[32,64,128]{2,1,0:T(8,128)(4,1)S(1)} %get-tuple-element.113, pred[32,64,128]{2,1,0:T(8,128)(4,1)S(1)} %get-tuple-element.112, ...), kind=kLoop, calls=%fused_computation.33 | loop fusion | flops 3670016 | bytes 3145760 | tf_op jit(solution)/shard_map/add | solution.py:295
  16.0 1.6 fusion.100
  17.9 5.6 %collective-permute-start.3 = (f32[8,128]{1,0:T(8,128)S(1)}, f32[8,128]{1,0:T(8,128)S(1)}, u32[]{:S(2)}, u32[]{:S(2)}) collective-permute-start(f32[8,128]{1,0:T(8,128)S(1)} %bitcast.364), channel_id=1, source_target_pairs={{0,2},{2,4},{4,6},{1,3},{3,5},{5,7},{8,10},{10,12},{12,14},{9,11},... | collective-permute-start | bytes 12296 | tf_op jit(solution)/shard_map/ppermute | solution.py:96
  28.9 5.0 %gather_fusion = s32[768]{0:T(1024)S(1)} fusion(s32[256]{0:T(256)S(1)} %reshape.1756, s32[1024]{0:T(1024)S(1)} %pad_clamp_fusion), kind=kCustom, calls=%fused_computation | custom fusion | bytes 9216 | tf_op jit(solution)/shard_map/gather | solution.py:261
  34.6 7.7 %all-to-all-start = ((s32[32,1,24]{2,1,0:T(1,128)}), s32[32,1,24]{2,1,0:T(1,128)S(1)}, u32[]{:S(2)}, u32[]{:S(2)}) async-start(s32[32,1,24]{2,1,0:T(1,128)} %bitcast.106), calls=%async_computation | async-start | bytes 32768 | tf_op jit(solution)/shard_map/all_to_all | solution.py:262
  42.2 1.7 fusion.101
  44.0 1.5 fusion.103
  45.5 1.5 fusion.104
  50.1 1.5 multiply_add_fusion.3
  56.4 2.6 iota_reduce_fusion
  61.7 4.7 %collective-permute-start.1 = (f32[32,128]{1,0:T(8,128)S(1)}, f32[32,128]{1,0:T(8,128)S(1)}, u32[]{:S(2)}, u32[]{:S(2)}) collective-permute-start(f32[32,128]{1,0:T(8,128)S(1)} %get-tuple-element.133), channel_id=1, source_target_pairs={{0,8},{8,16},{16,24},{1,9},{9,17},{17,25},{2,10},{10,18},{18,26},{... | collective-permute-start | bytes 49160 | tf_op jit(solution)/shard_map/ppermute | solution.py:96
  67.9 1.4 copy.2291
  73.4 2.8 multiply_add_fusion.2
  78.2 5.2 %collective-permute-start.6 = (f32[32,128]{1,0:T(8,128)S(1)}, f32[32,128]{1,0:T(8,128)S(1)}, u32[]{:S(2)}, u32[]{:S(2)}) collective-permute-start(f32[32,128]{1,0:T(8,128)S(1)} %get-tuple-element.193), channel_id=1, source_target_pairs={{0,8},{8,16},{16,24},{1,9},{9,17},{17,25},{2,10},{10,18},{18,26},{... | collective-permute-start | bytes 49160 | tf_op jit(solution)/shard_map/ppermute | solution.py:96
  84.7 4.5 %collective-permute-start.8 = (f32[8,128]{1,0:T(8,128)S(1)}, f32[8,128]{1,0:T(8,128)S(1)}, u32[]{:S(2)}, u32[]{:S(2)}) collective-permute-start(f32[8,128]{1,0:T(8,128)S(1)} %bitcast.365), channel_id=1, source_target_pairs={{0,2},{2,4},{4,6},{1,3},{3,5},{5,7},{8,10},{10,12},{12,14},{9,11},... | collective-permute-start | bytes 12296 | tf_op jit(solution)/shard_map/ppermute | solution.py:96
  96.5 1.4 fusion.35
  98.0 4.2 %multiply_add_fusion.1 = f32[18,8,32,128]{3,2,1,0:T(8,128)S(1)} fusion(f32[8,32,128]{2,1,0:T(8,128)S(1)} %bitcast.305, f32[18]{0:T(128)S(1)} %copy-done.81, f32[18]{0:T(128)S(1)} %copy-done.84, f32[18]{0:T(128)S(1)} %copy-done.87, f32[8,32,128]{2,1,0:T(8,128)S(1)} %bitcast.297, f32[19,8,32,128]{3,2,1,0:T(8,128)S(1)} %copy-done.4, ...), kind=kLoop, calls=%fused_computation.9 | loop fusion | flops 19464192 | bytes 5112024 | tf_op jit(solution)/shard_map/add | solution.py:59
  102.8 4.8 %collective-permute-start.11 = (f32[32,128]{1,0:T(8,128)S(1)}, f32[32,128]{1,0:T(8,128)S(1)}, u32[]{:S(2)}, u32[]{:S(2)}) collective-permute-start(f32[32,128]{1,0:T(8,128)S(1)} %get-tuple-element.177), channel_id=1, source_target_pairs={{0,8},{8,16},{16,24},{1,9},{9,17},{17,25},{2,10},{10,18},{18,26},{... | collective-permute-start | bytes 49160 | tf_op jit(solution)/shard_map/ppermute | solution.py:96
  111.2 4.5 %collective-permute-start.13 = (f32[8,128]{1,0:T(8,128)S(1)}, f32[8,128]{1,0:T(8,128)S(1)}, u32[]{:S(2)}, u32[]{:S(2)}) collective-permute-start(f32[8,128]{1,0:T(8,128)S(1)} %bitcast.368), channel_id=1, source_target_pairs={{0,2},{2,4},{4,6},{1,3},{3,5},{5,7},{8,10},{10,12},{12,14},{9,11},... | collective-permute-start | bytes 12296 | tf_op jit(solution)/shard_map/ppermute | solution.py:96
  122.2 5.2 %collective-permute-start.16 = (f32[32,128]{1,0:T(8,128)S(1)}, f32[32,128]{1,0:T(8,128)S(1)}, u32[]{:S(2)}, u32[]{:S(2)}) collective-permute-start(f32[32,128]{1,0:T(8,128)S(1)} %get-tuple-element.161), channel_id=1, source_target_pairs={{0,8},{8,16},{16,24},{1,9},{9,17},{17,25},{2,10},{10,18},{18,26},{... | collective-permute-start | bytes 49160 | tf_op jit(solution)/shard_map/ppermute | solution.py:96
  128.7 4.8 %collective-permute-start.18 = (f32[8,128]{1,0:T(8,128)S(1)}, f32[8,128]{1,0:T(8,128)S(1)}, u32[]{:S(2)}, u32[]{:S(2)}) collective-permute-start(f32[8,128]{1,0:T(8,128)S(1)} %bitcast.366), channel_id=1, source_target_pairs={{0,2},{2,4},{4,6},{1,3},{3,5},{5,7},{8,10},{10,12},{12,14},{9,11},... | collective-permute-start | bytes 12296 | tf_op jit(solution)/shard_map/ppermute | solution.py:96
  133.9 4.5 %collective-permute-start.23 = (f32[32,128]{1,0:T(8,128)}, f32[32,128]{1,0:T(8,128)}, u32[]{:S(2)}, u32[]{:S(2)}) collective-permute-start(f32[32,128]{1,0:T(8,128)} %bitcast.148), channel_id=1, source_target_pairs={{0,2},{2,4},{4,6},{1,3},{3,5},{5,7},{8,10},{10,12},{12,14},{9,11},... | collective-permute-start | bytes 49160 | tf_op jit(solution)/shard_map/ppermute | solution.py:96
  139.7 6.1 %collective-permute-start.21 = (f32[64,128]{1,0:T(8,128)}, f32[64,128]{1,0:T(8,128)}, u32[]{:S(2)}, u32[]{:S(2)}) collective-permute-start(f32[64,128]{1,0:T(8,128)} %get-tuple-element.143), channel_id=1, source_target_pairs={{0,8},{8,16},{16,24},{1,9},{9,17},{17,25},{2,10},{10,18},{18,26},{... | collective-permute-start | bytes 98312 | tf_op jit(solution)/shard_map/ppermute | solution.py:96
  148.0 3.0 gather_fusion.1
  150.9 4.9 %select_select_fusion.1 = f32[4,32,24,128]{3,0,2,1:T(4,128)} fusion(f32[4,32,24,128]{3,0,2,1:T(4,128)S(1)} %bitcast.290, pred[32,24]{1,0:T(8,128)(4,1)} %broadcast_in_dim.390, pred[32,24]{1,0:T(8,128)(4,1)} %broadcast_in_dim.388), kind=kLoop, calls=%fused_computation.12 | loop fusion | flops 786432 | bytes 3147264 | tf_op jit(solution)/shard_map/jit(_where)/select_n | solution.py:280
  155.9 3.4 all-to-all-start.1
  159.4 8.8 %add_add_fusion = (f32[32,64,128]{2,1,0:T(8,128)}, f32[32,64,128]{2,1,0:T(8,128)}, f32[32,64,128]{2,1,0:T(8,128)}, f32[32,64,128]{2,1,0:T(8,128)}, f32[32,64,128...) fusion(f32[32,64,128]{2,1,0:T(8,128)} %copy-done.1, f32[1,64,128]{2,1,0:T(8,128)} %bitcast.139, ...), kind=kLoop, calls=%fused_computation.32 | loop fusion | flops 6291456 | bytes 16777216 | tf_op jit(solution)/shard_map/add | solution.py:303
  169.9 7.5 %multiply_add_fusion = f32[18,8,32,128]{3,2,1,0:T(8,128)} fusion(f32[8,32,128]{2,1,0:T(8,128)S(1)} %bitcast.308, f32[18]{0:T(128)} %param.15, f32[18]{0:T(128)} %param.13, f32[18]{0:T(128)} %copy-done.85, f32[8,32,128]{2,1,0:T(8,128)S(1)} %bitcast.307, f32[8,32,128]{2,1,0:T(8,128)S(1)} %bitcast.298, f32[19,8,32,128]{3,2,1,0:T(8,128)} %param.11, ...), kind=kLoop, calls=%fused_computation.8 | loop fusion | flops 25952256 | bytes 5243096 | tf_op jit(solution)/shard_map/add | solution.py:59
  177.4 20.6 %all-to-all-done.1 = f32[4,32,24,128]{3,0,2,1:T(4,128)S(1)} async-done(((f32[4,32,24,128]{3,0,2,1:T(4,128)}), f32[4,32,24,128]{3,0,2,1:T(4,128)S(1)}, u32[]{:S(2)}, u32[]{:S(2)}) %all-to-all-start.1) | async-done | bytes 1572896 | tf_op jit(solution)/shard_map/all_to_all | solution.py:281
  198.0 15.2 %gather_fusion.2 = f32[2048,4,128]{2,1,0:T(4,128)} fusion(f32[4,768,128]{2,0,1:T(4,128)S(1)} %bitcast.287, s32[2048]{0:T(1024)S(1)} %copy-done.56), kind=kCustom, calls=%fused_computation.2 | custom fusion | bytes 8396800 | tf_op jit(solution)/shard_map/jit(_take)/gather | solution.py:288
  213.2 2.5 copy.2287
  215.7 2.8 select_select_fusion.r_ref
  218.5 15.6 %chebyshev_start.1 = (f32[4,32,64,128]{3,2,1,0:T(8,128)}, f32[4,64,128]{2,1,0:T(8,128)}, f32[4,64,128]{2,1,0:T(8,128)}, f32[4,32,1,128]{3,2,1,0:T(1,128)}, f32[4...) custom-call(f32[4,32,64,128]{3,2,1,0:T(8,128)} %select_select_fusion.r_ref, ...), custom_call_target="tpu_custom_call" | custom-call | flops 2097152 | bytes 9437184 | tf_op jit(solution)/shard_map/chebyshev_start/pallas_call | solution.py:199
  236.0 2.7 collective-permute-start.25
  243.5 4.2 %collective-permute-done.28.yhi = f32[4,32,1,128]{3,2,1,0:T(1,128)S(1)} collective-permute-done((f32[4,32,1,128]{3,2,1,0:T(1,128)}, f32[4,32,1,128]{3,2,1,0:T(1,128)S(1)}, u32[]{:S(2)}, u32[]{:S(2)}) %collective-permute-start.28) | collective-permute-done | bytes 65568 | tf_op jit(solution)/shard_map/ppermute | solution.py:96
  248.4 32.6 %chebyshev_sweep.3 = (f32[4,32,64,128]{3,2,1,0:T(8,128)}, f32[4,32,64,128]{3,2,1,0:T(8,128)}, f32[4,32,64,128]{3,2,1,0:T(8,128)}, f32[4,64,128]{2,1,0:T(8,128)},...) custom-call(f32[4,32,64,128]{3,2,1,0:T(8,128)} %get-tuple-element.32, ...), custom_call_target="tpu_custom_call" | custom-call | flops 31457280 | bytes 36700160 | tf_op jit(solution)/shard_map/chebyshev_sweep/pallas_call | solution.py:217
  283.2 4.6 %collective-permute-start.30 = (f32[4,64,128]{2,1,0:T(8,128)}, f32[4,64,128]{2,1,0:T(8,128)S(1)}, u32[]{:S(2)}, u32[]{:S(2)}) collective-permute-start(f32[4,64,128]{2,1,0:T(8,128)} %get-tuple-element.42), channel_id=1, source_target_pairs={{0,8},{8,16},{16,24},{1,9},{9,17},{17,25},{2,10},{10,18},{18,26},{... | collective-permute-start | bytes 393224 | tf_op jit(solution)/shard_map/ppermute | solution.py:96
  289.1 2.8 collective-permute-start.32
  294.1 4.2 %collective-permute-done.33.yhi = f32[4,32,1,128]{3,2,1,0:T(1,128)S(1)} collective-permute-done((f32[4,32,1,128]{3,2,1,0:T(1,128)}, f32[4,32,1,128]{3,2,1,0:T(1,128)S(1)}, u32[]{:S(2)}, u32[]{:S(2)}) %collective-permute-start.33) | collective-permute-done | bytes 65568 | tf_op jit(solution)/shard_map/ppermute | solution.py:96
  298.9 32.5 %chebyshev_sweep.4 = (f32[4,32,64,128]{3,2,1,0:T(8,128)}, f32[4,32,64,128]{3,2,1,0:T(8,128)}, f32[4,32,64,128]{3,2,1,0:T(8,128)}, f32[4,64,128]{2,1,0:T(8,128)},...) custom-call(f32[4,32,64,128]{3,2,1,0:T(8,128)} %get-tuple-element.39, ...), custom_call_target="tpu_custom_call" | custom-call | flops 31457280 | bytes 36700160 | tf_op jit(solution)/shard_map/chebyshev_sweep/pallas_call | solution.py:217
  332.5 1.8 pad_maximum_fusion
  334.2 4.9 %collective-permute-start.35 = (f32[4,64,128]{2,1,0:T(8,128)S(1)}, f32[4,64,128]{2,1,0:T(8,128)S(1)}, u32[]{:S(2)}, u32[]{:S(2)}) collective-permute-start(f32[4,64,128]{2,1,0:T(8,128)S(1)} %copy-done.90), channel_id=1, source_target_pairs={{0,8},{8,16},{16,24},{1,9},{9,17},{17,25},{2,10},{10,18},{18,26},{... | collective-permute-start | bytes 393224 | tf_op jit(solution)/shard_map/ppermute | solution.py:96
  340.5 3.5 collective-permute-start.37
  346.0 4.2 %collective-permute-done.38.yhi = f32[4,32,1,128]{3,2,1,0:T(1,128)S(1)} collective-permute-done((f32[4,32,1,128]{3,2,1,0:T(1,128)S(1)}, f32[4,32,1,128]{3,2,1,0:T(1,128)S(1)}, u32[]{:S(2)}, u32[]{:S(2)}) %collective-permute-start.38) | collective-permute-done | bytes 65568 | tf_op jit(solution)/shard_map/ppermute | solution.py:96
  350.9 32.5 %chebyshev_sweep.5 = (f32[4,32,64,128]{3,2,1,0:T(8,128)}, f32[4,32,64,128]{3,2,1,0:T(8,128)}, f32[4,32,64,128]{3,2,1,0:T(8,128)}, f32[4,64,128]{2,1,0:T(8,128)},...) custom-call(f32[4,32,64,128]{3,2,1,0:T(8,128)} %get-tuple-element.48, ...), custom_call_target="tpu_custom_call" | custom-call | flops 31457280 | bytes 36700160 | tf_op jit(solution)/shard_map/chebyshev_sweep/pallas_call | solution.py:217
  383.4 7.8 %copy.2292 = f32[32,64,4,128]{3,2,1,0:T(4,128)} copy(f32[32,64,4,128]{3,1,0,2:T(8,128)} %bitcast.291) | data formatting | bytes 8388608
  (363 shorter events, 71.0 us)
Async XLA Ops:
  7.0 40.0 %copy-start.1 = (f32[32,64,128]{2,1,0:T(8,128)}, f32[32,64,128]{2,1,0:T(8,128)S(1)}, u32[]{:S(2)}) copy-start(f32[32,64,128]{2,1,0:T(8,128)S(1)} %get-tuple-element.111) | copy-start | bytes 3145732
  13.5 48.2 %collective-permute-start.24 = (f32[32,64]{1,0:T(8,128)S(1)}, f32[32,64]{1,0:T(8,128)S(1)}, u32[]{:S(2)}, u32[]{:S(2)}) collective-permute-start(f32[32,64]{1,0:T(8,128)S(1)} %fusion.1), channel_id=1, source_target_pairs={{0,1},{1,0},{2,3},{3,2},{4,5},{5,4},{6,7},{7,6},{8,9},{9,8},{10,11... | collective-permute-start | bytes 24584 | tf_op jit(solution)/shard_map/ppermute | solution.py:91
  14.7 144.6 %collective-permute-start.22 = (f32[32,128]{1,0:T(8,128)}, f32[32,128]{1,0:T(8,128)}, u32[]{:S(2)}, u32[]{:S(2)}) collective-permute-start(f32[32,128]{1,0:T(8,128)} %bitcast.146), channel_id=1, source_target_pairs={{2,0},{4,2},{6,4},{3,1},{5,3},{7,5},{10,8},{12,10},{14,12},{11,9},... | collective-permute-start | bytes 49160 | tf_op jit(solution)/shard_map/ppermute | solution.py:96
  17.8 35.8 %collective-permute-start.4 = (f32[8,32]{1,0:T(8,128)S(1)}, f32[8,32]{1,0:T(8,128)S(1)}, u32[]{:S(2)}, u32[]{:S(2)}) collective-permute-start(f32[8,32]{1,0:T(8,128)S(1)} %fusion.12), channel_id=1, source_target_pairs={{0,1},{1,0},{2,3},{3,2},{4,5},{5,4},{6,7},{7,6},{8,9},{9,8},{10,11... | collective-permute-start | bytes 3080 | tf_op jit(solution)/shard_map/ppermute | solution.py:91
  17.9 51.5 %collective-permute-start.3 = (f32[8,128]{1,0:T(8,128)S(1)}, f32[8,128]{1,0:T(8,128)S(1)}, u32[]{:S(2)}, u32[]{:S(2)}) collective-permute-start(f32[8,128]{1,0:T(8,128)S(1)} %bitcast.364), channel_id=1, source_target_pairs={{0,2},{2,4},{4,6},{1,3},{3,5},{5,7},{8,10},{10,12},{12,14},{9,11},... | collective-permute-start | bytes 12296 | tf_op jit(solution)/shard_map/ppermute | solution.py:96
  23.4 45.9 %collective-permute-start.2 = (f32[8,128]{1,0:T(8,128)S(1)}, f32[8,128]{1,0:T(8,128)S(1)}, u32[]{:S(2)}, u32[]{:S(2)}) collective-permute-start(f32[8,128]{1,0:T(8,128)S(1)} %bitcast.363), channel_id=1, source_target_pairs={{2,0},{4,2},{6,4},{3,1},{5,3},{7,5},{10,8},{12,10},{14,12},{11,9},... | collective-permute-start | bytes 12296 | tf_op jit(solution)/shard_map/ppermute | solution.py:96
  34.6 21.1 %all-to-all-start = ((s32[32,1,24]{2,1,0:T(1,128)}), s32[32,1,24]{2,1,0:T(1,128)S(1)}, u32[]{:S(2)}, u32[]{:S(2)}) async-start(s32[32,1,24]{2,1,0:T(1,128)} %bitcast.106), calls=%async_computation | async-start | bytes 32768 | tf_op jit(solution)/shard_map/all_to_all | solution.py:262
  50.0 52.1 %copy-start.8 = (pred[8,32,128]{2,1,0:T(8,128)(4,1)}, pred[8,32,128]{2,1,0:T(8,128)(4,1)S(1)}, u32[]{:S(2)}) copy-start(pred[8,32,128]{2,1,0:T(8,128)(4,1)S(1)} %get-tuple-element.203) | copy-start | bytes 98308
  50.0 52.1 %copy-start.10 = (pred[8,32,128]{2,1,0:T(8,128)(4,1)}, pred[8,32,128]{2,1,0:T(8,128)(4,1)S(1)}, u32[]{:S(2)}) copy-start(pred[8,32,128]{2,1,0:T(8,128)(4,1)S(1)} %get-tuple-element.204) | copy-start | bytes 98308
  50.0 52.1 %copy-start.12 = (pred[8,32,128]{2,1,0:T(8,128)(4,1)}, pred[8,32,128]{2,1,0:T(8,128)(4,1)S(1)}, u32[]{:S(2)}) copy-start(pred[8,32,128]{2,1,0:T(8,128)(4,1)S(1)} %get-tuple-element.205) | copy-start | bytes 98308
  50.1 52.1 %copy-start.66 = (f32[9]{0:T(128)}, f32[9]{0:T(128)S(1)}, u32[]{:S(2)}) copy-start(f32[9]{0:T(128)S(1)} %get-tuple-element.236) | copy-start | bytes 112
  50.1 52.1 %copy-start.68 = (f32[9]{0:T(128)}, f32[9]{0:T(128)S(1)}, u32[]{:S(2)}) copy-start(f32[9]{0:T(128)S(1)} %get-tuple-element.237) | copy-start | bytes 112
  53.6 15.8 %collective-permute-start = (f32[32,128]{1,0:T(8,128)S(1)}, f32[32,128]{1,0:T(8,128)S(1)}, u32[]{:S(2)}, u32[]{:S(2)}) collective-permute-start(f32[32,128]{1,0:T(8,128)S(1)} %get-tuple-element.134), channel_id=1, source_target_pairs={{8,0},{16,8},{24,16},{9,1},{17,9},{25,17},{10,2},{18,10},{26,18},{... | collective-permute-start | bytes 49160 | tf_op jit(solution)/shard_map/ppermute | solution.py:96
  61.7 7.6 %collective-permute-start.1 = (f32[32,128]{1,0:T(8,128)S(1)}, f32[32,128]{1,0:T(8,128)S(1)}, u32[]{:S(2)}, u32[]{:S(2)}) collective-permute-start(f32[32,128]{1,0:T(8,128)S(1)} %get-tuple-element.133), channel_id=1, source_target_pairs={{0,8},{8,16},{16,24},{1,9},{9,17},{17,25},{2,10},{10,18},{18,26},{... | collective-permute-start | bytes 49160 | tf_op jit(solution)/shard_map/ppermute | solution.py:96
  76.8 7.9 %collective-permute-start.9 = (f32[8,32]{1,0:T(8,128)S(1)}, f32[8,32]{1,0:T(8,128)S(1)}, u32[]{:S(2)}, u32[]{:S(2)}) collective-permute-start(f32[8,32]{1,0:T(8,128)S(1)} %fusion.11), channel_id=1, source_target_pairs={{0,1},{1,0},{2,3},{3,2},{4,5},{5,4},{6,7},{7,6},{8,9},{9,8},{10,11... | collective-permute-start | bytes 3080 | tf_op jit(solution)/shard_map/ppermute | solution.py:91
  76.9 15.8 %collective-permute-start.5 = (f32[32,128]{1,0:T(8,128)S(1)}, f32[32,128]{1,0:T(8,128)S(1)}, u32[]{:S(2)}, u32[]{:S(2)}) collective-permute-start(f32[32,128]{1,0:T(8,128)S(1)} %get-tuple-element.194), channel_id=1, source_target_pairs={{8,0},{16,8},{24,16},{9,1},{17,9},{25,17},{10,2},{18,10},{26,18},{... | collective-permute-start | bytes 49160 | tf_op jit(solution)/shard_map/ppermute | solution.py:96
  78.2 14.5 %collective-permute-start.6 = (f32[32,128]{1,0:T(8,128)S(1)}, f32[32,128]{1,0:T(8,128)S(1)}, u32[]{:S(2)}, u32[]{:S(2)}) collective-permute-start(f32[32,128]{1,0:T(8,128)S(1)} %get-tuple-element.193), channel_id=1, source_target_pairs={{0,8},{8,16},{16,24},{1,9},{9,17},{17,25},{2,10},{10,18},{18,26},{... | collective-permute-start | bytes 49160 | tf_op jit(solution)/shard_map/ppermute | solution.py:96
  83.4 9.3 %collective-permute-start.7 = (f32[8,128]{1,0:T(8,128)S(1)}, f32[8,128]{1,0:T(8,128)S(1)}, u32[]{:S(2)}, u32[]{:S(2)}) collective-permute-start(f32[8,128]{1,0:T(8,128)S(1)} %bitcast.367), channel_id=1, source_target_pairs={{2,0},{4,2},{6,4},{3,1},{5,3},{7,5},{10,8},{12,10},{14,12},{11,9},... | collective-permute-start | bytes 12296 | tf_op jit(solution)/shard_map/ppermute | solution.py:96
  84.7 8.0 %collective-permute-start.8 = (f32[8,128]{1,0:T(8,128)S(1)}, f32[8,128]{1,0:T(8,128)S(1)}, u32[]{:S(2)}, u32[]{:S(2)}) collective-permute-start(f32[8,128]{1,0:T(8,128)S(1)} %bitcast.365), channel_id=1, source_target_pairs={{0,2},{2,4},{4,6},{1,3},{3,5},{5,7},{8,10},{10,12},{12,14},{9,11},... | collective-permute-start | bytes 12296 | tf_op jit(solution)/shard_map/ppermute | solution.py:96
  102.7 8.4 %collective-permute-start.14 = (f32[8,32]{1,0:T(8,128)S(1)}, f32[8,32]{1,0:T(8,128)S(1)}, u32[]{:S(2)}, u32[]{:S(2)}) collective-permute-start(f32[8,32]{1,0:T(8,128)S(1)} %fusion.10), channel_id=1, source_target_pairs={{0,1},{1,0},{2,3},{3,2},{4,5},{5,4},{6,7},{7,6},{8,9},{9,8},{10,11... | collective-permute-start | bytes 3080 | tf_op jit(solution)/shard_map/ppermute | solution.py:91
  102.8 14.2 %collective-permute-start.11 = (f32[32,128]{1,0:T(8,128)S(1)}, f32[32,128]{1,0:T(8,128)S(1)}, u32[]{:S(2)}, u32[]{:S(2)}) collective-permute-start(f32[32,128]{1,0:T(8,128)S(1)} %get-tuple-element.177), channel_id=1, source_target_pairs={{0,8},{8,16},{16,24},{1,9},{9,17},{17,25},{2,10},{10,18},{18,26},{... | collective-permute-start | bytes 49160 | tf_op jit(solution)/shard_map/ppermute | solution.py:96
  108.6 8.5 %collective-permute-start.10 = (f32[32,128]{1,0:T(8,128)S(1)}, f32[32,128]{1,0:T(8,128)S(1)}, u32[]{:S(2)}, u32[]{:S(2)}) collective-permute-start(f32[32,128]{1,0:T(8,128)S(1)} %get-tuple-element.178), channel_id=1, source_target_pairs={{8,0},{16,8},{24,16},{9,1},{17,9},{25,17},{10,2},{18,10},{26,18},{... | collective-permute-start | bytes 49160 | tf_op jit(solution)/shard_map/ppermute | solution.py:96
  109.9 6.4 %collective-permute-start.12 = (f32[8,128]{1,0:T(8,128)S(1)}, f32[8,128]{1,0:T(8,128)S(1)}, u32[]{:S(2)}, u32[]{:S(2)}) collective-permute-start(f32[8,128]{1,0:T(8,128)S(1)} %bitcast.370), channel_id=1, source_target_pairs={{2,0},{4,2},{6,4},{3,1},{5,3},{7,5},{10,8},{12,10},{14,12},{11,9},... | collective-permute-start | bytes 12296 | tf_op jit(solution)/shard_map/ppermute | solution.py:96
  111.2 5.9 %collective-permute-start.13 = (f32[8,128]{1,0:T(8,128)S(1)}, f32[8,128]{1,0:T(8,128)S(1)}, u32[]{:S(2)}, u32[]{:S(2)}) collective-permute-start(f32[8,128]{1,0:T(8,128)S(1)} %bitcast.368), channel_id=1, source_target_pairs={{0,2},{2,4},{4,6},{1,3},{3,5},{5,7},{8,10},{10,12},{12,14},{9,11},... | collective-permute-start | bytes 12296 | tf_op jit(solution)/shard_map/ppermute | solution.py:96
  120.8 7.9 %collective-permute-start.19 = (f32[8,32]{1,0:T(8,128)S(1)}, f32[8,32]{1,0:T(8,128)S(1)}, u32[]{:S(2)}, u32[]{:S(2)}) collective-permute-start(f32[8,32]{1,0:T(8,128)S(1)} %fusion.9), channel_id=1, source_target_pairs={{0,1},{1,0},{2,3},{3,2},{4,5},{5,4},{6,7},{7,6},{8,9},{9,8},{10,11... | collective-permute-start | bytes 3080 | tf_op jit(solution)/shard_map/ppermute | solution.py:91
  120.9 18.8 %collective-permute-start.15 = (f32[32,128]{1,0:T(8,128)S(1)}, f32[32,128]{1,0:T(8,128)S(1)}, u32[]{:S(2)}, u32[]{:S(2)}) collective-permute-start(f32[32,128]{1,0:T(8,128)S(1)} %get-tuple-element.162), channel_id=1, source_target_pairs={{8,0},{16,8},{24,16},{9,1},{17,9},{25,17},{10,2},{18,10},{26,18},{... | collective-permute-start | bytes 49160 | tf_op jit(solution)/shard_map/ppermute | solution.py:96
  122.2 23.5 %collective-permute-start.16 = (f32[32,128]{1,0:T(8,128)S(1)}, f32[32,128]{1,0:T(8,128)S(1)}, u32[]{:S(2)}, u32[]{:S(2)}) collective-permute-start(f32[32,128]{1,0:T(8,128)S(1)} %get-tuple-element.161), channel_id=1, source_target_pairs={{0,8},{8,16},{16,24},{1,9},{9,17},{17,25},{2,10},{10,18},{18,26},{... | collective-permute-start | bytes 49160 | tf_op jit(solution)/shard_map/ppermute | solution.py:96
  127.4 6.4 %collective-permute-start.17 = (f32[8,128]{1,0:T(8,128)S(1)}, f32[8,128]{1,0:T(8,128)S(1)}, u32[]{:S(2)}, u32[]{:S(2)}) collective-permute-start(f32[8,128]{1,0:T(8,128)S(1)} %bitcast.369), channel_id=1, source_target_pairs={{2,0},{4,2},{6,4},{3,1},{5,3},{7,5},{10,8},{12,10},{14,12},{11,9},... | collective-permute-start | bytes 12296 | tf_op jit(solution)/shard_map/ppermute | solution.py:96
  128.7 9.7 %collective-permute-start.18 = (f32[8,128]{1,0:T(8,128)S(1)}, f32[8,128]{1,0:T(8,128)S(1)}, u32[]{:S(2)}, u32[]{:S(2)}) collective-permute-start(f32[8,128]{1,0:T(8,128)S(1)} %bitcast.366), channel_id=1, source_target_pairs={{0,2},{2,4},{4,6},{1,3},{3,5},{5,7},{8,10},{10,12},{12,14},{9,11},... | collective-permute-start | bytes 12296 | tf_op jit(solution)/shard_map/ppermute | solution.py:96
  133.9 25.4 %collective-permute-start.23 = (f32[32,128]{1,0:T(8,128)}, f32[32,128]{1,0:T(8,128)}, u32[]{:S(2)}, u32[]{:S(2)}) collective-permute-start(f32[32,128]{1,0:T(8,128)} %bitcast.148), channel_id=1, source_target_pairs={{0,2},{2,4},{4,6},{1,3},{3,5},{5,7},{8,10},{10,12},{12,14},{9,11},... | collective-permute-start | bytes 49160 | tf_op jit(solution)/shard_map/ppermute | solution.py:96
  138.4 20.9 %collective-permute-start.20 = (f32[64,128]{1,0:T(8,128)}, f32[64,128]{1,0:T(8,128)}, u32[]{:S(2)}, u32[]{:S(2)}) collective-permute-start(f32[64,128]{1,0:T(8,128)} %get-tuple-element.144), channel_id=1, source_target_pairs={{8,0},{16,8},{24,16},{9,1},{17,9},{25,17},{10,2},{18,10},{26,18},{... | collective-permute-start | bytes 98312 | tf_op jit(solution)/shard_map/ppermute | solution.py:96
  139.7 19.6 %collective-permute-start.21 = (f32[64,128]{1,0:T(8,128)}, f32[64,128]{1,0:T(8,128)}, u32[]{:S(2)}, u32[]{:S(2)}) collective-permute-start(f32[64,128]{1,0:T(8,128)} %get-tuple-element.143), channel_id=1, source_target_pairs={{0,8},{8,16},{16,24},{1,9},{9,17},{17,25},{2,10},{10,18},{18,26},{... | collective-permute-start | bytes 98312 | tf_op jit(solution)/shard_map/ppermute | solution.py:96
  155.9 42.1 %all-to-all-start.1 = ((f32[4,32,24,128]{3,0,2,1:T(4,128)}), f32[4,32,24,128]{3,0,2,1:T(4,128)S(1)}, u32[]{:S(2)}, u32[]{:S(2)}) async-start(f32[4,32,24,128]{3,0,2,1:T(4,128)} %select_select_fusion.1), calls=%async_computation.1 | async-start | bytes 3145728 | tf_op jit(solution)/shard_map/all_to_all | solution.py:281
  235.1 7.6 %collective-permute-start.29 = (f32[4,32,64]{2,1,0:T(8,128)S(1)}, f32[4,32,64]{2,1,0:T(8,128)S(1)}, u32[]{:S(2)}, u32[]{:S(2)}) collective-permute-start(f32[4,32,64]{2,1,0:T(8,128)S(1)} %broadcast_select_fusion.8), channel_id=1, source_target_pairs={{0,1},{1,0},{2,3},{3,2},{4,5},{5,4},{6,7},{7,6},{8,9},{9,8},{10,11... | collective-permute-start | bytes 98312 | tf_op jit(solution)/shard_map/ppermute | solution.py:91
  236.0 11.7 %collective-permute-start.25 = (f32[4,64,128]{2,1,0:T(8,128)S(1)}, f32[4,64,128]{2,1,0:T(8,128)S(1)}, u32[]{:S(2)}, u32[]{:S(2)}) collective-permute-start(f32[4,64,128]{2,1,0:T(8,128)S(1)} %copy-done.92), channel_id=1, source_target_pairs={{0,8},{8,16},{16,24},{1,9},{9,17},{17,25},{2,10},{10,18},{18,26},{... | collective-permute-start | bytes 393224 | tf_op jit(solution)/shard_map/ppermute | solution.py:96
  238.7 9.0 %collective-permute-start.26 = (f32[4,64,128]{2,1,0:T(8,128)S(1)}, f32[4,64,128]{2,1,0:T(8,128)S(1)}, u32[]{:S(2)}, u32[]{:S(2)}) collective-permute-start(f32[4,64,128]{2,1,0:T(8,128)S(1)} %copy-done.91), channel_id=1, source_target_pairs={{8,0},{16,8},{24,16},{9,1},{17,9},{25,17},{10,2},{18,10},{26,18},{... | collective-permute-start | bytes 393224 | tf_op jit(solution)/shard_map/ppermute | solution.py:96
  240.0 3.5 collective-permute-start.27
  241.3 6.4 %collective-permute-start.28 = (f32[4,32,1,128]{3,2,1,0:T(1,128)}, f32[4,32,1,128]{3,2,1,0:T(1,128)S(1)}, u32[]{:S(2)}, u32[]{:S(2)}) collective-permute-start(f32[4,32,1,128]{3,2,1,0:T(1,128)} %get-tuple-element.36), channel_id=1, source_target_pairs={{2,0},{4,2},{6,4},{3,1},{5,3},{7,5},{10,8},{12,10},{14,12},{11,9},... | collective-permute-start | bytes 196616 | tf_op jit(solution)/shard_map/ppermute | solution.py:96
  281.9 11.3 %collective-permute-start.34 = (f32[4,32,64]{2,1,0:T(8,128)S(1)}, f32[4,32,64]{2,1,0:T(8,128)S(1)}, u32[]{:S(2)}, u32[]{:S(2)}) collective-permute-start(f32[4,32,64]{2,1,0:T(8,128)S(1)} %broadcast_select_fusion.7), channel_id=1, source_target_pairs={{0,1},{1,0},{2,3},{3,2},{4,5},{5,4},{6,7},{7,6},{8,9},{9,8},{10,11... | collective-permute-start | bytes 98312 | tf_op jit(solution)/shard_map/ppermute | solution.py:91
  283.2 15.0 %collective-permute-start.30 = (f32[4,64,128]{2,1,0:T(8,128)}, f32[4,64,128]{2,1,0:T(8,128)S(1)}, u32[]{:S(2)}, u32[]{:S(2)}) collective-permute-start(f32[4,64,128]{2,1,0:T(8,128)} %get-tuple-element.42), channel_id=1, source_target_pairs={{0,8},{8,16},{16,24},{1,9},{9,17},{17,25},{2,10},{10,18},{18,26},{... | collective-permute-start | bytes 393224 | tf_op jit(solution)/shard_map/ppermute | solution.py:96
  287.8 10.4 %collective-permute-start.31 = (f32[4,64,128]{2,1,0:T(8,128)}, f32[4,64,128]{2,1,0:T(8,128)S(1)}, u32[]{:S(2)}, u32[]{:S(2)}) collective-permute-start(f32[4,64,128]{2,1,0:T(8,128)} %get-tuple-element.43), channel_id=1, source_target_pairs={{8,0},{16,8},{24,16},{9,1},{17,9},{25,17},{10,2},{18,10},{26,18},{... | collective-permute-start | bytes 393224 | tf_op jit(solution)/shard_map/ppermute | solution.py:96
  289.1 5.0 %collective-permute-start.32 = (f32[4,32,1,128]{3,2,1,0:T(1,128)}, f32[4,32,1,128]{3,2,1,0:T(1,128)S(1)}, u32[]{:S(2)}, u32[]{:S(2)}) collective-permute-start(f32[4,32,1,128]{3,2,1,0:T(1,128)} %get-tuple-element.44), channel_id=1, source_target_pairs={{0,2},{2,4},{4,6},{1,3},{3,5},{5,7},{8,10},{10,12},{12,14},{9,11},... | collective-permute-start | bytes 196616 | tf_op jit(solution)/shard_map/ppermute | solution.py:96
  291.9 6.4 %collective-permute-start.33 = (f32[4,32,1,128]{3,2,1,0:T(1,128)}, f32[4,32,1,128]{3,2,1,0:T(1,128)S(1)}, u32[]{:S(2)}, u32[]{:S(2)}) collective-permute-start(f32[4,32,1,128]{3,2,1,0:T(1,128)} %get-tuple-element.45), channel_id=1, source_target_pairs={{2,0},{4,2},{6,4},{3,1},{5,3},{7,5},{10,8},{12,10},{14,12},{11,9},... | collective-permute-start | bytes 196616 | tf_op jit(solution)/shard_map/ppermute | solution.py:96
  332.4 12.9 %collective-permute-start.39 = (f32[4,32,64]{2,1,0:T(8,128)S(1)}, f32[4,32,64]{2,1,0:T(8,128)S(1)}, u32[]{:S(2)}, u32[]{:S(2)}) collective-permute-start(f32[4,32,64]{2,1,0:T(8,128)S(1)} %broadcast_select_fusion.6), channel_id=1, source_target_pairs={{0,1},{1,0},{2,3},{3,2},{4,5},{5,4},{6,7},{7,6},{8,9},{9,8},{10,11... | collective-permute-start | bytes 98312 | tf_op jit(solution)/shard_map/ppermute | solution.py:91
  334.2 15.9 %collective-permute-start.35 = (f32[4,64,128]{2,1,0:T(8,128)S(1)}, f32[4,64,128]{2,1,0:T(8,128)S(1)}, u32[]{:S(2)}, u32[]{:S(2)}) collective-permute-start(f32[4,64,128]{2,1,0:T(8,128)S(1)} %copy-done.90), channel_id=1, source_target_pairs={{0,8},{8,16},{16,24},{1,9},{9,17},{17,25},{2,10},{10,18},{18,26},{... | collective-permute-start | bytes 393224 | tf_op jit(solution)/shard_map/ppermute | solution.py:96
  339.2 11.0 %collective-permute-start.36 = (f32[4,64,128]{2,1,0:T(8,128)S(1)}, f32[4,64,128]{2,1,0:T(8,128)S(1)}, u32[]{:S(2)}, u32[]{:S(2)}) collective-permute-start(f32[4,64,128]{2,1,0:T(8,128)S(1)} %copy-done.89), channel_id=1, source_target_pairs={{8,0},{16,8},{24,16},{9,1},{17,9},{25,17},{10,2},{18,10},{26,18},{... | collective-permute-start | bytes 393224 | tf_op jit(solution)/shard_map/ppermute | solution.py:96
  340.5 5.5 %collective-permute-start.37 = (f32[4,32,1,128]{3,2,1,0:T(1,128)S(1)}, f32[4,32,1,128]{3,2,1,0:T(1,128)S(1)}, u32[]{:S(2)}, u32[]{:S(2)}) collective-permute-start(f32[4,32,1,128]{3,2,1,0:T(1,128)S(1)} %copy-done.94), channel_id=1, source_target_pairs={{0,2},{2,4},{4,6},{1,3},{3,5},{5,7},{8,10},{10,12},{12,14},{9,11},... | collective-permute-start | bytes 196616 | tf_op jit(solution)/shard_map/ppermute | solution.py:96
  344.0 6.2 %collective-permute-start.38 = (f32[4,32,1,128]{3,2,1,0:T(1,128)S(1)}, f32[4,32,1,128]{3,2,1,0:T(1,128)S(1)}, u32[]{:S(2)}, u32[]{:S(2)}) collective-permute-start(f32[4,32,1,128]{3,2,1,0:T(1,128)S(1)} %copy-done.93), channel_id=1, source_target_pairs={{2,0},{4,2},{6,4},{3,1},{5,3},{7,5},{10,8},{12,10},{14,12},{11,9},... | collective-permute-start | bytes 196616 | tf_op jit(solution)/shard_map/ppermute | solution.py:96
  (90 other events, 806.2 us)

commit v2 on v1

--- a/solution.py
+++ b/solution.py
@@ -72,16 +72,27 @@
     return (gate_state, ion_current)
 
 
-def heart_laplace(voltage):
+def faces_of(block, dim):
+    top = lax.index_in_dim(block, block.shape[dim] - 1, axis=dim, keepdims=False)
+    bottom = lax.index_in_dim(block, 0, axis=dim, keepdims=False)
+    return top, bottom
+
+
+def heart_laplace(voltage, riders=None):
     parts = []
-    for axis, dim in (("gx", 0), ("gy", 1), ("gz", 2)):
-        low, high = face_halos(voltage, axis, dim)
-        minus, plus = shifted(voltage, low, high, dim)
+    carried = []
+    for index, (axis, dim) in enumerate((("gx", 0), ("gy", 1), ("gz", 2))):
+        pairs = [faces_of(voltage, dim)]
+        if riders is not None:
+            pairs.append(riders[index])
+        got = exchange_group(pairs, axis)
+        minus, plus = shifted(voltage, got[0][0], got[0][1], dim)
         parts.append((plus, minus))
+        carried.append(got[1:])
     total = parts[0][0] + parts[0][1]
     total = total + parts[1][0] + parts[1][1]
     total = total + parts[2][0] + parts[2][1]
-    return total - 6.0 * voltage
+    return total - 6.0 * voltage, carried
 
 
 def exchange(top, bottom, axis):
@@ -96,6 +107,21 @@
     return lax.ppermute(top, axis, forward), lax.ppermute(bottom, axis, backward)
 
 
+def exchange_group(pairs, axis):
+    if len(pairs) == 1:
+        return [exchange(pairs[0][0], pairs[0][1], axis)]
+    top = jnp.concatenate([item.reshape(-1) for item, _ in pairs])
+    bottom = jnp.concatenate([item.reshape(-1) for _, item in pairs])
+    low, high = exchange(top, bottom, axis)
+    result = []
+    offset = 0
+    for item, _ in pairs:
+        size = item.size
+        result.append((low[offset:offset + size].reshape(item.shape), high[offset:offset + size].reshape(item.shape)))
+        offset += size
+    return result
+
+
 def write_faces(x, value, columns, xf_lo, xf_hi, yf_lo, yf_hi, zf_lo, zf_hi):
     nx = yf_lo.shape[1]
     ny, nz = value.shape
@@ -125,7 +151,7 @@
     zf_hi[0] = flipped[half:half + nx, :]
 
 
-def sweep_kernel(first, second, d_ref, r_ref, p_ref, fxp, fxm, fyp, fym, fzp, fzm, dg_ref,
+def sweep_kernel(first, second, d_ref, r_ref, p_ref, fxp, fxm, fyp, fym, fzp, fzm, dg_ref, inv_ref,
                  xlo, xhi, ylo, yhi, zlo, zhi, r_out, d_out, p_out, *face_out):
     nx, ny, nz = d_ref.shape[1], d_ref.shape[2], d_ref.shape[3]
     row = lax.broadcasted_iota(jnp.int32, (ny, nz), 0)
@@ -151,25 +177,25 @@
         beside = beside + fzp[x] * z_plus + fzm[x] * z_minus
         diag = dg_ref[x]
         residual = r_ref[0, x] - (diag * centre - beside)
-        step_dir = first * centre + second * (residual / diag)
+        step_dir = first * centre + second * (residual * inv_ref[x])
         r_out[0, x] = residual
         d_out[0, x] = step_dir
         p_out[0, x] = p_ref[0, x] + step_dir
         return write_faces(x, step_dir, carry, *face_out)
 
-    columns = lax.fori_loop(0, nx, body, jnp.zeros((ny, nz), jnp.float32))
+    columns = lax.fori_loop(0, nx, body, jnp.zeros((ny, nz), jnp.float32), unroll=2)
     finish_faces(columns, *face_out)
 
 
-def initial_kernel(mid, r_ref, dg_ref, d_out, *face_out):
+def initial_kernel(mid, r_ref, inv_ref, d_out, *face_out):
     nx, ny, nz = r_ref.shape[1], r_ref.shape[2], r_ref.shape[3]
 
     def body(x, carry):
-        step_dir = r_ref[0, x] / dg_ref[x] / mid
+        step_dir = r_ref[0, x] * inv_ref[x] * (1.0 / mid)
         d_out[0, x] = step_dir
         return write_faces(x, step_dir, carry, *face_out)
 
-    columns = lax.fori_loop(0, nx, body, jnp.zeros((ny, nz), jnp.float32))
+    columns = lax.fori_loop(0, nx, body, jnp.zeros((ny, nz), jnp.float32), unroll=2)
     finish_faces(columns, *face_out)
 
 
@@ -192,7 +218,7 @@
     return full, fixed, face_specs, face_shapes
 
 
-def run_initial(mid, source, diagonal):
+def run_initial(mid, source, inverse):
     full, fixed, face_specs, face_shapes = specs(source.shape)
     shape = jax.ShapeDtypeStruct(source.shape, jnp.float32)
     size = source.size
@@ -204,11 +230,11 @@
         out_shape=[shape] + face_shapes,
         cost_estimate=pl.CostEstimate(flops=2 * size, transcendentals=0, bytes_accessed=8 * size + 4 * size // source.shape[0]),
         name="chebyshev_start",
-    )(source, diagonal)
+    )(source, inverse)
     return outs[0], outs[1:]
 
 
-def run_sweep(first, second, step_dir, residual, potential, faces, diagonal, halos):
+def run_sweep(first, second, step_dir, residual, potential, faces, diagonal, inverse, halos):
     full, fixed, face_specs, face_shapes = specs(step_dir.shape)
     steps, nx, ny, nz = step_dir.shape
     x_face, y_face = face_specs[0], face_specs[2]
@@ -217,12 +243,12 @@
     outs = pl.pallas_call(
         functools.partial(sweep_kernel, first, second),
         grid=(steps,),
-        in_specs=[full, full, full] + [fixed] * 7 + [x_face, x_face, y_face, y_face, face_specs[4], face_specs[4]],
+        in_specs=[full, full, full] + [fixed] * 8 + [x_face, x_face, y_face, y_face, face_specs[4], face_specs[4]],
         out_specs=[full, full, full] + face_specs,
         out_shape=[shape, shape, shape] + face_shapes,
         cost_estimate=pl.CostEstimate(flops=30 * size, transcendentals=0, bytes_accessed=4 * 7 * size + 4 * 7 * size // steps),
         name="chebyshev_sweep",
-    )(step_dir, residual, potential, *faces, diagonal, *halos)
+    )(step_dir, residual, potential, *faces, diagonal, inverse, *halos)
     return outs[0], outs[1], outs[2], outs[3:]
 
 
@@ -266,12 +292,23 @@
     row_used = jnp.any(row_match, axis=1)
     row_slot = jnp.argmax(row_match, axis=1).astype(jnp.int32)
 
+    sigma = []
+    for dim_index in range(3):
+        value = jnp.zeros(tissue.shape, jnp.float32)
+        for tissue_kind in range(tissue_sigma.shape[0]):
+            value = value + jnp.where(tissue == tissue_kind, tissue_sigma[tissue_kind, dim_index], 0.0)
+        sigma.append(value)
+    riders = [faces_of(sigma[dim_index], dim_index) for dim_index in range(3)]
+
     currents = []
     for time_step in range(STEPS):
         gate_state, ion_current = membrane(
             voltage, gate_state, cell_type, gate_half, gate_slope, gate_tau, conduct, reversal
         )
-        current = SIGMA_HEART * heart_laplace(voltage)
+        laplace, carried = heart_laplace(voltage, riders if time_step == 0 else None)
+        if time_step == 0:
+            sigma_halos = [item[0] for item in carried]
+        current = SIGMA_HEART * laplace
         currents.append(current)
         voltage = voltage + DT_HEART * (current - ion_current)
     heart_next = jnp.concatenate([voltage[None], gate_state], axis=0)
@@ -288,15 +325,9 @@
     source = jnp.where(row_used[None, :, None], jnp.take(received, row_slot, axis=1), 0.0)
     source = source.reshape(STEPS, torso_x, torso_y, torso_z)
 
-    sigma = []
+    faces = []
     for dim_index in range(3):
-        value = jnp.zeros(tissue.shape, jnp.float32)
-        for tissue_kind in range(tissue_sigma.shape[0]):
-            value = value + jnp.where(tissue == tissue_kind, tissue_sigma[tissue_kind, dim_index], 0.0)
-        sigma.append(value)
-    faces = []
-    for dim_index, axis in enumerate(("gx", "gy", "gz")):
-        low, high = face_halos(sigma[dim_index], axis, dim_index)
+        low, high = sigma_halos[dim_index]
         minus, plus = shifted(sigma[dim_index], low, high, dim_index)
         faces.append(0.5 * (sigma[dim_index] + plus))
         faces.append(0.5 * (sigma[dim_index] + minus))
@@ -304,7 +335,8 @@
 
     spectrum_mid, first_coef, second_coef = chebyshev_weights(SWEEPS)
     residual = source
-    step_dir, dir_faces = run_initial(spectrum_mid, residual, diagonal)
+    inverse = 1.0 / diagonal
+    step_dir, dir_faces = run_initial(spectrum_mid, residual, inverse)
     potential = step_dir
     for sweep in range(1, SWEEPS):
         x_low, x_high = exchange(dir_faces[1], dir_faces[0], "gx")
@@ -312,7 +344,7 @@
         z_low, z_high = exchange(dir_faces[5], dir_faces[4], "gz")
         halos = (x_low, x_high, y_low, y_high, z_low, z_high)
         residual, step_dir, potential, dir_faces = run_sweep(
-            first_coef[sweep - 1], second_coef[sweep - 1], step_dir, residual, potential, faces, diagonal, halos
+            first_coef[sweep - 1], second_coef[sweep - 1], step_dir, residual, potential, faces, diagonal, inverse, halos
         )
     return (heart_next, jnp.transpose(potential, (1, 2, 0, 3)))
 

time: 395 us -> 379 us (0.959)
  Pallas kernels: 113 us -> 98.3 us
  starting transfers between devices: 102 us -> 90.8 us
  local copies, waits for them, and re-layouts: 68.3 us -> 73.1 us
    pallas_call x3, Pallas kernels: 97.6 us -> 84 us  [run_sweep(): pl.pallas_call(functools.partial(sweep_kernel, first, second), grid=(step...]
    ppermute x16 -> x14, starting transfers between devices: 69.7 us -> 58.3 us  [exchange(): lax.ppermute(top, axis, forward)]
    add x1 -> x0, other arithmetic: 8.81 us -> none  [local(): SCREEN + faces[0] + faces[1] + faces[2] + faces[3] + faces[4] + faces[5]]
    div x0 -> x1, other arithmetic: none -> 6.99 us  [local(): inverse = 1.0 / diagonal]
    slice x6 -> x24, local copies, waits for them, and re-layouts: 0.84 us -> 5.54 us  [the longest x8 2.13 us: exchange_group(): low[offset:offset + size].reshape(item.shape)]
    ppermute x16 -> x14, starting transfers between devices: 20.6 us -> 18.3 us  [exchange(): lax.ppermute(bottom, axis, backward)]
    unnamed x194 -> x200, local copies, waits for them, and re-layouts: 11.4 us -> 12.5 us
    ppermute x16 -> x14, waiting for transfers between devices: 12.6 us -> 12.3 us  [exchange(): lax.ppermute(bottom, axis, backward)]
  transfers between devices with their start and end apart: 42 -> 37, of which waited for: 7 -> 8; matrix products, arithmetic and copies ran while one was open for 23% -> 17% of each run, Pallas kernels for 0% -> 0%
where the time goes in v2:
time: 379 us; the launch traced here: 375 us
  Pallas kernels  98.3 us (26%)
  starting transfers between devices  90.8 us (24%)
  local copies, waits for them, and re-layouts  73.1 us (19%)
  other arithmetic  72.9 us (19%)
  waiting for transfers between devices  36.8 us (10%)
    pallas_call x3, Pallas kernels, run_sweep(): pl.pallas_call(functools.partial(sweep_kernel, first, second), grid=(step...  84 us
    ppermute x14, starting transfers between devices, exchange(): lax.ppermute(top, axis, forward)  58.3 us
    all_to_all x1, waiting for transfers between devices, local(): lax.all_to_all(send_values.reshape(STEPS, devices, capacity, row_len), ('...  22.6 us
    ppermute x14, starting transfers between devices, exchange(): lax.ppermute(bottom, axis, backward)  18.3 us
    gather x2, local copies, waits for them, and re-layouts, local(): jnp.take(received, row_slot, axis=1)  17.7 us
    add x4, other arithmetic, membrane(): steady + (gate_state - steady) * jnp.exp(-DT_HEART / time_const)  16.1 us
    pallas_call x1, Pallas kernels, run_initial(): pl.pallas_call(functools.partial(initial_kernel, mid), grid=(source.shape...  14.3 us
    unnamed x200, local copies, waits for them, and re-layouts  12.5 us
  transfers between devices with their start and end apart: 37, of which 8 were waited for; matrix products, arithmetic and copies ran while one was open for 17% of the time, Pallas kernels for 0%

profile of v2, /device:TPU:0, one launch (start us, length us, event | category | flops | bytes accessed | tf_op | source)
XLA Modules:
  0.0 374.6 jit_solution(5960971614579254739)
XLA Ops:
  0.6 1.8 fusion.118
  2.4 4.6 %select_add_fusion.1 = (f32[32,64,128]{2,1,0:T(8,128)S(1)}, pred[32,64,128]{2,1,0:T(8,128)(4,1)S(1)}, pred[32,64,128]{2,1,0:T(8,128)(4,1)S(1)}, pred[32,64,128]{2,1,0:T(8,128)(4,1)S(1)}, pred[32,64,128]{2,1,0:T(8,128)(4,1)S(1)}) fusion(f32[]{:T(128)} %bitcast.29, f32[]{:T(128)} %bitcast.28, f32[]{:T(128)} %bitcast.27, f32[]{:T(128)} %bitcast.26, ...), kind=kLoop, calls=%fused_computation.33 | loop fusion | flops 2883584 | bytes 3145744 | tf_op jit(solution)/shard_map/add | solution.py:299
  7.0 5.8 %select_add_fusion.2 = (f32[32,64,128]{2,1,0:T(8,128)S(1)}, f32[32,64,128]{2,1,0:T(8,128)S(1)}) fusion(pred[32,64,128]{2,1,0:T(8,128)(4,1)S(1)} %get-tuple-element.119, pred[32,64,128]{2,1,0:T(8,128)(4,1)S(1)} %get-tuple-element.118, pred[32,64,128]{2,1,0:T(8,128)(4,1)S(1)} %get-tuple-element.117, pred[32,64,128]{2,1,0:T(8,128)(4,1)S(1)} %get-tuple-element.116, ...), kind=kLoop, calls=%fused_computation.34 | loop fusion | flops 3670016 | bytes 3145760 | tf_op jit(solution)/shard_map/add | solution.py:299
  12.9 1.8 fusion.98
  17.2 5.5 %collective-permute-start.3 = (f32[5120]{0:T(1024)}, f32[5120]{0:T(1024)S(1)}, u32[]{:S(2)}, u32[]{:S(2)}) collective-permute-start(f32[5120]{0:T(1024)} %pad_maximum_fusion.5), channel_id=1, source_target_pairs={{0,2},{2,4},{4,6},{1,3},{3,5},{5,7},{8,10},{10,12},{12,14},{9,11},... | collective-permute-start | bytes 61448 | tf_op jit(solution)/shard_map/ppermute | solution.py:107
  23.5 3.8 %collective-permute-start.1 = (f32[12288]{0:T(1024)S(1)}, f32[12288]{0:T(1024)S(1)}, u32[]{:S(2)}, u32[]{:S(2)}) collective-permute-start(f32[12288]{0:T(1024)S(1)} %pad_maximum_fusion.3), channel_id=1, source_target_pairs={{0,8},{8,16},{16,24},{1,9},{9,17},{17,25},{2,10},{10,18},{18,26},{... | collective-permute-start | bytes 147464 | tf_op jit(solution)/shard_map/ppermute | solution.py:107
  36.2 5.0 %gather_fusion = s32[768]{0:T(1024)S(1)} fusion(s32[256]{0:T(256)S(1)} %reshape.1868, s32[1024]{0:T(1024)S(1)} %pad_clamp_fusion), kind=kCustom, calls=%fused_computation | custom fusion | bytes 9216 | tf_op jit(solution)/shard_map/gather | solution.py:287
  41.9 6.1 %all-to-all-start = ((s32[32,1,24]{2,1,0:T(1,128)}), s32[32,1,24]{2,1,0:T(1,128)S(1)}, u32[]{:S(2)}, u32[]{:S(2)}) async-start(s32[32,1,24]{2,1,0:T(1,128)} %bitcast.116), calls=%async_computation | async-start | bytes 32768 | tf_op jit(solution)/shard_map/all_to_all | solution.py:288
  48.0 1.5 fusion.100
  49.5 1.6 fusion.101
  51.1 1.7 fusion.99
  55.3 1.5 multiply_add_fusion.3
  59.6 2.8 iota_reduce_fusion
  66.6 1.9 slice.567
  68.5 1.9 slice.568
  76.7 2.8 multiply_add_fusion.2
  81.7 4.5 %collective-permute-start.6 = (f32[32,128]{1,0:T(8,128)S(1)}, f32[32,128]{1,0:T(8,128)S(1)}, u32[]{:S(2)}, u32[]{:S(2)}) collective-permute-start(f32[32,128]{1,0:T(8,128)S(1)} %get-tuple-element.186), channel_id=1, source_target_pairs={{0,8},{8,16},{16,24},{1,9},{9,17},{17,25},{2,10},{10,18},{18,26},{... | collective-permute-start | bytes 49160 | tf_op jit(solution)/shard_map/ppermute | solution.py:107
  87.5 4.5 %collective-permute-start.8 = (f32[8,128]{1,0:T(8,128)S(1)}, f32[8,128]{1,0:T(8,128)S(1)}, u32[]{:S(2)}, u32[]{:S(2)}) collective-permute-start(f32[8,128]{1,0:T(8,128)S(1)} %bitcast.359), channel_id=1, source_target_pairs={{0,2},{2,4},{4,6},{1,3},{3,5},{5,7},{8,10},{10,12},{12,14},{9,11},... | collective-permute-start | bytes 12296 | tf_op jit(solution)/shard_map/ppermute | solution.py:107
  100.6 1.4 fusion.33
  102.1 4.2 %multiply_add_fusion.1 = f32[18,8,32,128]{3,2,1,0:T(8,128)S(1)} fusion(f32[8,32,128]{2,1,0:T(8,128)S(1)} %bitcast.301, f32[18]{0:T(128)S(1)} %copy-done.84, f32[18]{0:T(128)S(1)} %copy-done.87, f32[18]{0:T(128)S(1)} %copy-done.90, f32[8,32,128]{2,1,0:T(8,128)S(1)} %bitcast.293, f32[19,8,32,128]{3,2,1,0:T(8,128)S(1)} %copy-done.4, ...), kind=kLoop, calls=%fused_computation.9 | loop fusion | flops 19464192 | bytes 5112024 | tf_op jit(solution)/shard_map/add | solution.py:59
  109.5 5.1 %collective-permute-start.11 = (f32[32,128]{1,0:T(8,128)S(1)}, f32[32,128]{1,0:T(8,128)S(1)}, u32[]{:S(2)}, u32[]{:S(2)}) collective-permute-start(f32[32,128]{1,0:T(8,128)S(1)} %get-tuple-element.170), channel_id=1, source_target_pairs={{0,8},{8,16},{16,24},{1,9},{9,17},{17,25},{2,10},{10,18},{18,26},{... | collective-permute-start | bytes 49160 | tf_op jit(solution)/shard_map/ppermute | solution.py:107
  116.0 4.8 %collective-permute-start.13 = (f32[8,128]{1,0:T(8,128)S(1)}, f32[8,128]{1,0:T(8,128)S(1)}, u32[]{:S(2)}, u32[]{:S(2)}) collective-permute-start(f32[8,128]{1,0:T(8,128)S(1)} %bitcast.361), channel_id=1, source_target_pairs={{0,2},{2,4},{4,6},{1,3},{3,5},{5,7},{8,10},{10,12},{12,14},{9,11},... | collective-permute-start | bytes 12296 | tf_op jit(solution)/shard_map/ppermute | solution.py:107
  127.0 5.4 %collective-permute-start.16 = (f32[32,128]{1,0:T(8,128)S(1)}, f32[32,128]{1,0:T(8,128)S(1)}, u32[]{:S(2)}, u32[]{:S(2)}) collective-permute-start(f32[32,128]{1,0:T(8,128)S(1)} %get-tuple-element.154), channel_id=1, source_target_pairs={{0,8},{8,16},{16,24},{1,9},{9,17},{17,25},{2,10},{10,18},{18,26},{... | collective-permute-start | bytes 49160 | tf_op jit(solution)/shard_map/ppermute | solution.py:107
  133.8 4.8 %collective-permute-start.18 = (f32[8,128]{1,0:T(8,128)S(1)}, f32[8,128]{1,0:T(8,128)S(1)}, u32[]{:S(2)}, u32[]{:S(2)}) collective-permute-start(f32[8,128]{1,0:T(8,128)S(1)} %bitcast.362), channel_id=1, source_target_pairs={{0,2},{2,4},{4,6},{1,3},{3,5},{5,7},{8,10},{10,12},{12,14},{9,11},... | collective-permute-start | bytes 12296 | tf_op jit(solution)/shard_map/ppermute | solution.py:107
  142.1 3.0 gather_fusion.1
  145.1 4.9 %select_select_fusion.1 = f32[4,32,24,128]{3,0,2,1:T(4,128)} fusion(f32[4,32,24,128]{3,0,2,1:T(4,128)S(1)} %bitcast.286, pred[32,24]{1,0:T(8,128)(4,1)} %broadcast_in_dim.362, pred[32,24]{1,0:T(8,128)(4,1)} %broadcast_in_dim.360), kind=kLoop, calls=%fused_computation.12 | loop fusion | flops 786432 | bytes 3147264 | tf_op jit(solution)/shard_map/jit(_where)/select_n | solution.py:317
  150.0 7.4 %all-to-all-start.1 = ((f32[4,32,24,128]{3,0,2,1:T(4,128)}), f32[4,32,24,128]{3,0,2,1:T(4,128)S(1)}, u32[]{:S(2)}, u32[]{:S(2)}) async-start(f32[4,32,24,128]{3,0,2,1:T(4,128)} %select_select_fusion.1), calls=%async_computation.1 | async-start | bytes 3145728 | tf_op jit(solution)/shard_map/all_to_all | solution.py:318
  157.4 7.0 %broadcast_divide_fusion = (f32[32,64,128]{2,1,0:T(8,128)}, f32[32,64,128]{2,1,0:T(8,128)}, f32[32,64,128]{2,1,0:T(8,128)}, f32[32,64,128]{2,1,0:T(8,128)}, f32[...) fusion(f32[32,64,128]{2,1,0:T(8,128)} %copy-done.1, ...), kind=kLoop, calls=%fused_computation.40 | loop fusion | flops 6553600 | bytes 17825792 | tf_op jit(solution)/shard_map/div | solution.py:338
  166.1 7.5 %multiply_add_fusion = f32[18,8,32,128]{3,2,1,0:T(8,128)} fusion(f32[8,32,128]{2,1,0:T(8,128)S(1)} %bitcast.304, f32[18]{0:T(128)} %param.15, f32[18]{0:T(128)} %param.13, f32[18]{0:T(128)} %copy-done.88, f32[8,32,128]{2,1,0:T(8,128)S(1)} %bitcast.303, f32[8,32,128]{2,1,0:T(8,128)S(1)} %bitcast.294, f32[19,8,32,128]{3,2,1,0:T(8,128)} %param.11, ...), kind=kLoop, calls=%fused_computation.8 | loop fusion | flops 25952256 | bytes 5243096 | tf_op jit(solution)/shard_map/add | solution.py:59
  173.6 22.6 %all-to-all-done.1 = f32[4,32,24,128]{3,0,2,1:T(4,128)S(1)} async-done(((f32[4,32,24,128]{3,0,2,1:T(4,128)}), f32[4,32,24,128]{3,0,2,1:T(4,128)S(1)}, u32[]{:S(2)}, u32[]{:S(2)}) %all-to-all-start.1) | async-done | bytes 1572896 | tf_op jit(solution)/shard_map/all_to_all | solution.py:318
  196.2 15.3 %gather_fusion.2 = f32[2048,4,128]{2,1,0:T(4,128)} fusion(f32[4,768,128]{2,0,1:T(4,128)S(1)} %bitcast.283, s32[2048]{0:T(1024)S(1)} %copy-done.58), kind=kCustom, calls=%fused_computation.2 | custom fusion | bytes 8396800 | tf_op jit(solution)/shard_map/jit(_take)/gather | solution.py:325
  211.5 2.5 copy.1568
  214.0 2.8 select_select_fusion.r_ref
  216.8 14.3 %chebyshev_start.1 = (f32[4,32,64,128]{3,2,1,0:T(8,128)}, f32[4,64,128]{2,1,0:T(8,128)}, f32[4,64,128]{2,1,0:T(8,128)}, f32[4,32,1,128]{3,2,1,0:T(1,128)}, f32[4...) custom-call(f32[4,32,64,128]{3,2,1,0:T(8,128)} %select_select_fusion.r_ref, ...), custom_call_target="tpu_custom_call" | custom-call | flops 2097152 | bytes 9437184 | tf_op jit(solution)/shard_map/chebyshev_start/pallas_call | solution.py:225
  232.9 2.7 collective-permute-start.20
  240.5 4.2 %collective-permute-done.23.yhi = f32[4,32,1,128]{3,2,1,0:T(1,128)S(1)} collective-permute-done((f32[4,32,1,128]{3,2,1,0:T(1,128)}, f32[4,32,1,128]{3,2,1,0:T(1,128)S(1)}, u32[]{:S(2)}, u32[]{:S(2)}) %collective-permute-start.23) | collective-permute-done | bytes 65568 | tf_op jit(solution)/shard_map/ppermute | solution.py:107
  245.4 28.1 %chebyshev_sweep.3 = (f32[4,32,64,128]{3,2,1,0:T(8,128)}, f32[4,32,64,128]{3,2,1,0:T(8,128)}, f32[4,32,64,128]{3,2,1,0:T(8,128)}, f32[4,64,128]{2,1,0:T(8,128)},...) custom-call(f32[4,32,64,128]{3,2,1,0:T(8,128)} %get-tuple-element.32, ...), custom_call_target="tpu_custom_call" | custom-call | flops 31457280 | bytes 36700160 | tf_op jit(solution)/shard_map/chebyshev_sweep/pallas_call | solution.py:243
  275.7 4.6 %collective-permute-start.25 = (f32[4,64,128]{2,1,0:T(8,128)}, f32[4,64,128]{2,1,0:T(8,128)S(1)}, u32[]{:S(2)}, u32[]{:S(2)}) collective-permute-start(f32[4,64,128]{2,1,0:T(8,128)} %get-tuple-element.42), channel_id=1, source_target_pairs={{0,8},{8,16},{16,24},{1,9},{9,17},{17,25},{2,10},{10,18},{18,26},{... | collective-permute-start | bytes 393224 | tf_op jit(solution)/shard_map/ppermute | solution.py:107
  281.6 2.7 collective-permute-start.27
  286.5 4.2 %collective-permute-done.28.yhi = f32[4,32,1,128]{3,2,1,0:T(1,128)S(1)} collective-permute-done((f32[4,32,1,128]{3,2,1,0:T(1,128)}, f32[4,32,1,128]{3,2,1,0:T(1,128)S(1)}, u32[]{:S(2)}, u32[]{:S(2)}) %collective-permute-start.28) | collective-permute-done | bytes 65568 | tf_op jit(solution)/shard_map/ppermute | solution.py:107
  291.4 28.0 %chebyshev_sweep.4 = (f32[4,32,64,128]{3,2,1,0:T(8,128)}, f32[4,32,64,128]{3,2,1,0:T(8,128)}, f32[4,32,64,128]{3,2,1,0:T(8,128)}, f32[4,64,128]{2,1,0:T(8,128)},...) custom-call(f32[4,32,64,128]{3,2,1,0:T(8,128)} %get-tuple-element.39, ...), custom_call_target="tpu_custom_call" | custom-call | flops 31457280 | bytes 36700160 | tf_op jit(solution)/shard_map/chebyshev_sweep/pallas_call | solution.py:243
  320.4 1.8 pad_maximum_fusion
  322.1 4.9 %collective-permute-start.30 = (f32[4,64,128]{2,1,0:T(8,128)S(1)}, f32[4,64,128]{2,1,0:T(8,128)S(1)}, u32[]{:S(2)}, u32[]{:S(2)}) collective-permute-start(f32[4,64,128]{2,1,0:T(8,128)S(1)} %copy-done.93), channel_id=1, source_target_pairs={{0,8},{8,16},{16,24},{1,9},{9,17},{17,25},{2,10},{10,18},{18,26},{... | collective-permute-start | bytes 393224 | tf_op jit(solution)/shard_map/ppermute | solution.py:107
  328.4 3.5 collective-permute-start.32
  331.9 1.6 collective-permute-start.33
  334.2 3.9 %collective-permute-done.33.yhi = f32[4,32,1,128]{3,2,1,0:T(1,128)S(1)} collective-permute-done((f32[4,32,1,128]{3,2,1,0:T(1,128)S(1)}, f32[4,32,1,128]{3,2,1,0:T(1,128)S(1)}, u32[]{:S(2)}, u32[]{:S(2)}) %collective-permute-start.33) | collective-permute-done | bytes 65568 | tf_op jit(solution)/shard_map/ppermute | solution.py:107
  338.8 28.0 %chebyshev_sweep.5 = (f32[4,32,64,128]{3,2,1,0:T(8,128)}, f32[4,32,64,128]{3,2,1,0:T(8,128)}, f32[4,32,64,128]{3,2,1,0:T(8,128)}, f32[4,64,128]{2,1,0:T(8,128)},...) custom-call(f32[4,32,64,128]{3,2,1,0:T(8,128)} %get-tuple-element.48, ...), custom_call_target="tpu_custom_call" | custom-call | flops 31457280 | bytes 36700160 | tf_op jit(solution)/shard_map/chebyshev_sweep/pallas_call | solution.py:243
  366.8 7.8 %copy.1571 = f32[32,64,4,128]{3,2,1,0:T(4,128)} copy(f32[32,64,4,128]{3,1,0,2:T(8,128)} %bitcast.287) | data formatting | bytes 8388608
  (381 shorter events, 74.1 us)
Async XLA Ops:
  12.8 35.2 %copy-start = (f32[32,64,128]{2,1,0:T(8,128)}, f32[32,64,128]{2,1,0:T(8,128)S(1)}, u32[]{:S(2)}) copy-start(f32[32,64,128]{2,1,0:T(8,128)S(1)} %get-tuple-element.136) | copy-start | bytes 3145732
  12.8 36.7 %copy-start.1 = (f32[32,64,128]{2,1,0:T(8,128)}, f32[32,64,128]{2,1,0:T(8,128)S(1)}, u32[]{:S(2)}) copy-start(f32[32,64,128]{2,1,0:T(8,128)S(1)} %get-tuple-element.137) | copy-start | bytes 3145732
  15.3 55.4 %collective-permute-start.2 = (f32[5120]{0:T(1024)}, f32[5120]{0:T(1024)S(1)}, u32[]{:S(2)}, u32[]{:S(2)}) collective-permute-start(f32[5120]{0:T(1024)} %pad_maximum_fusion.4), channel_id=1, source_target_pairs={{2,0},{4,2},{6,4},{3,1},{5,3},{7,5},{10,8},{12,10},{14,12},{11,9},... | collective-permute-start | bytes 61448 | tf_op jit(solution)/shard_map/ppermute | solution.py:107
  17.2 53.6 %collective-permute-start.3 = (f32[5120]{0:T(1024)}, f32[5120]{0:T(1024)S(1)}, u32[]{:S(2)}, u32[]{:S(2)}) collective-permute-start(f32[5120]{0:T(1024)} %pad_maximum_fusion.5), channel_id=1, source_target_pairs={{0,2},{2,4},{4,6},{1,3},{3,5},{5,7},{8,10},{10,12},{12,14},{9,11},... | collective-permute-start | bytes 61448 | tf_op jit(solution)/shard_map/ppermute | solution.py:107
  23.5 47.9 %collective-permute-start.1 = (f32[12288]{0:T(1024)S(1)}, f32[12288]{0:T(1024)S(1)}, u32[]{:S(2)}, u32[]{:S(2)}) collective-permute-start(f32[12288]{0:T(1024)S(1)} %pad_maximum_fusion.3), channel_id=1, source_target_pairs={{0,8},{8,16},{16,24},{1,9},{9,17},{17,25},{2,10},{10,18},{18,26},{... | collective-permute-start | bytes 147464 | tf_op jit(solution)/shard_map/ppermute | solution.py:107
  28.0 43.4 %collective-permute-start = (f32[12288]{0:T(1024)}, f32[12288]{0:T(1024)S(1)}, u32[]{:S(2)}, u32[]{:S(2)}) collective-permute-start(f32[12288]{0:T(1024)} %pad_maximum_fusion.2), channel_id=1, source_target_pairs={{8,0},{16,8},{24,16},{9,1},{17,9},{25,17},{10,2},{18,10},{26,18},{... | collective-permute-start | bytes 147464 | tf_op jit(solution)/shard_map/ppermute | solution.py:107
  31.3 33.8 %collective-permute-start.4 = (f32[2304]{0:T(1024)}, f32[2304]{0:T(1024)}, u32[]{:S(2)}, u32[]{:S(2)}) collective-permute-start(f32[2304]{0:T(1024)} %maximum_select_fusion), channel_id=1, source_target_pairs={{0,1},{1,0},{2,3},{3,2},{4,5},{5,4},{6,7},{7,6},{8,9},{9,8},{10,11... | collective-permute-start | bytes 27656 | tf_op jit(solution)/shard_map/ppermute | solution.py:102
  41.9 16.9 %all-to-all-start = ((s32[32,1,24]{2,1,0:T(1,128)}), s32[32,1,24]{2,1,0:T(1,128)S(1)}, u32[]{:S(2)}, u32[]{:S(2)}) async-start(s32[32,1,24]{2,1,0:T(1,128)} %bitcast.116), calls=%async_computation | async-start | bytes 32768 | tf_op jit(solution)/shard_map/all_to_all | solution.py:288
  55.2 51.1 %copy-start.8 = (pred[8,32,128]{2,1,0:T(8,128)(4,1)}, pred[8,32,128]{2,1,0:T(8,128)(4,1)S(1)}, u32[]{:S(2)}) copy-start(pred[8,32,128]{2,1,0:T(8,128)(4,1)S(1)} %get-tuple-element.196) | copy-start | bytes 98308
  55.2 51.1 %copy-start.10 = (pred[8,32,128]{2,1,0:T(8,128)(4,1)}, pred[8,32,128]{2,1,0:T(8,128)(4,1)S(1)}, u32[]{:S(2)}) copy-start(pred[8,32,128]{2,1,0:T(8,128)(4,1)S(1)} %get-tuple-element.197) | copy-start | bytes 98308
  55.2 51.1 %copy-start.12 = (pred[8,32,128]{2,1,0:T(8,128)(4,1)}, pred[8,32,128]{2,1,0:T(8,128)(4,1)S(1)}, u32[]{:S(2)}) copy-start(pred[8,32,128]{2,1,0:T(8,128)(4,1)S(1)} %get-tuple-element.198) | copy-start | bytes 98308
  80.1 13.3 %collective-permute-start.9 = (f32[8,32]{1,0:T(8,128)S(1)}, f32[8,32]{1,0:T(8,128)S(1)}, u32[]{:S(2)}, u32[]{:S(2)}) collective-permute-start(f32[8,32]{1,0:T(8,128)S(1)} %fusion.10), channel_id=1, source_target_pairs={{0,1},{1,0},{2,3},{3,2},{4,5},{5,4},{6,7},{7,6},{8,9},{9,8},{10,11... | collective-permute-start | bytes 3080 | tf_op jit(solution)/shard_map/ppermute | solution.py:102
  80.4 16.4 %collective-permute-start.5 = (f32[32,128]{1,0:T(8,128)S(1)}, f32[32,128]{1,0:T(8,128)S(1)}, u32[]{:S(2)}, u32[]{:S(2)}) collective-permute-start(f32[32,128]{1,0:T(8,128)S(1)} %get-tuple-element.187), channel_id=1, source_target_pairs={{8,0},{16,8},{24,16},{9,1},{17,9},{25,17},{10,2},{18,10},{26,18},{... | collective-permute-start | bytes 49160 | tf_op jit(solution)/shard_map/ppermute | solution.py:107
  81.7 15.1 %collective-permute-start.6 = (f32[32,128]{1,0:T(8,128)S(1)}, f32[32,128]{1,0:T(8,128)S(1)}, u32[]{:S(2)}, u32[]{:S(2)}) collective-permute-start(f32[32,128]{1,0:T(8,128)S(1)} %get-tuple-element.186), channel_id=1, source_target_pairs={{0,8},{8,16},{16,24},{1,9},{9,17},{17,25},{2,10},{10,18},{18,26},{... | collective-permute-start | bytes 49160 | tf_op jit(solution)/shard_map/ppermute | solution.py:107
  86.2 10.5 %collective-permute-start.7 = (f32[8,128]{1,0:T(8,128)S(1)}, f32[8,128]{1,0:T(8,128)S(1)}, u32[]{:S(2)}, u32[]{:S(2)}) collective-permute-start(f32[8,128]{1,0:T(8,128)S(1)} %bitcast.360), channel_id=1, source_target_pairs={{2,0},{4,2},{6,4},{3,1},{5,3},{7,5},{10,8},{12,10},{14,12},{11,9},... | collective-permute-start | bytes 12296 | tf_op jit(solution)/shard_map/ppermute | solution.py:107
  87.5 9.2 %collective-permute-start.8 = (f32[8,128]{1,0:T(8,128)S(1)}, f32[8,128]{1,0:T(8,128)S(1)}, u32[]{:S(2)}, u32[]{:S(2)}) collective-permute-start(f32[8,128]{1,0:T(8,128)S(1)} %bitcast.359), channel_id=1, source_target_pairs={{0,2},{2,4},{4,6},{1,3},{3,5},{5,7},{8,10},{10,12},{12,14},{9,11},... | collective-permute-start | bytes 12296 | tf_op jit(solution)/shard_map/ppermute | solution.py:107
  106.8 13.9 %collective-permute-start.14 = (f32[8,32]{1,0:T(8,128)S(1)}, f32[8,32]{1,0:T(8,128)S(1)}, u32[]{:S(2)}, u32[]{:S(2)}) collective-permute-start(f32[8,32]{1,0:T(8,128)S(1)} %fusion.9), channel_id=1, source_target_pairs={{0,1},{1,0},{2,3},{3,2},{4,5},{5,4},{6,7},{7,6},{8,9},{9,8},{10,11... | collective-permute-start | bytes 3080 | tf_op jit(solution)/shard_map/ppermute | solution.py:102
  108.2 13.6 %collective-permute-start.10 = (f32[32,128]{1,0:T(8,128)S(1)}, f32[32,128]{1,0:T(8,128)S(1)}, u32[]{:S(2)}, u32[]{:S(2)}) collective-permute-start(f32[32,128]{1,0:T(8,128)S(1)} %get-tuple-element.171), channel_id=1, source_target_pairs={{8,0},{16,8},{24,16},{9,1},{17,9},{25,17},{10,2},{18,10},{26,18},{... | collective-permute-start | bytes 49160 | tf_op jit(solution)/shard_map/ppermute | solution.py:107
  109.5 12.3 %collective-permute-start.11 = (f32[32,128]{1,0:T(8,128)S(1)}, f32[32,128]{1,0:T(8,128)S(1)}, u32[]{:S(2)}, u32[]{:S(2)}) collective-permute-start(f32[32,128]{1,0:T(8,128)S(1)} %get-tuple-element.170), channel_id=1, source_target_pairs={{0,8},{8,16},{16,24},{1,9},{9,17},{17,25},{2,10},{10,18},{18,26},{... | collective-permute-start | bytes 49160 | tf_op jit(solution)/shard_map/ppermute | solution.py:107
  114.7 6.7 %collective-permute-start.12 = (f32[8,128]{1,0:T(8,128)S(1)}, f32[8,128]{1,0:T(8,128)S(1)}, u32[]{:S(2)}, u32[]{:S(2)}) collective-permute-start(f32[8,128]{1,0:T(8,128)S(1)} %bitcast.363), channel_id=1, source_target_pairs={{2,0},{4,2},{6,4},{3,1},{5,3},{7,5},{10,8},{12,10},{14,12},{11,9},... | collective-permute-start | bytes 12296 | tf_op jit(solution)/shard_map/ppermute | solution.py:107
  116.0 5.9 %collective-permute-start.13 = (f32[8,128]{1,0:T(8,128)S(1)}, f32[8,128]{1,0:T(8,128)S(1)}, u32[]{:S(2)}, u32[]{:S(2)}) collective-permute-start(f32[8,128]{1,0:T(8,128)S(1)} %bitcast.361), channel_id=1, source_target_pairs={{0,2},{2,4},{4,6},{1,3},{3,5},{5,7},{8,10},{10,12},{12,14},{9,11},... | collective-permute-start | bytes 12296 | tf_op jit(solution)/shard_map/ppermute | solution.py:107
  125.6 13.0 %collective-permute-start.19 = (f32[8,32]{1,0:T(8,128)S(1)}, f32[8,32]{1,0:T(8,128)S(1)}, u32[]{:S(2)}, u32[]{:S(2)}) collective-permute-start(f32[8,32]{1,0:T(8,128)S(1)} %fusion.8), channel_id=1, source_target_pairs={{0,1},{1,0},{2,3},{3,2},{4,5},{5,4},{6,7},{7,6},{8,9},{9,8},{10,11... | collective-permute-start | bytes 3080 | tf_op jit(solution)/shard_map/ppermute | solution.py:102
  125.7 14.2 %collective-permute-start.15 = (f32[32,128]{1,0:T(8,128)S(1)}, f32[32,128]{1,0:T(8,128)S(1)}, u32[]{:S(2)}, u32[]{:S(2)}) collective-permute-start(f32[32,128]{1,0:T(8,128)S(1)} %get-tuple-element.155), channel_id=1, source_target_pairs={{8,0},{16,8},{24,16},{9,1},{17,9},{25,17},{10,2},{18,10},{26,18},{... | collective-permute-start | bytes 49160 | tf_op jit(solution)/shard_map/ppermute | solution.py:107
  127.0 12.9 %collective-permute-start.16 = (f32[32,128]{1,0:T(8,128)S(1)}, f32[32,128]{1,0:T(8,128)S(1)}, u32[]{:S(2)}, u32[]{:S(2)}) collective-permute-start(f32[32,128]{1,0:T(8,128)S(1)} %get-tuple-element.154), channel_id=1, source_target_pairs={{0,8},{8,16},{16,24},{1,9},{9,17},{17,25},{2,10},{10,18},{18,26},{... | collective-permute-start | bytes 49160 | tf_op jit(solution)/shard_map/ppermute | solution.py:107
  132.5 6.4 %collective-permute-start.17 = (f32[8,128]{1,0:T(8,128)S(1)}, f32[8,128]{1,0:T(8,128)S(1)}, u32[]{:S(2)}, u32[]{:S(2)}) collective-permute-start(f32[8,128]{1,0:T(8,128)S(1)} %bitcast.364), channel_id=1, source_target_pairs={{2,0},{4,2},{6,4},{3,1},{5,3},{7,5},{10,8},{12,10},{14,12},{11,9},... | collective-permute-start | bytes 12296 | tf_op jit(solution)/shard_map/ppermute | solution.py:107
  133.8 6.1 %collective-permute-start.18 = (f32[8,128]{1,0:T(8,128)S(1)}, f32[8,128]{1,0:T(8,128)S(1)}, u32[]{:S(2)}, u32[]{:S(2)}) collective-permute-start(f32[8,128]{1,0:T(8,128)S(1)} %bitcast.362), channel_id=1, source_target_pairs={{0,2},{2,4},{4,6},{1,3},{3,5},{5,7},{8,10},{10,12},{12,14},{9,11},... | collective-permute-start | bytes 12296 | tf_op jit(solution)/shard_map/ppermute | solution.py:107
  150.0 46.2 %all-to-all-start.1 = ((f32[4,32,24,128]{3,0,2,1:T(4,128)}), f32[4,32,24,128]{3,0,2,1:T(4,128)S(1)}, u32[]{:S(2)}, u32[]{:S(2)}) async-start(f32[4,32,24,128]{3,0,2,1:T(4,128)} %select_select_fusion.1), calls=%async_computation.1 | async-start | bytes 3145728 | tf_op jit(solution)/shard_map/all_to_all | solution.py:318
  166.1 30.1 %copy-start.58 = (s32[2048]{0:T(1024)S(1)}, s32[2048]{0:T(1024)}, u32[]{:S(2)}) copy-start(s32[2048]{0:T(1024)} %fusion.84) | copy-start | bytes 24580
  232.0 7.6 %collective-permute-start.24 = (f32[4,32,64]{2,1,0:T(8,128)S(1)}, f32[4,32,64]{2,1,0:T(8,128)S(1)}, u32[]{:S(2)}, u32[]{:S(2)}) collective-permute-start(f32[4,32,64]{2,1,0:T(8,128)S(1)} %broadcast_select_fusion.8), channel_id=1, source_target_pairs={{0,1},{1,0},{2,3},{3,2},{4,5},{5,4},{6,7},{7,6},{8,9},{9,8},{10,11... | collective-permute-start | bytes 98312 | tf_op jit(solution)/shard_map/ppermute | solution.py:102
  232.9 11.7 %collective-permute-start.20 = (f32[4,64,128]{2,1,0:T(8,128)S(1)}, f32[4,64,128]{2,1,0:T(8,128)S(1)}, u32[]{:S(2)}, u32[]{:S(2)}) collective-permute-start(f32[4,64,128]{2,1,0:T(8,128)S(1)} %copy-done.95), channel_id=1, source_target_pairs={{0,8},{8,16},{16,24},{1,9},{9,17},{17,25},{2,10},{10,18},{18,26},{... | collective-permute-start | bytes 393224 | tf_op jit(solution)/shard_map/ppermute | solution.py:107
  235.7 9.0 %collective-permute-start.21 = (f32[4,64,128]{2,1,0:T(8,128)S(1)}, f32[4,64,128]{2,1,0:T(8,128)S(1)}, u32[]{:S(2)}, u32[]{:S(2)}) collective-permute-start(f32[4,64,128]{2,1,0:T(8,128)S(1)} %copy-done.94), channel_id=1, source_target_pairs={{8,0},{16,8},{24,16},{9,1},{17,9},{25,17},{10,2},{18,10},{26,18},{... | collective-permute-start | bytes 393224 | tf_op jit(solution)/shard_map/ppermute | solution.py:107
  237.0 3.5 collective-permute-start.22
  238.3 6.4 %collective-permute-start.23 = (f32[4,32,1,128]{3,2,1,0:T(1,128)}, f32[4,32,1,128]{3,2,1,0:T(1,128)S(1)}, u32[]{:S(2)}, u32[]{:S(2)}) collective-permute-start(f32[4,32,1,128]{3,2,1,0:T(1,128)} %get-tuple-element.36), channel_id=1, source_target_pairs={{2,0},{4,2},{6,4},{3,1},{5,3},{7,5},{10,8},{12,10},{14,12},{11,9},... | collective-permute-start | bytes 196616 | tf_op jit(solution)/shard_map/ppermute | solution.py:107
  245.4 29.1 %copy-start.22 = (f32[1,8,32,127]{3,2,1,0:T(8,128)S(1)}, f32[1,8,32,127]{3,2,1,0:T(8,128)}, u32[]{:S(2)}) copy-start(f32[1,8,32,127]{3,2,1,0:T(8,128)} %get-tuple-element.149) | copy-start | bytes 390148
  245.4 29.1 %copy-start.42 = (f32[32,128]{1,0:T(8,128)S(1)}, f32[32,128]{1,0:T(8,128)}, u32[]{:S(2)}) copy-start(f32[32,128]{1,0:T(8,128)} %copy-done.41) | copy-start | bytes 49156
  245.4 29.1 %copy-start.44 = (f32[32,128]{1,0:T(8,128)S(1)}, f32[32,128]{1,0:T(8,128)}, u32[]{:S(2)}) copy-start(f32[32,128]{1,0:T(8,128)} %copy-done.43) | copy-start | bytes 49156
  245.4 29.1 %copy-start.65 = (f32[8,128]{1,0:T(8,128)S(1)}, f32[8,128]{1,0:T(8,128)}, u32[]{:S(2)}) copy-start(f32[8,128]{1,0:T(8,128)} %copy-done.64) | copy-start | bytes 12292
  245.4 29.1 %copy-start.67 = (f32[8,128]{1,0:T(8,128)S(1)}, f32[8,128]{1,0:T(8,128)}, u32[]{:S(2)}) copy-start(f32[8,128]{1,0:T(8,128)} %copy-done.66) | copy-start | bytes 12292
  274.4 11.2 %collective-permute-start.29 = (f32[4,32,64]{2,1,0:T(8,128)S(1)}, f32[4,32,64]{2,1,0:T(8,128)S(1)}, u32[]{:S(2)}, u32[]{:S(2)}) collective-permute-start(f32[4,32,64]{2,1,0:T(8,128)S(1)} %broadcast_select_fusion.7), channel_id=1, source_target_pairs={{0,1},{1,0},{2,3},{3,2},{4,5},{5,4},{6,7},{7,6},{8,9},{9,8},{10,11... | collective-permute-start | bytes 98312 | tf_op jit(solution)/shard_map/ppermute | solution.py:102
  275.7 15.0 %collective-permute-start.25 = (f32[4,64,128]{2,1,0:T(8,128)}, f32[4,64,128]{2,1,0:T(8,128)S(1)}, u32[]{:S(2)}, u32[]{:S(2)}) collective-permute-start(f32[4,64,128]{2,1,0:T(8,128)} %get-tuple-element.42), channel_id=1, source_target_pairs={{0,8},{8,16},{16,24},{1,9},{9,17},{17,25},{2,10},{10,18},{18,26},{... | collective-permute-start | bytes 393224 | tf_op jit(solution)/shard_map/ppermute | solution.py:107
  280.3 10.4 %collective-permute-start.26 = (f32[4,64,128]{2,1,0:T(8,128)}, f32[4,64,128]{2,1,0:T(8,128)S(1)}, u32[]{:S(2)}, u32[]{:S(2)}) collective-permute-start(f32[4,64,128]{2,1,0:T(8,128)} %get-tuple-element.43), channel_id=1, source_target_pairs={{8,0},{16,8},{24,16},{9,1},{17,9},{25,17},{10,2},{18,10},{26,18},{... | collective-permute-start | bytes 393224 | tf_op jit(solution)/shard_map/ppermute | solution.py:107
  281.6 4.9 %collective-permute-start.27 = (f32[4,32,1,128]{3,2,1,0:T(1,128)}, f32[4,32,1,128]{3,2,1,0:T(1,128)S(1)}, u32[]{:S(2)}, u32[]{:S(2)}) collective-permute-start(f32[4,32,1,128]{3,2,1,0:T(1,128)} %get-tuple-element.44), channel_id=1, source_target_pairs={{0,2},{2,4},{4,6},{1,3},{3,5},{5,7},{8,10},{10,12},{12,14},{9,11},... | collective-permute-start | bytes 196616 | tf_op jit(solution)/shard_map/ppermute | solution.py:107
  284.3 6.4 %collective-permute-start.28 = (f32[4,32,1,128]{3,2,1,0:T(1,128)}, f32[4,32,1,128]{3,2,1,0:T(1,128)S(1)}, u32[]{:S(2)}, u32[]{:S(2)}) collective-permute-start(f32[4,32,1,128]{3,2,1,0:T(1,128)} %get-tuple-element.45), channel_id=1, source_target_pairs={{2,0},{4,2},{6,4},{3,1},{5,3},{7,5},{10,8},{12,10},{14,12},{11,9},... | collective-permute-start | bytes 196616 | tf_op jit(solution)/shard_map/ppermute | solution.py:107
  320.3 13.2 %collective-permute-start.34 = (f32[4,32,64]{2,1,0:T(8,128)S(1)}, f32[4,32,64]{2,1,0:T(8,128)S(1)}, u32[]{:S(2)}, u32[]{:S(2)}) collective-permute-start(f32[4,32,64]{2,1,0:T(8,128)S(1)} %broadcast_select_fusion.6), channel_id=1, source_target_pairs={{0,1},{1,0},{2,3},{3,2},{4,5},{5,4},{6,7},{7,6},{8,9},{9,8},{10,11... | collective-permute-start | bytes 98312 | tf_op jit(solution)/shard_map/ppermute | solution.py:102
  322.1 15.9 %collective-permute-start.30 = (f32[4,64,128]{2,1,0:T(8,128)S(1)}, f32[4,64,128]{2,1,0:T(8,128)S(1)}, u32[]{:S(2)}, u32[]{:S(2)}) collective-permute-start(f32[4,64,128]{2,1,0:T(8,128)S(1)} %copy-done.93), channel_id=1, source_target_pairs={{0,8},{8,16},{16,24},{1,9},{9,17},{17,25},{2,10},{10,18},{18,26},{... | collective-permute-start | bytes 393224 | tf_op jit(solution)/shard_map/ppermute | solution.py:107
  327.1 11.0 %collective-permute-start.31 = (f32[4,64,128]{2,1,0:T(8,128)S(1)}, f32[4,64,128]{2,1,0:T(8,128)S(1)}, u32[]{:S(2)}, u32[]{:S(2)}) collective-permute-start(f32[4,64,128]{2,1,0:T(8,128)S(1)} %copy-done.92), channel_id=1, source_target_pairs={{8,0},{16,8},{24,16},{9,1},{17,9},{25,17},{10,2},{18,10},{26,18},{... | collective-permute-start | bytes 393224 | tf_op jit(solution)/shard_map/ppermute | solution.py:107
  328.4 5.8 %collective-permute-start.32 = (f32[4,32,1,128]{3,2,1,0:T(1,128)S(1)}, f32[4,32,1,128]{3,2,1,0:T(1,128)S(1)}, u32[]{:S(2)}, u32[]{:S(2)}) collective-permute-start(f32[4,32,1,128]{3,2,1,0:T(1,128)S(1)} %copy-done.97), channel_id=1, source_target_pairs={{0,2},{2,4},{4,6},{1,3},{3,5},{5,7},{8,10},{10,12},{12,14},{9,11},... | collective-permute-start | bytes 196616 | tf_op jit(solution)/shard_map/ppermute | solution.py:107
  331.9 6.2 %collective-permute-start.33 = (f32[4,32,1,128]{3,2,1,0:T(1,128)S(1)}, f32[4,32,1,128]{3,2,1,0:T(1,128)S(1)}, u32[]{:S(2)}, u32[]{:S(2)}) collective-permute-start(f32[4,32,1,128]{3,2,1,0:T(1,128)S(1)} %copy-done.96), channel_id=1, source_target_pairs={{2,0},{4,2},{6,4},{3,1},{5,3},{7,5},{10,8},{12,10},{14,12},{11,9},... | collective-permute-start | bytes 196616 | tf_op jit(solution)/shard_map/ppermute | solution.py:107
  (90 other events, 518.5 us)

commit v3 on v2

--- a/solution.py
+++ b/solution.py
@@ -187,11 +187,24 @@
     finish_faces(columns, *face_out)
 
 
-def initial_kernel(mid, r_ref, inv_ref, d_out, *face_out):
-    nx, ny, nz = r_ref.shape[1], r_ref.shape[2], r_ref.shape[3]
+def initial_kernel(mid, rows_ref, recv_ref, inv_ref, r_out, d_out, *face_out):
+    nx, ny, nz = r_out.shape[1], r_out.shape[2], r_out.shape[3]
+    slots = rows_ref.shape[0]
+    r_out[...] = jnp.zeros(r_out.shape, jnp.float32)
+
+    def place(k, carry):
+        row = rows_ref[k]
+
+        @pl.when(row < nx * ny)
+        def _():
+            r_out[0, row // ny, pl.ds(row % ny, 1), :] = recv_ref[0, pl.ds(k, 1), :]
+
+        return carry
+
+    lax.fori_loop(0, slots, place, 0)
 
     def body(x, carry):
-        step_dir = r_ref[0, x] * inv_ref[x] * (1.0 / mid)
+        step_dir = r_out[0, x] * inv_ref[x] * (1.0 / mid)
         d_out[0, x] = step_dir
         return write_faces(x, step_dir, carry, *face_out)
 
@@ -218,20 +231,25 @@
     return full, fixed, face_specs, face_shapes
 
 
-def run_initial(mid, source, inverse):
-    full, fixed, face_specs, face_shapes = specs(source.shape)
-    shape = jax.ShapeDtypeStruct(source.shape, jnp.float32)
-    size = source.size
+def run_initial(mid, recv_rows, received, inverse):
+    steps, slots, nz = received.shape
+    nx, ny = inverse.shape[0], inverse.shape[1]
+    shape4 = (steps, nx, ny, nz)
+    full, fixed, face_specs, face_shapes = specs(shape4)
+    shape = jax.ShapeDtypeStruct(shape4, jnp.float32)
+    size = steps * nx * ny * nz
+    rows_spec = pl.BlockSpec(memory_space=pltpu.SMEM)
+    recv_spec = pl.BlockSpec((1, slots, nz), lambda s: (s, 0, 0))
     outs = pl.pallas_call(
         functools.partial(initial_kernel, mid),
-        grid=(source.shape[0],),
-        in_specs=[full, fixed],
-        out_specs=[full] + face_specs,
-        out_shape=[shape] + face_shapes,
-        cost_estimate=pl.CostEstimate(flops=2 * size, transcendentals=0, bytes_accessed=8 * size + 4 * size // source.shape[0]),
+        grid=(steps,),
+        in_specs=[rows_spec, recv_spec, fixed],
+        out_specs=[full, full] + face_specs,
+        out_shape=[shape, shape] + face_shapes,
+        cost_estimate=pl.CostEstimate(flops=2 * size, transcendentals=0, bytes_accessed=8 * size + 4 * size // steps + 4 * received.size),
         name="chebyshev_start",
-    )(source, inverse)
-    return outs[0], outs[1:]
+    )(recv_rows, received, inverse)
+    return outs[0], outs[1], outs[2:]
 
 
 def run_sweep(first, second, step_dir, residual, potential, faces, diagonal, inverse, halos):
@@ -288,9 +306,6 @@
     recv_rows = lax.all_to_all(
         send_rows.reshape(devices, capacity), ("gx", "gy", "gz"), 0, 0, tiled=True
     ).reshape(slots)
-    row_match = recv_rows[None, :] == jnp.arange(torso_rows, dtype=jnp.int32)[:, None]
-    row_used = jnp.any(row_match, axis=1)
-    row_slot = jnp.argmax(row_match, axis=1).astype(jnp.int32)
 
     sigma = []
     for dim_index in range(3):
@@ -322,8 +337,6 @@
         1,
         tiled=True,
     ).reshape(STEPS, slots, row_len)
-    source = jnp.where(row_used[None, :, None], jnp.take(received, row_slot, axis=1), 0.0)
-    source = source.reshape(STEPS, torso_x, torso_y, torso_z)
 
     faces = []
     for dim_index in range(3):
@@ -334,9 +347,8 @@
     diagonal = SCREEN + faces[0] + faces[1] + faces[2] + faces[3] + faces[4] + faces[5]
 
     spectrum_mid, first_coef, second_coef = chebyshev_weights(SWEEPS)
-    residual = source
     inverse = 1.0 / diagonal
-    step_dir, dir_faces = run_initial(spectrum_mid, residual, inverse)
+    residual, step_dir, dir_faces = run_initial(spectrum_mid, recv_rows, received, inverse)
     potential = step_dir
     for sweep in range(1, SWEEPS):
         x_low, x_high = exchange(dir_faces[1], dir_faces[0], "gx")

time: 379 us -> 439 us (1.16)
  Pallas kernels: 98.3 us -> 142 us
  starting transfers between devices: 90.8 us -> 106 us
  local copies, waits for them, and re-layouts: 73.1 us -> 82.4 us
  other arithmetic: 72.9 us -> 68.3 us
    pallas_call x1, Pallas kernels: 14.3 us -> 58.2 us  [run_initial(): pl.pallas_call(functools.partial(initial_kernel, mid), grid=(steps,), in_...]
    gather x2 -> x0, local copies, waits for them, and re-layouts: 17.7 us -> none  [local(): jnp.take(received, row_slot, axis=1)]
    ppermute x14, starting transfers between devices: 58.3 us -> 76 us  [exchange(): lax.ppermute(top, axis, forward)]
    concatenate x8, local copies, waits for them, and re-layouts: 2.43 us -> 7.12 us  [shifted(): jnp.concatenate([lax.slice_in_dim(block, 1, n, axis=dim), high], axis=dim)]
    concatenate x8, local copies, waits for them, and re-layouts: 2.42 us -> 7.02 us  [shifted(): jnp.concatenate([low, lax.slice_in_dim(block, 0, n - 1, axis=dim)], axis=...]
    unnamed x200 -> x198, local copies, waits for them, and re-layouts: 12.5 us -> 12.7 us
  transfers between devices with their start and end apart: 37 -> 37, of which waited for: 8 -> 6; matrix products, arithmetic and copies ran while one was open for 17% -> 18% of each run, Pallas kernels for 0% -> 0%
where the time goes in v3:
time: 439 us; the launch traced here: 435 us
  Pallas kernels  142 us (32%)
  starting transfers between devices  106 us (24%)
  local copies, waits for them, and re-layouts  82.4 us (19%)
  other arithmetic  68.3 us (16%)
  waiting for transfers between devices  34.6 us (8%)
    pallas_call x3, Pallas kernels, run_sweep(): pl.pallas_call(functools.partial(sweep_kernel, first, second), grid=(step...  84 us
    ppermute x14, starting transfers between devices, exchange(): lax.ppermute(top, axis, forward)  76 us
    pallas_call x1, Pallas kernels, run_initial(): pl.pallas_call(functools.partial(initial_kernel, mid), grid=(steps,), in_...  58.2 us
    all_to_all x1, waiting for transfers between devices, local(): lax.all_to_all(send_values.reshape(STEPS, devices, capacity, row_len), ('...  21.8 us
    ppermute x14, starting transfers between devices, exchange(): lax.ppermute(bottom, axis, backward)  18 us
    add x4, other arithmetic, membrane(): steady + (gate_state - steady) * jnp.exp(-DT_HEART / time_const)  15.3 us
    unnamed x198, local copies, waits for them, and re-layouts  12.7 us
    ppermute x14, waiting for transfers between devices, exchange(): lax.ppermute(bottom, axis, backward)  12.3 us
  transfers between devices with their start and end apart: 37, of which 6 were waited for; matrix products, arithmetic and copies ran while one was open for 18% of the time, Pallas kernels for 0%

profile of v3, /device:TPU:0, one launch (start us, length us, event | category | flops | bytes accessed | tf_op | source)
XLA Modules:
  0.0 435.5 jit_solution(4425839803492826274)
XLA Ops:
  0.6 1.8 fusion.117
  2.4 4.4 %select_add_fusion.1 = (f32[32,64,128]{2,1,0:T(8,128)S(1)}, pred[32,64,128]{2,1,0:T(8,128)(4,1)S(1)}, pred[32,64,128]{2,1,0:T(8,128)(4,1)S(1)}, pred[32,64,128]{2,1,0:T(8,128)(4,1)S(1)}, pred[32,64,128]{2,1,0:T(8,128)(4,1)S(1)}) fusion(f32[]{:T(128)} %bitcast.29, f32[]{:T(128)} %bitcast.28, f32[]{:T(128)} %bitcast.27, f32[]{:T(128)} %bitcast.26, ...), kind=kLoop, calls=%fused_computation.29 | loop fusion | flops 2883584 | bytes 3145744 | tf_op jit(solution)/shard_map/add | solution.py:314
  6.9 5.7 %select_add_fusion.2 = (f32[32,64,128]{2,1,0:T(8,128)S(1)}, f32[32,64,128]{2,1,0:T(8,128)S(1)}) fusion(pred[32,64,128]{2,1,0:T(8,128)(4,1)S(1)} %get-tuple-element.119, pred[32,64,128]{2,1,0:T(8,128)(4,1)S(1)} %get-tuple-element.118, pred[32,64,128]{2,1,0:T(8,128)(4,1)S(1)} %get-tuple-element.117, pred[32,64,128]{2,1,0:T(8,128)(4,1)S(1)} %get-tuple-element.116, ...), kind=kLoop, calls=%fused_computation.30 | loop fusion | flops 3670016 | bytes 3145760 | tf_op jit(solution)/shard_map/add | solution.py:314
  12.6 1.6 fusion.97
  16.7 6.1 %collective-permute-start.3 = (f32[5120]{0:T(1024)}, f32[5120]{0:T(1024)}, u32[]{:S(2)}, u32[]{:S(2)}) collective-permute-start(f32[5120]{0:T(1024)} %pad_maximum_fusion.5), channel_id=1, source_target_pairs={{0,2},{2,4},{4,6},{1,3},{3,5},{5,7},{8,10},{10,12},{12,14},{9,11},... | collective-permute-start | bytes 61448 | tf_op jit(solution)/shard_map/ppermute | solution.py:107
  24.2 3.8 collective-permute-start.1
  36.1 5.0 %gather_fusion = s32[768]{0:T(1024)S(1)} fusion(s32[256]{0:T(256)S(1)} %reshape.1858, s32[1024]{0:T(1024)S(1)} %pad_clamp_fusion), kind=kCustom, calls=%fused_computation | custom fusion | bytes 9216 | tf_op jit(solution)/shard_map/gather | solution.py:305
  41.8 6.3 %all-to-all-start = ((s32[32,1,24]{2,1,0:T(1,128)}), s32[32,1,24]{2,1,0:T(1,128)S(1)}, u32[]{:S(2)}, u32[]{:S(2)}) async-start(s32[32,1,24]{2,1,0:T(1,128)} %bitcast.116), calls=%async_computation | async-start | bytes 32768 | tf_op jit(solution)/shard_map/all_to_all | solution.py:306
  48.0 1.5 fusion.99
  49.6 1.5 fusion.100
  51.2 1.7 fusion.98
  55.5 1.5 multiply_add_fusion.3
  64.5 1.9 slice.567
  66.5 2.0 slice.568
  74.8 2.0 fusion.25
  82.3 2.8 multiply_add_fusion.2
  87.8 4.5 %collective-permute-start.6 = (f32[32,128]{1,0:T(8,128)}, f32[32,128]{1,0:T(8,128)S(1)}, u32[]{:S(2)}, u32[]{:S(2)}) collective-permute-start(f32[32,128]{1,0:T(8,128)} %get-tuple-element.186), channel_id=1, source_target_pairs={{0,8},{8,16},{16,24},{1,9},{9,17},{17,25},{2,10},{10,18},{18,26},{... | collective-permute-start | bytes 49160 | tf_op jit(solution)/shard_map/ppermute | solution.py:107
  93.6 4.8 %collective-permute-start.8 = (f32[8,128]{1,0:T(8,128)}, f32[8,128]{1,0:T(8,128)S(1)}, u32[]{:S(2)}, u32[]{:S(2)}) collective-permute-start(f32[8,128]{1,0:T(8,128)} %bitcast.52), channel_id=1, source_target_pairs={{0,2},{2,4},{4,6},{1,3},{3,5},{5,7},{8,10},{10,12},{12,14},{9,11},... | collective-permute-start | bytes 12296 | tf_op jit(solution)/shard_map/ppermute | solution.py:107
  109.9 1.5 fusion.33
  111.5 4.2 multiply_add_fusion.1
  120.1 5.7 %collective-permute-start.11 = (f32[32,128]{1,0:T(8,128)}, f32[32,128]{1,0:T(8,128)}, u32[]{:S(2)}, u32[]{:S(2)}) collective-permute-start(f32[32,128]{1,0:T(8,128)} %get-tuple-element.170), channel_id=1, source_target_pairs={{0,8},{8,16},{16,24},{1,9},{9,17},{17,25},{2,10},{10,18},{18,26},{... | collective-permute-start | bytes 49160 | tf_op jit(solution)/shard_map/ppermute | solution.py:107
  127.1 5.1 %collective-permute-start.13 = (f32[8,128]{1,0:T(8,128)}, f32[8,128]{1,0:T(8,128)}, u32[]{:S(2)}, u32[]{:S(2)}) collective-permute-start(f32[8,128]{1,0:T(8,128)} %bitcast.78), channel_id=1, source_target_pairs={{0,2},{2,4},{4,6},{1,3},{3,5},{5,7},{8,10},{10,12},{12,14},{9,11},... | collective-permute-start | bytes 12296 | tf_op jit(solution)/shard_map/ppermute | solution.py:107
  138.6 2.0 fusion.55
  145.9 5.5 %collective-permute-start.16 = (f32[32,128]{1,0:T(8,128)}, f32[32,128]{1,0:T(8,128)}, u32[]{:S(2)}, u32[]{:S(2)}) collective-permute-start(f32[32,128]{1,0:T(8,128)} %get-tuple-element.154), channel_id=1, source_target_pairs={{0,8},{8,16},{16,24},{1,9},{9,17},{17,25},{2,10},{10,18},{18,26},{... | collective-permute-start | bytes 49160 | tf_op jit(solution)/shard_map/ppermute | solution.py:107
  152.7 5.1 %collective-permute-start.18 = (f32[8,128]{1,0:T(8,128)}, f32[8,128]{1,0:T(8,128)}, u32[]{:S(2)}, u32[]{:S(2)}) collective-permute-start(f32[8,128]{1,0:T(8,128)} %bitcast.105), channel_id=1, source_target_pairs={{0,2},{2,4},{4,6},{1,3},{3,5},{5,7},{8,10},{10,12},{12,14},{9,11},... | collective-permute-start | bytes 12296 | tf_op jit(solution)/shard_map/ppermute | solution.py:107
  162.6 1.5 fusion.73
  165.4 4.2 gather_fusion.1
  169.6 2.8 fusion
  172.4 4.9 %all-to-all-start.1 = ((f32[4,32,24,128]{3,2,0,1:T(8,128)}), f32[4,32,24,128]{3,2,0,1:T(8,128)}, u32[]{:S(2)}, u32[]{:S(2)}) async-start(f32[4,32,24,128]{3,2,0,1:T(8,128)} %fusion), calls=%async_computation.1 | async-start | bytes 3145728 | tf_op jit(solution)/shard_map/all_to_all | solution.py:333
  177.3 7.0 %broadcast_divide_fusion = (f32[32,64,128]{2,1,0:T(8,128)}, f32[32,64,128]{2,1,0:T(8,128)}, f32[32,64,128]{2,1,0:T(8,128)}, f32[32,64,128]{2,1,0:T(8,128)}, f32[...) fusion(f32[32,64,128]{2,1,0:T(8,128)S(1)} %get-tuple-element.137, ...), kind=kLoop, calls=%fused_computation.36 | loop fusion | flops 6553600 | bytes 17825792 | tf_op jit(solution)/shard_map/div | solution.py:350
  187.4 6.7 %multiply_add_fusion = f32[18,8,32,128]{3,2,1,0:T(8,128)S(1)} fusion(f32[8,32,128]{2,1,0:T(8,128)S(1)} %bitcast.300, f32[18]{0:T(128)} %param.15, f32[18]{0:T(128)} %param.13, f32[18]{0:T(128)} %copy-done.88, f32[8,32,128]{2,1,0:T(8,128)} %bitcast.299, f32[8,32,128]{2,1,0:T(8,128)} %bitcast.289, f32[19,8,32,128]{3,2,1,0:T(8,128)} %param.11, ...), kind=kLoop, calls=%fused_computation.3 | loop fusion | flops 25952256 | bytes 5243096 | tf_op jit(solution)/shard_map/add | solution.py:59
  194.2 21.8 %all-to-all-done.1 = f32[4,32,24,128]{3,2,0,1:T(8,128)} async-done(((f32[4,32,24,128]{3,2,0,1:T(8,128)}), f32[4,32,24,128]{3,2,0,1:T(8,128)}, u32[]{:S(2)}, u32[]{:S(2)}) %all-to-all-start.1) | async-done | bytes 1572896 | tf_op jit(solution)/shard_map/all_to_all | solution.py:333
  215.9 2.7 copy.1571
  218.6 58.2 %chebyshev_start.1 = (f32[4,32,64,128]{3,2,1,0:T(8,128)}, f32[4,32,64,128]{3,2,1,0:T(8,128)}, f32[4,64,128]{2,1,0:T(8,128)}, f32[4,64,128]{2,1,0:T(8,128)}, f32[...) custom-call(s32[768]{0:T(1024)} %reshape.1859.rows_ref, ...), custom_call_target="tpu_custom_call" | custom-call | flops 2097152 | bytes 11010048 | tf_op jit(solution)/shard_map/chebyshev_start/pallas_call | solution.py:243
  278.6 6.9 %collective-permute-start.20 = (f32[4,64,128]{2,1,0:T(8,128)}, f32[4,64,128]{2,1,0:T(8,128)S(1)}, u32[]{:S(2)}, u32[]{:S(2)}) collective-permute-start(f32[4,64,128]{2,1,0:T(8,128)} %get-tuple-element.33), channel_id=1, source_target_pairs={{0,8},{8,16},{16,24},{1,9},{9,17},{17,25},{2,10},{10,18},{18,26},{... | collective-permute-start | bytes 393224 | tf_op jit(solution)/shard_map/ppermute | solution.py:107
  286.8 13.1 %collective-permute-start.22 = (f32[4,32,1,128]{3,2,1,0:T(1,128)}, f32[4,32,1,128]{3,2,1,0:T(1,128)S(1)}, u32[]{:S(2)}, u32[]{:S(2)}) collective-permute-start(f32[4,32,1,128]{3,2,1,0:T(1,128)} %get-tuple-element.35), channel_id=1, source_target_pairs={{0,2},{2,4},{4,6},{1,3},{3,5},{5,7},{8,10},{10,12},{12,14},{9,11},... | collective-permute-start | bytes 196616 | tf_op jit(solution)/shard_map/ppermute | solution.py:107
  302.1 4.0 collective-permute-done.23.yhi
  306.8 28.1 %chebyshev_sweep.3 = (f32[4,32,64,128]{3,2,1,0:T(8,128)}, f32[4,32,64,128]{3,2,1,0:T(8,128)}, f32[4,32,64,128]{3,2,1,0:T(8,128)}, f32[4,64,128]{2,1,0:T(8,128)},...) custom-call(f32[4,32,64,128]{3,2,1,0:T(8,128)} %get-tuple-element.31, ...), custom_call_target="tpu_custom_call" | custom-call | flops 31457280 | bytes 36700160 | tf_op jit(solution)/shard_map/chebyshev_sweep/pallas_call | solution.py:261
  337.1 4.6 %collective-permute-start.25 = (f32[4,64,128]{2,1,0:T(8,128)}, f32[4,64,128]{2,1,0:T(8,128)S(1)}, u32[]{:S(2)}, u32[]{:S(2)}) collective-permute-start(f32[4,64,128]{2,1,0:T(8,128)} %get-tuple-element.42), channel_id=1, source_target_pairs={{0,8},{8,16},{16,24},{1,9},{9,17},{17,25},{2,10},{10,18},{18,26},{... | collective-permute-start | bytes 393224 | tf_op jit(solution)/shard_map/ppermute | solution.py:107
  343.0 2.2 collective-permute-start.27
  347.4 4.2 collective-permute-done.28.yhi
  352.3 28.0 %chebyshev_sweep.4 = (f32[4,32,64,128]{3,2,1,0:T(8,128)}, f32[4,32,64,128]{3,2,1,0:T(8,128)}, f32[4,32,64,128]{3,2,1,0:T(8,128)}, f32[4,64,128]{2,1,0:T(8,128)},...) custom-call(f32[4,32,64,128]{3,2,1,0:T(8,128)} %get-tuple-element.39, ...), custom_call_target="tpu_custom_call" | custom-call | flops 31457280 | bytes 36700160 | tf_op jit(solution)/shard_map/chebyshev_sweep/pallas_call | solution.py:261
  381.2 1.8 pad_maximum_fusion
  383.0 4.7 %collective-permute-start.30 = (f32[4,64,128]{2,1,0:T(8,128)S(1)}, f32[4,64,128]{2,1,0:T(8,128)S(1)}, u32[]{:S(2)}, u32[]{:S(2)}) collective-permute-start(f32[4,64,128]{2,1,0:T(8,128)S(1)} %copy-done.93), channel_id=1, source_target_pairs={{0,8},{8,16},{16,24},{1,9},{9,17},{17,25},{2,10},{10,18},{18,26},{... | collective-permute-start | bytes 393224 | tf_op jit(solution)/shard_map/ppermute | solution.py:107
  389.1 3.7 collective-permute-start.32
  394.8 4.2 collective-permute-done.33.yhi
  399.7 28.0 %chebyshev_sweep.5 = (f32[4,32,64,128]{3,2,1,0:T(8,128)}, f32[4,32,64,128]{3,2,1,0:T(8,128)}, f32[4,32,64,128]{3,2,1,0:T(8,128)}, f32[4,64,128]{2,1,0:T(8,128)},...) custom-call(f32[4,32,64,128]{3,2,1,0:T(8,128)} %get-tuple-element.48, ...), custom_call_target="tpu_custom_call" | custom-call | flops 31457280 | bytes 36700160 | tf_op jit(solution)/shard_map/chebyshev_sweep/pallas_call | solution.py:261
  427.7 7.8 %copy.1574 = f32[32,64,4,128]{3,2,1,0:T(4,128)} copy(f32[32,64,4,128]{3,1,0,2:T(8,128)} %bitcast.283) | data formatting | bytes 8388608
  (369 shorter events, 93.9 us)
Async XLA Ops:
  14.8 55.2 %collective-permute-start.2 = (f32[5120]{0:T(1024)}, f32[5120]{0:T(1024)}, u32[]{:S(2)}, u32[]{:S(2)}) collective-permute-start(f32[5120]{0:T(1024)} %pad_maximum_fusion.4), channel_id=1, source_target_pairs={{2,0},{4,2},{6,4},{3,1},{5,3},{7,5},{10,8},{12,10},{14,12},{11,9},... | collective-permute-start | bytes 61448 | tf_op jit(solution)/shard_map/ppermute | solution.py:107
  16.7 55.5 %collective-permute-start.3 = (f32[5120]{0:T(1024)}, f32[5120]{0:T(1024)}, u32[]{:S(2)}, u32[]{:S(2)}) collective-permute-start(f32[5120]{0:T(1024)} %pad_maximum_fusion.5), channel_id=1, source_target_pairs={{0,2},{2,4},{4,6},{1,3},{3,5},{5,7},{8,10},{10,12},{12,14},{9,11},... | collective-permute-start | bytes 61448 | tf_op jit(solution)/shard_map/ppermute | solution.py:107
  24.2 50.0 %collective-permute-start.1 = (f32[12288]{0:T(1024)}, f32[12288]{0:T(1024)S(1)}, u32[]{:S(2)}, u32[]{:S(2)}) collective-permute-start(f32[12288]{0:T(1024)} %pad_maximum_fusion.3), channel_id=1, source_target_pairs={{0,8},{8,16},{16,24},{1,9},{9,17},{17,25},{2,10},{10,18},{18,26},{... | collective-permute-start | bytes 147464 | tf_op jit(solution)/shard_map/ppermute | solution.py:107
  28.7 45.5 %collective-permute-start = (f32[12288]{0:T(1024)}, f32[12288]{0:T(1024)S(1)}, u32[]{:S(2)}, u32[]{:S(2)}) collective-permute-start(f32[12288]{0:T(1024)} %pad_maximum_fusion.2), channel_id=1, source_target_pairs={{8,0},{16,8},{24,16},{9,1},{17,9},{25,17},{10,2},{18,10},{26,18},{... | collective-permute-start | bytes 147464 | tf_op jit(solution)/shard_map/ppermute | solution.py:107
  32.0 28.4 %collective-permute-start.4 = (f32[2304]{0:T(1024)}, f32[2304]{0:T(1024)}, u32[]{:S(2)}, u32[]{:S(2)}) collective-permute-start(f32[2304]{0:T(1024)} %maximum_select_fusion), channel_id=1, source_target_pairs={{0,1},{1,0},{2,3},{3,2},{4,5},{5,4},{6,7},{7,6},{8,9},{9,8},{10,11... | collective-permute-start | bytes 27656 | tf_op jit(solution)/shard_map/ppermute | solution.py:102
  41.8 17.3 %all-to-all-start = ((s32[32,1,24]{2,1,0:T(1,128)}), s32[32,1,24]{2,1,0:T(1,128)S(1)}, u32[]{:S(2)}, u32[]{:S(2)}) async-start(s32[32,1,24]{2,1,0:T(1,128)} %bitcast.116), calls=%async_computation | async-start | bytes 32768 | tf_op jit(solution)/shard_map/all_to_all | solution.py:306
  55.5 29.7 %copy-start.68 = (f32[9]{0:T(128)}, f32[9]{0:T(128)S(1)}, u32[]{:S(2)}) copy-start(f32[9]{0:T(128)S(1)} %get-tuple-element.219) | copy-start | bytes 112
  55.5 29.7 %copy-start.71 = (f32[9]{0:T(128)}, f32[9]{0:T(128)S(1)}, u32[]{:S(2)}) copy-start(f32[9]{0:T(128)S(1)} %get-tuple-element.220) | copy-start | bytes 112
  86.4 13.2 %collective-permute-start.9 = (f32[8,32]{1,0:T(8,128)S(1)}, f32[8,32]{1,0:T(8,128)S(1)}, u32[]{:S(2)}, u32[]{:S(2)}) collective-permute-start(f32[8,32]{1,0:T(8,128)S(1)} %fusion.10), channel_id=1, source_target_pairs={{0,1},{1,0},{2,3},{3,2},{4,5},{5,4},{6,7},{7,6},{8,9},{9,8},{10,11... | collective-permute-start | bytes 3080 | tf_op jit(solution)/shard_map/ppermute | solution.py:102
  86.5 17.9 %collective-permute-start.5 = (f32[32,128]{1,0:T(8,128)}, f32[32,128]{1,0:T(8,128)S(1)}, u32[]{:S(2)}, u32[]{:S(2)}) collective-permute-start(f32[32,128]{1,0:T(8,128)} %get-tuple-element.187), channel_id=1, source_target_pairs={{8,0},{16,8},{24,16},{9,1},{17,9},{25,17},{10,2},{18,10},{26,18},{... | collective-permute-start | bytes 49160 | tf_op jit(solution)/shard_map/ppermute | solution.py:107
  87.8 16.6 %collective-permute-start.6 = (f32[32,128]{1,0:T(8,128)}, f32[32,128]{1,0:T(8,128)S(1)}, u32[]{:S(2)}, u32[]{:S(2)}) collective-permute-start(f32[32,128]{1,0:T(8,128)} %get-tuple-element.186), channel_id=1, source_target_pairs={{0,8},{8,16},{16,24},{1,9},{9,17},{17,25},{2,10},{10,18},{18,26},{... | collective-permute-start | bytes 49160 | tf_op jit(solution)/shard_map/ppermute | solution.py:107
  92.3 12.0 %collective-permute-start.7 = (f32[8,128]{1,0:T(8,128)}, f32[8,128]{1,0:T(8,128)S(1)}, u32[]{:S(2)}, u32[]{:S(2)}) collective-permute-start(f32[8,128]{1,0:T(8,128)} %bitcast.50), channel_id=1, source_target_pairs={{2,0},{4,2},{6,4},{3,1},{5,3},{7,5},{10,8},{12,10},{14,12},{11,9},... | collective-permute-start | bytes 12296 | tf_op jit(solution)/shard_map/ppermute | solution.py:107
  93.6 10.7 %collective-permute-start.8 = (f32[8,128]{1,0:T(8,128)}, f32[8,128]{1,0:T(8,128)S(1)}, u32[]{:S(2)}, u32[]{:S(2)}) collective-permute-start(f32[8,128]{1,0:T(8,128)} %bitcast.52), channel_id=1, source_target_pairs={{0,2},{2,4},{4,6},{1,3},{3,5},{5,7},{8,10},{10,12},{12,14},{9,11},... | collective-permute-start | bytes 12296 | tf_op jit(solution)/shard_map/ppermute | solution.py:107
  116.4 15.9 %collective-permute-start.14 = (f32[8,32]{1,0:T(8,128)S(1)}, f32[8,32]{1,0:T(8,128)S(1)}, u32[]{:S(2)}, u32[]{:S(2)}) collective-permute-start(f32[8,32]{1,0:T(8,128)S(1)} %fusion.9), channel_id=1, source_target_pairs={{0,1},{1,0},{2,3},{3,2},{4,5},{5,4},{6,7},{7,6},{8,9},{9,8},{10,11... | collective-permute-start | bytes 3080 | tf_op jit(solution)/shard_map/ppermute | solution.py:102
  118.8 19.9 %collective-permute-start.10 = (f32[32,128]{1,0:T(8,128)}, f32[32,128]{1,0:T(8,128)S(1)}, u32[]{:S(2)}, u32[]{:S(2)}) collective-permute-start(f32[32,128]{1,0:T(8,128)} %get-tuple-element.171), channel_id=1, source_target_pairs={{8,0},{16,8},{24,16},{9,1},{17,9},{25,17},{10,2},{18,10},{26,18},{... | collective-permute-start | bytes 49160 | tf_op jit(solution)/shard_map/ppermute | solution.py:107
  120.1 18.6 %collective-permute-start.11 = (f32[32,128]{1,0:T(8,128)}, f32[32,128]{1,0:T(8,128)}, u32[]{:S(2)}, u32[]{:S(2)}) collective-permute-start(f32[32,128]{1,0:T(8,128)} %get-tuple-element.170), channel_id=1, source_target_pairs={{0,8},{8,16},{16,24},{1,9},{9,17},{17,25},{2,10},{10,18},{18,26},{... | collective-permute-start | bytes 49160 | tf_op jit(solution)/shard_map/ppermute | solution.py:107
  125.8 12.9 %collective-permute-start.12 = (f32[8,128]{1,0:T(8,128)}, f32[8,128]{1,0:T(8,128)}, u32[]{:S(2)}, u32[]{:S(2)}) collective-permute-start(f32[8,128]{1,0:T(8,128)} %bitcast.76), channel_id=1, source_target_pairs={{2,0},{4,2},{6,4},{3,1},{5,3},{7,5},{10,8},{12,10},{14,12},{11,9},... | collective-permute-start | bytes 12296 | tf_op jit(solution)/shard_map/ppermute | solution.py:107
  127.1 11.6 %collective-permute-start.13 = (f32[8,128]{1,0:T(8,128)}, f32[8,128]{1,0:T(8,128)}, u32[]{:S(2)}, u32[]{:S(2)}) collective-permute-start(f32[8,128]{1,0:T(8,128)} %bitcast.78), channel_id=1, source_target_pairs={{0,2},{2,4},{4,6},{1,3},{3,5},{5,7},{8,10},{10,12},{12,14},{9,11},... | collective-permute-start | bytes 12296 | tf_op jit(solution)/shard_map/ppermute | solution.py:107
  144.0 13.9 %collective-permute-start.19 = (f32[8,32]{1,0:T(8,128)S(1)}, f32[8,32]{1,0:T(8,128)S(1)}, u32[]{:S(2)}, u32[]{:S(2)}) collective-permute-start(f32[8,32]{1,0:T(8,128)S(1)} %fusion.8), channel_id=1, source_target_pairs={{0,1},{1,0},{2,3},{3,2},{4,5},{5,4},{6,7},{7,6},{8,9},{9,8},{10,11... | collective-permute-start | bytes 3080 | tf_op jit(solution)/shard_map/ppermute | solution.py:102
  144.6 16.7 %collective-permute-start.15 = (f32[32,128]{1,0:T(8,128)}, f32[32,128]{1,0:T(8,128)}, u32[]{:S(2)}, u32[]{:S(2)}) collective-permute-start(f32[32,128]{1,0:T(8,128)} %get-tuple-element.155), channel_id=1, source_target_pairs={{8,0},{16,8},{24,16},{9,1},{17,9},{25,17},{10,2},{18,10},{26,18},{... | collective-permute-start | bytes 49160 | tf_op jit(solution)/shard_map/ppermute | solution.py:107
  145.9 15.5 %collective-permute-start.16 = (f32[32,128]{1,0:T(8,128)}, f32[32,128]{1,0:T(8,128)}, u32[]{:S(2)}, u32[]{:S(2)}) collective-permute-start(f32[32,128]{1,0:T(8,128)} %get-tuple-element.154), channel_id=1, source_target_pairs={{0,8},{8,16},{16,24},{1,9},{9,17},{17,25},{2,10},{10,18},{18,26},{... | collective-permute-start | bytes 49160 | tf_op jit(solution)/shard_map/ppermute | solution.py:107
  151.4 10.0 %collective-permute-start.17 = (f32[8,128]{1,0:T(8,128)}, f32[8,128]{1,0:T(8,128)}, u32[]{:S(2)}, u32[]{:S(2)}) collective-permute-start(f32[8,128]{1,0:T(8,128)} %bitcast.102), channel_id=1, source_target_pairs={{2,0},{4,2},{6,4},{3,1},{5,3},{7,5},{10,8},{12,10},{14,12},{11,9},... | collective-permute-start | bytes 12296 | tf_op jit(solution)/shard_map/ppermute | solution.py:107
  152.7 8.7 %collective-permute-start.18 = (f32[8,128]{1,0:T(8,128)}, f32[8,128]{1,0:T(8,128)}, u32[]{:S(2)}, u32[]{:S(2)}) collective-permute-start(f32[8,128]{1,0:T(8,128)} %bitcast.105), channel_id=1, source_target_pairs={{0,2},{2,4},{4,6},{1,3},{3,5},{5,7},{8,10},{10,12},{12,14},{9,11},... | collective-permute-start | bytes 12296 | tf_op jit(solution)/shard_map/ppermute | solution.py:107
  172.4 43.5 %all-to-all-start.1 = ((f32[4,32,24,128]{3,2,0,1:T(8,128)}), f32[4,32,24,128]{3,2,0,1:T(8,128)}, u32[]{:S(2)}, u32[]{:S(2)}) async-start(f32[4,32,24,128]{3,2,0,1:T(8,128)} %fusion), calls=%async_computation.1 | async-start | bytes 3145728 | tf_op jit(solution)/shard_map/all_to_all | solution.py:333
  194.1 83.7 %copy-start.18 = (pred[8,32,128]{2,1,0:T(8,128)(4,1)S(1)}, pred[8,32,128]{2,1,0:T(8,128)(4,1)}, u32[]{:S(2)}) copy-start(pred[8,32,128]{2,1,0:T(8,128)(4,1)} %copy-done.15) | copy-start | bytes 98308
  194.1 83.7 %copy-start.22 = (pred[8,32,128]{2,1,0:T(8,128)(4,1)S(1)}, pred[8,32,128]{2,1,0:T(8,128)(4,1)}, u32[]{:S(2)}) copy-start(pred[8,32,128]{2,1,0:T(8,128)(4,1)} %copy-done.19) | copy-start | bytes 98308
  194.1 83.7 %copy-start.26 = (pred[8,32,128]{2,1,0:T(8,128)(4,1)S(1)}, pred[8,32,128]{2,1,0:T(8,128)(4,1)}, u32[]{:S(2)}) copy-start(pred[8,32,128]{2,1,0:T(8,128)(4,1)} %copy-done.23) | copy-start | bytes 98308
  194.1 83.7 %copy-start.70 = (f32[9]{0:T(128)S(1)}, f32[9]{0:T(128)}, u32[]{:S(2)}) copy-start(f32[9]{0:T(128)} %copy-done.68) | copy-start | bytes 112
  194.1 83.7 %copy-start.73 = (f32[9]{0:T(128)S(1)}, f32[9]{0:T(128)}, u32[]{:S(2)}) copy-start(f32[9]{0:T(128)} %copy-done.71) | copy-start | bytes 112
  194.1 83.7 %copy-start.76 = (f32[9]{0:T(128)S(1)}, f32[9]{0:T(128)}, u32[]{:S(2)}) copy-start(f32[9]{0:T(128)} %copy-done.74) | copy-start | bytes 112
  194.1 83.7 %copy-start.80 = (f32[9]{0:T(128)S(1)}, f32[9]{0:T(128)}, u32[]{:S(2)}) copy-start(f32[9]{0:T(128)} %param.17) | copy-start | bytes 112
  218.6 59.7 %copy-start.59 = (f32[8,32]{1,0:T(8,128)S(1)}, f32[8,32]{1,0:T(8,128)}, u32[]{:S(2)}) copy-start(f32[8,32]{1,0:T(8,128)} %get-tuple-element.214) | copy-start | bytes 3076
  218.6 59.9 %copy-start.58 = (f32[8,32]{1,0:T(8,128)S(1)}, f32[8,32]{1,0:T(8,128)}, u32[]{:S(2)}) copy-start(f32[8,32]{1,0:T(8,128)} %get-tuple-element.213) | copy-start | bytes 3076
  277.7 23.6 %collective-permute-start.24 = (f32[4,32,64]{2,1,0:T(8,128)S(1)}, f32[4,32,64]{2,1,0:T(8,128)S(1)}, u32[]{:S(2)}, u32[]{:S(2)}) collective-permute-start(f32[4,32,64]{2,1,0:T(8,128)S(1)} %broadcast_select_fusion.8), channel_id=1, source_target_pairs={{0,1},{1,0},{2,3},{3,2},{4,5},{5,4},{6,7},{7,6},{8,9},{9,8},{10,11... | collective-permute-start | bytes 98312 | tf_op jit(solution)/shard_map/ppermute | solution.py:102
  278.6 27.5 %collective-permute-start.20 = (f32[4,64,128]{2,1,0:T(8,128)}, f32[4,64,128]{2,1,0:T(8,128)S(1)}, u32[]{:S(2)}, u32[]{:S(2)}) collective-permute-start(f32[4,64,128]{2,1,0:T(8,128)} %get-tuple-element.33), channel_id=1, source_target_pairs={{0,8},{8,16},{16,24},{1,9},{9,17},{17,25},{2,10},{10,18},{18,26},{... | collective-permute-start | bytes 393224 | tf_op jit(solution)/shard_map/ppermute | solution.py:107
  285.5 20.6 %collective-permute-start.21 = (f32[4,64,128]{2,1,0:T(8,128)}, f32[4,64,128]{2,1,0:T(8,128)S(1)}, u32[]{:S(2)}, u32[]{:S(2)}) collective-permute-start(f32[4,64,128]{2,1,0:T(8,128)} %get-tuple-element.34), channel_id=1, source_target_pairs={{8,0},{16,8},{24,16},{9,1},{17,9},{25,17},{10,2},{18,10},{26,18},{... | collective-permute-start | bytes 393224 | tf_op jit(solution)/shard_map/ppermute | solution.py:107
  286.8 15.3 %collective-permute-start.22 = (f32[4,32,1,128]{3,2,1,0:T(1,128)}, f32[4,32,1,128]{3,2,1,0:T(1,128)S(1)}, u32[]{:S(2)}, u32[]{:S(2)}) collective-permute-start(f32[4,32,1,128]{3,2,1,0:T(1,128)} %get-tuple-element.35), channel_id=1, source_target_pairs={{0,2},{2,4},{4,6},{1,3},{3,5},{5,7},{8,10},{10,12},{12,14},{9,11},... | collective-permute-start | bytes 196616 | tf_op jit(solution)/shard_map/ppermute | solution.py:107
  299.9 6.2 %collective-permute-start.23 = (f32[4,32,1,128]{3,2,1,0:T(1,128)S(1)}, f32[4,32,1,128]{3,2,1,0:T(1,128)S(1)}, u32[]{:S(2)}, u32[]{:S(2)}) collective-permute-start(f32[4,32,1,128]{3,2,1,0:T(1,128)S(1)} %copy-done.95), channel_id=1, source_target_pairs={{2,0},{4,2},{6,4},{3,1},{5,3},{7,5},{10,8},{12,10},{14,12},{11,9},... | collective-permute-start | bytes 196616 | tf_op jit(solution)/shard_map/ppermute | solution.py:107
  335.8 10.7 %collective-permute-start.29 = (f32[4,32,64]{2,1,0:T(8,128)S(1)}, f32[4,32,64]{2,1,0:T(8,128)S(1)}, u32[]{:S(2)}, u32[]{:S(2)}) collective-permute-start(f32[4,32,64]{2,1,0:T(8,128)S(1)} %broadcast_select_fusion.7), channel_id=1, source_target_pairs={{0,1},{1,0},{2,3},{3,2},{4,5},{5,4},{6,7},{7,6},{8,9},{9,8},{10,11... | collective-permute-start | bytes 98312 | tf_op jit(solution)/shard_map/ppermute | solution.py:102
  337.1 14.5 %collective-permute-start.25 = (f32[4,64,128]{2,1,0:T(8,128)}, f32[4,64,128]{2,1,0:T(8,128)S(1)}, u32[]{:S(2)}, u32[]{:S(2)}) collective-permute-start(f32[4,64,128]{2,1,0:T(8,128)} %get-tuple-element.42), channel_id=1, source_target_pairs={{0,8},{8,16},{16,24},{1,9},{9,17},{17,25},{2,10},{10,18},{18,26},{... | collective-permute-start | bytes 393224 | tf_op jit(solution)/shard_map/ppermute | solution.py:107
  341.7 9.9 %collective-permute-start.26 = (f32[4,64,128]{2,1,0:T(8,128)}, f32[4,64,128]{2,1,0:T(8,128)S(1)}, u32[]{:S(2)}, u32[]{:S(2)}) collective-permute-start(f32[4,64,128]{2,1,0:T(8,128)} %get-tuple-element.43), channel_id=1, source_target_pairs={{8,0},{16,8},{24,16},{9,1},{17,9},{25,17},{10,2},{18,10},{26,18},{... | collective-permute-start | bytes 393224 | tf_op jit(solution)/shard_map/ppermute | solution.py:107
  343.0 4.4 %collective-permute-start.27 = (f32[4,32,1,128]{3,2,1,0:T(1,128)}, f32[4,32,1,128]{3,2,1,0:T(1,128)S(1)}, u32[]{:S(2)}, u32[]{:S(2)}) collective-permute-start(f32[4,32,1,128]{3,2,1,0:T(1,128)} %get-tuple-element.44), channel_id=1, source_target_pairs={{0,2},{2,4},{4,6},{1,3},{3,5},{5,7},{8,10},{10,12},{12,14},{9,11},... | collective-permute-start | bytes 196616 | tf_op jit(solution)/shard_map/ppermute | solution.py:107
  345.2 6.4 %collective-permute-start.28 = (f32[4,32,1,128]{3,2,1,0:T(1,128)}, f32[4,32,1,128]{3,2,1,0:T(1,128)S(1)}, u32[]{:S(2)}, u32[]{:S(2)}) collective-permute-start(f32[4,32,1,128]{3,2,1,0:T(1,128)} %get-tuple-element.45), channel_id=1, source_target_pairs={{2,0},{4,2},{6,4},{3,1},{5,3},{7,5},{10,8},{12,10},{14,12},{11,9},... | collective-permute-start | bytes 196616 | tf_op jit(solution)/shard_map/ppermute | solution.py:107
  381.1 13.0 %collective-permute-start.34 = (f32[4,32,64]{2,1,0:T(8,128)S(1)}, f32[4,32,64]{2,1,0:T(8,128)S(1)}, u32[]{:S(2)}, u32[]{:S(2)}) collective-permute-start(f32[4,32,64]{2,1,0:T(8,128)S(1)} %broadcast_select_fusion.6), channel_id=1, source_target_pairs={{0,1},{1,0},{2,3},{3,2},{4,5},{5,4},{6,7},{7,6},{8,9},{9,8},{10,11... | collective-permute-start | bytes 98312 | tf_op jit(solution)/shard_map/ppermute | solution.py:102
  383.0 16.0 %collective-permute-start.30 = (f32[4,64,128]{2,1,0:T(8,128)S(1)}, f32[4,64,128]{2,1,0:T(8,128)S(1)}, u32[]{:S(2)}, u32[]{:S(2)}) collective-permute-start(f32[4,64,128]{2,1,0:T(8,128)S(1)} %copy-done.93), channel_id=1, source_target_pairs={{0,8},{8,16},{16,24},{1,9},{9,17},{17,25},{2,10},{10,18},{18,26},{... | collective-permute-start | bytes 393224 | tf_op jit(solution)/shard_map/ppermute | solution.py:107
  387.8 11.2 %collective-permute-start.31 = (f32[4,64,128]{2,1,0:T(8,128)S(1)}, f32[4,64,128]{2,1,0:T(8,128)S(1)}, u32[]{:S(2)}, u32[]{:S(2)}) collective-permute-start(f32[4,64,128]{2,1,0:T(8,128)S(1)} %copy-done.92), channel_id=1, source_target_pairs={{8,0},{16,8},{24,16},{9,1},{17,9},{25,17},{10,2},{18,10},{26,18},{... | collective-permute-start | bytes 393224 | tf_op jit(solution)/shard_map/ppermute | solution.py:107
  389.1 5.7 %collective-permute-start.32 = (f32[4,32,1,128]{3,2,1,0:T(1,128)S(1)}, f32[4,32,1,128]{3,2,1,0:T(1,128)S(1)}, u32[]{:S(2)}, u32[]{:S(2)}) collective-permute-start(f32[4,32,1,128]{3,2,1,0:T(1,128)S(1)} %copy-done.96), channel_id=1, source_target_pairs={{0,2},{2,4},{4,6},{1,3},{3,5},{5,7},{8,10},{10,12},{12,14},{9,11},... | collective-permute-start | bytes 196616 | tf_op jit(solution)/shard_map/ppermute | solution.py:107
  392.8 6.2 %collective-permute-start.33 = (f32[4,32,1,128]{3,2,1,0:T(1,128)S(1)}, f32[4,32,1,128]{3,2,1,0:T(1,128)S(1)}, u32[]{:S(2)}, u32[]{:S(2)}) collective-permute-start(f32[4,32,1,128]{3,2,1,0:T(1,128)S(1)} %copy-done.94), channel_id=1, source_target_pairs={{2,0},{4,2},{6,4},{3,1},{5,3},{7,5},{10,8},{12,10},{14,12},{11,9},... | collective-permute-start | bytes 196616 | tf_op jit(solution)/shard_map/ppermute | solution.py:107
  (87 other events, 511.8 us)

commit v4 on v2

--- a/solution.py
+++ b/solution.py
@@ -122,81 +122,93 @@
     return result
 
 
-def write_faces(x, value, columns, xf_lo, xf_hi, yf_lo, yf_hi, zf_lo, zf_hi):
+def group_faces(x, g, step, columns, lane, xf_lo, xf_hi, yf_lo, yf_hi):
     nx = yf_lo.shape[1]
-    ny, nz = value.shape
+    groups = xf_lo.shape[1] // 8
+    nz = step.shape[1]
     half = nz // 2
-    lane = lax.broadcasted_iota(jnp.int32, (ny, nz), 1)
-
-    @pl.when(x == 0)
-    def _():
-        xf_lo[0] = value
-
-    @pl.when(x == nx - 1)
-    def _():
-        xf_hi[0] = value
-
-    yf_lo[0, x] = value[0:1, :]
-    yf_hi[0, x] = value[ny - 1:ny, :]
-    columns = jnp.where(lane == x, jnp.broadcast_to(value[:, 0:1], (ny, nz)), columns)
-    columns = jnp.where(lane == half + x, jnp.broadcast_to(value[:, nz - 1:nz], (ny, nz)), columns)
-    return columns
-
-
-def finish_faces(columns, xf_lo, xf_hi, yf_lo, yf_hi, zf_lo, zf_hi):
-    nx = yf_lo.shape[1]
-    half = columns.shape[1] // 2
-    flipped = columns.T
+    rows = pl.ds(8 * g, 8)
+
+    if g == 0:
+        yf_lo[0, x] = step[0:1, :]
+    if g == groups - 1:
+        yf_hi[0, x] = step[7:8, :]
+    columns = jnp.where(lane == x, jnp.broadcast_to(step[:, 0:1], step.shape), columns)
+    return jnp.where(lane == half + x, jnp.broadcast_to(step[:, nz - 1:nz], step.shape), columns)
+
+
+def finish_faces(d_out, xf_lo, xf_hi, col_scr, zf_lo, zf_hi):
+    nx = zf_lo.shape[1]
+    xf_lo[0] = d_out[0, 0]
+    xf_hi[0] = d_out[0, nx - 1]
+    half = col_scr.shape[1] // 2
+    flipped = col_scr[...].T
     zf_lo[0] = flipped[0:nx, :]
     zf_hi[0] = flipped[half:half + nx, :]
 
 
 def sweep_kernel(first, second, d_ref, r_ref, p_ref, fxp, fxm, fyp, fym, fzp, fzm, dg_ref, inv_ref,
-                 xlo, xhi, ylo, yhi, zlo, zhi, r_out, d_out, p_out, *face_out):
+                 xlo, xhi, ylo, yhi, zlo, zhi, r_out, d_out, p_out, xf_lo, xf_hi, yf_lo, yf_hi,
+                 zf_lo, zf_hi, low_scr, high_scr, col_scr):
     nx, ny, nz = d_ref.shape[1], d_ref.shape[2], d_ref.shape[3]
-    row = lax.broadcasted_iota(jnp.int32, (ny, nz), 0)
-    lane = lax.broadcasted_iota(jnp.int32, (ny, nz), 1)
+    groups = ny // 8
+    sub = lax.broadcasted_iota(jnp.int32, (8, nz), 0)
+    lane = lax.broadcasted_iota(jnp.int32, (8, nz), 1)
     blank = jnp.zeros((nz - nx, ny), jnp.float32)
-    low_cols = jnp.concatenate([zlo[0], blank], axis=0).T
+    low_scr[...] = jnp.concatenate([zlo[0], blank], axis=0).T
     high_rows = zhi[0]
-    high_cols = jnp.concatenate([high_rows[1:nx], blank, high_rows[0:1]], axis=0).T
+    high_scr[...] = jnp.concatenate([high_rows[1:nx], blank, high_rows[0:1]], axis=0).T
+    col_scr[...] = jnp.zeros(col_scr.shape, jnp.float32)
 
     def body(x, carry):
-        centre = d_ref[0, x]
-        below = d_ref[0, jnp.maximum(x - 1, 0)]
-        above = d_ref[0, jnp.minimum(x + 1, nx - 1)]
-        x_minus = jnp.where(x == 0, xlo[0], below)
-        x_plus = jnp.where(x == nx - 1, xhi[0], above)
-        y_minus = jnp.where(row == 0, ylo[0, x], pltpu.roll(centre, 1, 0))
-        y_plus = jnp.where(row == ny - 1, yhi[0, x], pltpu.roll(centre, ny - 1, 0))
         turn = lax.rem(nz - x, nz)
-        z_minus = jnp.where(lane == 0, pltpu.roll(low_cols, turn, 1), pltpu.roll(centre, 1, 1))
-        z_plus = jnp.where(lane == nz - 1, pltpu.roll(high_cols, turn, 1), pltpu.roll(centre, nz - 1, 1))
-        beside = fxp[x] * x_plus + fxm[x] * x_minus
-        beside = beside + fyp[x] * y_plus + fym[x] * y_minus
-        beside = beside + fzp[x] * z_plus + fzm[x] * z_minus
-        diag = dg_ref[x]
-        residual = r_ref[0, x] - (diag * centre - beside)
-        step_dir = first * centre + second * (residual * inv_ref[x])
-        r_out[0, x] = residual
-        d_out[0, x] = step_dir
-        p_out[0, x] = p_ref[0, x] + step_dir
-        return write_faces(x, step_dir, carry, *face_out)
-
-    columns = lax.fori_loop(0, nx, body, jnp.zeros((ny, nz), jnp.float32), unroll=2)
-    finish_faces(columns, *face_out)
-
-
-def initial_kernel(mid, r_ref, inv_ref, d_out, *face_out):
+        below = jnp.maximum(x - 1, 0)
+        above = jnp.minimum(x + 1, nx - 1)
+        cs = [d_ref[0, x, pl.ds(8 * g, 8), :] for g in range(groups)]
+        r1 = [pltpu.roll(c, 1, 0) for c in cs]
+        r7 = [pltpu.roll(c, 7, 0) for c in cs]
+        for g in range(groups):
+            rows = pl.ds(8 * g, 8)
+            centre = cs[g]
+            x_minus = jnp.where(x == 0, xlo[0, rows], d_ref[0, below, rows])
+            x_plus = jnp.where(x == nx - 1, xhi[0, rows], d_ref[0, above, rows])
+            up = ylo[0, x] if g == 0 else r1[g - 1]
+            down = yhi[0, x] if g == groups - 1 else r7[g + 1]
+            y_minus = jnp.where(sub == 0, up, r1[g])
+            y_plus = jnp.where(sub == 7, down, r7[g])
+            z_minus = jnp.where(lane == 0, pltpu.roll(low_scr[rows], turn, 1), pltpu.roll(centre, 1, 1))
+            z_plus = jnp.where(lane == nz - 1, pltpu.roll(high_scr[rows], turn, 1), pltpu.roll(centre, nz - 1, 1))
+            beside = fxp[x, rows] * x_plus + fxm[x, rows] * x_minus
+            beside = beside + fyp[x, rows] * y_plus + fym[x, rows] * y_minus
+            beside = beside + fzp[x, rows] * z_plus + fzm[x, rows] * z_minus
+            residual = r_ref[0, x, rows] - (dg_ref[x, rows] * centre - beside)
+            step_dir = first * centre + second * (residual * inv_ref[x, rows])
+            r_out[0, x, rows] = residual
+            d_out[0, x, rows] = step_dir
+            p_out[0, x, rows] = p_ref[0, x, rows] + step_dir
+            col_scr[rows] = group_faces(x, g, step_dir, col_scr[rows], lane, xf_lo, xf_hi, yf_lo, yf_hi)
+        return carry
+
+    lax.fori_loop(0, nx, body, 0)
+    finish_faces(d_out, xf_lo, xf_hi, col_scr, zf_lo, zf_hi)
+
+
+def initial_kernel(mid, r_ref, inv_ref, d_out, xf_lo, xf_hi, yf_lo, yf_hi, zf_lo, zf_hi, col_scr):
     nx, ny, nz = r_ref.shape[1], r_ref.shape[2], r_ref.shape[3]
+    groups = ny // 8
+    lane = lax.broadcasted_iota(jnp.int32, (8, nz), 1)
+    col_scr[...] = jnp.zeros(col_scr.shape, jnp.float32)
 
     def body(x, carry):
-        step_dir = r_ref[0, x] * inv_ref[x] * (1.0 / mid)
-        d_out[0, x] = step_dir
-        return write_faces(x, step_dir, carry, *face_out)
-
-    columns = lax.fori_loop(0, nx, body, jnp.zeros((ny, nz), jnp.float32), unroll=2)
-    finish_faces(columns, *face_out)
+        for g in range(groups):
+            rows = pl.ds(8 * g, 8)
+            step_dir = r_ref[0, x, rows] * inv_ref[x, rows] * (1.0 / mid)
+            d_out[0, x, rows] = step_dir
+            col_scr[rows] = group_faces(x, g, step_dir, col_scr[rows], lane, xf_lo, xf_hi, yf_lo, yf_hi)
+        return carry
+
+    lax.fori_loop(0, nx, body, 0)
+    finish_faces(d_out, xf_lo, xf_hi, col_scr, zf_lo, zf_hi)
 
 
 def specs(shape):
@@ -229,6 +241,7 @@
         out_specs=[full] + face_specs,
         out_shape=[shape] + face_shapes,
         cost_estimate=pl.CostEstimate(flops=2 * size, transcendentals=0, bytes_accessed=8 * size + 4 * size // source.shape[0]),
+        scratch_shapes=[pltpu.VMEM((source.shape[2], source.shape[3]), jnp.float32)],
         name="chebyshev_start",
     )(source, inverse)
     return outs[0], outs[1:]
@@ -247,6 +260,7 @@
         out_specs=[full, full, full] + face_specs,
         out_shape=[shape, shape, shape] + face_shapes,
         cost_estimate=pl.CostEstimate(flops=30 * size, transcendentals=0, bytes_accessed=4 * 7 * size + 4 * 7 * size // steps),
+        scratch_shapes=[pltpu.VMEM((ny, nz), jnp.float32)] * 3,
         name="chebyshev_sweep",
     )(step_dir, residual, potential, *faces, diagonal, inverse, *halos)
     return outs[0], outs[1], outs[2], outs[3:]

time: 379 us -> 389 us (1.026)
  Pallas kernels: 98.3 us -> 108 us
    pallas_call x3, Pallas kernels: 84 us -> 94.2 us  [run_sweep(): pl.pallas_call(functools.partial(sweep_kernel, first, second), grid=(step...]
where the time goes in v4:
time: 389 us; the launch traced here: 385 us
  Pallas kernels  108 us (28%)
  starting transfers between devices  90.8 us (23%)
  local copies, waits for them, and re-layouts  73.1 us (19%)
  other arithmetic  72.9 us (19%)
  waiting for transfers between devices  36.8 us (9%)
    pallas_call x3, Pallas kernels, run_sweep(): pl.pallas_call(functools.partial(sweep_kernel, first, second), grid=(step...  94.2 us
    ppermute x14, starting transfers between devices, exchange(): lax.ppermute(top, axis, forward)  58.4 us
    all_to_all x1, waiting for transfers between devices, local(): lax.all_to_all(send_values.reshape(STEPS, devices, capacity, row_len), ('...  22.6 us
    ppermute x14, starting transfers between devices, exchange(): lax.ppermute(bottom, axis, backward)  18.3 us
    gather x2, local copies, waits for them, and re-layouts, local(): jnp.take(received, row_slot, axis=1)  17.7 us
    add x4, other arithmetic, membrane(): steady + (gate_state - steady) * jnp.exp(-DT_HEART / time_const)  16.1 us
    pallas_call x1, Pallas kernels, run_initial(): pl.pallas_call(functools.partial(initial_kernel, mid), grid=(source.shape...  14.2 us
    unnamed x200, local copies, waits for them, and re-layouts  12.5 us
  transfers between devices with their start and end apart: 37, of which 8 were waited for; matrix products, arithmetic and copies ran while one was open for 17% of the time, Pallas kernels for 0%

profile of v4, /device:TPU:0, one launch (start us, length us, event | category | flops | bytes accessed | tf_op | source)
XLA Modules:
  0.0 384.7 jit_solution(12994592858487153668)
XLA Ops:
  0.6 1.8 fusion.118
  2.4 4.6 %select_add_fusion.1 = (f32[32,64,128]{2,1,0:T(8,128)S(1)}, pred[32,64,128]{2,1,0:T(8,128)(4,1)S(1)}, pred[32,64,128]{2,1,0:T(8,128)(4,1)S(1)}, pred[32,64,128]{2,1,0:T(8,128)(4,1)S(1)}, pred[32,64,128]{2,1,0:T(8,128)(4,1)S(1)}) fusion(f32[]{:T(128)} %bitcast.29, f32[]{:T(128)} %bitcast.28, f32[]{:T(128)} %bitcast.27, f32[]{:T(128)} %bitcast.26, ...), kind=kLoop, calls=%fused_computation.33 | loop fusion | flops 2883584 | bytes 3145744 | tf_op jit(solution)/shard_map/add | solution.py:313
  7.0 5.8 %select_add_fusion.2 = (f32[32,64,128]{2,1,0:T(8,128)S(1)}, f32[32,64,128]{2,1,0:T(8,128)S(1)}) fusion(pred[32,64,128]{2,1,0:T(8,128)(4,1)S(1)} %get-tuple-element.119, pred[32,64,128]{2,1,0:T(8,128)(4,1)S(1)} %get-tuple-element.118, pred[32,64,128]{2,1,0:T(8,128)(4,1)S(1)} %get-tuple-element.117, pred[32,64,128]{2,1,0:T(8,128)(4,1)S(1)} %get-tuple-element.116, ...), kind=kLoop, calls=%fused_computation.34 | loop fusion | flops 3670016 | bytes 3145760 | tf_op jit(solution)/shard_map/add | solution.py:313
  12.9 1.8 fusion.98
  17.2 5.5 %collective-permute-start.3 = (f32[5120]{0:T(1024)}, f32[5120]{0:T(1024)S(1)}, u32[]{:S(2)}, u32[]{:S(2)}) collective-permute-start(f32[5120]{0:T(1024)} %pad_maximum_fusion.5), channel_id=1, source_target_pairs={{0,2},{2,4},{4,6},{1,3},{3,5},{5,7},{8,10},{10,12},{12,14},{9,11},... | collective-permute-start | bytes 61448 | tf_op jit(solution)/shard_map/ppermute | solution.py:107
  23.5 3.8 collective-permute-start.1
  36.2 5.0 %gather_fusion = s32[768]{0:T(1024)S(1)} fusion(s32[256]{0:T(256)S(1)} %reshape.1868, s32[1024]{0:T(1024)S(1)} %pad_clamp_fusion), kind=kCustom, calls=%fused_computation | custom fusion | bytes 9216 | tf_op jit(solution)/shard_map/gather | solution.py:301
  41.9 6.1 %all-to-all-start = ((s32[32,1,24]{2,1,0:T(1,128)}), s32[32,1,24]{2,1,0:T(1,128)S(1)}, u32[]{:S(2)}, u32[]{:S(2)}) async-start(s32[32,1,24]{2,1,0:T(1,128)} %bitcast.116), calls=%async_computation | async-start | bytes 32768 | tf_op jit(solution)/shard_map/all_to_all | solution.py:302
  48.0 1.5 fusion.100
  49.5 1.6 fusion.101
  51.1 1.7 fusion.99
  55.3 1.5 multiply_add_fusion.3
  59.6 2.8 iota_reduce_fusion
  66.6 1.9 slice.567
  68.5 1.9 slice.568
  76.7 2.8 multiply_add_fusion.2
  81.7 4.5 %collective-permute-start.6 = (f32[32,128]{1,0:T(8,128)S(1)}, f32[32,128]{1,0:T(8,128)S(1)}, u32[]{:S(2)}, u32[]{:S(2)}) collective-permute-start(f32[32,128]{1,0:T(8,128)S(1)} %get-tuple-element.186), channel_id=1, source_target_pairs={{0,8},{8,16},{16,24},{1,9},{9,17},{17,25},{2,10},{10,18},{18,26},{... | collective-permute-start | bytes 49160 | tf_op jit(solution)/shard_map/ppermute | solution.py:107
  87.5 4.5 %collective-permute-start.8 = (f32[8,128]{1,0:T(8,128)S(1)}, f32[8,128]{1,0:T(8,128)S(1)}, u32[]{:S(2)}, u32[]{:S(2)}) collective-permute-start(f32[8,128]{1,0:T(8,128)S(1)} %bitcast.359), channel_id=1, source_target_pairs={{0,2},{2,4},{4,6},{1,3},{3,5},{5,7},{8,10},{10,12},{12,14},{9,11},... | collective-permute-start | bytes 12296 | tf_op jit(solution)/shard_map/ppermute | solution.py:107
  100.6 1.4 fusion.33
  102.1 4.2 %multiply_add_fusion.1 = f32[18,8,32,128]{3,2,1,0:T(8,128)S(1)} fusion(f32[8,32,128]{2,1,0:T(8,128)S(1)} %bitcast.301, f32[18]{0:T(128)S(1)} %copy-done.84, f32[18]{0:T(128)S(1)} %copy-done.87, f32[18]{0:T(128)S(1)} %copy-done.90, f32[8,32,128]{2,1,0:T(8,128)S(1)} %bitcast.293, f32[19,8,32,128]{3,2,1,0:T(8,128)S(1)} %copy-done.4, ...), kind=kLoop, calls=%fused_computation.9 | loop fusion | flops 19464192 | bytes 5112024 | tf_op jit(solution)/shard_map/add | solution.py:59
  109.5 5.1 %collective-permute-start.11 = (f32[32,128]{1,0:T(8,128)S(1)}, f32[32,128]{1,0:T(8,128)S(1)}, u32[]{:S(2)}, u32[]{:S(2)}) collective-permute-start(f32[32,128]{1,0:T(8,128)S(1)} %get-tuple-element.170), channel_id=1, source_target_pairs={{0,8},{8,16},{16,24},{1,9},{9,17},{17,25},{2,10},{10,18},{18,26},{... | collective-permute-start | bytes 49160 | tf_op jit(solution)/shard_map/ppermute | solution.py:107
  116.0 4.8 %collective-permute-start.13 = (f32[8,128]{1,0:T(8,128)S(1)}, f32[8,128]{1,0:T(8,128)S(1)}, u32[]{:S(2)}, u32[]{:S(2)}) collective-permute-start(f32[8,128]{1,0:T(8,128)S(1)} %bitcast.361), channel_id=1, source_target_pairs={{0,2},{2,4},{4,6},{1,3},{3,5},{5,7},{8,10},{10,12},{12,14},{9,11},... | collective-permute-start | bytes 12296 | tf_op jit(solution)/shard_map/ppermute | solution.py:107
  127.0 5.4 %collective-permute-start.16 = (f32[32,128]{1,0:T(8,128)S(1)}, f32[32,128]{1,0:T(8,128)S(1)}, u32[]{:S(2)}, u32[]{:S(2)}) collective-permute-start(f32[32,128]{1,0:T(8,128)S(1)} %get-tuple-element.154), channel_id=1, source_target_pairs={{0,8},{8,16},{16,24},{1,9},{9,17},{17,25},{2,10},{10,18},{18,26},{... | collective-permute-start | bytes 49160 | tf_op jit(solution)/shard_map/ppermute | solution.py:107
  133.8 4.8 %collective-permute-start.18 = (f32[8,128]{1,0:T(8,128)S(1)}, f32[8,128]{1,0:T(8,128)S(1)}, u32[]{:S(2)}, u32[]{:S(2)}) collective-permute-start(f32[8,128]{1,0:T(8,128)S(1)} %bitcast.362), channel_id=1, source_target_pairs={{0,2},{2,4},{4,6},{1,3},{3,5},{5,7},{8,10},{10,12},{12,14},{9,11},... | collective-permute-start | bytes 12296 | tf_op jit(solution)/shard_map/ppermute | solution.py:107
  142.1 3.0 gather_fusion.1
  145.1 4.9 %select_select_fusion.1 = f32[4,32,24,128]{3,0,2,1:T(4,128)} fusion(f32[4,32,24,128]{3,0,2,1:T(4,128)S(1)} %bitcast.286, pred[32,24]{1,0:T(8,128)(4,1)} %broadcast_in_dim.362, pred[32,24]{1,0:T(8,128)(4,1)} %broadcast_in_dim.360), kind=kLoop, calls=%fused_computation.12 | loop fusion | flops 786432 | bytes 3147264 | tf_op jit(solution)/shard_map/jit(_where)/select_n | solution.py:331
  150.0 7.4 %all-to-all-start.1 = ((f32[4,32,24,128]{3,0,2,1:T(4,128)}), f32[4,32,24,128]{3,0,2,1:T(4,128)S(1)}, u32[]{:S(2)}, u32[]{:S(2)}) async-start(f32[4,32,24,128]{3,0,2,1:T(4,128)} %select_select_fusion.1), calls=%async_computation.1 | async-start | bytes 3145728 | tf_op jit(solution)/shard_map/all_to_all | solution.py:332
  157.4 7.0 %broadcast_divide_fusion = (f32[32,64,128]{2,1,0:T(8,128)}, f32[32,64,128]{2,1,0:T(8,128)}, f32[32,64,128]{2,1,0:T(8,128)}, f32[32,64,128]{2,1,0:T(8,128)}, f32[...) fusion(f32[32,64,128]{2,1,0:T(8,128)} %copy-done.1, ...), kind=kLoop, calls=%fused_computation.40 | loop fusion | flops 6553600 | bytes 17825792 | tf_op jit(solution)/shard_map/div | solution.py:352
  166.1 7.5 %multiply_add_fusion = f32[18,8,32,128]{3,2,1,0:T(8,128)} fusion(f32[8,32,128]{2,1,0:T(8,128)S(1)} %bitcast.304, f32[18]{0:T(128)} %param.15, f32[18]{0:T(128)} %param.13, f32[18]{0:T(128)} %copy-done.88, f32[8,32,128]{2,1,0:T(8,128)S(1)} %bitcast.303, f32[8,32,128]{2,1,0:T(8,128)S(1)} %bitcast.294, f32[19,8,32,128]{3,2,1,0:T(8,128)} %param.11, ...), kind=kLoop, calls=%fused_computation.8 | loop fusion | flops 25952256 | bytes 5243096 | tf_op jit(solution)/shard_map/add | solution.py:59
  173.6 22.6 %all-to-all-done.1 = f32[4,32,24,128]{3,0,2,1:T(4,128)S(1)} async-done(((f32[4,32,24,128]{3,0,2,1:T(4,128)}), f32[4,32,24,128]{3,0,2,1:T(4,128)S(1)}, u32[]{:S(2)}, u32[]{:S(2)}) %all-to-all-start.1) | async-done | bytes 1572896 | tf_op jit(solution)/shard_map/all_to_all | solution.py:332
  196.2 15.2 %gather_fusion.2 = f32[2048,4,128]{2,1,0:T(4,128)} fusion(f32[4,768,128]{2,0,1:T(4,128)S(1)} %bitcast.283, s32[2048]{0:T(1024)S(1)} %copy-done.58), kind=kCustom, calls=%fused_computation.2 | custom fusion | bytes 8396800 | tf_op jit(solution)/shard_map/jit(_take)/gather | solution.py:339
  211.5 2.5 copy.1568
  214.0 2.8 select_select_fusion.r_ref
  216.8 14.2 %chebyshev_start.1 = (f32[4,32,64,128]{3,2,1,0:T(8,128)}, f32[4,64,128]{2,1,0:T(8,128)}, f32[4,64,128]{2,1,0:T(8,128)}, f32[4,32,1,128]{3,2,1,0:T(1,128)}, f32[4...) custom-call(f32[4,32,64,128]{3,2,1,0:T(8,128)} %select_select_fusion.r_ref, ...), custom_call_target="tpu_custom_call" | custom-call | flops 2097152 | bytes 9437184 | tf_op jit(solution)/shard_map/chebyshev_start/pallas_call | solution.py:237
  232.9 2.7 collective-permute-start.20
  240.4 4.2 %collective-permute-done.23.yhi = f32[4,32,1,128]{3,2,1,0:T(1,128)S(1)} collective-permute-done((f32[4,32,1,128]{3,2,1,0:T(1,128)}, f32[4,32,1,128]{3,2,1,0:T(1,128)S(1)}, u32[]{:S(2)}, u32[]{:S(2)}) %collective-permute-start.23) | collective-permute-done | bytes 65568 | tf_op jit(solution)/shard_map/ppermute | solution.py:107
  245.4 31.5 %chebyshev_sweep.3 = (f32[4,32,64,128]{3,2,1,0:T(8,128)}, f32[4,32,64,128]{3,2,1,0:T(8,128)}, f32[4,32,64,128]{3,2,1,0:T(8,128)}, f32[4,64,128]{2,1,0:T(8,128)},...) custom-call(f32[4,32,64,128]{3,2,1,0:T(8,128)} %get-tuple-element.32, ...), custom_call_target="tpu_custom_call" | custom-call | flops 31457280 | bytes 36700160 | tf_op jit(solution)/shard_map/chebyshev_sweep/pallas_call | solution.py:256
  279.0 4.6 %collective-permute-start.25 = (f32[4,64,128]{2,1,0:T(8,128)}, f32[4,64,128]{2,1,0:T(8,128)S(1)}, u32[]{:S(2)}, u32[]{:S(2)}) collective-permute-start(f32[4,64,128]{2,1,0:T(8,128)} %get-tuple-element.42), channel_id=1, source_target_pairs={{0,8},{8,16},{16,24},{1,9},{9,17},{17,25},{2,10},{10,18},{18,26},{... | collective-permute-start | bytes 393224 | tf_op jit(solution)/shard_map/ppermute | solution.py:107
  284.9 2.8 collective-permute-start.27
  289.9 4.2 %collective-permute-done.28.yhi = f32[4,32,1,128]{3,2,1,0:T(1,128)S(1)} collective-permute-done((f32[4,32,1,128]{3,2,1,0:T(1,128)}, f32[4,32,1,128]{3,2,1,0:T(1,128)S(1)}, u32[]{:S(2)}, u32[]{:S(2)}) %collective-permute-start.28) | collective-permute-done | bytes 65568 | tf_op jit(solution)/shard_map/ppermute | solution.py:107
  294.8 31.4 %chebyshev_sweep.4 = (f32[4,32,64,128]{3,2,1,0:T(8,128)}, f32[4,32,64,128]{3,2,1,0:T(8,128)}, f32[4,32,64,128]{3,2,1,0:T(8,128)}, f32[4,64,128]{2,1,0:T(8,128)},...) custom-call(f32[4,32,64,128]{3,2,1,0:T(8,128)} %get-tuple-element.39, ...), custom_call_target="tpu_custom_call" | custom-call | flops 31457280 | bytes 36700160 | tf_op jit(solution)/shard_map/chebyshev_sweep/pallas_call | solution.py:256
  327.1 1.8 pad_maximum_fusion
  328.9 4.9 %collective-permute-start.30 = (f32[4,64,128]{2,1,0:T(8,128)S(1)}, f32[4,64,128]{2,1,0:T(8,128)S(1)}, u32[]{:S(2)}, u32[]{:S(2)}) collective-permute-start(f32[4,64,128]{2,1,0:T(8,128)S(1)} %copy-done.93), channel_id=1, source_target_pairs={{0,8},{8,16},{16,24},{1,9},{9,17},{17,25},{2,10},{10,18},{18,26},{... | collective-permute-start | bytes 393224 | tf_op jit(solution)/shard_map/ppermute | solution.py:107
  335.1 3.5 collective-permute-start.32
  338.7 1.6 collective-permute-start.33
  340.9 3.9 %collective-permute-done.33.yhi = f32[4,32,1,128]{3,2,1,0:T(1,128)S(1)} collective-permute-done((f32[4,32,1,128]{3,2,1,0:T(1,128)S(1)}, f32[4,32,1,128]{3,2,1,0:T(1,128)S(1)}, u32[]{:S(2)}, u32[]{:S(2)}) %collective-permute-start.33) | collective-permute-done | bytes 65568 | tf_op jit(solution)/shard_map/ppermute | solution.py:107
  345.6 31.4 %chebyshev_sweep.5 = (f32[4,32,64,128]{3,2,1,0:T(8,128)}, f32[4,32,64,128]{3,2,1,0:T(8,128)}, f32[4,32,64,128]{3,2,1,0:T(8,128)}, f32[4,64,128]{2,1,0:T(8,128)},...) custom-call(f32[4,32,64,128]{3,2,1,0:T(8,128)} %get-tuple-element.48, ...), custom_call_target="tpu_custom_call" | custom-call | flops 31457280 | bytes 36700160 | tf_op jit(solution)/shard_map/chebyshev_sweep/pallas_call | solution.py:256
  376.9 7.8 %copy.1571 = f32[32,64,4,128]{3,2,1,0:T(4,128)} copy(f32[32,64,4,128]{3,1,0,2:T(8,128)} %bitcast.287) | data formatting | bytes 8388608
  (381 shorter events, 74.1 us)
Async XLA Ops:
  12.8 35.2 %copy-start = (f32[32,64,128]{2,1,0:T(8,128)}, f32[32,64,128]{2,1,0:T(8,128)S(1)}, u32[]{:S(2)}) copy-start(f32[32,64,128]{2,1,0:T(8,128)S(1)} %get-tuple-element.136) | copy-start | bytes 3145732
  12.8 36.7 %copy-start.1 = (f32[32,64,128]{2,1,0:T(8,128)}, f32[32,64,128]{2,1,0:T(8,128)S(1)}, u32[]{:S(2)}) copy-start(f32[32,64,128]{2,1,0:T(8,128)S(1)} %get-tuple-element.137) | copy-start | bytes 3145732
  15.3 55.4 %collective-permute-start.2 = (f32[5120]{0:T(1024)}, f32[5120]{0:T(1024)S(1)}, u32[]{:S(2)}, u32[]{:S(2)}) collective-permute-start(f32[5120]{0:T(1024)} %pad_maximum_fusion.4), channel_id=1, source_target_pairs={{2,0},{4,2},{6,4},{3,1},{5,3},{7,5},{10,8},{12,10},{14,12},{11,9},... | collective-permute-start | bytes 61448 | tf_op jit(solution)/shard_map/ppermute | solution.py:107
  17.2 53.6 %collective-permute-start.3 = (f32[5120]{0:T(1024)}, f32[5120]{0:T(1024)S(1)}, u32[]{:S(2)}, u32[]{:S(2)}) collective-permute-start(f32[5120]{0:T(1024)} %pad_maximum_fusion.5), channel_id=1, source_target_pairs={{0,2},{2,4},{4,6},{1,3},{3,5},{5,7},{8,10},{10,12},{12,14},{9,11},... | collective-permute-start | bytes 61448 | tf_op jit(solution)/shard_map/ppermute | solution.py:107
  23.5 47.9 %collective-permute-start.1 = (f32[12288]{0:T(1024)S(1)}, f32[12288]{0:T(1024)S(1)}, u32[]{:S(2)}, u32[]{:S(2)}) collective-permute-start(f32[12288]{0:T(1024)S(1)} %pad_maximum_fusion.3), channel_id=1, source_target_pairs={{0,8},{8,16},{16,24},{1,9},{9,17},{17,25},{2,10},{10,18},{18,26},{... | collective-permute-start | bytes 147464 | tf_op jit(solution)/shard_map/ppermute | solution.py:107
  28.0 43.4 %collective-permute-start = (f32[12288]{0:T(1024)}, f32[12288]{0:T(1024)S(1)}, u32[]{:S(2)}, u32[]{:S(2)}) collective-permute-start(f32[12288]{0:T(1024)} %pad_maximum_fusion.2), channel_id=1, source_target_pairs={{8,0},{16,8},{24,16},{9,1},{17,9},{25,17},{10,2},{18,10},{26,18},{... | collective-permute-start | bytes 147464 | tf_op jit(solution)/shard_map/ppermute | solution.py:107
  31.3 33.8 %collective-permute-start.4 = (f32[2304]{0:T(1024)}, f32[2304]{0:T(1024)}, u32[]{:S(2)}, u32[]{:S(2)}) collective-permute-start(f32[2304]{0:T(1024)} %maximum_select_fusion), channel_id=1, source_target_pairs={{0,1},{1,0},{2,3},{3,2},{4,5},{5,4},{6,7},{7,6},{8,9},{9,8},{10,11... | collective-permute-start | bytes 27656 | tf_op jit(solution)/shard_map/ppermute | solution.py:102
  41.9 16.9 %all-to-all-start = ((s32[32,1,24]{2,1,0:T(1,128)}), s32[32,1,24]{2,1,0:T(1,128)S(1)}, u32[]{:S(2)}, u32[]{:S(2)}) async-start(s32[32,1,24]{2,1,0:T(1,128)} %bitcast.116), calls=%async_computation | async-start | bytes 32768 | tf_op jit(solution)/shard_map/all_to_all | solution.py:302
  55.2 51.1 %copy-start.8 = (pred[8,32,128]{2,1,0:T(8,128)(4,1)}, pred[8,32,128]{2,1,0:T(8,128)(4,1)S(1)}, u32[]{:S(2)}) copy-start(pred[8,32,128]{2,1,0:T(8,128)(4,1)S(1)} %get-tuple-element.196) | copy-start | bytes 98308
  55.2 51.1 %copy-start.10 = (pred[8,32,128]{2,1,0:T(8,128)(4,1)}, pred[8,32,128]{2,1,0:T(8,128)(4,1)S(1)}, u32[]{:S(2)}) copy-start(pred[8,32,128]{2,1,0:T(8,128)(4,1)S(1)} %get-tuple-element.197) | copy-start | bytes 98308
  55.2 51.1 %copy-start.12 = (pred[8,32,128]{2,1,0:T(8,128)(4,1)}, pred[8,32,128]{2,1,0:T(8,128)(4,1)S(1)}, u32[]{:S(2)}) copy-start(pred[8,32,128]{2,1,0:T(8,128)(4,1)S(1)} %get-tuple-element.198) | copy-start | bytes 98308
  80.1 13.3 %collective-permute-start.9 = (f32[8,32]{1,0:T(8,128)S(1)}, f32[8,32]{1,0:T(8,128)S(1)}, u32[]{:S(2)}, u32[]{:S(2)}) collective-permute-start(f32[8,32]{1,0:T(8,128)S(1)} %fusion.10), channel_id=1, source_target_pairs={{0,1},{1,0},{2,3},{3,2},{4,5},{5,4},{6,7},{7,6},{8,9},{9,8},{10,11... | collective-permute-start | bytes 3080 | tf_op jit(solution)/shard_map/ppermute | solution.py:102
  80.4 16.4 %collective-permute-start.5 = (f32[32,128]{1,0:T(8,128)S(1)}, f32[32,128]{1,0:T(8,128)S(1)}, u32[]{:S(2)}, u32[]{:S(2)}) collective-permute-start(f32[32,128]{1,0:T(8,128)S(1)} %get-tuple-element.187), channel_id=1, source_target_pairs={{8,0},{16,8},{24,16},{9,1},{17,9},{25,17},{10,2},{18,10},{26,18},{... | collective-permute-start | bytes 49160 | tf_op jit(solution)/shard_map/ppermute | solution.py:107
  81.7 15.1 %collective-permute-start.6 = (f32[32,128]{1,0:T(8,128)S(1)}, f32[32,128]{1,0:T(8,128)S(1)}, u32[]{:S(2)}, u32[]{:S(2)}) collective-permute-start(f32[32,128]{1,0:T(8,128)S(1)} %get-tuple-element.186), channel_id=1, source_target_pairs={{0,8},{8,16},{16,24},{1,9},{9,17},{17,25},{2,10},{10,18},{18,26},{... | collective-permute-start | bytes 49160 | tf_op jit(solution)/shard_map/ppermute | solution.py:107
  86.2 10.5 %collective-permute-start.7 = (f32[8,128]{1,0:T(8,128)S(1)}, f32[8,128]{1,0:T(8,128)S(1)}, u32[]{:S(2)}, u32[]{:S(2)}) collective-permute-start(f32[8,128]{1,0:T(8,128)S(1)} %bitcast.360), channel_id=1, source_target_pairs={{2,0},{4,2},{6,4},{3,1},{5,3},{7,5},{10,8},{12,10},{14,12},{11,9},... | collective-permute-start | bytes 12296 | tf_op jit(solution)/shard_map/ppermute | solution.py:107
  87.5 9.2 %collective-permute-start.8 = (f32[8,128]{1,0:T(8,128)S(1)}, f32[8,128]{1,0:T(8,128)S(1)}, u32[]{:S(2)}, u32[]{:S(2)}) collective-permute-start(f32[8,128]{1,0:T(8,128)S(1)} %bitcast.359), channel_id=1, source_target_pairs={{0,2},{2,4},{4,6},{1,3},{3,5},{5,7},{8,10},{10,12},{12,14},{9,11},... | collective-permute-start | bytes 12296 | tf_op jit(solution)/shard_map/ppermute | solution.py:107
  106.8 13.9 %collective-permute-start.14 = (f32[8,32]{1,0:T(8,128)S(1)}, f32[8,32]{1,0:T(8,128)S(1)}, u32[]{:S(2)}, u32[]{:S(2)}) collective-permute-start(f32[8,32]{1,0:T(8,128)S(1)} %fusion.9), channel_id=1, source_target_pairs={{0,1},{1,0},{2,3},{3,2},{4,5},{5,4},{6,7},{7,6},{8,9},{9,8},{10,11... | collective-permute-start | bytes 3080 | tf_op jit(solution)/shard_map/ppermute | solution.py:102
  108.2 13.6 %collective-permute-start.10 = (f32[32,128]{1,0:T(8,128)S(1)}, f32[32,128]{1,0:T(8,128)S(1)}, u32[]{:S(2)}, u32[]{:S(2)}) collective-permute-start(f32[32,128]{1,0:T(8,128)S(1)} %get-tuple-element.171), channel_id=1, source_target_pairs={{8,0},{16,8},{24,16},{9,1},{17,9},{25,17},{10,2},{18,10},{26,18},{... | collective-permute-start | bytes 49160 | tf_op jit(solution)/shard_map/ppermute | solution.py:107
  109.5 12.3 %collective-permute-start.11 = (f32[32,128]{1,0:T(8,128)S(1)}, f32[32,128]{1,0:T(8,128)S(1)}, u32[]{:S(2)}, u32[]{:S(2)}) collective-permute-start(f32[32,128]{1,0:T(8,128)S(1)} %get-tuple-element.170), channel_id=1, source_target_pairs={{0,8},{8,16},{16,24},{1,9},{9,17},{17,25},{2,10},{10,18},{18,26},{... | collective-permute-start | bytes 49160 | tf_op jit(solution)/shard_map/ppermute | solution.py:107
  114.7 6.7 %collective-permute-start.12 = (f32[8,128]{1,0:T(8,128)S(1)}, f32[8,128]{1,0:T(8,128)S(1)}, u32[]{:S(2)}, u32[]{:S(2)}) collective-permute-start(f32[8,128]{1,0:T(8,128)S(1)} %bitcast.363), channel_id=1, source_target_pairs={{2,0},{4,2},{6,4},{3,1},{5,3},{7,5},{10,8},{12,10},{14,12},{11,9},... | collective-permute-start | bytes 12296 | tf_op jit(solution)/shard_map/ppermute | solution.py:107
  116.0 5.9 %collective-permute-start.13 = (f32[8,128]{1,0:T(8,128)S(1)}, f32[8,128]{1,0:T(8,128)S(1)}, u32[]{:S(2)}, u32[]{:S(2)}) collective-permute-start(f32[8,128]{1,0:T(8,128)S(1)} %bitcast.361), channel_id=1, source_target_pairs={{0,2},{2,4},{4,6},{1,3},{3,5},{5,7},{8,10},{10,12},{12,14},{9,11},... | collective-permute-start | bytes 12296 | tf_op jit(solution)/shard_map/ppermute | solution.py:107
  125.6 13.0 %collective-permute-start.19 = (f32[8,32]{1,0:T(8,128)S(1)}, f32[8,32]{1,0:T(8,128)S(1)}, u32[]{:S(2)}, u32[]{:S(2)}) collective-permute-start(f32[8,32]{1,0:T(8,128)S(1)} %fusion.8), channel_id=1, source_target_pairs={{0,1},{1,0},{2,3},{3,2},{4,5},{5,4},{6,7},{7,6},{8,9},{9,8},{10,11... | collective-permute-start | bytes 3080 | tf_op jit(solution)/shard_map/ppermute | solution.py:102
  125.7 14.2 %collective-permute-start.15 = (f32[32,128]{1,0:T(8,128)S(1)}, f32[32,128]{1,0:T(8,128)S(1)}, u32[]{:S(2)}, u32[]{:S(2)}) collective-permute-start(f32[32,128]{1,0:T(8,128)S(1)} %get-tuple-element.155), channel_id=1, source_target_pairs={{8,0},{16,8},{24,16},{9,1},{17,9},{25,17},{10,2},{18,10},{26,18},{... | collective-permute-start | bytes 49160 | tf_op jit(solution)/shard_map/ppermute | solution.py:107
  127.0 12.9 %collective-permute-start.16 = (f32[32,128]{1,0:T(8,128)S(1)}, f32[32,128]{1,0:T(8,128)S(1)}, u32[]{:S(2)}, u32[]{:S(2)}) collective-permute-start(f32[32,128]{1,0:T(8,128)S(1)} %get-tuple-element.154), channel_id=1, source_target_pairs={{0,8},{8,16},{16,24},{1,9},{9,17},{17,25},{2,10},{10,18},{18,26},{... | collective-permute-start | bytes 49160 | tf_op jit(solution)/shard_map/ppermute | solution.py:107
  132.5 6.4 %collective-permute-start.17 = (f32[8,128]{1,0:T(8,128)S(1)}, f32[8,128]{1,0:T(8,128)S(1)}, u32[]{:S(2)}, u32[]{:S(2)}) collective-permute-start(f32[8,128]{1,0:T(8,128)S(1)} %bitcast.364), channel_id=1, source_target_pairs={{2,0},{4,2},{6,4},{3,1},{5,3},{7,5},{10,8},{12,10},{14,12},{11,9},... | collective-permute-start | bytes 12296 | tf_op jit(solution)/shard_map/ppermute | solution.py:107
  133.8 6.1 %collective-permute-start.18 = (f32[8,128]{1,0:T(8,128)S(1)}, f32[8,128]{1,0:T(8,128)S(1)}, u32[]{:S(2)}, u32[]{:S(2)}) collective-permute-start(f32[8,128]{1,0:T(8,128)S(1)} %bitcast.362), channel_id=1, source_target_pairs={{0,2},{2,4},{4,6},{1,3},{3,5},{5,7},{8,10},{10,12},{12,14},{9,11},... | collective-permute-start | bytes 12296 | tf_op jit(solution)/shard_map/ppermute | solution.py:107
  150.0 46.2 %all-to-all-start.1 = ((f32[4,32,24,128]{3,0,2,1:T(4,128)}), f32[4,32,24,128]{3,0,2,1:T(4,128)S(1)}, u32[]{:S(2)}, u32[]{:S(2)}) async-start(f32[4,32,24,128]{3,0,2,1:T(4,128)} %select_select_fusion.1), calls=%async_computation.1 | async-start | bytes 3145728 | tf_op jit(solution)/shard_map/all_to_all | solution.py:332
  232.0 7.6 %collective-permute-start.24 = (f32[4,32,64]{2,1,0:T(8,128)S(1)}, f32[4,32,64]{2,1,0:T(8,128)S(1)}, u32[]{:S(2)}, u32[]{:S(2)}) collective-permute-start(f32[4,32,64]{2,1,0:T(8,128)S(1)} %broadcast_select_fusion.8), channel_id=1, source_target_pairs={{0,1},{1,0},{2,3},{3,2},{4,5},{5,4},{6,7},{7,6},{8,9},{9,8},{10,11... | collective-permute-start | bytes 98312 | tf_op jit(solution)/shard_map/ppermute | solution.py:102
  232.9 11.7 %collective-permute-start.20 = (f32[4,64,128]{2,1,0:T(8,128)S(1)}, f32[4,64,128]{2,1,0:T(8,128)S(1)}, u32[]{:S(2)}, u32[]{:S(2)}) collective-permute-start(f32[4,64,128]{2,1,0:T(8,128)S(1)} %copy-done.95), channel_id=1, source_target_pairs={{0,8},{8,16},{16,24},{1,9},{9,17},{17,25},{2,10},{10,18},{18,26},{... | collective-permute-start | bytes 393224 | tf_op jit(solution)/shard_map/ppermute | solution.py:107
  235.6 9.0 %collective-permute-start.21 = (f32[4,64,128]{2,1,0:T(8,128)S(1)}, f32[4,64,128]{2,1,0:T(8,128)S(1)}, u32[]{:S(2)}, u32[]{:S(2)}) collective-permute-start(f32[4,64,128]{2,1,0:T(8,128)S(1)} %copy-done.94), channel_id=1, source_target_pairs={{8,0},{16,8},{24,16},{9,1},{17,9},{25,17},{10,2},{18,10},{26,18},{... | collective-permute-start | bytes 393224 | tf_op jit(solution)/shard_map/ppermute | solution.py:107
  236.9 3.5 collective-permute-start.22
  238.2 6.4 %collective-permute-start.23 = (f32[4,32,1,128]{3,2,1,0:T(1,128)}, f32[4,32,1,128]{3,2,1,0:T(1,128)S(1)}, u32[]{:S(2)}, u32[]{:S(2)}) collective-permute-start(f32[4,32,1,128]{3,2,1,0:T(1,128)} %get-tuple-element.36), channel_id=1, source_target_pairs={{2,0},{4,2},{6,4},{3,1},{5,3},{7,5},{10,8},{12,10},{14,12},{11,9},... | collective-permute-start | bytes 196616 | tf_op jit(solution)/shard_map/ppermute | solution.py:107
  245.3 32.5 %copy-start.21 = (f32[1,8,31,128]{3,2,1,0:T(8,128)S(1)}, f32[1,8,31,128]{3,2,1,0:T(8,128)}, u32[]{:S(2)}) copy-start(f32[1,8,31,128]{3,2,1,0:T(8,128)} %get-tuple-element.142) | copy-start | bytes 380932
  245.3 32.5 %copy-start.22 = (f32[1,8,32,127]{3,2,1,0:T(8,128)S(1)}, f32[1,8,32,127]{3,2,1,0:T(8,128)}, u32[]{:S(2)}) copy-start(f32[1,8,32,127]{3,2,1,0:T(8,128)} %get-tuple-element.149) | copy-start | bytes 390148
  245.3 32.5 %copy-start.42 = (f32[32,128]{1,0:T(8,128)S(1)}, f32[32,128]{1,0:T(8,128)}, u32[]{:S(2)}) copy-start(f32[32,128]{1,0:T(8,128)} %copy-done.41) | copy-start | bytes 49156
  245.3 32.5 %copy-start.44 = (f32[32,128]{1,0:T(8,128)S(1)}, f32[32,128]{1,0:T(8,128)}, u32[]{:S(2)}) copy-start(f32[32,128]{1,0:T(8,128)} %copy-done.43) | copy-start | bytes 49156
  245.4 32.5 %copy-start.65 = (f32[8,128]{1,0:T(8,128)S(1)}, f32[8,128]{1,0:T(8,128)}, u32[]{:S(2)}) copy-start(f32[8,128]{1,0:T(8,128)} %copy-done.64) | copy-start | bytes 12292
  245.4 32.5 %copy-start.67 = (f32[8,128]{1,0:T(8,128)S(1)}, f32[8,128]{1,0:T(8,128)}, u32[]{:S(2)}) copy-start(f32[8,128]{1,0:T(8,128)} %copy-done.66) | copy-start | bytes 12292
  277.7 11.3 %collective-permute-start.29 = (f32[4,32,64]{2,1,0:T(8,128)S(1)}, f32[4,32,64]{2,1,0:T(8,128)S(1)}, u32[]{:S(2)}, u32[]{:S(2)}) collective-permute-start(f32[4,32,64]{2,1,0:T(8,128)S(1)} %broadcast_select_fusion.7), channel_id=1, source_target_pairs={{0,1},{1,0},{2,3},{3,2},{4,5},{5,4},{6,7},{7,6},{8,9},{9,8},{10,11... | collective-permute-start | bytes 98312 | tf_op jit(solution)/shard_map/ppermute | solution.py:102
  279.0 15.0 %collective-permute-start.25 = (f32[4,64,128]{2,1,0:T(8,128)}, f32[4,64,128]{2,1,0:T(8,128)S(1)}, u32[]{:S(2)}, u32[]{:S(2)}) collective-permute-start(f32[4,64,128]{2,1,0:T(8,128)} %get-tuple-element.42), channel_id=1, source_target_pairs={{0,8},{8,16},{16,24},{1,9},{9,17},{17,25},{2,10},{10,18},{18,26},{... | collective-permute-start | bytes 393224 | tf_op jit(solution)/shard_map/ppermute | solution.py:107
  283.6 10.4 %collective-permute-start.26 = (f32[4,64,128]{2,1,0:T(8,128)}, f32[4,64,128]{2,1,0:T(8,128)S(1)}, u32[]{:S(2)}, u32[]{:S(2)}) collective-permute-start(f32[4,64,128]{2,1,0:T(8,128)} %get-tuple-element.43), channel_id=1, source_target_pairs={{8,0},{16,8},{24,16},{9,1},{17,9},{25,17},{10,2},{18,10},{26,18},{... | collective-permute-start | bytes 393224 | tf_op jit(solution)/shard_map/ppermute | solution.py:107
  284.9 5.0 %collective-permute-start.27 = (f32[4,32,1,128]{3,2,1,0:T(1,128)}, f32[4,32,1,128]{3,2,1,0:T(1,128)S(1)}, u32[]{:S(2)}, u32[]{:S(2)}) collective-permute-start(f32[4,32,1,128]{3,2,1,0:T(1,128)} %get-tuple-element.44), channel_id=1, source_target_pairs={{0,2},{2,4},{4,6},{1,3},{3,5},{5,7},{8,10},{10,12},{12,14},{9,11},... | collective-permute-start | bytes 196616 | tf_op jit(solution)/shard_map/ppermute | solution.py:107
  287.7 6.4 %collective-permute-start.28 = (f32[4,32,1,128]{3,2,1,0:T(1,128)}, f32[4,32,1,128]{3,2,1,0:T(1,128)S(1)}, u32[]{:S(2)}, u32[]{:S(2)}) collective-permute-start(f32[4,32,1,128]{3,2,1,0:T(1,128)} %get-tuple-element.45), channel_id=1, source_target_pairs={{2,0},{4,2},{6,4},{3,1},{5,3},{7,5},{10,8},{12,10},{14,12},{11,9},... | collective-permute-start | bytes 196616 | tf_op jit(solution)/shard_map/ppermute | solution.py:107
  327.0 13.2 %collective-permute-start.34 = (f32[4,32,64]{2,1,0:T(8,128)S(1)}, f32[4,32,64]{2,1,0:T(8,128)S(1)}, u32[]{:S(2)}, u32[]{:S(2)}) collective-permute-start(f32[4,32,64]{2,1,0:T(8,128)S(1)} %broadcast_select_fusion.6), channel_id=1, source_target_pairs={{0,1},{1,0},{2,3},{3,2},{4,5},{5,4},{6,7},{7,6},{8,9},{9,8},{10,11... | collective-permute-start | bytes 98312 | tf_op jit(solution)/shard_map/ppermute | solution.py:102
  328.9 15.9 %collective-permute-start.30 = (f32[4,64,128]{2,1,0:T(8,128)S(1)}, f32[4,64,128]{2,1,0:T(8,128)S(1)}, u32[]{:S(2)}, u32[]{:S(2)}) collective-permute-start(f32[4,64,128]{2,1,0:T(8,128)S(1)} %copy-done.93), channel_id=1, source_target_pairs={{0,8},{8,16},{16,24},{1,9},{9,17},{17,25},{2,10},{10,18},{18,26},{... | collective-permute-start | bytes 393224 | tf_op jit(solution)/shard_map/ppermute | solution.py:107
  333.8 11.0 %collective-permute-start.31 = (f32[4,64,128]{2,1,0:T(8,128)S(1)}, f32[4,64,128]{2,1,0:T(8,128)S(1)}, u32[]{:S(2)}, u32[]{:S(2)}) collective-permute-start(f32[4,64,128]{2,1,0:T(8,128)S(1)} %copy-done.92), channel_id=1, source_target_pairs={{8,0},{16,8},{24,16},{9,1},{17,9},{25,17},{10,2},{18,10},{26,18},{... | collective-permute-start | bytes 393224 | tf_op jit(solution)/shard_map/ppermute | solution.py:107
  335.1 5.8 %collective-permute-start.32 = (f32[4,32,1,128]{3,2,1,0:T(1,128)S(1)}, f32[4,32,1,128]{3,2,1,0:T(1,128)S(1)}, u32[]{:S(2)}, u32[]{:S(2)}) collective-permute-start(f32[4,32,1,128]{3,2,1,0:T(1,128)S(1)} %copy-done.97), channel_id=1, source_target_pairs={{0,2},{2,4},{4,6},{1,3},{3,5},{5,7},{8,10},{10,12},{12,14},{9,11},... | collective-permute-start | bytes 196616 | tf_op jit(solution)/shard_map/ppermute | solution.py:107
  338.7 6.2 %collective-permute-start.33 = (f32[4,32,1,128]{3,2,1,0:T(1,128)S(1)}, f32[4,32,1,128]{3,2,1,0:T(1,128)S(1)}, u32[]{:S(2)}, u32[]{:S(2)}) collective-permute-start(f32[4,32,1,128]{3,2,1,0:T(1,128)S(1)} %copy-done.96), channel_id=1, source_target_pairs={{2,0},{4,2},{6,4},{3,1},{5,3},{7,5},{10,8},{12,10},{14,12},{11,9},... | collective-permute-start | bytes 196616 | tf_op jit(solution)/shard_map/ppermute | solution.py:107
  (90 other events, 522.6 us)

commit v5 on v2

--- a/solution.py
+++ b/solution.py
@@ -151,8 +151,9 @@
     zf_hi[0] = flipped[half:half + nx, :]
 
 
-def sweep_kernel(first, second, d_ref, r_ref, p_ref, fxp, fxm, fyp, fym, fzp, fzm, dg_ref, inv_ref,
+def sweep_kernel(first, second, final, d_ref, r_ref, p_ref, fxp, fxm, fyp, fym, fzp, fzm, dg_ref, inv_ref,
                  xlo, xhi, ylo, yhi, zlo, zhi, r_out, d_out, p_out, *face_out):
+    snapshot = pl.program_id(0)
     nx, ny, nz = d_ref.shape[1], d_ref.shape[2], d_ref.shape[3]
     row = lax.broadcasted_iota(jnp.int32, (ny, nz), 0)
     lane = lax.broadcasted_iota(jnp.int32, (ny, nz), 1)
@@ -180,7 +181,10 @@
         step_dir = first * centre + second * (residual * inv_ref[x])
         r_out[0, x] = residual
         d_out[0, x] = step_dir
-        p_out[0, x] = p_ref[0, x] + step_dir
+        if final:
+            p_out[x, :, snapshot, :] = p_ref[0, x] + step_dir
+        else:
+            p_out[0, x] = p_ref[0, x] + step_dir
         return write_faces(x, step_dir, carry, *face_out)
 
     columns = lax.fori_loop(0, nx, body, jnp.zeros((ny, nz), jnp.float32), unroll=2)
@@ -234,18 +238,23 @@
     return outs[0], outs[1:]
 
 
-def run_sweep(first, second, step_dir, residual, potential, faces, diagonal, inverse, halos):
+def run_sweep(first, second, step_dir, residual, potential, faces, diagonal, inverse, halos, final=False):
     full, fixed, face_specs, face_shapes = specs(step_dir.shape)
     steps, nx, ny, nz = step_dir.shape
     x_face, y_face = face_specs[0], face_specs[2]
     shape = jax.ShapeDtypeStruct(step_dir.shape, jnp.float32)
+    if final:
+        out_spec = pl.BlockSpec((nx, ny, steps, nz), lambda s: (0, 0, 0, 0))
+        out_shape = jax.ShapeDtypeStruct((nx, ny, steps, nz), jnp.float32)
+    else:
+        out_spec, out_shape = full, shape
     size = step_dir.size
     outs = pl.pallas_call(
-        functools.partial(sweep_kernel, first, second),
+        functools.partial(sweep_kernel, first, second, final),
         grid=(steps,),
         in_specs=[full, full, full] + [fixed] * 8 + [x_face, x_face, y_face, y_face, face_specs[4], face_specs[4]],
-        out_specs=[full, full, full] + face_specs,
-        out_shape=[shape, shape, shape] + face_shapes,
+        out_specs=[full, full, out_spec] + face_specs,
+        out_shape=[shape, shape, out_shape] + face_shapes,
         cost_estimate=pl.CostEstimate(flops=30 * size, transcendentals=0, bytes_accessed=4 * 7 * size + 4 * 7 * size // steps),
         name="chebyshev_sweep",
     )(step_dir, residual, potential, *faces, diagonal, inverse, *halos)
@@ -344,9 +353,10 @@
         z_low, z_high = exchange(dir_faces[5], dir_faces[4], "gz")
         halos = (x_low, x_high, y_low, y_high, z_low, z_high)
         residual, step_dir, potential, dir_faces = run_sweep(
-            first_coef[sweep - 1], second_coef[sweep - 1], step_dir, residual, potential, faces, diagonal, inverse, halos
+            first_coef[sweep - 1], second_coef[sweep - 1], step_dir, residual, potential, faces, diagonal, inverse, halos,
+            final=sweep == SWEEPS - 1,
         )
-    return (heart_next, jnp.transpose(potential, (1, 2, 0, 3)))
+    return (heart_next, potential)
 
 
 def solution(mesh):

time: 379 us -> 374 us (0.987)
  local copies, waits for them, and re-layouts: 73.1 us -> 65.8 us
    unnamed x200 -> x197, local copies, waits for them, and re-layouts: 12.5 us -> 4.58 us
  transfers between devices with their start and end apart: 37 -> 37, of which waited for: 8 -> 8; matrix products, arithmetic and copies ran while one was open for 17% -> 18% of each run, Pallas kernels for 0% -> 0%
where the time goes in v5:
time: 374 us; the launch traced here: 370 us
  Pallas kernels  101 us (27%)
  starting transfers between devices  90.5 us (24%)
  other arithmetic  72.7 us (19%)
  local copies, waits for them, and re-layouts  65.8 us (18%)
  waiting for transfers between devices  36.2 us (10%)
    pallas_call x3, Pallas kernels, run_sweep(): pl.pallas_call(functools.partial(sweep_kernel, first, second, final), gri...  87.1 us
    ppermute x14, starting transfers between devices, exchange(): lax.ppermute(top, axis, forward)  58.4 us
    all_to_all x1, waiting for transfers between devices, local(): lax.all_to_all(send_values.reshape(STEPS, devices, capacity, row_len), ('...  21.9 us
    ppermute x14, starting transfers between devices, exchange(): lax.ppermute(bottom, axis, backward)  18.1 us
    gather x2, local copies, waits for them, and re-layouts, local(): jnp.take(received, row_slot, axis=1)  17.7 us
    add x4, other arithmetic, membrane(): steady + (gate_state - steady) * jnp.exp(-DT_HEART / time_const)  16.1 us
    pallas_call x1, Pallas kernels, run_initial(): pl.pallas_call(functools.partial(initial_kernel, mid), grid=(source.shape...  14.3 us
    ppermute x14, waiting for transfers between devices, exchange(): lax.ppermute(bottom, axis, backward)  12.3 us
  transfers between devices with their start and end apart: 37, of which 8 were waited for; matrix products, arithmetic and copies ran while one was open for 18% of the time, Pallas kernels for 0%

profile of v5, /device:TPU:0, one launch (start us, length us, event | category | flops | bytes accessed | tf_op | source)
XLA Modules:
  0.0 369.6 jit_solution(15838728920516266068)
XLA Ops:
  0.6 1.8 fusion.118
  2.4 4.5 %select_add_fusion.1 = (f32[32,64,128]{2,1,0:T(8,128)S(1)}, pred[32,64,128]{2,1,0:T(8,128)(4,1)S(1)}, pred[32,64,128]{2,1,0:T(8,128)(4,1)S(1)}, pred[32,64,128]{2,1,0:T(8,128)(4,1)S(1)}, pred[32,64,128]{2,1,0:T(8,128)(4,1)S(1)}) fusion(f32[]{:T(128)} %bitcast.29, f32[]{:T(128)} %bitcast.28, f32[]{:T(128)} %bitcast.27, f32[]{:T(128)} %bitcast.26, ...), kind=kLoop, calls=%fused_computation.33 | loop fusion | flops 2883584 | bytes 3145744 | tf_op jit(solution)/shard_map/add | solution.py:308
  6.9 5.9 %select_add_fusion.2 = (f32[32,64,128]{2,1,0:T(8,128)S(1)}, f32[32,64,128]{2,1,0:T(8,128)S(1)}) fusion(pred[32,64,128]{2,1,0:T(8,128)(4,1)S(1)} %get-tuple-element.85, pred[32,64,128]{2,1,0:T(8,128)(4,1)S(1)} %get-tuple-element.84, pred[32,64,128]{2,1,0:T(8,128)(4,1)S(1)} %get-tuple-element.83, pred[32,64,128]{2,1,0:T(8,128)(4,1)S(1)} %get-tuple-element.82, ...), kind=kLoop, calls=%fused_computation.34 | loop fusion | flops 3670016 | bytes 3145760 | tf_op jit(solution)/shard_map/add | solution.py:308
  12.9 1.8 fusion.98
  17.1 5.5 %collective-permute-start.3 = (f32[5120]{0:T(1024)}, f32[5120]{0:T(1024)S(1)}, u32[]{:S(2)}, u32[]{:S(2)}) collective-permute-start(f32[5120]{0:T(1024)} %pad_maximum_fusion.5), channel_id=1, source_target_pairs={{0,2},{2,4},{4,6},{1,3},{3,5},{5,7},{8,10},{10,12},{12,14},{9,11},... | collective-permute-start | bytes 61448 | tf_op jit(solution)/shard_map/ppermute | solution.py:107
  23.4 3.8 %collective-permute-start.1 = (f32[12288]{0:T(1024)S(1)}, f32[12288]{0:T(1024)S(1)}, u32[]{:S(2)}, u32[]{:S(2)}) collective-permute-start(f32[12288]{0:T(1024)S(1)} %pad_maximum_fusion.3), channel_id=1, source_target_pairs={{0,8},{8,16},{16,24},{1,9},{9,17},{17,25},{2,10},{10,18},{18,26},{... | collective-permute-start | bytes 147464 | tf_op jit(solution)/shard_map/ppermute | solution.py:107
  34.6 1.3 reduce.66
  36.0 5.0 %gather_fusion = s32[768]{0:T(1024)S(1)} fusion(s32[256]{0:T(256)S(1)} %reshape.1868, s32[1024]{0:T(1024)S(1)} %pad_clamp_fusion), kind=kCustom, calls=%fused_computation | custom fusion | bytes 9216 | tf_op jit(solution)/shard_map/gather | solution.py:296
  41.7 6.1 %all-to-all-start = ((s32[32,1,24]{2,1,0:T(1,128)}), s32[32,1,24]{2,1,0:T(1,128)S(1)}, u32[]{:S(2)}, u32[]{:S(2)}) async-start(s32[32,1,24]{2,1,0:T(1,128)} %bitcast.116), calls=%async_computation | async-start | bytes 32768 | tf_op jit(solution)/shard_map/all_to_all | solution.py:297
  47.8 1.5 fusion.100
  49.3 1.6 fusion.101
  50.9 1.7 fusion.99
  55.1 1.5 multiply_add_fusion.3
  59.4 2.8 iota_reduce_fusion
  66.5 1.8 slice.567
  68.3 1.9 slice.568
  75.0 1.4 fusion.18
  76.5 2.8 multiply_add_fusion.2
  81.5 4.5 %collective-permute-start.6 = (f32[32,128]{1,0:T(8,128)S(1)}, f32[32,128]{1,0:T(8,128)S(1)}, u32[]{:S(2)}, u32[]{:S(2)}) collective-permute-start(f32[32,128]{1,0:T(8,128)S(1)} %get-tuple-element.152), channel_id=1, source_target_pairs={{0,8},{8,16},{16,24},{1,9},{9,17},{17,25},{2,10},{10,18},{18,26},{... | collective-permute-start | bytes 49160 | tf_op jit(solution)/shard_map/ppermute | solution.py:107
  87.3 4.5 %collective-permute-start.8 = (f32[8,128]{1,0:T(8,128)S(1)}, f32[8,128]{1,0:T(8,128)S(1)}, u32[]{:S(2)}, u32[]{:S(2)}) collective-permute-start(f32[8,128]{1,0:T(8,128)S(1)} %bitcast.357), channel_id=1, source_target_pairs={{0,2},{2,4},{4,6},{1,3},{3,5},{5,7},{8,10},{10,12},{12,14},{9,11},... | collective-permute-start | bytes 12296 | tf_op jit(solution)/shard_map/ppermute | solution.py:107
  100.4 1.4 fusion.33
  101.9 4.2 %multiply_add_fusion.1 = f32[18,8,32,128]{3,2,1,0:T(8,128)S(1)} fusion(f32[8,32,128]{2,1,0:T(8,128)S(1)} %bitcast.299, f32[18]{0:T(128)S(1)} %copy-done.84, f32[18]{0:T(128)S(1)} %copy-done.87, f32[18]{0:T(128)S(1)} %copy-done.90, f32[8,32,128]{2,1,0:T(8,128)S(1)} %bitcast.291, f32[19,8,32,128]{3,2,1,0:T(8,128)S(1)} %copy-done.4, ...), kind=kLoop, calls=%fused_computation.9 | loop fusion | flops 19464192 | bytes 5112024 | tf_op jit(solution)/shard_map/add | solution.py:59
  109.3 5.1 %collective-permute-start.11 = (f32[32,128]{1,0:T(8,128)S(1)}, f32[32,128]{1,0:T(8,128)S(1)}, u32[]{:S(2)}, u32[]{:S(2)}) collective-permute-start(f32[32,128]{1,0:T(8,128)S(1)} %get-tuple-element.136), channel_id=1, source_target_pairs={{0,8},{8,16},{16,24},{1,9},{9,17},{17,25},{2,10},{10,18},{18,26},{... | collective-permute-start | bytes 49160 | tf_op jit(solution)/shard_map/ppermute | solution.py:107
  115.7 4.8 %collective-permute-start.13 = (f32[8,128]{1,0:T(8,128)S(1)}, f32[8,128]{1,0:T(8,128)S(1)}, u32[]{:S(2)}, u32[]{:S(2)}) collective-permute-start(f32[8,128]{1,0:T(8,128)S(1)} %bitcast.359), channel_id=1, source_target_pairs={{0,2},{2,4},{4,6},{1,3},{3,5},{5,7},{8,10},{10,12},{12,14},{9,11},... | collective-permute-start | bytes 12296 | tf_op jit(solution)/shard_map/ppermute | solution.py:107
  126.8 5.4 %collective-permute-start.16 = (f32[32,128]{1,0:T(8,128)S(1)}, f32[32,128]{1,0:T(8,128)S(1)}, u32[]{:S(2)}, u32[]{:S(2)}) collective-permute-start(f32[32,128]{1,0:T(8,128)S(1)} %get-tuple-element.120), channel_id=1, source_target_pairs={{0,8},{8,16},{16,24},{1,9},{9,17},{17,25},{2,10},{10,18},{18,26},{... | collective-permute-start | bytes 49160 | tf_op jit(solution)/shard_map/ppermute | solution.py:107
  133.5 4.8 %collective-permute-start.18 = (f32[8,128]{1,0:T(8,128)S(1)}, f32[8,128]{1,0:T(8,128)S(1)}, u32[]{:S(2)}, u32[]{:S(2)}) collective-permute-start(f32[8,128]{1,0:T(8,128)S(1)} %bitcast.360), channel_id=1, source_target_pairs={{0,2},{2,4},{4,6},{1,3},{3,5},{5,7},{8,10},{10,12},{12,14},{9,11},... | collective-permute-start | bytes 12296 | tf_op jit(solution)/shard_map/ppermute | solution.py:107
  141.9 3.0 gather_fusion.1
  144.8 4.9 %select_select_fusion.1 = f32[4,32,24,128]{3,0,2,1:T(4,128)} fusion(f32[4,32,24,128]{3,0,2,1:T(4,128)S(1)} %bitcast.285, pred[32,24]{1,0:T(8,128)(4,1)} %broadcast_in_dim.362, pred[32,24]{1,0:T(8,128)(4,1)} %broadcast_in_dim.360), kind=kLoop, calls=%fused_computation.12 | loop fusion | flops 786432 | bytes 3147264 | tf_op jit(solution)/shard_map/jit(_where)/select_n | solution.py:326
  149.8 7.4 %all-to-all-start.1 = ((f32[4,32,24,128]{3,0,2,1:T(4,128)}), f32[4,32,24,128]{3,0,2,1:T(4,128)S(1)}, u32[]{:S(2)}, u32[]{:S(2)}) async-start(f32[4,32,24,128]{3,0,2,1:T(4,128)} %select_select_fusion.1), calls=%async_computation.1 | async-start | bytes 3145728 | tf_op jit(solution)/shard_map/all_to_all | solution.py:327
  157.2 7.1 %broadcast_divide_fusion = (f32[32,64,128]{2,1,0:T(8,128)}, f32[32,64,128]{2,1,0:T(8,128)}, f32[32,64,128]{2,1,0:T(8,128)}, f32[32,64,128]{2,1,0:T(8,128)}, f32[...) fusion(f32[32,64,128]{2,1,0:T(8,128)} %copy-done.1, ...), kind=kLoop, calls=%fused_computation.40 | loop fusion | flops 6553600 | bytes 17825792 | tf_op jit(solution)/shard_map/div | solution.py:347
  166.6 7.5 %multiply_add_fusion = f32[18,8,32,128]{3,2,1,0:T(8,128)} fusion(f32[8,32,128]{2,1,0:T(8,128)S(1)} %bitcast.302, f32[18]{0:T(128)} %param.15, f32[18]{0:T(128)} %param.13, f32[18]{0:T(128)} %copy-done.88, f32[8,32,128]{2,1,0:T(8,128)S(1)} %bitcast.301, f32[8,32,128]{2,1,0:T(8,128)S(1)} %bitcast.292, f32[19,8,32,128]{3,2,1,0:T(8,128)} %param.11, ...), kind=kLoop, calls=%fused_computation.8 | loop fusion | flops 25952256 | bytes 5243096 | tf_op jit(solution)/shard_map/add | solution.py:59
  174.1 21.9 %all-to-all-done.1 = f32[4,32,24,128]{3,0,2,1:T(4,128)S(1)} async-done(((f32[4,32,24,128]{3,0,2,1:T(4,128)}), f32[4,32,24,128]{3,0,2,1:T(4,128)S(1)}, u32[]{:S(2)}, u32[]{:S(2)}) %all-to-all-start.1) | async-done | bytes 1572896 | tf_op jit(solution)/shard_map/all_to_all | solution.py:327
  196.0 15.2 %gather_fusion.2 = f32[2048,4,128]{2,1,0:T(4,128)} fusion(f32[4,768,128]{2,0,1:T(4,128)S(1)} %bitcast.282, s32[2048]{0:T(1024)S(1)} %copy-done.58), kind=kCustom, calls=%fused_computation.2 | custom fusion | bytes 8396800 | tf_op jit(solution)/shard_map/jit(_take)/gather | solution.py:334
  211.3 2.5 copy.1552
  213.8 2.8 select_select_fusion.r_ref
  216.6 14.3 %chebyshev_start.1 = (f32[4,32,64,128]{3,2,1,0:T(8,128)}, f32[4,64,128]{2,1,0:T(8,128)}, f32[4,64,128]{2,1,0:T(8,128)}, f32[4,32,1,128]{3,2,1,0:T(1,128)}, f32[4...) custom-call(f32[4,32,64,128]{3,2,1,0:T(8,128)} %select_select_fusion.r_ref, ...), custom_call_target="tpu_custom_call" | custom-call | flops 2097152 | bytes 9437184 | tf_op jit(solution)/shard_map/chebyshev_start/pallas_call | solution.py:229
  232.7 2.7 collective-permute-start.20
  240.2 4.0 %collective-permute-done.23.yhi = f32[4,32,1,128]{3,2,1,0:T(1,128)S(1)} collective-permute-done((f32[4,32,1,128]{3,2,1,0:T(1,128)S(1)}, f32[4,32,1,128]{3,2,1,0:T(1,128)S(1)}, u32[]{:S(2)}, u32[]{:S(2)}) %collective-permute-start.23) | collective-permute-done | bytes 65568 | tf_op jit(solution)/shard_map/ppermute | solution.py:107
  245.0 28.0 %chebyshev_sweep.3 = (f32[4,32,64,128]{3,2,1,0:T(8,128)}, f32[4,32,64,128]{3,2,1,0:T(8,128)}, f32[4,32,64,128]{3,2,1,0:T(8,128)}, f32[4,64,128]{2,1,0:T(8,128)},...) custom-call(f32[4,32,64,128]{3,2,1,0:T(8,128)} %get-tuple-element.32, ...), custom_call_target="tpu_custom_call" | custom-call | flops 31457280 | bytes 36700160 | tf_op jit(solution)/shard_map/chebyshev_sweep/pallas_call | solution.py:252
  275.2 4.6 %collective-permute-start.25 = (f32[4,64,128]{2,1,0:T(8,128)}, f32[4,64,128]{2,1,0:T(8,128)S(1)}, u32[]{:S(2)}, u32[]{:S(2)}) collective-permute-start(f32[4,64,128]{2,1,0:T(8,128)} %get-tuple-element.42), channel_id=1, source_target_pairs={{0,8},{8,16},{16,24},{1,9},{9,17},{17,25},{2,10},{10,18},{18,26},{... | collective-permute-start | bytes 393224 | tf_op jit(solution)/shard_map/ppermute | solution.py:107
  281.0 2.8 collective-permute-start.27
  286.0 4.2 %collective-permute-done.28.yhi = f32[4,32,1,128]{3,2,1,0:T(1,128)S(1)} collective-permute-done((f32[4,32,1,128]{3,2,1,0:T(1,128)}, f32[4,32,1,128]{3,2,1,0:T(1,128)S(1)}, u32[]{:S(2)}, u32[]{:S(2)}) %collective-permute-start.28) | collective-permute-done | bytes 65568 | tf_op jit(solution)/shard_map/ppermute | solution.py:107
  290.9 28.0 %chebyshev_sweep.4 = (f32[4,32,64,128]{3,2,1,0:T(8,128)}, f32[4,32,64,128]{3,2,1,0:T(8,128)}, f32[4,32,64,128]{3,2,1,0:T(8,128)}, f32[4,64,128]{2,1,0:T(8,128)},...) custom-call(f32[4,32,64,128]{3,2,1,0:T(8,128)} %get-tuple-element.39, ...), custom_call_target="tpu_custom_call" | custom-call | flops 31457280 | bytes 36700160 | tf_op jit(solution)/shard_map/chebyshev_sweep/pallas_call | solution.py:252
  319.8 1.8 pad_maximum_fusion
  321.6 4.9 %collective-permute-start.30 = (f32[4,64,128]{2,1,0:T(8,128)S(1)}, f32[4,64,128]{2,1,0:T(8,128)S(1)}, u32[]{:S(2)}, u32[]{:S(2)}) collective-permute-start(f32[4,64,128]{2,1,0:T(8,128)S(1)} %copy-done.93), channel_id=1, source_target_pairs={{0,8},{8,16},{16,24},{1,9},{9,17},{17,25},{2,10},{10,18},{18,26},{... | collective-permute-start | bytes 393224 | tf_op jit(solution)/shard_map/ppermute | solution.py:107
  327.8 3.5 collective-permute-start.32
  333.4 4.2 %collective-permute-done.33.yhi = f32[4,32,1,128]{3,2,1,0:T(1,128)S(1)} collective-permute-done((f32[4,32,1,128]{3,2,1,0:T(1,128)S(1)}, f32[4,32,1,128]{3,2,1,0:T(1,128)S(1)}, u32[]{:S(2)}, u32[]{:S(2)}) %collective-permute-start.33) | collective-permute-done | bytes 65568 | tf_op jit(solution)/shard_map/ppermute | solution.py:107
  338.3 31.1 %chebyshev_sweep.5 = (f32[4,32,64,128]{3,2,1,0:T(8,128)}, f32[4,32,64,128]{3,2,1,0:T(8,128)}, f32[32,64,4,128]{3,2,1,0:T(4,128)}, f32[4,64,128]{2,1,0:T(8,128)},...) custom-call(f32[4,32,64,128]{3,2,1,0:T(8,128)} %get-tuple-element.48, ...), custom_call_target="tpu_custom_call" | custom-call | flops 31457280 | bytes 36700160 | tf_op jit(solution)/shard_map/chebyshev_sweep/pallas_call | solution.py:252
  (378 shorter events, 73.0 us)
Async XLA Ops:
  12.8 35.0 %copy-start = (f32[32,64,128]{2,1,0:T(8,128)}, f32[32,64,128]{2,1,0:T(8,128)S(1)}, u32[]{:S(2)}) copy-start(f32[32,64,128]{2,1,0:T(8,128)S(1)} %get-tuple-element.102) | copy-start | bytes 3145732
  12.8 36.5 %copy-start.1 = (f32[32,64,128]{2,1,0:T(8,128)}, f32[32,64,128]{2,1,0:T(8,128)S(1)}, u32[]{:S(2)}) copy-start(f32[32,64,128]{2,1,0:T(8,128)S(1)} %get-tuple-element.103) | copy-start | bytes 3145732
  15.2 55.3 %collective-permute-start.2 = (f32[5120]{0:T(1024)}, f32[5120]{0:T(1024)S(1)}, u32[]{:S(2)}, u32[]{:S(2)}) collective-permute-start(f32[5120]{0:T(1024)} %pad_maximum_fusion.4), channel_id=1, source_target_pairs={{2,0},{4,2},{6,4},{3,1},{5,3},{7,5},{10,8},{12,10},{14,12},{11,9},... | collective-permute-start | bytes 61448 | tf_op jit(solution)/shard_map/ppermute | solution.py:107
  17.1 53.4 %collective-permute-start.3 = (f32[5120]{0:T(1024)}, f32[5120]{0:T(1024)S(1)}, u32[]{:S(2)}, u32[]{:S(2)}) collective-permute-start(f32[5120]{0:T(1024)} %pad_maximum_fusion.5), channel_id=1, source_target_pairs={{0,2},{2,4},{4,6},{1,3},{3,5},{5,7},{8,10},{10,12},{12,14},{9,11},... | collective-permute-start | bytes 61448 | tf_op jit(solution)/shard_map/ppermute | solution.py:107
  23.4 47.7 %collective-permute-start.1 = (f32[12288]{0:T(1024)S(1)}, f32[12288]{0:T(1024)S(1)}, u32[]{:S(2)}, u32[]{:S(2)}) collective-permute-start(f32[12288]{0:T(1024)S(1)} %pad_maximum_fusion.3), channel_id=1, source_target_pairs={{0,8},{8,16},{16,24},{1,9},{9,17},{17,25},{2,10},{10,18},{18,26},{... | collective-permute-start | bytes 147464 | tf_op jit(solution)/shard_map/ppermute | solution.py:107
  27.9 43.3 %collective-permute-start = (f32[12288]{0:T(1024)}, f32[12288]{0:T(1024)S(1)}, u32[]{:S(2)}, u32[]{:S(2)}) collective-permute-start(f32[12288]{0:T(1024)} %pad_maximum_fusion.2), channel_id=1, source_target_pairs={{8,0},{16,8},{24,16},{9,1},{17,9},{25,17},{10,2},{18,10},{26,18},{... | collective-permute-start | bytes 147464 | tf_op jit(solution)/shard_map/ppermute | solution.py:107
  31.2 33.7 %collective-permute-start.4 = (f32[2304]{0:T(1024)}, f32[2304]{0:T(1024)}, u32[]{:S(2)}, u32[]{:S(2)}) collective-permute-start(f32[2304]{0:T(1024)} %maximum_select_fusion), channel_id=1, source_target_pairs={{0,1},{1,0},{2,3},{3,2},{4,5},{5,4},{6,7},{7,6},{8,9},{9,8},{10,11... | collective-permute-start | bytes 27656 | tf_op jit(solution)/shard_map/ppermute | solution.py:102
  41.7 16.9 %all-to-all-start = ((s32[32,1,24]{2,1,0:T(1,128)}), s32[32,1,24]{2,1,0:T(1,128)S(1)}, u32[]{:S(2)}, u32[]{:S(2)}) async-start(s32[32,1,24]{2,1,0:T(1,128)} %bitcast.116), calls=%async_computation | async-start | bytes 32768 | tf_op jit(solution)/shard_map/all_to_all | solution.py:297
  55.0 51.0 %copy-start.8 = (pred[8,32,128]{2,1,0:T(8,128)(4,1)}, pred[8,32,128]{2,1,0:T(8,128)(4,1)S(1)}, u32[]{:S(2)}) copy-start(pred[8,32,128]{2,1,0:T(8,128)(4,1)S(1)} %get-tuple-element.162) | copy-start | bytes 98308
  55.0 51.0 %copy-start.10 = (pred[8,32,128]{2,1,0:T(8,128)(4,1)}, pred[8,32,128]{2,1,0:T(8,128)(4,1)S(1)}, u32[]{:S(2)}) copy-start(pred[8,32,128]{2,1,0:T(8,128)(4,1)S(1)} %get-tuple-element.163) | copy-start | bytes 98308
  55.0 51.0 %copy-start.12 = (pred[8,32,128]{2,1,0:T(8,128)(4,1)}, pred[8,32,128]{2,1,0:T(8,128)(4,1)S(1)}, u32[]{:S(2)}) copy-start(pred[8,32,128]{2,1,0:T(8,128)(4,1)S(1)} %get-tuple-element.164) | copy-start | bytes 98308
  79.9 13.3 %collective-permute-start.9 = (f32[8,32]{1,0:T(8,128)S(1)}, f32[8,32]{1,0:T(8,128)S(1)}, u32[]{:S(2)}, u32[]{:S(2)}) collective-permute-start(f32[8,32]{1,0:T(8,128)S(1)} %fusion.10), channel_id=1, source_target_pairs={{0,1},{1,0},{2,3},{3,2},{4,5},{5,4},{6,7},{7,6},{8,9},{9,8},{10,11... | collective-permute-start | bytes 3080 | tf_op jit(solution)/shard_map/ppermute | solution.py:102
  80.2 16.4 %collective-permute-start.5 = (f32[32,128]{1,0:T(8,128)S(1)}, f32[32,128]{1,0:T(8,128)S(1)}, u32[]{:S(2)}, u32[]{:S(2)}) collective-permute-start(f32[32,128]{1,0:T(8,128)S(1)} %get-tuple-element.153), channel_id=1, source_target_pairs={{8,0},{16,8},{24,16},{9,1},{17,9},{25,17},{10,2},{18,10},{26,18},{... | collective-permute-start | bytes 49160 | tf_op jit(solution)/shard_map/ppermute | solution.py:107
  81.5 15.1 %collective-permute-start.6 = (f32[32,128]{1,0:T(8,128)S(1)}, f32[32,128]{1,0:T(8,128)S(1)}, u32[]{:S(2)}, u32[]{:S(2)}) collective-permute-start(f32[32,128]{1,0:T(8,128)S(1)} %get-tuple-element.152), channel_id=1, source_target_pairs={{0,8},{8,16},{16,24},{1,9},{9,17},{17,25},{2,10},{10,18},{18,26},{... | collective-permute-start | bytes 49160 | tf_op jit(solution)/shard_map/ppermute | solution.py:107
  86.0 10.5 %collective-permute-start.7 = (f32[8,128]{1,0:T(8,128)S(1)}, f32[8,128]{1,0:T(8,128)S(1)}, u32[]{:S(2)}, u32[]{:S(2)}) collective-permute-start(f32[8,128]{1,0:T(8,128)S(1)} %bitcast.358), channel_id=1, source_target_pairs={{2,0},{4,2},{6,4},{3,1},{5,3},{7,5},{10,8},{12,10},{14,12},{11,9},... | collective-permute-start | bytes 12296 | tf_op jit(solution)/shard_map/ppermute | solution.py:107
  87.3 9.2 %collective-permute-start.8 = (f32[8,128]{1,0:T(8,128)S(1)}, f32[8,128]{1,0:T(8,128)S(1)}, u32[]{:S(2)}, u32[]{:S(2)}) collective-permute-start(f32[8,128]{1,0:T(8,128)S(1)} %bitcast.357), channel_id=1, source_target_pairs={{0,2},{2,4},{4,6},{1,3},{3,5},{5,7},{8,10},{10,12},{12,14},{9,11},... | collective-permute-start | bytes 12296 | tf_op jit(solution)/shard_map/ppermute | solution.py:107
  106.6 13.9 %collective-permute-start.14 = (f32[8,32]{1,0:T(8,128)S(1)}, f32[8,32]{1,0:T(8,128)S(1)}, u32[]{:S(2)}, u32[]{:S(2)}) collective-permute-start(f32[8,32]{1,0:T(8,128)S(1)} %fusion.9), channel_id=1, source_target_pairs={{0,1},{1,0},{2,3},{3,2},{4,5},{5,4},{6,7},{7,6},{8,9},{9,8},{10,11... | collective-permute-start | bytes 3080 | tf_op jit(solution)/shard_map/ppermute | solution.py:102
  108.0 13.6 %collective-permute-start.10 = (f32[32,128]{1,0:T(8,128)S(1)}, f32[32,128]{1,0:T(8,128)S(1)}, u32[]{:S(2)}, u32[]{:S(2)}) collective-permute-start(f32[32,128]{1,0:T(8,128)S(1)} %get-tuple-element.137), channel_id=1, source_target_pairs={{8,0},{16,8},{24,16},{9,1},{17,9},{25,17},{10,2},{18,10},{26,18},{... | collective-permute-start | bytes 49160 | tf_op jit(solution)/shard_map/ppermute | solution.py:107
  109.3 12.3 %collective-permute-start.11 = (f32[32,128]{1,0:T(8,128)S(1)}, f32[32,128]{1,0:T(8,128)S(1)}, u32[]{:S(2)}, u32[]{:S(2)}) collective-permute-start(f32[32,128]{1,0:T(8,128)S(1)} %get-tuple-element.136), channel_id=1, source_target_pairs={{0,8},{8,16},{16,24},{1,9},{9,17},{17,25},{2,10},{10,18},{18,26},{... | collective-permute-start | bytes 49160 | tf_op jit(solution)/shard_map/ppermute | solution.py:107
  114.4 6.7 %collective-permute-start.12 = (f32[8,128]{1,0:T(8,128)S(1)}, f32[8,128]{1,0:T(8,128)S(1)}, u32[]{:S(2)}, u32[]{:S(2)}) collective-permute-start(f32[8,128]{1,0:T(8,128)S(1)} %bitcast.361), channel_id=1, source_target_pairs={{2,0},{4,2},{6,4},{3,1},{5,3},{7,5},{10,8},{12,10},{14,12},{11,9},... | collective-permute-start | bytes 12296 | tf_op jit(solution)/shard_map/ppermute | solution.py:107
  115.7 5.9 %collective-permute-start.13 = (f32[8,128]{1,0:T(8,128)S(1)}, f32[8,128]{1,0:T(8,128)S(1)}, u32[]{:S(2)}, u32[]{:S(2)}) collective-permute-start(f32[8,128]{1,0:T(8,128)S(1)} %bitcast.359), channel_id=1, source_target_pairs={{0,2},{2,4},{4,6},{1,3},{3,5},{5,7},{8,10},{10,12},{12,14},{9,11},... | collective-permute-start | bytes 12296 | tf_op jit(solution)/shard_map/ppermute | solution.py:107
  125.4 13.0 %collective-permute-start.19 = (f32[8,32]{1,0:T(8,128)S(1)}, f32[8,32]{1,0:T(8,128)S(1)}, u32[]{:S(2)}, u32[]{:S(2)}) collective-permute-start(f32[8,32]{1,0:T(8,128)S(1)} %fusion.8), channel_id=1, source_target_pairs={{0,1},{1,0},{2,3},{3,2},{4,5},{5,4},{6,7},{7,6},{8,9},{9,8},{10,11... | collective-permute-start | bytes 3080 | tf_op jit(solution)/shard_map/ppermute | solution.py:102
  125.5 14.2 %collective-permute-start.15 = (f32[32,128]{1,0:T(8,128)S(1)}, f32[32,128]{1,0:T(8,128)S(1)}, u32[]{:S(2)}, u32[]{:S(2)}) collective-permute-start(f32[32,128]{1,0:T(8,128)S(1)} %get-tuple-element.121), channel_id=1, source_target_pairs={{8,0},{16,8},{24,16},{9,1},{17,9},{25,17},{10,2},{18,10},{26,18},{... | collective-permute-start | bytes 49160 | tf_op jit(solution)/shard_map/ppermute | solution.py:107
  126.8 12.9 %collective-permute-start.16 = (f32[32,128]{1,0:T(8,128)S(1)}, f32[32,128]{1,0:T(8,128)S(1)}, u32[]{:S(2)}, u32[]{:S(2)}) collective-permute-start(f32[32,128]{1,0:T(8,128)S(1)} %get-tuple-element.120), channel_id=1, source_target_pairs={{0,8},{8,16},{16,24},{1,9},{9,17},{17,25},{2,10},{10,18},{18,26},{... | collective-permute-start | bytes 49160 | tf_op jit(solution)/shard_map/ppermute | solution.py:107
  132.2 6.4 %collective-permute-start.17 = (f32[8,128]{1,0:T(8,128)S(1)}, f32[8,128]{1,0:T(8,128)S(1)}, u32[]{:S(2)}, u32[]{:S(2)}) collective-permute-start(f32[8,128]{1,0:T(8,128)S(1)} %bitcast.362), channel_id=1, source_target_pairs={{2,0},{4,2},{6,4},{3,1},{5,3},{7,5},{10,8},{12,10},{14,12},{11,9},... | collective-permute-start | bytes 12296 | tf_op jit(solution)/shard_map/ppermute | solution.py:107
  133.5 6.1 %collective-permute-start.18 = (f32[8,128]{1,0:T(8,128)S(1)}, f32[8,128]{1,0:T(8,128)S(1)}, u32[]{:S(2)}, u32[]{:S(2)}) collective-permute-start(f32[8,128]{1,0:T(8,128)S(1)} %bitcast.360), channel_id=1, source_target_pairs={{0,2},{2,4},{4,6},{1,3},{3,5},{5,7},{8,10},{10,12},{12,14},{9,11},... | collective-permute-start | bytes 12296 | tf_op jit(solution)/shard_map/ppermute | solution.py:107
  149.8 46.2 %all-to-all-start.1 = ((f32[4,32,24,128]{3,0,2,1:T(4,128)}), f32[4,32,24,128]{3,0,2,1:T(4,128)S(1)}, u32[]{:S(2)}, u32[]{:S(2)}) async-start(f32[4,32,24,128]{3,0,2,1:T(4,128)} %select_select_fusion.1), calls=%async_computation.1 | async-start | bytes 3145728 | tf_op jit(solution)/shard_map/all_to_all | solution.py:327
  166.6 29.5 %copy-start.58 = (s32[2048]{0:T(1024)S(1)}, s32[2048]{0:T(1024)}, u32[]{:S(2)}) copy-start(s32[2048]{0:T(1024)} %fusion.84) | copy-start | bytes 24580
  231.8 7.5 %collective-permute-start.24 = (f32[4,32,64]{2,1,0:T(8,128)S(1)}, f32[4,32,64]{2,1,0:T(8,128)S(1)}, u32[]{:S(2)}, u32[]{:S(2)}) collective-permute-start(f32[4,32,64]{2,1,0:T(8,128)S(1)} %broadcast_select_fusion.8), channel_id=1, source_target_pairs={{0,1},{1,0},{2,3},{3,2},{4,5},{5,4},{6,7},{7,6},{8,9},{9,8},{10,11... | collective-permute-start | bytes 98312 | tf_op jit(solution)/shard_map/ppermute | solution.py:102
  232.7 11.5 %collective-permute-start.20 = (f32[4,64,128]{2,1,0:T(8,128)}, f32[4,64,128]{2,1,0:T(8,128)S(1)}, u32[]{:S(2)}, u32[]{:S(2)}) collective-permute-start(f32[4,64,128]{2,1,0:T(8,128)} %get-tuple-element.33), channel_id=1, source_target_pairs={{0,8},{8,16},{16,24},{1,9},{9,17},{17,25},{2,10},{10,18},{18,26},{... | collective-permute-start | bytes 393224 | tf_op jit(solution)/shard_map/ppermute | solution.py:107
  235.4 8.8 %collective-permute-start.21 = (f32[4,64,128]{2,1,0:T(8,128)}, f32[4,64,128]{2,1,0:T(8,128)S(1)}, u32[]{:S(2)}, u32[]{:S(2)}) collective-permute-start(f32[4,64,128]{2,1,0:T(8,128)} %get-tuple-element.34), channel_id=1, source_target_pairs={{8,0},{16,8},{24,16},{9,1},{17,9},{25,17},{10,2},{18,10},{26,18},{... | collective-permute-start | bytes 393224 | tf_op jit(solution)/shard_map/ppermute | solution.py:107
  236.7 3.5 collective-permute-start.22
  238.0 6.2 %collective-permute-start.23 = (f32[4,32,1,128]{3,2,1,0:T(1,128)S(1)}, f32[4,32,1,128]{3,2,1,0:T(1,128)S(1)}, u32[]{:S(2)}, u32[]{:S(2)}) collective-permute-start(f32[4,32,1,128]{3,2,1,0:T(1,128)S(1)} %copy-done.96), channel_id=1, source_target_pairs={{2,0},{4,2},{6,4},{3,1},{5,3},{7,5},{10,8},{12,10},{14,12},{11,9},... | collective-permute-start | bytes 196616 | tf_op jit(solution)/shard_map/ppermute | solution.py:107
  244.9 29.0 %copy-start.23 = (f32[1,8,32,127]{3,2,1,0:T(8,128)S(1)}, f32[1,8,32,127]{3,2,1,0:T(8,128)}, u32[]{:S(2)}) copy-start(f32[1,8,32,127]{3,2,1,0:T(8,128)} %get-tuple-element.115) | copy-start | bytes 390148
  244.9 29.1 %copy-start.43 = (f32[32,128]{1,0:T(8,128)S(1)}, f32[32,128]{1,0:T(8,128)}, u32[]{:S(2)}) copy-start(f32[32,128]{1,0:T(8,128)} %copy-done.42) | copy-start | bytes 49156
  244.9 29.1 %copy-start.45 = (f32[32,128]{1,0:T(8,128)S(1)}, f32[32,128]{1,0:T(8,128)}, u32[]{:S(2)}) copy-start(f32[32,128]{1,0:T(8,128)} %copy-done.44) | copy-start | bytes 49156
  244.9 29.1 %copy-start.65 = (f32[8,128]{1,0:T(8,128)S(1)}, f32[8,128]{1,0:T(8,128)}, u32[]{:S(2)}) copy-start(f32[8,128]{1,0:T(8,128)} %copy-done.64) | copy-start | bytes 12292
  244.9 29.1 %copy-start.67 = (f32[8,128]{1,0:T(8,128)S(1)}, f32[8,128]{1,0:T(8,128)}, u32[]{:S(2)}) copy-start(f32[8,128]{1,0:T(8,128)} %copy-done.66) | copy-start | bytes 12292
  273.9 11.2 %collective-permute-start.29 = (f32[4,32,64]{2,1,0:T(8,128)S(1)}, f32[4,32,64]{2,1,0:T(8,128)S(1)}, u32[]{:S(2)}, u32[]{:S(2)}) collective-permute-start(f32[4,32,64]{2,1,0:T(8,128)S(1)} %broadcast_select_fusion.7), channel_id=1, source_target_pairs={{0,1},{1,0},{2,3},{3,2},{4,5},{5,4},{6,7},{7,6},{8,9},{9,8},{10,11... | collective-permute-start | bytes 98312 | tf_op jit(solution)/shard_map/ppermute | solution.py:102
  275.2 15.0 %collective-permute-start.25 = (f32[4,64,128]{2,1,0:T(8,128)}, f32[4,64,128]{2,1,0:T(8,128)S(1)}, u32[]{:S(2)}, u32[]{:S(2)}) collective-permute-start(f32[4,64,128]{2,1,0:T(8,128)} %get-tuple-element.42), channel_id=1, source_target_pairs={{0,8},{8,16},{16,24},{1,9},{9,17},{17,25},{2,10},{10,18},{18,26},{... | collective-permute-start | bytes 393224 | tf_op jit(solution)/shard_map/ppermute | solution.py:107
  279.7 10.4 %collective-permute-start.26 = (f32[4,64,128]{2,1,0:T(8,128)}, f32[4,64,128]{2,1,0:T(8,128)S(1)}, u32[]{:S(2)}, u32[]{:S(2)}) collective-permute-start(f32[4,64,128]{2,1,0:T(8,128)} %get-tuple-element.43), channel_id=1, source_target_pairs={{8,0},{16,8},{24,16},{9,1},{17,9},{25,17},{10,2},{18,10},{26,18},{... | collective-permute-start | bytes 393224 | tf_op jit(solution)/shard_map/ppermute | solution.py:107
  281.0 5.0 %collective-permute-start.27 = (f32[4,32,1,128]{3,2,1,0:T(1,128)}, f32[4,32,1,128]{3,2,1,0:T(1,128)S(1)}, u32[]{:S(2)}, u32[]{:S(2)}) collective-permute-start(f32[4,32,1,128]{3,2,1,0:T(1,128)} %get-tuple-element.44), channel_id=1, source_target_pairs={{0,2},{2,4},{4,6},{1,3},{3,5},{5,7},{8,10},{10,12},{12,14},{9,11},... | collective-permute-start | bytes 196616 | tf_op jit(solution)/shard_map/ppermute | solution.py:107
  283.8 6.4 %collective-permute-start.28 = (f32[4,32,1,128]{3,2,1,0:T(1,128)}, f32[4,32,1,128]{3,2,1,0:T(1,128)S(1)}, u32[]{:S(2)}, u32[]{:S(2)}) collective-permute-start(f32[4,32,1,128]{3,2,1,0:T(1,128)} %get-tuple-element.45), channel_id=1, source_target_pairs={{2,0},{4,2},{6,4},{3,1},{5,3},{7,5},{10,8},{12,10},{14,12},{11,9},... | collective-permute-start | bytes 196616 | tf_op jit(solution)/shard_map/ppermute | solution.py:107
  319.8 12.9 %collective-permute-start.34 = (f32[4,32,64]{2,1,0:T(8,128)S(1)}, f32[4,32,64]{2,1,0:T(8,128)S(1)}, u32[]{:S(2)}, u32[]{:S(2)}) collective-permute-start(f32[4,32,64]{2,1,0:T(8,128)S(1)} %broadcast_select_fusion.6), channel_id=1, source_target_pairs={{0,1},{1,0},{2,3},{3,2},{4,5},{5,4},{6,7},{7,6},{8,9},{9,8},{10,11... | collective-permute-start | bytes 98312 | tf_op jit(solution)/shard_map/ppermute | solution.py:102
  321.6 15.9 %collective-permute-start.30 = (f32[4,64,128]{2,1,0:T(8,128)S(1)}, f32[4,64,128]{2,1,0:T(8,128)S(1)}, u32[]{:S(2)}, u32[]{:S(2)}) collective-permute-start(f32[4,64,128]{2,1,0:T(8,128)S(1)} %copy-done.93), channel_id=1, source_target_pairs={{0,8},{8,16},{16,24},{1,9},{9,17},{17,25},{2,10},{10,18},{18,26},{... | collective-permute-start | bytes 393224 | tf_op jit(solution)/shard_map/ppermute | solution.py:107
  326.5 11.0 %collective-permute-start.31 = (f32[4,64,128]{2,1,0:T(8,128)S(1)}, f32[4,64,128]{2,1,0:T(8,128)S(1)}, u32[]{:S(2)}, u32[]{:S(2)}) collective-permute-start(f32[4,64,128]{2,1,0:T(8,128)S(1)} %copy-done.92), channel_id=1, source_target_pairs={{8,0},{16,8},{24,16},{9,1},{17,9},{25,17},{10,2},{18,10},{26,18},{... | collective-permute-start | bytes 393224 | tf_op jit(solution)/shard_map/ppermute | solution.py:107
  327.8 5.5 %collective-permute-start.32 = (f32[4,32,1,128]{3,2,1,0:T(1,128)S(1)}, f32[4,32,1,128]{3,2,1,0:T(1,128)S(1)}, u32[]{:S(2)}, u32[]{:S(2)}) collective-permute-start(f32[4,32,1,128]{3,2,1,0:T(1,128)S(1)} %copy-done.95), channel_id=1, source_target_pairs={{0,2},{2,4},{4,6},{1,3},{3,5},{5,7},{8,10},{10,12},{12,14},{9,11},... | collective-permute-start | bytes 196616 | tf_op jit(solution)/shard_map/ppermute | solution.py:107
  331.4 6.2 %collective-permute-start.33 = (f32[4,32,1,128]{3,2,1,0:T(1,128)S(1)}, f32[4,32,1,128]{3,2,1,0:T(1,128)S(1)}, u32[]{:S(2)}, u32[]{:S(2)}) collective-permute-start(f32[4,32,1,128]{3,2,1,0:T(1,128)S(1)} %copy-done.94), channel_id=1, source_target_pairs={{2,0},{4,2},{6,4},{3,1},{5,3},{7,5},{10,8},{12,10},{14,12},{11,9},... | collective-permute-start | bytes 196616 | tf_op jit(solution)/shard_map/ppermute | solution.py:107
  (89 other events, 520.3 us)

commit v6 on v5

--- a/solution.py
+++ b/solution.py
@@ -261,6 +261,99 @@
     return outs[0], outs[1], outs[2], outs[3:]
 
 
+def heart_kernel(kinds, coef, v_ref, g_ref, ct_ref, xlo, xhi, ylo, yhi, zlo, zhi,
+                 g_out, c_out, v_out, xf_lo, xf_hi, yf_lo, yf_hi, zf_lo, zf_hi):
+    i = pl.program_id(0)
+    hx, hy, row = v_ref.shape
+    gates = g_ref.shape[0]
+    channels = gates // 2
+    sub = lax.broadcasted_iota(jnp.int32, (hy, row), 0)
+    lane = lax.broadcasted_iota(jnp.int32, (hy, row), 1)
+    centre = v_ref[i]
+    below = v_ref[jnp.maximum(i - 1, 0)]
+    above = v_ref[jnp.minimum(i + 1, hx - 1)]
+    x_minus = jnp.where(i == 0, xlo[...], below)
+    x_plus = jnp.where(i == hx - 1, xhi[...], above)
+    y_minus = jnp.where(sub == 0, ylo[i], pltpu.roll(centre, 1, 0))
+    y_plus = jnp.where(sub == hy - 1, yhi[i], pltpu.roll(centre, hy - 1, 0))
+    z_minus = jnp.where(lane == 0, pltpu.roll(zlo[...], lax.rem(row - i, row), 1), pltpu.roll(centre, 1, 1))
+    z_plus = jnp.where(lane == row - 1, pltpu.roll(zhi[...], lax.rem(row - 1 - i + row, row), 1), pltpu.roll(centre, row - 1, 1))
+    total = x_plus + x_minus
+    total = total + y_plus + y_minus
+    total = total + z_plus + z_minus
+    current = SIGMA_HEART * (total - 6.0 * centre)
+    cell = ct_ref[0]
+    ion = None
+    for channel in range(channels):
+        updated = []
+        for gate in (2 * channel, 2 * channel + 1):
+            exponent = coef[gate] * (centre - coef[gates + gate])
+            steady = 1.0 / (1.0 + jnp.exp(-exponent))
+            time_const = coef[2 * gates + gate] * (0.5 + steady)
+            value = steady + (g_ref[gate, 0] - steady) * jnp.exp(-DT_HEART / time_const)
+            g_out[gate, 0] = value
+            updated.append(value)
+        weight = jnp.zeros((hy, row), jnp.float32)
+        for kind in range(kinds):
+            weight = weight + jnp.where(cell == kind, coef[3 * gates + kind * channels + channel], 0.0)
+        term = weight * updated[0] * updated[1] * (centre - coef[3 * gates + kinds * channels + channel])
+        ion = term if ion is None else ion + term
+    new_v = centre + DT_HEART * (current - ion)
+    c_out[0] = current
+    v_out[0] = new_v
+
+    @pl.when(i == 0)
+    def _():
+        xf_lo[...] = new_v
+        zf_lo[...] = jnp.zeros(zf_lo.shape, jnp.float32)
+        zf_hi[...] = jnp.zeros(zf_hi.shape, jnp.float32)
+
+    @pl.when(i == hx - 1)
+    def _():
+        xf_hi[...] = new_v
+
+    yf_lo[i] = new_v[0:1, :]
+    yf_hi[i] = new_v[hy - 1:hy, :]
+    zf_lo[...] = jnp.where(lane == i, jnp.broadcast_to(new_v[:, 0:1], (hy, row)), zf_lo[...])
+    zf_hi[...] = jnp.where(lane == i, jnp.broadcast_to(new_v[:, row - 1:row], (hy, row)), zf_hi[...])
+
+
+def heart_step(coef, kinds, voltage, gate_state, cell_type, halos):
+    hx, hy, row = voltage.shape
+    gates = gate_state.shape[0]
+    whole = lambda shape: pl.BlockSpec(shape, lambda i: (0,) * len(shape))
+    slab = pl.BlockSpec((1, hy, row), lambda i: (i, 0, 0))
+    gate_slab = pl.BlockSpec((gates, 1, hy, row), lambda i: (0, i, 0, 0))
+    plane = whole((hy, row))
+    rows = whole((hx, 1, row))
+    f32 = lambda shape: jax.ShapeDtypeStruct(shape, jnp.float32)
+    size = voltage.size
+    return pl.pallas_call(
+        functools.partial(heart_kernel, kinds),
+        grid=(hx,),
+        in_specs=[pl.BlockSpec(memory_space=pltpu.SMEM), whole((hx, hy, row)), gate_slab, slab,
+                  plane, plane, rows, rows, plane, plane],
+        out_specs=[gate_slab, slab, slab, plane, plane, rows, rows, plane, plane],
+        out_shape=[f32(gate_state.shape), f32(voltage.shape), f32(voltage.shape),
+                   f32((hy, row)), f32((hy, row)), f32((hx, 1, row)), f32((hx, 1, row)),
+                   f32((hy, row)), f32((hy, row))],
+        cost_estimate=pl.CostEstimate(flops=40 * gates * size, transcendentals=3 * gates * size,
+                                      bytes_accessed=4 * (2 * gates + 5) * size),
+        name="heart_step",
+    )(coef, voltage, gate_state, cell_type, *halos)
+
+
+def voltage_faces(voltage):
+    hx, hy, row = voltage.shape
+    pad = jnp.zeros((hy, row - hx), jnp.float32)
+    return (
+        voltage[0], voltage[hx - 1],
+        voltage[:, 0:1, :], voltage[:, hy - 1:hy, :],
+        jnp.concatenate([voltage[:, :, 0].T, pad], axis=1),
+        jnp.concatenate([voltage[:, :, row - 1].T, pad], axis=1),
+    )
+
+
 def local(
     heart_state,
     cell_type,
@@ -309,17 +402,30 @@
         sigma.append(value)
     riders = [faces_of(sigma[dim_index], dim_index) for dim_index in range(3)]
 
+    gate_count = gate_half.shape[0]
+    gate_sign = jnp.where(jnp.arange(gate_count) % 2 == 0, 1.0, -1.0).astype(jnp.float32)
+    coef = jnp.concatenate(
+        [gate_sign / gate_slope, gate_half, gate_tau, conduct.reshape(-1), reversal]
+    ).astype(jnp.float32)
+    kinds = conduct.shape[0]
+    faces_now = voltage_faces(voltage)
     currents = []
     for time_step in range(STEPS):
-        gate_state, ion_current = membrane(
-            voltage, gate_state, cell_type, gate_half, gate_slope, gate_tau, conduct, reversal
-        )
-        laplace, carried = heart_laplace(voltage, riders if time_step == 0 else None)
-        if time_step == 0:
-            sigma_halos = [item[0] for item in carried]
-        current = SIGMA_HEART * laplace
+        halos = []
+        for index, axis in enumerate(("gx", "gy", "gz")):
+            pairs = [(faces_now[2 * index + 1], faces_now[2 * index])]
+            if time_step == 0:
+                pairs.append(riders[index])
+            got = exchange_group(pairs, axis)
+            halos.extend(got[0])
+            if time_step == 0:
+                if index == 0:
+                    sigma_halos = []
+                sigma_halos.append(got[1])
+        outs = heart_step(coef, kinds, voltage, gate_state, cell_type, halos)
+        gate_state, current, voltage = outs[0], outs[1], outs[2]
+        faces_now = outs[3:]
         currents.append(current)
-        voltage = voltage + DT_HEART * (current - ion_current)
     heart_next = jnp.concatenate([voltage[None], gate_state], axis=0)
 
     payload = jnp.stack([item.reshape(blocks, row_len) for item in currents], axis=0)

time: 374 us -> 380 us (1.016)
  Pallas kernels: 101 us -> 130 us
  other arithmetic: 72.7 us -> 52.9 us
  waiting for transfers between devices: 36.2 us -> 42.6 us
  starting transfers between devices: 90.5 us -> 85.2 us
    pallas_call x0 -> x4, Pallas kernels: none -> 28.5 us  [heart_step(): pl.pallas_call(functools.partial(heart_kernel, kinds), grid=(hx,), in_spe...]
    add x13 -> x0, other arithmetic: 26.7 us -> none  [the longest x4 16.1 us: membrane(): steady + (gate_state - steady) * jnp.exp(-DT_HEART / time_const)]
    ppermute x14, waiting for transfers between devices: 12.3 us -> 24.9 us  [exchange(): lax.ppermute(bottom, axis, backward)]
    all_to_all x1, waiting for transfers between devices: 21.9 us -> 14.4 us  [local(): lax.all_to_all(send_values.reshape(STEPS, devices, capacity, row_len), ('...]
    ppermute x14, starting transfers between devices: 58.4 us -> 53.3 us  [exchange(): lax.ppermute(top, axis, forward)]
    concatenate x16 -> x1, local copies, waits for them, and re-layouts: 5.51 us -> 1.29 us  [local(): jnp.concatenate([gate_sign / gate_slope, gate_half, gate_tau, conduct.res...]
    slice x9 -> x3, local copies, waits for them, and re-layouts: 9.38 us -> 6.35 us  [shifted(): lax.slice_in_dim(block, 0, n - 1, axis=dim)]
  transfers between devices with their start and end apart: 37 -> 37, of which waited for: 8 -> 11; matrix products, arithmetic and copies ran while one was open for 18% -> 19% of each run, Pallas kernels for 0% -> 4%
where the time goes in v6:
time: 380 us; the launch traced here: 377 us
  Pallas kernels  130 us (34%)
  starting transfers between devices  85.2 us (22%)
  local copies, waits for them, and re-layouts  64.8 us (17%)
  other arithmetic  52.9 us (14%)
  waiting for transfers between devices  42.6 us (11%)
    pallas_call x3, Pallas kernels, run_sweep(): pl.pallas_call(functools.partial(sweep_kernel, first, second, final), gri...  87.3 us
    ppermute x14, starting transfers between devices, exchange(): lax.ppermute(top, axis, forward)  53.3 us
    pallas_call x4, Pallas kernels, heart_step(): pl.pallas_call(functools.partial(heart_kernel, kinds), grid=(hx,), in_spe...  28.5 us
    ppermute x14, waiting for transfers between devices, exchange(): lax.ppermute(bottom, axis, backward)  24.9 us
    ppermute x14, starting transfers between devices, exchange(): lax.ppermute(bottom, axis, backward)  18.2 us
    gather x2, local copies, waits for them, and re-layouts, local(): jnp.take(received, row_slot, axis=1)  17.7 us
    all_to_all x1, waiting for transfers between devices, local(): lax.all_to_all(send_values.reshape(STEPS, devices, capacity, row_len), ('...  14.4 us
    pallas_call x1, Pallas kernels, run_initial(): pl.pallas_call(functools.partial(initial_kernel, mid), grid=(source.shape...  14.1 us
  transfers between devices with their start and end apart: 37, of which 11 were waited for; matrix products, arithmetic and copies ran while one was open for 19% of the time, Pallas kernels for 4%

profile of v6, /device:TPU:0, one launch (start us, length us, event | category | flops | bytes accessed | tf_op | source)
XLA Modules:
  0.0 377.2 jit_solution(1390365377132226175)
XLA Ops:
  0.6 1.8 fusion.24
  4.9 5.4 %select_add_fusion = (f32[32,64,128]{2,1,0:T(8,128)S(1)}, pred[32,64,128]{2,1,0:T(8,128)(4,1)}, pred[32,64,128]{2,1,0:T(8,128)(4,1)}, pred[32,64,128]{2,1,0:T(8,128)(4,1)}, pred[32,64,128]{2,1,0:T(8,128)(4,1)}) fusion(f32[]{:T(128)} %bitcast.26, f32[]{:T(128)} %bitcast.25, f32[]{:T(128)} %bitcast.24, f32[]{:T(128)} %bitcast.23, s32[32,64,128]{2,1,0:T(8,128)} %param.20), kind=kLoop, calls=%fused_computation.24 | loop fusion | flops 2883584 | bytes 3145744 | tf_op jit(solution)/shard_map/add | solution.py:401
  17.0 6.8 %select_add_fusion.1 = (f32[32,64,128]{2,1,0:T(8,128)S(1)}, f32[32,64,128]{2,1,0:T(8,128)S(1)}) fusion(pred[32,64,128]{2,1,0:T(8,128)(4,1)} %get-tuple-element.134, pred[32,64,128]{2,1,0:T(8,128)(4,1)} %get-tuple-element.133, pred[32,64,128]{2,1,0:T(8,128)(4,1)} %get-tuple-element.132, pred[32,64,128]{2,1,0:T(8,128)(4,1)} %get-tuple-element.131, ...), kind=kLoop, calls=%fused_computation.25 | loop fusion | flops 3670016 | bytes 3145760 | tf_op jit(solution)/shard_map/add | solution.py:401
  25.4 5.1 %collective-permute-start.2 = (f32[5120]{0:T(1024)}, f32[5120]{0:T(1024)}, u32[]{:S(2)}, u32[]{:S(2)}) collective-permute-start(f32[5120]{0:T(1024)} %pad_maximum_fusion.4), channel_id=1, source_target_pairs={{0,2},{2,4},{4,6},{1,3},{3,5},{5,7},{8,10},{10,12},{12,14},{9,11},... | collective-permute-start | bytes 61448 | tf_op jit(solution)/shard_map/ppermute | solution.py:107
  33.0 4.0 %collective-permute-start = (f32[12288]{0:T(1024)}, f32[12288]{0:T(1024)}, u32[]{:S(2)}, u32[]{:S(2)}) collective-permute-start(f32[12288]{0:T(1024)} %pad_maximum_fusion.2), channel_id=1, source_target_pairs={{0,8},{8,16},{16,24},{1,9},{9,17},{17,25},{2,10},{10,18},{18,26},{... | collective-permute-start | bytes 147464 | tf_op jit(solution)/shard_map/ppermute | solution.py:107
  41.6 1.9 reduce-window.6
  46.4 1.7 slice.243.g_ref
  56.6 7.1 %heart_step.4 = (f32[18,8,32,128]{3,2,1,0:T(8,128)}, f32[8,32,128]{2,1,0:T(8,128)}, f32[8,32,128]{2,1,0:T(8,128)}, f32[32,128]{1,0:T(8,128)}, f32[32,128]{1,0:T(...) custom-call(f32[90]{0:T(128)} %concatenate.48.coef, ...), custom_call_target="tpu_custom_call" | custom-call | flops 23592960 | bytes 5373952 | tf_op jit(solution)/shard_map/heart_step/pallas_call | solution.py:331
  65.2 5.0 %gather_fusion = s32[768]{0:T(1024)S(1)} fusion(s32[256]{0:T(256)S(1)} %reshape.202, s32[1024]{0:T(1024)S(1)} %pad_clamp_fusion), kind=kCustom, calls=%fused_computation | custom fusion | bytes 9216 | tf_op jit(solution)/shard_map/gather | solution.py:389
  70.2 4.5 %collective-permute-start.7 = (f32[8,1,128]{2,1,0:T(1,128)S(1)}, f32[8,1,128]{2,1,0:T(1,128)S(1)}, u32[]{:S(2)}, u32[]{:S(2)}) collective-permute-start(f32[8,1,128]{2,1,0:T(1,128)S(1)} %copy-done.38), channel_id=1, source_target_pairs={{0,2},{2,4},{4,6},{1,3},{3,5},{5,7},{8,10},{10,12},{12,14},{9,11},... | collective-permute-start | bytes 12296 | tf_op jit(solution)/shard_map/ppermute | solution.py:107
  76.1 4.5 %collective-permute-start.5 = (f32[32,128]{1,0:T(8,128)S(1)}, f32[32,128]{1,0:T(8,128)S(1)}, u32[]{:S(2)}, u32[]{:S(2)}) collective-permute-start(f32[32,128]{1,0:T(8,128)S(1)} %copy-done.30), channel_id=1, source_target_pairs={{0,8},{8,16},{16,24},{1,9},{9,17},{17,25},{2,10},{10,18},{18,26},{... | collective-permute-start | bytes 49160 | tf_op jit(solution)/shard_map/ppermute | solution.py:107
  82.6 3.7 collective-permute-done.6.xhi
  86.9 7.1 %heart_step.5 = (f32[18,8,32,128]{3,2,1,0:T(8,128)}, f32[8,32,128]{2,1,0:T(8,128)}, f32[8,32,128]{2,1,0:T(8,128)}, f32[32,128]{1,0:T(8,128)}, f32[32,128]{1,0:T(...) custom-call(f32[90]{0:T(128)} %concatenate.48.coef, ...), custom_call_target="tpu_custom_call" | custom-call | flops 23592960 | bytes 5373952 | tf_op jit(solution)/shard_map/heart_step/pallas_call | solution.py:331
  95.5 7.3 %all-to-all-start = ((s32[32,1,24]{2,1,0:T(1,128)}), s32[32,1,24]{2,1,0:T(1,128)S(1)}, u32[]{:S(2)}, u32[]{:S(2)}) async-start(s32[32,1,24]{2,1,0:T(1,128)} %bitcast.33), calls=%async_computation | async-start | bytes 32768 | tf_op jit(solution)/shard_map/all_to_all | solution.py:390
  102.8 3.7 collective-permute-start.12
  107.7 3.4 collective-permute-start.10
  113.1 3.9 %collective-permute-done.11.xhi = f32[32,128]{1,0:T(8,128)S(1)} collective-permute-done((f32[32,128]{1,0:T(8,128)}, f32[32,128]{1,0:T(8,128)S(1)}, u32[]{:S(2)}, u32[]{:S(2)}) %collective-permute-start.11) | collective-permute-done | bytes 16416 | tf_op jit(solution)/shard_map/ppermute | solution.py:107
  117.6 7.1 %heart_step.6 = (f32[18,8,32,128]{3,2,1,0:T(8,128)}, f32[8,32,128]{2,1,0:T(8,128)}, f32[8,32,128]{2,1,0:T(8,128)}, f32[32,128]{1,0:T(8,128)}, f32[32,128]{1,0:T(...) custom-call(f32[90]{0:T(128)} %concatenate.48.coef, ...), custom_call_target="tpu_custom_call" | custom-call | flops 23592960 | bytes 5373952 | tf_op jit(solution)/shard_map/heart_step/pallas_call | solution.py:331
  125.7 4.5 %collective-permute-start.17 = (f32[8,1,128]{2,1,0:T(1,128)}, f32[8,1,128]{2,1,0:T(1,128)S(1)}, u32[]{:S(2)}, u32[]{:S(2)}) collective-permute-start(f32[8,1,128]{2,1,0:T(1,128)} %get-tuple-element.80), channel_id=1, source_target_pairs={{0,2},{2,4},{4,6},{1,3},{3,5},{5,7},{8,10},{10,12},{12,14},{9,11},... | collective-permute-start | bytes 12296 | tf_op jit(solution)/shard_map/ppermute | solution.py:107
  131.6 4.3 %collective-permute-start.15 = (f32[32,128]{1,0:T(8,128)}, f32[32,128]{1,0:T(8,128)S(1)}, u32[]{:S(2)}, u32[]{:S(2)}) collective-permute-start(f32[32,128]{1,0:T(8,128)} %get-tuple-element.78), channel_id=1, source_target_pairs={{0,8},{8,16},{16,24},{1,9},{9,17},{17,25},{2,10},{10,18},{18,26},{... | collective-permute-start | bytes 49160 | tf_op jit(solution)/shard_map/ppermute | solution.py:107
  137.8 3.9 %collective-permute-done.16.xhi = f32[32,128]{1,0:T(8,128)S(1)} collective-permute-done((f32[32,128]{1,0:T(8,128)}, f32[32,128]{1,0:T(8,128)S(1)}, u32[]{:S(2)}, u32[]{:S(2)}) %collective-permute-start.16) | collective-permute-done | bytes 16416 | tf_op jit(solution)/shard_map/ppermute | solution.py:107
  142.3 7.1 %heart_step.7 = (f32[18,8,32,128]{3,2,1,0:T(8,128)}, f32[8,32,128]{2,1,0:T(8,128)}, f32[8,32,128]{2,1,0:T(8,128)}, f32[32,128]{1,0:T(8,128)}, f32[32,128]{1,0:T(...) custom-call(f32[90]{0:T(128)} %concatenate.48.coef, ...), custom_call_target="tpu_custom_call" | custom-call | flops 23592960 | bytes 5373952 | tf_op jit(solution)/shard_map/heart_step/pallas_call | solution.py:331
  150.9 2.8 gather_fusion.1
  153.7 4.1 %select_select_fusion.1 = f32[4,32,24,128]{3,0,2,1:T(4,128)} fusion(f32[4,32,24,128]{3,0,2,1:T(4,128)S(1)} %bitcast.89, pred[32,24]{1,0:T(8,128)(4,1)S(1)} %broadcast_in_dim.159, pred[32,24]{1,0:T(8,128)(4,1)S(1)} %broadcast_in_dim.157), kind=kLoop, calls=%fused_computation.8 | loop fusion | flops 786432 | bytes 3147264 | tf_op jit(solution)/shard_map/jit(_where)/select_n | solution.py:432
  157.8 5.8 %all-to-all-start.1 = ((f32[4,32,24,128]{3,0,2,1:T(4,128)}), f32[4,32,24,128]{3,0,2,1:T(4,128)S(1)}, u32[]{:S(2)}, u32[]{:S(2)}) async-start(f32[4,32,24,128]{3,0,2,1:T(4,128)} %select_select_fusion.1), calls=%async_computation.1 | async-start | bytes 3145728 | tf_op jit(solution)/shard_map/all_to_all | solution.py:433
  163.7 3.1 fusion.21
  168.3 1.7 fusion.19
  171.6 2.8 iota_reduce_fusion
  175.9 1.9 slice.299
  177.8 1.8 slice.298
  181.2 6.9 %broadcast_divide_fusion = (f32[32,64,128]{2,1,0:T(8,128)}, f32[32,64,128]{2,1,0:T(8,128)}, f32[32,64,128]{2,1,0:T(8,128)}, f32[32,64,128]{2,1,0:T(8,128)}, f32[...) fusion(f32[32,64,128]{2,1,0:T(8,128)} %copy-done.2, ...), kind=kLoop, calls=%fused_computation.31 | loop fusion | flops 6553600 | bytes 17825792 | tf_op jit(solution)/shard_map/div | solution.py:453
  188.1 14.4 %all-to-all-done.1 = f32[4,32,24,128]{3,0,2,1:T(4,128)S(1)} async-done(((f32[4,32,24,128]{3,0,2,1:T(4,128)}), f32[4,32,24,128]{3,0,2,1:T(4,128)S(1)}, u32[]{:S(2)}, u32[]{:S(2)}) %all-to-all-start.1) | async-done | bytes 1572896 | tf_op jit(solution)/shard_map/all_to_all | solution.py:433
  202.5 15.3 %gather_fusion.2 = f32[2048,4,128]{2,1,0:T(4,128)} fusion(f32[4,768,128]{2,0,1:T(4,128)S(1)} %bitcast.86, s32[2048]{0:T(1024)S(1)} %fusion.11), kind=kCustom, calls=%fused_computation.2 | custom fusion | bytes 8396800 | tf_op jit(solution)/shard_map/jit(_take)/gather | solution.py:440
  217.8 2.5 copy.42
  220.2 2.8 select_select_fusion.r_ref
  223.0 14.1 %chebyshev_start.1 = (f32[4,32,64,128]{3,2,1,0:T(8,128)}, f32[4,64,128]{2,1,0:T(8,128)}, f32[4,64,128]{2,1,0:T(8,128)}, f32[4,32,1,128]{3,2,1,0:T(1,128)}, f32[4...) custom-call(f32[4,32,64,128]{3,2,1,0:T(8,128)} %select_select_fusion.r_ref, ...), custom_call_target="tpu_custom_call" | custom-call | flops 2097152 | bytes 9437184 | tf_op jit(solution)/shard_map/chebyshev_start/pallas_call | solution.py:229
  240.7 2.7 collective-permute-start.20
  246.7 4.8 %collective-permute-done.21.xhi = f32[4,64,128]{2,1,0:T(8,128)S(1)} collective-permute-done((f32[4,64,128]{2,1,0:T(8,128)}, f32[4,64,128]{2,1,0:T(8,128)S(1)}, u32[]{:S(2)}, u32[]{:S(2)}) %collective-permute-start.21) | collective-permute-done | bytes 131104 | tf_op jit(solution)/shard_map/ppermute | solution.py:107
  252.1 28.0 %chebyshev_sweep.3 = (f32[4,32,64,128]{3,2,1,0:T(8,128)}, f32[4,32,64,128]{3,2,1,0:T(8,128)}, f32[4,32,64,128]{3,2,1,0:T(8,128)}, f32[4,64,128]{2,1,0:T(8,128)},...) custom-call(f32[4,32,64,128]{3,2,1,0:T(8,128)} %get-tuple-element.92, ...), custom_call_target="tpu_custom_call" | custom-call | flops 31457280 | bytes 36700160 | tf_op jit(solution)/shard_map/chebyshev_sweep/pallas_call | solution.py:252
  281.1 4.3 %collective-permute-start.27 = (f32[4,32,1,128]{3,2,1,0:T(1,128)}, f32[4,32,1,128]{3,2,1,0:T(1,128)S(1)}, u32[]{:S(2)}, u32[]{:S(2)}) collective-permute-start(f32[4,32,1,128]{3,2,1,0:T(1,128)} %get-tuple-element.104), channel_id=1, source_target_pairs={{0,2},{2,4},{4,6},{1,3},{3,5},{5,7},{8,10},{10,12},{12,14},{9,11},... | collective-permute-start | bytes 196616 | tf_op jit(solution)/shard_map/ppermute | solution.py:107
  286.6 3.7 collective-permute-start.25
  293.7 4.0 %collective-permute-done.26.xhi = f32[4,64,128]{2,1,0:T(8,128)S(1)} collective-permute-done((f32[4,64,128]{2,1,0:T(8,128)}, f32[4,64,128]{2,1,0:T(8,128)S(1)}, u32[]{:S(2)}, u32[]{:S(2)}) %collective-permute-start.26) | collective-permute-done | bytes 131104 | tf_op jit(solution)/shard_map/ppermute | solution.py:107
  298.4 28.1 %chebyshev_sweep.4 = (f32[4,32,64,128]{3,2,1,0:T(8,128)}, f32[4,32,64,128]{3,2,1,0:T(8,128)}, f32[4,32,64,128]{3,2,1,0:T(8,128)}, f32[4,64,128]{2,1,0:T(8,128)},...) custom-call(f32[4,32,64,128]{3,2,1,0:T(8,128)} %get-tuple-element.99, ...), custom_call_target="tpu_custom_call" | custom-call | flops 31457280 | bytes 36700160 | tf_op jit(solution)/shard_map/chebyshev_sweep/pallas_call | solution.py:252
  327.5 1.8 pad_maximum_fusion
  329.3 4.3 %collective-permute-start.32 = (f32[4,32,1,128]{3,2,1,0:T(1,128)S(1)}, f32[4,32,1,128]{3,2,1,0:T(1,128)S(1)}, u32[]{:S(2)}, u32[]{:S(2)}) collective-permute-start(f32[4,32,1,128]{3,2,1,0:T(1,128)S(1)} %copy-done.28), channel_id=1, source_target_pairs={{0,2},{2,4},{4,6},{1,3},{3,5},{5,7},{8,10},{10,12},{12,14},{9,11},... | collective-permute-start | bytes 196616 | tf_op jit(solution)/shard_map/ppermute | solution.py:107
  334.9 3.1 collective-permute-start.30
  341.1 4.1 %collective-permute-done.31.xhi = f32[4,64,128]{2,1,0:T(8,128)S(1)} collective-permute-done((f32[4,64,128]{2,1,0:T(8,128)S(1)}, f32[4,64,128]{2,1,0:T(8,128)S(1)}, u32[]{:S(2)}, u32[]{:S(2)}) %collective-permute-start.31) | collective-permute-done | bytes 131104 | tf_op jit(solution)/shard_map/ppermute | solution.py:107
  345.8 31.1 %chebyshev_sweep.5 = (f32[4,32,64,128]{3,2,1,0:T(8,128)}, f32[4,32,64,128]{3,2,1,0:T(8,128)}, f32[32,64,4,128]{3,2,1,0:T(4,128)}, f32[4,64,128]{2,1,0:T(8,128)},...) custom-call(f32[4,32,64,128]{3,2,1,0:T(8,128)} %get-tuple-element.10, ...), custom_call_target="tpu_custom_call" | custom-call | flops 31457280 | bytes 36700160 | tf_op jit(solution)/shard_map/chebyshev_sweep/pallas_call | solution.py:252
  (219 shorter events, 71.6 us)
Async XLA Ops:
  10.4 22.0 %copy-start.3 = (f32[19,8,32,128]{3,2,1,0:T(8,128)S(1)}, f32[19,8,32,128]{3,2,1,0:T(8,128)}, u32[]{:S(2)}) copy-start(f32[19,8,32,128]{3,2,1,0:T(8,128)} %param.11) | copy-start | bytes 7471108
  13.6 25.4 %copy-start.45 = (f32[18]{0:T(128)S(1)}, f32[18]{0:T(128)}, u32[]{:S(2)}) copy-start(f32[18]{0:T(128)} %param.14) | copy-start | bytes 220
  13.6 26.0 %copy-start.22 = (s32[8,32,1]{1,2,0:T(1,128)S(1)}, s32[8,32,1]{1,2,0:T(1,128)}, u32[]{:S(2)}) copy-start(s32[8,32,1]{1,2,0:T(1,128)} %param.18) | copy-start | bytes 3076
  15.7 36.3 %collective-permute-start.4 = (f32[6144]{0:T(1024)}, f32[6144]{0:T(1024)}, u32[]{:S(2)}, u32[]{:S(2)}) collective-permute-start(f32[6144]{0:T(1024)} %maximum_select_fusion), channel_id=1, source_target_pairs={{0,1},{1,0},{2,3},{3,2},{4,5},{5,4},{6,7},{7,6},{8,9},{9,8},{10,11... | collective-permute-start | bytes 73736 | tf_op jit(solution)/shard_map/ppermute | solution.py:102
  25.4 24.1 %collective-permute-start.2 = (f32[5120]{0:T(1024)}, f32[5120]{0:T(1024)}, u32[]{:S(2)}, u32[]{:S(2)}) collective-permute-start(f32[5120]{0:T(1024)} %pad_maximum_fusion.4), channel_id=1, source_target_pairs={{0,2},{2,4},{4,6},{1,3},{3,5},{5,7},{8,10},{10,12},{12,14},{9,11},... | collective-permute-start | bytes 61448 | tf_op jit(solution)/shard_map/ppermute | solution.py:107
  31.0 19.7 %collective-permute-start.3 = (f32[5120]{0:T(1024)}, f32[5120]{0:T(1024)}, u32[]{:S(2)}, u32[]{:S(2)}) collective-permute-start(f32[5120]{0:T(1024)} %pad_maximum_fusion.5), channel_id=1, source_target_pairs={{2,0},{4,2},{6,4},{3,1},{5,3},{7,5},{10,8},{12,10},{14,12},{11,9},... | collective-permute-start | bytes 61448 | tf_op jit(solution)/shard_map/ppermute | solution.py:107
  33.0 21.0 %collective-permute-start = (f32[12288]{0:T(1024)}, f32[12288]{0:T(1024)}, u32[]{:S(2)}, u32[]{:S(2)}) collective-permute-start(f32[12288]{0:T(1024)} %pad_maximum_fusion.2), channel_id=1, source_target_pairs={{0,8},{8,16},{16,24},{1,9},{9,17},{17,25},{2,10},{10,18},{18,26},{... | collective-permute-start | bytes 147464 | tf_op jit(solution)/shard_map/ppermute | solution.py:107
  37.6 17.7 %collective-permute-start.1 = (f32[12288]{0:T(1024)}, f32[12288]{0:T(1024)}, u32[]{:S(2)}, u32[]{:S(2)}) collective-permute-start(f32[12288]{0:T(1024)} %pad_maximum_fusion.3), channel_id=1, source_target_pairs={{8,0},{16,8},{24,16},{9,1},{17,9},{25,17},{10,2},{18,10},{26,18},{... | collective-permute-start | bytes 147464 | tf_op jit(solution)/shard_map/ppermute | solution.py:107
  48.1 16.4 %copy-start.23 = (s32[8,32,1]{1,2,0:T(1,128)S(1)}, s32[8,32,1]{1,2,0:T(1,128)}, u32[]{:S(2)}) copy-start(s32[8,32,1]{1,2,0:T(1,128)} %param.19) | copy-start | bytes 3076
  63.8 12.3 %copy-start.30 = (f32[32,128]{1,0:T(8,128)S(1)}, f32[32,128]{1,0:T(8,128)}, u32[]{:S(2)}) copy-start(f32[32,128]{1,0:T(8,128)} %get-tuple-element.62) | copy-start | bytes 49156
  63.8 16.9 %copy-start.29 = (f32[32,128]{1,0:T(8,128)S(1)}, f32[32,128]{1,0:T(8,128)}, u32[]{:S(2)}) copy-start(f32[32,128]{1,0:T(8,128)} %get-tuple-element.63) | copy-start | bytes 49156
  64.5 17.5 %collective-permute-start.9 = (f32[32,128]{1,0:T(8,128)S(1)}, f32[32,128]{1,0:T(8,128)S(1)}, u32[]{:S(2)}, u32[]{:S(2)}) collective-permute-start(f32[32,128]{1,0:T(8,128)S(1)} %broadcast_select_fusion.19), channel_id=1, source_target_pairs={{0,1},{1,0},{2,3},{3,2},{4,5},{5,4},{6,7},{7,6},{8,9},{9,8},{10,11... | collective-permute-start | bytes 49160 | tf_op jit(solution)/shard_map/ppermute | solution.py:102
  70.2 12.4 %collective-permute-start.7 = (f32[8,1,128]{2,1,0:T(1,128)S(1)}, f32[8,1,128]{2,1,0:T(1,128)S(1)}, u32[]{:S(2)}, u32[]{:S(2)}) collective-permute-start(f32[8,1,128]{2,1,0:T(1,128)S(1)} %copy-done.38), channel_id=1, source_target_pairs={{0,2},{2,4},{4,6},{1,3},{3,5},{5,7},{8,10},{10,12},{12,14},{9,11},... | collective-permute-start | bytes 12296 | tf_op jit(solution)/shard_map/ppermute | solution.py:107
  74.8 7.8 %collective-permute-start.8 = (f32[8,1,128]{2,1,0:T(1,128)S(1)}, f32[8,1,128]{2,1,0:T(1,128)S(1)}, u32[]{:S(2)}, u32[]{:S(2)}) collective-permute-start(f32[8,1,128]{2,1,0:T(1,128)S(1)} %copy-done.37), channel_id=1, source_target_pairs={{2,0},{4,2},{6,4},{3,1},{5,3},{7,5},{10,8},{12,10},{14,12},{11,9},... | collective-permute-start | bytes 12296 | tf_op jit(solution)/shard_map/ppermute | solution.py:107
  76.1 6.5 %collective-permute-start.5 = (f32[32,128]{1,0:T(8,128)S(1)}, f32[32,128]{1,0:T(8,128)S(1)}, u32[]{:S(2)}, u32[]{:S(2)}) collective-permute-start(f32[32,128]{1,0:T(8,128)S(1)} %copy-done.30), channel_id=1, source_target_pairs={{0,8},{8,16},{16,24},{1,9},{9,17},{17,25},{2,10},{10,18},{18,26},{... | collective-permute-start | bytes 49160 | tf_op jit(solution)/shard_map/ppermute | solution.py:107
  80.7 5.6 %collective-permute-start.6 = (f32[32,128]{1,0:T(8,128)S(1)}, f32[32,128]{1,0:T(8,128)S(1)}, u32[]{:S(2)}, u32[]{:S(2)}) collective-permute-start(f32[32,128]{1,0:T(8,128)S(1)} %copy-done.29), channel_id=1, source_target_pairs={{8,0},{16,8},{24,16},{9,1},{17,9},{25,17},{10,2},{18,10},{26,18},{... | collective-permute-start | bytes 49160 | tf_op jit(solution)/shard_map/ppermute | solution.py:107
  94.8 17.6 %collective-permute-start.14 = (f32[32,128]{1,0:T(8,128)S(1)}, f32[32,128]{1,0:T(8,128)S(1)}, u32[]{:S(2)}, u32[]{:S(2)}) collective-permute-start(f32[32,128]{1,0:T(8,128)S(1)} %broadcast_select_fusion.18), channel_id=1, source_target_pairs={{0,1},{1,0},{2,3},{3,2},{4,5},{5,4},{6,7},{7,6},{8,9},{9,8},{10,11... | collective-permute-start | bytes 49160 | tf_op jit(solution)/shard_map/ppermute | solution.py:102
  95.5 62.3 %all-to-all-start = ((s32[32,1,24]{2,1,0:T(1,128)}), s32[32,1,24]{2,1,0:T(1,128)S(1)}, u32[]{:S(2)}, u32[]{:S(2)}) async-start(s32[32,1,24]{2,1,0:T(1,128)} %bitcast.33), calls=%async_computation | async-start | bytes 32768 | tf_op jit(solution)/shard_map/all_to_all | solution.py:390
  102.8 10.3 %collective-permute-start.12 = (f32[8,1,128]{2,1,0:T(1,128)}, f32[8,1,128]{2,1,0:T(1,128)S(1)}, u32[]{:S(2)}, u32[]{:S(2)}) collective-permute-start(f32[8,1,128]{2,1,0:T(1,128)} %get-tuple-element.72), channel_id=1, source_target_pairs={{0,2},{2,4},{4,6},{1,3},{3,5},{5,7},{8,10},{10,12},{12,14},{9,11},... | collective-permute-start | bytes 12296 | tf_op jit(solution)/shard_map/ppermute | solution.py:107
  106.4 6.6 %collective-permute-start.13 = (f32[8,1,128]{2,1,0:T(1,128)}, f32[8,1,128]{2,1,0:T(1,128)S(1)}, u32[]{:S(2)}, u32[]{:S(2)}) collective-permute-start(f32[8,1,128]{2,1,0:T(1,128)} %get-tuple-element.73), channel_id=1, source_target_pairs={{2,0},{4,2},{6,4},{3,1},{5,3},{7,5},{10,8},{12,10},{14,12},{11,9},... | collective-permute-start | bytes 12296 | tf_op jit(solution)/shard_map/ppermute | solution.py:107
  107.7 5.3 %collective-permute-start.10 = (f32[32,128]{1,0:T(8,128)}, f32[32,128]{1,0:T(8,128)S(1)}, u32[]{:S(2)}, u32[]{:S(2)}) collective-permute-start(f32[32,128]{1,0:T(8,128)} %get-tuple-element.70), channel_id=1, source_target_pairs={{0,8},{8,16},{16,24},{1,9},{9,17},{17,25},{2,10},{10,18},{18,26},{... | collective-permute-start | bytes 49160 | tf_op jit(solution)/shard_map/ppermute | solution.py:107
  111.1 5.8 %collective-permute-start.11 = (f32[32,128]{1,0:T(8,128)}, f32[32,128]{1,0:T(8,128)S(1)}, u32[]{:S(2)}, u32[]{:S(2)}) collective-permute-start(f32[32,128]{1,0:T(8,128)} %get-tuple-element.71), channel_id=1, source_target_pairs={{8,0},{16,8},{24,16},{9,1},{17,9},{25,17},{10,2},{18,10},{26,18},{... | collective-permute-start | bytes 49160 | tf_op jit(solution)/shard_map/ppermute | solution.py:107
  124.7 24.7 %copy-start.13 = (f32[8,32,128]{2,1,0:T(8,128)S(1)}, f32[8,32,128]{2,1,0:T(8,128)}, u32[]{:S(2)}) copy-start(f32[8,32,128]{2,1,0:T(8,128)} %get-tuple-element.88) | copy-start | bytes 393220
  124.7 24.7 %copy-start.14 = (f32[8,32,128]{2,1,0:T(8,128)S(1)}, f32[8,32,128]{2,1,0:T(8,128)}, u32[]{:S(2)}) copy-start(f32[8,32,128]{2,1,0:T(8,128)} %get-tuple-element.89) | copy-start | bytes 393220
  124.7 24.7 %copy-start.15 = (f32[8,32,128]{2,1,0:T(8,128)S(1)}, f32[8,32,128]{2,1,0:T(8,128)}, u32[]{:S(2)}) copy-start(f32[8,32,128]{2,1,0:T(8,128)} %get-tuple-element.90) | copy-start | bytes 393220
  125.5 11.6 %collective-permute-start.19 = (f32[32,128]{1,0:T(8,128)S(1)}, f32[32,128]{1,0:T(8,128)S(1)}, u32[]{:S(2)}, u32[]{:S(2)}) collective-permute-start(f32[32,128]{1,0:T(8,128)S(1)} %broadcast_select_fusion.17), channel_id=1, source_target_pairs={{0,1},{1,0},{2,3},{3,2},{4,5},{5,4},{6,7},{7,6},{8,9},{9,8},{10,11... | collective-permute-start | bytes 49160 | tf_op jit(solution)/shard_map/ppermute | solution.py:102
  125.7 12.1 %collective-permute-start.17 = (f32[8,1,128]{2,1,0:T(1,128)}, f32[8,1,128]{2,1,0:T(1,128)S(1)}, u32[]{:S(2)}, u32[]{:S(2)}) collective-permute-start(f32[8,1,128]{2,1,0:T(1,128)} %get-tuple-element.80), channel_id=1, source_target_pairs={{0,2},{2,4},{4,6},{1,3},{3,5},{5,7},{8,10},{10,12},{12,14},{9,11},... | collective-permute-start | bytes 12296 | tf_op jit(solution)/shard_map/ppermute | solution.py:107
  130.3 7.5 %collective-permute-start.18 = (f32[8,1,128]{2,1,0:T(1,128)}, f32[8,1,128]{2,1,0:T(1,128)S(1)}, u32[]{:S(2)}, u32[]{:S(2)}) collective-permute-start(f32[8,1,128]{2,1,0:T(1,128)} %get-tuple-element.81), channel_id=1, source_target_pairs={{2,0},{4,2},{6,4},{3,1},{5,3},{7,5},{10,8},{12,10},{14,12},{11,9},... | collective-permute-start | bytes 12296 | tf_op jit(solution)/shard_map/ppermute | solution.py:107
  131.6 6.2 %collective-permute-start.15 = (f32[32,128]{1,0:T(8,128)}, f32[32,128]{1,0:T(8,128)S(1)}, u32[]{:S(2)}, u32[]{:S(2)}) collective-permute-start(f32[32,128]{1,0:T(8,128)} %get-tuple-element.78), channel_id=1, source_target_pairs={{0,8},{8,16},{16,24},{1,9},{9,17},{17,25},{2,10},{10,18},{18,26},{... | collective-permute-start | bytes 49160 | tf_op jit(solution)/shard_map/ppermute | solution.py:107
  135.9 5.8 %collective-permute-start.16 = (f32[32,128]{1,0:T(8,128)}, f32[32,128]{1,0:T(8,128)S(1)}, u32[]{:S(2)}, u32[]{:S(2)}) collective-permute-start(f32[32,128]{1,0:T(8,128)} %get-tuple-element.79), channel_id=1, source_target_pairs={{8,0},{16,8},{24,16},{9,1},{17,9},{25,17},{10,2},{18,10},{26,18},{... | collective-permute-start | bytes 49160 | tf_op jit(solution)/shard_map/ppermute | solution.py:107
  157.8 44.7 %all-to-all-start.1 = ((f32[4,32,24,128]{3,0,2,1:T(4,128)}), f32[4,32,24,128]{3,0,2,1:T(4,128)S(1)}, u32[]{:S(2)}, u32[]{:S(2)}) async-start(f32[4,32,24,128]{3,0,2,1:T(4,128)} %select_select_fusion.1), calls=%async_computation.1 | async-start | bytes 3145728 | tf_op jit(solution)/shard_map/all_to_all | solution.py:433
  238.0 6.7 %collective-permute-start.24 = (f32[4,32,64]{2,1,0:T(8,128)S(1)}, f32[4,32,64]{2,1,0:T(8,128)S(1)}, u32[]{:S(2)}, u32[]{:S(2)}) collective-permute-start(f32[4,32,64]{2,1,0:T(8,128)S(1)} %broadcast_select_fusion.8), channel_id=1, source_target_pairs={{0,1},{1,0},{2,3},{3,2},{4,5},{5,4},{6,7},{7,6},{8,9},{9,8},{10,11... | collective-permute-start | bytes 98312 | tf_op jit(solution)/shard_map/ppermute | solution.py:102
  238.1 7.3 %collective-permute-start.22 = (f32[4,32,1,128]{3,2,1,0:T(1,128)}, f32[4,32,1,128]{3,2,1,0:T(1,128)S(1)}, u32[]{:S(2)}, u32[]{:S(2)}) collective-permute-start(f32[4,32,1,128]{3,2,1,0:T(1,128)} %get-tuple-element.95), channel_id=1, source_target_pairs={{0,2},{2,4},{4,6},{1,3},{3,5},{5,7},{8,10},{10,12},{12,14},{9,11},... | collective-permute-start | bytes 196616 | tf_op jit(solution)/shard_map/ppermute | solution.py:107
  239.4 6.6 %collective-permute-start.23 = (f32[4,32,1,128]{3,2,1,0:T(1,128)}, f32[4,32,1,128]{3,2,1,0:T(1,128)S(1)}, u32[]{:S(2)}, u32[]{:S(2)}) collective-permute-start(f32[4,32,1,128]{3,2,1,0:T(1,128)} %get-tuple-element.96), channel_id=1, source_target_pairs={{2,0},{4,2},{6,4},{3,1},{5,3},{7,5},{10,8},{12,10},{14,12},{11,9},... | collective-permute-start | bytes 196616 | tf_op jit(solution)/shard_map/ppermute | solution.py:107
  240.7 6.0 %collective-permute-start.20 = (f32[4,64,128]{2,1,0:T(8,128)}, f32[4,64,128]{2,1,0:T(8,128)S(1)}, u32[]{:S(2)}, u32[]{:S(2)}) collective-permute-start(f32[4,64,128]{2,1,0:T(8,128)} %get-tuple-element.93), channel_id=1, source_target_pairs={{0,8},{8,16},{16,24},{1,9},{9,17},{17,25},{2,10},{10,18},{18,26},{... | collective-permute-start | bytes 393224 | tf_op jit(solution)/shard_map/ppermute | solution.py:107
  243.4 8.0 %collective-permute-start.21 = (f32[4,64,128]{2,1,0:T(8,128)}, f32[4,64,128]{2,1,0:T(8,128)S(1)}, u32[]{:S(2)}, u32[]{:S(2)}) collective-permute-start(f32[4,64,128]{2,1,0:T(8,128)} %get-tuple-element.94), channel_id=1, source_target_pairs={{8,0},{16,8},{24,16},{9,1},{17,9},{25,17},{10,2},{18,10},{26,18},{... | collective-permute-start | bytes 393224 | tf_op jit(solution)/shard_map/ppermute | solution.py:107
  281.0 10.6 %collective-permute-start.29 = (f32[4,32,64]{2,1,0:T(8,128)S(1)}, f32[4,32,64]{2,1,0:T(8,128)S(1)}, u32[]{:S(2)}, u32[]{:S(2)}) collective-permute-start(f32[4,32,64]{2,1,0:T(8,128)S(1)} %broadcast_select_fusion.7), channel_id=1, source_target_pairs={{0,1},{1,0},{2,3},{3,2},{4,5},{5,4},{6,7},{7,6},{8,9},{9,8},{10,11... | collective-permute-start | bytes 98312 | tf_op jit(solution)/shard_map/ppermute | solution.py:102
  281.1 11.2 %collective-permute-start.27 = (f32[4,32,1,128]{3,2,1,0:T(1,128)}, f32[4,32,1,128]{3,2,1,0:T(1,128)S(1)}, u32[]{:S(2)}, u32[]{:S(2)}) collective-permute-start(f32[4,32,1,128]{3,2,1,0:T(1,128)} %get-tuple-element.104), channel_id=1, source_target_pairs={{0,2},{2,4},{4,6},{1,3},{3,5},{5,7},{8,10},{10,12},{12,14},{9,11},... | collective-permute-start | bytes 196616 | tf_op jit(solution)/shard_map/ppermute | solution.py:107
  285.3 7.0 %collective-permute-start.28 = (f32[4,32,1,128]{3,2,1,0:T(1,128)}, f32[4,32,1,128]{3,2,1,0:T(1,128)S(1)}, u32[]{:S(2)}, u32[]{:S(2)}) collective-permute-start(f32[4,32,1,128]{3,2,1,0:T(1,128)} %get-tuple-element.105), channel_id=1, source_target_pairs={{2,0},{4,2},{6,4},{3,1},{5,3},{7,5},{10,8},{12,10},{14,12},{11,9},... | collective-permute-start | bytes 196616 | tf_op jit(solution)/shard_map/ppermute | solution.py:107
  286.6 7.1 %collective-permute-start.25 = (f32[4,64,128]{2,1,0:T(8,128)}, f32[4,64,128]{2,1,0:T(8,128)S(1)}, u32[]{:S(2)}, u32[]{:S(2)}) collective-permute-start(f32[4,64,128]{2,1,0:T(8,128)} %get-tuple-element.102), channel_id=1, source_target_pairs={{0,8},{8,16},{16,24},{1,9},{9,17},{17,25},{2,10},{10,18},{18,26},{... | collective-permute-start | bytes 393224 | tf_op jit(solution)/shard_map/ppermute | solution.py:107
  290.3 7.4 %collective-permute-start.26 = (f32[4,64,128]{2,1,0:T(8,128)}, f32[4,64,128]{2,1,0:T(8,128)S(1)}, u32[]{:S(2)}, u32[]{:S(2)}) collective-permute-start(f32[4,64,128]{2,1,0:T(8,128)} %get-tuple-element.103), channel_id=1, source_target_pairs={{8,0},{16,8},{24,16},{9,1},{17,9},{25,17},{10,2},{18,10},{26,18},{... | collective-permute-start | bytes 393224 | tf_op jit(solution)/shard_map/ppermute | solution.py:107
  298.4 29.1 %copy-start.4 = (f32[18,8,32,128]{3,2,1,0:T(8,128)S(1)}, f32[18,8,32,128]{3,2,1,0:T(8,128)}, u32[]{:S(2)}) copy-start(f32[18,8,32,128]{3,2,1,0:T(8,128)} %get-tuple-element.85) | copy-start | bytes 7077892
  298.4 29.1 %copy-start.12 = (f32[8,32,128]{2,1,0:T(8,128)S(1)}, f32[8,32,128]{2,1,0:T(8,128)}, u32[]{:S(2)}) copy-start(f32[8,32,128]{2,1,0:T(8,128)} %get-tuple-element.84) | copy-start | bytes 393220
  327.4 11.9 %collective-permute-start.34 = (f32[4,32,64]{2,1,0:T(8,128)S(1)}, f32[4,32,64]{2,1,0:T(8,128)S(1)}, u32[]{:S(2)}, u32[]{:S(2)}) collective-permute-start(f32[4,32,64]{2,1,0:T(8,128)S(1)} %broadcast_select_fusion.6), channel_id=1, source_target_pairs={{0,1},{1,0},{2,3},{3,2},{4,5},{5,4},{6,7},{7,6},{8,9},{9,8},{10,11... | collective-permute-start | bytes 98312 | tf_op jit(solution)/shard_map/ppermute | solution.py:102
  329.3 10.7 %collective-permute-start.32 = (f32[4,32,1,128]{3,2,1,0:T(1,128)S(1)}, f32[4,32,1,128]{3,2,1,0:T(1,128)S(1)}, u32[]{:S(2)}, u32[]{:S(2)}) collective-permute-start(f32[4,32,1,128]{3,2,1,0:T(1,128)S(1)} %copy-done.28), channel_id=1, source_target_pairs={{0,2},{2,4},{4,6},{1,3},{3,5},{5,7},{8,10},{10,12},{12,14},{9,11},... | collective-permute-start | bytes 196616 | tf_op jit(solution)/shard_map/ppermute | solution.py:107
  333.6 6.4 %collective-permute-start.33 = (f32[4,32,1,128]{3,2,1,0:T(1,128)S(1)}, f32[4,32,1,128]{3,2,1,0:T(1,128)S(1)}, u32[]{:S(2)}, u32[]{:S(2)}) collective-permute-start(f32[4,32,1,128]{3,2,1,0:T(1,128)S(1)} %copy-done.27), channel_id=1, source_target_pairs={{2,0},{4,2},{6,4},{3,1},{5,3},{7,5},{10,8},{12,10},{14,12},{11,9},... | collective-permute-start | bytes 196616 | tf_op jit(solution)/shard_map/ppermute | solution.py:107
  334.9 6.2 %collective-permute-start.30 = (f32[4,64,128]{2,1,0:T(8,128)S(1)}, f32[4,64,128]{2,1,0:T(8,128)S(1)}, u32[]{:S(2)}, u32[]{:S(2)}) collective-permute-start(f32[4,64,128]{2,1,0:T(8,128)S(1)} %copy-done.26), channel_id=1, source_target_pairs={{0,8},{8,16},{16,24},{1,9},{9,17},{17,25},{2,10},{10,18},{18,26},{... | collective-permute-start | bytes 393224 | tf_op jit(solution)/shard_map/ppermute | solution.py:107
  338.0 7.2 %collective-permute-start.31 = (f32[4,64,128]{2,1,0:T(8,128)S(1)}, f32[4,64,128]{2,1,0:T(8,128)S(1)}, u32[]{:S(2)}, u32[]{:S(2)}) collective-permute-start(f32[4,64,128]{2,1,0:T(8,128)S(1)} %copy-done.25), channel_id=1, source_target_pairs={{8,0},{16,8},{24,16},{9,1},{17,9},{25,17},{10,2},{18,10},{26,18},{... | collective-permute-start | bytes 393224 | tf_op jit(solution)/shard_map/ppermute | solution.py:107
  (35 other events, 152.3 us)

commit v7 on v5

--- a/solution.py
+++ b/solution.py
@@ -261,6 +261,53 @@
     return outs[0], outs[1], outs[2], outs[3:]
 
 
+def sigma_kernel(sigma_ref, t_ref, sx, sy, sz, x_lo, x_hi, y_lo, y_hi, z_lo, z_hi):
+    nx, ny, nz = t_ref.shape
+    kinds = sigma_ref.shape[0] // 3
+    half = nz // 2
+    lane = lax.broadcasted_iota(jnp.int32, (ny, nz), 1)
+
+    def body(x, columns):
+        cls = t_ref[x]
+        values = []
+        for dim_index in range(3):
+            value = jnp.zeros((ny, nz), jnp.float32)
+            for kind in range(kinds):
+                value = value + jnp.where(cls == kind, sigma_ref[3 * kind + dim_index], 0.0)
+            values.append(value)
+        sx[x] = values[0]
+        sy[x] = values[1]
+        sz[x] = values[2]
+        y_lo[pl.ds(x, 1), :] = values[1][0:1, :]
+        y_hi[pl.ds(x, 1), :] = values[1][ny - 1:ny, :]
+        columns = jnp.where(lane == x, jnp.broadcast_to(values[2][:, 0:1], (ny, nz)), columns)
+        return jnp.where(lane == half + x, jnp.broadcast_to(values[2][:, nz - 1:nz], (ny, nz)), columns)
+
+    columns = lax.fori_loop(0, nx, body, jnp.zeros((ny, nz), jnp.float32))
+    x_lo[...] = sx[0]
+    x_hi[...] = sx[nx - 1]
+    flipped = columns.T
+    z_lo[...] = flipped[0:nx, :]
+    z_hi[...] = flipped[half:half + nx, :]
+
+
+def conductivity(tissue, tissue_sigma):
+    nx, ny, nz = tissue.shape
+    vmem = pl.BlockSpec(memory_space=pltpu.VMEM)
+    f32 = lambda shape: jax.ShapeDtypeStruct(shape, jnp.float32)
+    outs = pl.pallas_call(
+        sigma_kernel,
+        in_specs=[pl.BlockSpec(memory_space=pltpu.SMEM), vmem],
+        out_specs=[vmem] * 9,
+        out_shape=[f32(tissue.shape)] * 3 + [f32((ny, nz))] * 2 + [f32((nx, nz))] * 2 + [f32((nx, ny))] * 2,
+        cost_estimate=pl.CostEstimate(flops=24 * tissue.size, transcendentals=0, bytes_accessed=16 * tissue.size),
+        name="tissue_conductivity",
+    )(tissue_sigma.reshape(-1).astype(jnp.float32), tissue)
+    sigma = list(outs[0:3])
+    riders = [(outs[4], outs[3]), (outs[6], outs[5]), (outs[8], outs[7])]
+    return sigma, riders
+
+
 def local(
     heart_state,
     cell_type,
@@ -301,13 +348,7 @@
     row_used = jnp.any(row_match, axis=1)
     row_slot = jnp.argmax(row_match, axis=1).astype(jnp.int32)
 
-    sigma = []
-    for dim_index in range(3):
-        value = jnp.zeros(tissue.shape, jnp.float32)
-        for tissue_kind in range(tissue_sigma.shape[0]):
-            value = value + jnp.where(tissue == tissue_kind, tissue_sigma[tissue_kind, dim_index], 0.0)
-        sigma.append(value)
-    riders = [faces_of(sigma[dim_index], dim_index) for dim_index in range(3)]
+    sigma, riders = conductivity(tissue, tissue_sigma)
 
     currents = []
     for time_step in range(STEPS):

time: 374 us -> 382 us (1.021)
  local copies, waits for them, and re-layouts: 65.8 us -> 78.3 us
  other arithmetic: 72.7 us -> 60.4 us
  Pallas kernels: 101 us -> 108 us
    add x2 -> x0, other arithmetic: 10.3 us -> none  [local(): value + jnp.where(tissue == tissue_kind, tissue_sigma[tissue_kind, dim_in...]
    pallas_call x0 -> x1, Pallas kernels: none -> 6.33 us  [conductivity(): pl.pallas_call(sigma_kernel, in_specs=[pl.BlockSpec(memory_space=pltpu.SM...]
  transfers between devices with their start and end apart: 37 -> 37, of which waited for: 8 -> 8; matrix products, arithmetic and copies ran while one was open for 18% -> 20% of each run, Pallas kernels for 0% -> 0%
where the time goes in v7:
time: 382 us; the launch traced here: 378 us
  Pallas kernels  108 us (28%)
  starting transfers between devices  91.3 us (24%)
  local copies, waits for them, and re-layouts  78.3 us (20%)
  other arithmetic  60.4 us (16%)
  waiting for transfers between devices  36.9 us (10%)
    pallas_call x3, Pallas kernels, run_sweep(): pl.pallas_call(functools.partial(sweep_kernel, first, second, final), gri...  87.1 us
    ppermute x14, starting transfers between devices, exchange(): lax.ppermute(top, axis, forward)  59.8 us
    all_to_all x1, waiting for transfers between devices, local(): lax.all_to_all(send_values.reshape(STEPS, devices, capacity, row_len), ('...  22.4 us
    ppermute x14, starting transfers between devices, exchange(): lax.ppermute(bottom, axis, backward)  18.1 us
    gather x2, local copies, waits for them, and re-layouts, local(): jnp.take(received, row_slot, axis=1)  17.7 us
    add x4, other arithmetic, membrane(): steady + (gate_state - steady) * jnp.exp(-DT_HEART / time_const)  16 us
    pallas_call x1, Pallas kernels, run_initial(): pl.pallas_call(functools.partial(initial_kernel, mid), grid=(source.shape...  14.3 us
    ppermute x14, waiting for transfers between devices, exchange(): lax.ppermute(bottom, axis, backward)  12.5 us
  transfers between devices with their start and end apart: 37, of which 8 were waited for; matrix products, arithmetic and copies ran while one was open for 20% of the time, Pallas kernels for 0%

profile of v7, /device:TPU:0, one launch (start us, length us, event | category | flops | bytes accessed | tf_op | source)
XLA Modules:
  0.0 377.7 jit_solution(2955444139169713561)
XLA Ops:
  0.6 1.6 fusion.98
  3.9 6.3 %tissue_conductivity.1 = (f32[32,64,128]{2,1,0:T(8,128)}, f32[32,64,128]{2,1,0:T(8,128)}, f32[32,64,128]{2,1,0:T(8,128)}, f32[64,128]{1,0:T(8,128)}, f32[64,128]...) custom-call(f32[12]{0:T(128)} %reshape.1887.sigma_ref, ...), custom_call_target="tpu_custom_call" | custom-call | flops 6291456 | bytes 4194304 | tf_op jit(solution)/shard_map/tissue_conductivity/pallas_call | solution.py:298
  16.2 5.7 %collective-permute-start.3 = (f32[5120]{0:T(1024)}, f32[5120]{0:T(1024)}, u32[]{:S(2)}, u32[]{:S(2)}) collective-permute-start(f32[5120]{0:T(1024)} %pad_maximum_fusion.5), channel_id=1, source_target_pairs={{0,2},{2,4},{4,6},{1,3},{3,5},{5,7},{8,10},{10,12},{12,14},{9,11},... | collective-permute-start | bytes 61448 | tf_op jit(solution)/shard_map/ppermute | solution.py:107
  22.7 1.4 pad_maximum_fusion.2
  25.3 1.4 pad_maximum_fusion.3
  26.7 5.2 %collective-permute-start.1 = (f32[12288]{0:T(1024)}, f32[12288]{0:T(1024)}, u32[]{:S(2)}, u32[]{:S(2)}) collective-permute-start(f32[12288]{0:T(1024)} %pad_maximum_fusion.3), channel_id=1, source_target_pairs={{0,8},{8,16},{16,24},{1,9},{9,17},{17,25},{2,10},{10,18},{18,26},{... | collective-permute-start | bytes 147464 | tf_op jit(solution)/shard_map/ppermute | solution.py:107
  37.1 5.0 %gather_fusion = s32[768]{0:T(1024)S(1)} fusion(s32[256]{0:T(256)S(1)} %reshape.1896, s32[1024]{0:T(1024)S(1)} %pad_clamp_fusion), kind=kCustom, calls=%fused_computation | custom fusion | bytes 9216 | tf_op jit(solution)/shard_map/gather | solution.py:343
  42.8 4.6 %all-to-all-start = ((s32[32,1,24]{2,1,0:T(1,128)}), s32[32,1,24]{2,1,0:T(1,128)S(1)}, u32[]{:S(2)}, u32[]{:S(2)}) async-start(s32[32,1,24]{2,1,0:T(1,128)} %bitcast.104), calls=%async_computation | async-start | bytes 32768 | tf_op jit(solution)/shard_map/all_to_all | solution.py:344
  50.1 1.7 fusion.99
  51.8 1.5 fusion.100
  53.3 1.6 fusion.101
  54.9 1.5 multiply_add_fusion.3
  59.1 2.8 iota_reduce_fusion
  68.3 1.9 slice.495
  70.3 1.8 slice.496
  77.7 1.7 fusion.25
  83.1 2.8 multiply_add_fusion.2
  88.1 4.5 %collective-permute-start.6 = (f32[32,128]{1,0:T(8,128)S(1)}, f32[32,128]{1,0:T(8,128)S(1)}, u32[]{:S(2)}, u32[]{:S(2)}) collective-permute-start(f32[32,128]{1,0:T(8,128)S(1)} %get-tuple-element.157), channel_id=1, source_target_pairs={{0,8},{8,16},{16,24},{1,9},{9,17},{17,25},{2,10},{10,18},{18,26},{... | collective-permute-start | bytes 49160 | tf_op jit(solution)/shard_map/ppermute | solution.py:107
  93.9 4.8 %collective-permute-start.8 = (f32[8,128]{1,0:T(8,128)}, f32[8,128]{1,0:T(8,128)S(1)}, u32[]{:S(2)}, u32[]{:S(2)}) collective-permute-start(f32[8,128]{1,0:T(8,128)} %bitcast.40), channel_id=1, source_target_pairs={{0,2},{2,4},{4,6},{1,3},{3,5},{5,7},{8,10},{10,12},{12,14},{9,11},... | collective-permute-start | bytes 12296 | tf_op jit(solution)/shard_map/ppermute | solution.py:107
  106.8 1.4 fusion.40
  111.5 1.4 fusion.33
  113.0 4.2 %multiply_add_fusion.1 = f32[18,8,32,128]{3,2,1,0:T(8,128)S(1)} fusion(f32[8,32,128]{2,1,0:T(8,128)S(1)} %bitcast.285, f32[18]{0:T(128)S(1)} %copy-done.116, f32[18]{0:T(128)S(1)} %copy-done.119, f32[18]{0:T(128)S(1)} %copy-done.122, f32[8,32,128]{2,1,0:T(8,128)S(1)} %bitcast.277, f32[19,8,32,128]{3,2,1,0:T(8,128)S(1)} %copy-done, ...), kind=kLoop, calls=%fused_computation.9 | loop fusion | flops 19464192 | bytes 5112024 | tf_op jit(solution)/shard_map/add | solution.py:59
  120.2 5.1 %collective-permute-start.11 = (f32[32,128]{1,0:T(8,128)}, f32[32,128]{1,0:T(8,128)S(1)}, u32[]{:S(2)}, u32[]{:S(2)}) collective-permute-start(f32[32,128]{1,0:T(8,128)} %get-tuple-element.141), channel_id=1, source_target_pairs={{0,8},{8,16},{16,24},{1,9},{9,17},{17,25},{2,10},{10,18},{18,26},{... | collective-permute-start | bytes 49160 | tf_op jit(solution)/shard_map/ppermute | solution.py:107
  126.6 4.5 %collective-permute-start.13 = (f32[8,128]{1,0:T(8,128)S(1)}, f32[8,128]{1,0:T(8,128)S(1)}, u32[]{:S(2)}, u32[]{:S(2)}) collective-permute-start(f32[8,128]{1,0:T(8,128)S(1)} %bitcast.345), channel_id=1, source_target_pairs={{0,2},{2,4},{4,6},{1,3},{3,5},{5,7},{8,10},{10,12},{12,14},{9,11},... | collective-permute-start | bytes 12296 | tf_op jit(solution)/shard_map/ppermute | solution.py:107
  136.9 5.4 %collective-permute-start.16 = (f32[32,128]{1,0:T(8,128)S(1)}, f32[32,128]{1,0:T(8,128)S(1)}, u32[]{:S(2)}, u32[]{:S(2)}) collective-permute-start(f32[32,128]{1,0:T(8,128)S(1)} %get-tuple-element.125), channel_id=1, source_target_pairs={{0,8},{8,16},{16,24},{1,9},{9,17},{17,25},{2,10},{10,18},{18,26},{... | collective-permute-start | bytes 49160 | tf_op jit(solution)/shard_map/ppermute | solution.py:107
  143.7 4.8 %collective-permute-start.18 = (f32[8,128]{1,0:T(8,128)S(1)}, f32[8,128]{1,0:T(8,128)S(1)}, u32[]{:S(2)}, u32[]{:S(2)}) collective-permute-start(f32[8,128]{1,0:T(8,128)S(1)} %bitcast.346), channel_id=1, source_target_pairs={{0,2},{2,4},{4,6},{1,3},{3,5},{5,7},{8,10},{10,12},{12,14},{9,11},... | collective-permute-start | bytes 12296 | tf_op jit(solution)/shard_map/ppermute | solution.py:107
  150.6 2.8 gather_fusion.1
  153.5 4.1 %select_select_fusion.1 = f32[4,32,24,128]{3,0,2,1:T(4,128)} fusion(f32[4,32,24,128]{3,0,2,1:T(4,128)S(1)} %bitcast.271, pred[32,24]{1,0:T(8,128)(4,1)S(1)} %copy-done.96, pred[32,24]{1,0:T(8,128)(4,1)S(1)} %copy-done.95), kind=kLoop, calls=%fused_computation.12 | loop fusion | flops 786432 | bytes 3147264 | tf_op jit(solution)/shard_map/jit(_where)/select_n | solution.py:367
  157.6 7.6 %all-to-all-start.1 = ((f32[4,32,24,128]{3,0,2,1:T(4,128)}), f32[4,32,24,128]{3,0,2,1:T(4,128)S(1)}, u32[]{:S(2)}, u32[]{:S(2)}) async-start(f32[4,32,24,128]{3,0,2,1:T(4,128)} %select_select_fusion.1), calls=%async_computation.1 | async-start | bytes 3145728 | tf_op jit(solution)/shard_map/all_to_all | solution.py:368
  165.3 7.0 %broadcast_divide_fusion = (f32[32,64,128]{2,1,0:T(8,128)}, f32[32,64,128]{2,1,0:T(8,128)}, f32[32,64,128]{2,1,0:T(8,128)}, f32[32,64,128]{2,1,0:T(8,128)}, f32[...) fusion(f32[32,64,128]{2,1,0:T(8,128)} %get-tuple-element.47, ...), kind=kLoop, calls=%fused_computation.35 | loop fusion | flops 6553600 | bytes 17825792 | tf_op jit(solution)/shard_map/div | solution.py:388
  173.9 7.5 %multiply_add_fusion = f32[18,8,32,128]{3,2,1,0:T(8,128)} fusion(f32[8,32,128]{2,1,0:T(8,128)S(1)} %bitcast.288, f32[18]{0:T(128)} %param.15, f32[18]{0:T(128)} %param.13, f32[18]{0:T(128)} %copy-done.120, f32[8,32,128]{2,1,0:T(8,128)S(1)} %bitcast.287, f32[8,32,128]{2,1,0:T(8,128)S(1)} %bitcast.278, f32[19,8,32,128]{3,2,1,0:T(8,128)} %param.11, ...), kind=kLoop, calls=%fused_computation.8 | loop fusion | flops 25952256 | bytes 5243096 | tf_op jit(solution)/shard_map/add | solution.py:59
  181.4 22.4 %all-to-all-done.1 = f32[4,32,24,128]{3,0,2,1:T(4,128)S(1)} async-done(((f32[4,32,24,128]{3,0,2,1:T(4,128)}), f32[4,32,24,128]{3,0,2,1:T(4,128)S(1)}, u32[]{:S(2)}, u32[]{:S(2)}) %all-to-all-start.1) | async-done | bytes 1572896 | tf_op jit(solution)/shard_map/all_to_all | solution.py:368
  203.8 15.2 %gather_fusion.2 = f32[2048,4,128]{2,1,0:T(4,128)} fusion(f32[4,768,128]{2,0,1:T(4,128)S(1)} %bitcast.268, s32[2048]{0:T(1024)S(1)} %copy-done.86), kind=kCustom, calls=%fused_computation.2 | custom fusion | bytes 8396800 | tf_op jit(solution)/shard_map/jit(_take)/gather | solution.py:375
  219.1 2.5 copy.1552
  221.6 2.8 select_select_fusion.r_ref
  224.4 14.3 %chebyshev_start.1 = (f32[4,32,64,128]{3,2,1,0:T(8,128)}, f32[4,64,128]{2,1,0:T(8,128)}, f32[4,64,128]{2,1,0:T(8,128)}, f32[4,32,1,128]{3,2,1,0:T(1,128)}, f32[4...) custom-call(f32[4,32,64,128]{3,2,1,0:T(8,128)} %select_select_fusion.r_ref, ...), custom_call_target="tpu_custom_call" | custom-call | flops 2097152 | bytes 9437184 | tf_op jit(solution)/shard_map/chebyshev_start/pallas_call | solution.py:229
  240.6 2.7 collective-permute-start.20
  248.1 4.2 %collective-permute-done.23.yhi = f32[4,32,1,128]{3,2,1,0:T(1,128)S(1)} collective-permute-done((f32[4,32,1,128]{3,2,1,0:T(1,128)}, f32[4,32,1,128]{3,2,1,0:T(1,128)S(1)}, u32[]{:S(2)}, u32[]{:S(2)}) %collective-permute-start.23) | collective-permute-done | bytes 65568 | tf_op jit(solution)/shard_map/ppermute | solution.py:107
  253.0 28.0 %chebyshev_sweep.3 = (f32[4,32,64,128]{3,2,1,0:T(8,128)}, f32[4,32,64,128]{3,2,1,0:T(8,128)}, f32[4,32,64,128]{3,2,1,0:T(8,128)}, f32[4,64,128]{2,1,0:T(8,128)},...) custom-call(f32[4,32,64,128]{3,2,1,0:T(8,128)} %get-tuple-element.50, ...), custom_call_target="tpu_custom_call" | custom-call | flops 31457280 | bytes 36700160 | tf_op jit(solution)/shard_map/chebyshev_sweep/pallas_call | solution.py:252
  283.3 4.6 %collective-permute-start.25 = (f32[4,64,128]{2,1,0:T(8,128)}, f32[4,64,128]{2,1,0:T(8,128)S(1)}, u32[]{:S(2)}, u32[]{:S(2)}) collective-permute-start(f32[4,64,128]{2,1,0:T(8,128)} %get-tuple-element.60), channel_id=1, source_target_pairs={{0,8},{8,16},{16,24},{1,9},{9,17},{17,25},{2,10},{10,18},{18,26},{... | collective-permute-start | bytes 393224 | tf_op jit(solution)/shard_map/ppermute | solution.py:107
  289.1 2.8 collective-permute-start.27
  294.1 4.2 %collective-permute-done.28.yhi = f32[4,32,1,128]{3,2,1,0:T(1,128)S(1)} collective-permute-done((f32[4,32,1,128]{3,2,1,0:T(1,128)}, f32[4,32,1,128]{3,2,1,0:T(1,128)S(1)}, u32[]{:S(2)}, u32[]{:S(2)}) %collective-permute-start.28) | collective-permute-done | bytes 65568 | tf_op jit(solution)/shard_map/ppermute | solution.py:107
  299.0 27.9 %chebyshev_sweep.4 = (f32[4,32,64,128]{3,2,1,0:T(8,128)}, f32[4,32,64,128]{3,2,1,0:T(8,128)}, f32[4,32,64,128]{3,2,1,0:T(8,128)}, f32[4,64,128]{2,1,0:T(8,128)},...) custom-call(f32[4,32,64,128]{3,2,1,0:T(8,128)} %get-tuple-element.57, ...), custom_call_target="tpu_custom_call" | custom-call | flops 31457280 | bytes 36700160 | tf_op jit(solution)/shard_map/chebyshev_sweep/pallas_call | solution.py:252
  327.9 1.8 pad_maximum_fusion
  329.7 4.9 %collective-permute-start.30 = (f32[4,64,128]{2,1,0:T(8,128)S(1)}, f32[4,64,128]{2,1,0:T(8,128)S(1)}, u32[]{:S(2)}, u32[]{:S(2)}) collective-permute-start(f32[4,64,128]{2,1,0:T(8,128)S(1)} %copy-done.125), channel_id=1, source_target_pairs={{0,8},{8,16},{16,24},{1,9},{9,17},{17,25},{2,10},{10,18},{18,26},{... | collective-permute-start | bytes 393224 | tf_op jit(solution)/shard_map/ppermute | solution.py:107
  335.9 3.5 collective-permute-start.32
  341.4 4.2 %collective-permute-done.33.yhi = f32[4,32,1,128]{3,2,1,0:T(1,128)S(1)} collective-permute-done((f32[4,32,1,128]{3,2,1,0:T(1,128)S(1)}, f32[4,32,1,128]{3,2,1,0:T(1,128)S(1)}, u32[]{:S(2)}, u32[]{:S(2)}) %collective-permute-start.33) | collective-permute-done | bytes 65568 | tf_op jit(solution)/shard_map/ppermute | solution.py:107
  346.3 31.1 %chebyshev_sweep.5 = (f32[4,32,64,128]{3,2,1,0:T(8,128)}, f32[4,32,64,128]{3,2,1,0:T(8,128)}, f32[32,64,4,128]{3,2,1,0:T(4,128)}, f32[4,64,128]{2,1,0:T(8,128)},...) custom-call(f32[4,32,64,128]{3,2,1,0:T(8,128)} %get-tuple-element.66, ...), custom_call_target="tpu_custom_call" | custom-call | flops 31457280 | bytes 36700160 | tf_op jit(solution)/shard_map/chebyshev_sweep/pallas_call | solution.py:252
  (438 shorter events, 83.8 us)
Async XLA Ops:
  0.6 35.8 %copy-start.113 = (s32[8,32,1]{1,2,0:T(1,128)S(1)}, s32[8,32,1]{1,2,0:T(1,128)}, u32[]{:S(2)}) copy-start(s32[8,32,1]{1,2,0:T(1,128)} %param.19) | copy-start | bytes 3076
  11.8 52.8 %collective-permute-start.4 = (f32[2304]{0:T(1024)S(1)}, f32[2304]{0:T(1024)S(1)}, u32[]{:S(2)}, u32[]{:S(2)}) collective-permute-start(f32[2304]{0:T(1024)S(1)} %maximum_select_fusion), channel_id=1, source_target_pairs={{0,1},{1,0},{2,3},{3,2},{4,5},{5,4},{6,7},{7,6},{8,9},{9,8},{10,11... | collective-permute-start | bytes 27656 | tf_op jit(solution)/shard_map/ppermute | solution.py:102
  13.6 58.6 %collective-permute-start.2 = (f32[5120]{0:T(1024)}, f32[5120]{0:T(1024)}, u32[]{:S(2)}, u32[]{:S(2)}) collective-permute-start(f32[5120]{0:T(1024)} %pad_maximum_fusion.4), channel_id=1, source_target_pairs={{2,0},{4,2},{6,4},{3,1},{5,3},{7,5},{10,8},{12,10},{14,12},{11,9},... | collective-permute-start | bytes 61448 | tf_op jit(solution)/shard_map/ppermute | solution.py:107
  16.2 58.1 %collective-permute-start.3 = (f32[5120]{0:T(1024)}, f32[5120]{0:T(1024)}, u32[]{:S(2)}, u32[]{:S(2)}) collective-permute-start(f32[5120]{0:T(1024)} %pad_maximum_fusion.5), channel_id=1, source_target_pairs={{0,2},{2,4},{4,6},{1,3},{3,5},{5,7},{8,10},{10,12},{12,14},{9,11},... | collective-permute-start | bytes 61448 | tf_op jit(solution)/shard_map/ppermute | solution.py:107
  24.1 52.2 %collective-permute-start = (f32[12288]{0:T(1024)}, f32[12288]{0:T(1024)}, u32[]{:S(2)}, u32[]{:S(2)}) collective-permute-start(f32[12288]{0:T(1024)} %pad_maximum_fusion.2), channel_id=1, source_target_pairs={{8,0},{16,8},{24,16},{9,1},{17,9},{25,17},{10,2},{18,10},{26,18},{... | collective-permute-start | bytes 147464 | tf_op jit(solution)/shard_map/ppermute | solution.py:107
  26.7 50.3 %collective-permute-start.1 = (f32[12288]{0:T(1024)}, f32[12288]{0:T(1024)}, u32[]{:S(2)}, u32[]{:S(2)}) collective-permute-start(f32[12288]{0:T(1024)} %pad_maximum_fusion.3), channel_id=1, source_target_pairs={{0,8},{8,16},{16,24},{1,9},{9,17},{17,25},{2,10},{10,18},{18,26},{... | collective-permute-start | bytes 147464 | tf_op jit(solution)/shard_map/ppermute | solution.py:107
  42.8 15.6 %all-to-all-start = ((s32[32,1,24]{2,1,0:T(1,128)}), s32[32,1,24]{2,1,0:T(1,128)S(1)}, u32[]{:S(2)}, u32[]{:S(2)}) async-start(s32[32,1,24]{2,1,0:T(1,128)} %bitcast.104), calls=%async_computation | async-start | bytes 32768 | tf_op jit(solution)/shard_map/all_to_all | solution.py:344
  50.0 35.9 %copy-start.101 = (f32[9]{0:T(128)}, f32[9]{0:T(128)S(1)}, u32[]{:S(2)}) copy-start(f32[9]{0:T(128)S(1)} %get-tuple-element.190) | copy-start | bytes 112
  50.1 35.9 %copy-start.104 = (f32[9]{0:T(128)}, f32[9]{0:T(128)S(1)}, u32[]{:S(2)}) copy-start(f32[9]{0:T(128)S(1)} %get-tuple-element.191) | copy-start | bytes 112
  50.1 35.9 %copy-start.107 = (f32[9]{0:T(128)}, f32[9]{0:T(128)S(1)}, u32[]{:S(2)}) copy-start(f32[9]{0:T(128)S(1)} %get-tuple-element.192) | copy-start | bytes 112
  86.5 15.0 %collective-permute-start.9 = (f32[8,32]{1,0:T(8,128)S(1)}, f32[8,32]{1,0:T(8,128)S(1)}, u32[]{:S(2)}, u32[]{:S(2)}) collective-permute-start(f32[8,32]{1,0:T(8,128)S(1)} %fusion.10), channel_id=1, source_target_pairs={{0,1},{1,0},{2,3},{3,2},{4,5},{5,4},{6,7},{7,6},{8,9},{9,8},{10,11... | collective-permute-start | bytes 3080 | tf_op jit(solution)/shard_map/ppermute | solution.py:102
  86.8 19.4 %collective-permute-start.5 = (f32[32,128]{1,0:T(8,128)S(1)}, f32[32,128]{1,0:T(8,128)S(1)}, u32[]{:S(2)}, u32[]{:S(2)}) collective-permute-start(f32[32,128]{1,0:T(8,128)S(1)} %get-tuple-element.158), channel_id=1, source_target_pairs={{8,0},{16,8},{24,16},{9,1},{17,9},{25,17},{10,2},{18,10},{26,18},{... | collective-permute-start | bytes 49160 | tf_op jit(solution)/shard_map/ppermute | solution.py:107
  88.1 18.1 %collective-permute-start.6 = (f32[32,128]{1,0:T(8,128)S(1)}, f32[32,128]{1,0:T(8,128)S(1)}, u32[]{:S(2)}, u32[]{:S(2)}) collective-permute-start(f32[32,128]{1,0:T(8,128)S(1)} %get-tuple-element.157), channel_id=1, source_target_pairs={{0,8},{8,16},{16,24},{1,9},{9,17},{17,25},{2,10},{10,18},{18,26},{... | collective-permute-start | bytes 49160 | tf_op jit(solution)/shard_map/ppermute | solution.py:107
  92.6 13.5 %collective-permute-start.7 = (f32[8,128]{1,0:T(8,128)}, f32[8,128]{1,0:T(8,128)S(1)}, u32[]{:S(2)}, u32[]{:S(2)}) collective-permute-start(f32[8,128]{1,0:T(8,128)} %bitcast.38), channel_id=1, source_target_pairs={{2,0},{4,2},{6,4},{3,1},{5,3},{7,5},{10,8},{12,10},{14,12},{11,9},... | collective-permute-start | bytes 12296 | tf_op jit(solution)/shard_map/ppermute | solution.py:107
  93.9 12.2 %collective-permute-start.8 = (f32[8,128]{1,0:T(8,128)}, f32[8,128]{1,0:T(8,128)S(1)}, u32[]{:S(2)}, u32[]{:S(2)}) collective-permute-start(f32[8,128]{1,0:T(8,128)} %bitcast.40), channel_id=1, source_target_pairs={{0,2},{2,4},{4,6},{1,3},{3,5},{5,7},{8,10},{10,12},{12,14},{9,11},... | collective-permute-start | bytes 12296 | tf_op jit(solution)/shard_map/ppermute | solution.py:107
  117.9 13.3 %collective-permute-start.14 = (f32[8,32]{1,0:T(8,128)S(1)}, f32[8,32]{1,0:T(8,128)S(1)}, u32[]{:S(2)}, u32[]{:S(2)}) collective-permute-start(f32[8,32]{1,0:T(8,128)S(1)} %fusion.9), channel_id=1, source_target_pairs={{0,1},{1,0},{2,3},{3,2},{4,5},{5,4},{6,7},{7,6},{8,9},{9,8},{10,11... | collective-permute-start | bytes 3080 | tf_op jit(solution)/shard_map/ppermute | solution.py:102
  118.9 13.6 %collective-permute-start.10 = (f32[32,128]{1,0:T(8,128)}, f32[32,128]{1,0:T(8,128)S(1)}, u32[]{:S(2)}, u32[]{:S(2)}) collective-permute-start(f32[32,128]{1,0:T(8,128)} %get-tuple-element.142), channel_id=1, source_target_pairs={{8,0},{16,8},{24,16},{9,1},{17,9},{25,17},{10,2},{18,10},{26,18},{... | collective-permute-start | bytes 49160 | tf_op jit(solution)/shard_map/ppermute | solution.py:107
  120.2 12.3 %collective-permute-start.11 = (f32[32,128]{1,0:T(8,128)}, f32[32,128]{1,0:T(8,128)S(1)}, u32[]{:S(2)}, u32[]{:S(2)}) collective-permute-start(f32[32,128]{1,0:T(8,128)} %get-tuple-element.141), channel_id=1, source_target_pairs={{0,8},{8,16},{16,24},{1,9},{9,17},{17,25},{2,10},{10,18},{18,26},{... | collective-permute-start | bytes 49160 | tf_op jit(solution)/shard_map/ppermute | solution.py:107
  125.3 6.6 %collective-permute-start.12 = (f32[8,128]{1,0:T(8,128)S(1)}, f32[8,128]{1,0:T(8,128)S(1)}, u32[]{:S(2)}, u32[]{:S(2)}) collective-permute-start(f32[8,128]{1,0:T(8,128)S(1)} %bitcast.347), channel_id=1, source_target_pairs={{2,0},{4,2},{6,4},{3,1},{5,3},{7,5},{10,8},{12,10},{14,12},{11,9},... | collective-permute-start | bytes 12296 | tf_op jit(solution)/shard_map/ppermute | solution.py:107
  126.6 5.9 %collective-permute-start.13 = (f32[8,128]{1,0:T(8,128)S(1)}, f32[8,128]{1,0:T(8,128)S(1)}, u32[]{:S(2)}, u32[]{:S(2)}) collective-permute-start(f32[8,128]{1,0:T(8,128)S(1)} %bitcast.345), channel_id=1, source_target_pairs={{0,2},{2,4},{4,6},{1,3},{3,5},{5,7},{8,10},{10,12},{12,14},{9,11},... | collective-permute-start | bytes 12296 | tf_op jit(solution)/shard_map/ppermute | solution.py:107
  135.6 13.0 %collective-permute-start.19 = (f32[8,32]{1,0:T(8,128)S(1)}, f32[8,32]{1,0:T(8,128)S(1)}, u32[]{:S(2)}, u32[]{:S(2)}) collective-permute-start(f32[8,32]{1,0:T(8,128)S(1)} %fusion.8), channel_id=1, source_target_pairs={{0,1},{1,0},{2,3},{3,2},{4,5},{5,4},{6,7},{7,6},{8,9},{9,8},{10,11... | collective-permute-start | bytes 3080 | tf_op jit(solution)/shard_map/ppermute | solution.py:102
  135.6 14.2 %collective-permute-start.15 = (f32[32,128]{1,0:T(8,128)S(1)}, f32[32,128]{1,0:T(8,128)S(1)}, u32[]{:S(2)}, u32[]{:S(2)}) collective-permute-start(f32[32,128]{1,0:T(8,128)S(1)} %get-tuple-element.126), channel_id=1, source_target_pairs={{8,0},{16,8},{24,16},{9,1},{17,9},{25,17},{10,2},{18,10},{26,18},{... | collective-permute-start | bytes 49160 | tf_op jit(solution)/shard_map/ppermute | solution.py:107
  136.9 12.9 %collective-permute-start.16 = (f32[32,128]{1,0:T(8,128)S(1)}, f32[32,128]{1,0:T(8,128)S(1)}, u32[]{:S(2)}, u32[]{:S(2)}) collective-permute-start(f32[32,128]{1,0:T(8,128)S(1)} %get-tuple-element.125), channel_id=1, source_target_pairs={{0,8},{8,16},{16,24},{1,9},{9,17},{17,25},{2,10},{10,18},{18,26},{... | collective-permute-start | bytes 49160 | tf_op jit(solution)/shard_map/ppermute | solution.py:107
  142.4 6.5 %collective-permute-start.17 = (f32[8,128]{1,0:T(8,128)S(1)}, f32[8,128]{1,0:T(8,128)S(1)}, u32[]{:S(2)}, u32[]{:S(2)}) collective-permute-start(f32[8,128]{1,0:T(8,128)S(1)} %bitcast.348), channel_id=1, source_target_pairs={{2,0},{4,2},{6,4},{3,1},{5,3},{7,5},{10,8},{12,10},{14,12},{11,9},... | collective-permute-start | bytes 12296 | tf_op jit(solution)/shard_map/ppermute | solution.py:107
  143.7 6.1 %collective-permute-start.18 = (f32[8,128]{1,0:T(8,128)S(1)}, f32[8,128]{1,0:T(8,128)S(1)}, u32[]{:S(2)}, u32[]{:S(2)}) collective-permute-start(f32[8,128]{1,0:T(8,128)S(1)} %bitcast.346), channel_id=1, source_target_pairs={{0,2},{2,4},{4,6},{1,3},{3,5},{5,7},{8,10},{10,12},{12,14},{9,11},... | collective-permute-start | bytes 12296 | tf_op jit(solution)/shard_map/ppermute | solution.py:107
  157.6 46.2 %all-to-all-start.1 = ((f32[4,32,24,128]{3,0,2,1:T(4,128)}), f32[4,32,24,128]{3,0,2,1:T(4,128)S(1)}, u32[]{:S(2)}, u32[]{:S(2)}) async-start(f32[4,32,24,128]{3,0,2,1:T(4,128)} %select_select_fusion.1), calls=%async_computation.1 | async-start | bytes 3145728 | tf_op jit(solution)/shard_map/all_to_all | solution.py:368
  173.9 29.9 %copy-start.86 = (s32[2048]{0:T(1024)S(1)}, s32[2048]{0:T(1024)}, u32[]{:S(2)}) copy-start(s32[2048]{0:T(1024)} %fusion.84) | copy-start | bytes 24580
  239.6 7.6 %collective-permute-start.24 = (f32[4,32,64]{2,1,0:T(8,128)S(1)}, f32[4,32,64]{2,1,0:T(8,128)S(1)}, u32[]{:S(2)}, u32[]{:S(2)}) collective-permute-start(f32[4,32,64]{2,1,0:T(8,128)S(1)} %broadcast_select_fusion.8), channel_id=1, source_target_pairs={{0,1},{1,0},{2,3},{3,2},{4,5},{5,4},{6,7},{7,6},{8,9},{9,8},{10,11... | collective-permute-start | bytes 98312 | tf_op jit(solution)/shard_map/ppermute | solution.py:102
  240.6 11.7 %collective-permute-start.20 = (f32[4,64,128]{2,1,0:T(8,128)S(1)}, f32[4,64,128]{2,1,0:T(8,128)S(1)}, u32[]{:S(2)}, u32[]{:S(2)}) collective-permute-start(f32[4,64,128]{2,1,0:T(8,128)S(1)} %copy-done.127), channel_id=1, source_target_pairs={{0,8},{8,16},{16,24},{1,9},{9,17},{17,25},{2,10},{10,18},{18,26},{... | collective-permute-start | bytes 393224 | tf_op jit(solution)/shard_map/ppermute | solution.py:107
  243.3 9.0 %collective-permute-start.21 = (f32[4,64,128]{2,1,0:T(8,128)S(1)}, f32[4,64,128]{2,1,0:T(8,128)S(1)}, u32[]{:S(2)}, u32[]{:S(2)}) collective-permute-start(f32[4,64,128]{2,1,0:T(8,128)S(1)} %copy-done.126), channel_id=1, source_target_pairs={{8,0},{16,8},{24,16},{9,1},{17,9},{25,17},{10,2},{18,10},{26,18},{... | collective-permute-start | bytes 393224 | tf_op jit(solution)/shard_map/ppermute | solution.py:107
  244.6 3.5 collective-permute-start.22
  245.9 6.4 %collective-permute-start.23 = (f32[4,32,1,128]{3,2,1,0:T(1,128)}, f32[4,32,1,128]{3,2,1,0:T(1,128)S(1)}, u32[]{:S(2)}, u32[]{:S(2)}) collective-permute-start(f32[4,32,1,128]{3,2,1,0:T(1,128)} %get-tuple-element.54), channel_id=1, source_target_pairs={{2,0},{4,2},{6,4},{3,1},{5,3},{7,5},{10,8},{12,10},{14,12},{11,9},... | collective-permute-start | bytes 196616 | tf_op jit(solution)/shard_map/ppermute | solution.py:107
  253.0 29.0 %copy-start.40 = (f32[1,8,31,128]{3,2,1,0:T(8,128)S(1)}, f32[1,8,31,128]{3,2,1,0:T(8,128)}, u32[]{:S(2)}) copy-start(f32[1,8,31,128]{3,2,1,0:T(8,128)} %get-tuple-element.113) | copy-start | bytes 380932
  253.0 29.1 %copy-start.43 = (f32[1,8,32,127]{3,2,1,0:T(8,128)S(1)}, f32[1,8,32,127]{3,2,1,0:T(8,128)}, u32[]{:S(2)}) copy-start(f32[1,8,32,127]{3,2,1,0:T(8,128)} %get-tuple-element.120) | copy-start | bytes 390148
  253.0 29.1 %copy-start.73 = (f32[32,128]{1,0:T(8,128)S(1)}, f32[32,128]{1,0:T(8,128)}, u32[]{:S(2)}) copy-start(f32[32,128]{1,0:T(8,128)} %copy-done.72) | copy-start | bytes 49156
  253.0 29.1 %copy-start.75 = (f32[32,128]{1,0:T(8,128)S(1)}, f32[32,128]{1,0:T(8,128)}, u32[]{:S(2)}) copy-start(f32[32,128]{1,0:T(8,128)} %copy-done.74) | copy-start | bytes 49156
  253.0 29.1 %copy-start.98 = (f32[8,128]{1,0:T(8,128)S(1)}, f32[8,128]{1,0:T(8,128)}, u32[]{:S(2)}) copy-start(f32[8,128]{1,0:T(8,128)} %copy-done.97) | copy-start | bytes 12292
  253.0 29.1 %copy-start.100 = (f32[8,128]{1,0:T(8,128)S(1)}, f32[8,128]{1,0:T(8,128)}, u32[]{:S(2)}) copy-start(f32[8,128]{1,0:T(8,128)} %copy-done.99) | copy-start | bytes 12292
  281.9 11.3 %collective-permute-start.29 = (f32[4,32,64]{2,1,0:T(8,128)S(1)}, f32[4,32,64]{2,1,0:T(8,128)S(1)}, u32[]{:S(2)}, u32[]{:S(2)}) collective-permute-start(f32[4,32,64]{2,1,0:T(8,128)S(1)} %broadcast_select_fusion.7), channel_id=1, source_target_pairs={{0,1},{1,0},{2,3},{3,2},{4,5},{5,4},{6,7},{7,6},{8,9},{9,8},{10,11... | collective-permute-start | bytes 98312 | tf_op jit(solution)/shard_map/ppermute | solution.py:102
  283.3 15.0 %collective-permute-start.25 = (f32[4,64,128]{2,1,0:T(8,128)}, f32[4,64,128]{2,1,0:T(8,128)S(1)}, u32[]{:S(2)}, u32[]{:S(2)}) collective-permute-start(f32[4,64,128]{2,1,0:T(8,128)} %get-tuple-element.60), channel_id=1, source_target_pairs={{0,8},{8,16},{16,24},{1,9},{9,17},{17,25},{2,10},{10,18},{18,26},{... | collective-permute-start | bytes 393224 | tf_op jit(solution)/shard_map/ppermute | solution.py:107
  287.8 10.4 %collective-permute-start.26 = (f32[4,64,128]{2,1,0:T(8,128)}, f32[4,64,128]{2,1,0:T(8,128)S(1)}, u32[]{:S(2)}, u32[]{:S(2)}) collective-permute-start(f32[4,64,128]{2,1,0:T(8,128)} %get-tuple-element.61), channel_id=1, source_target_pairs={{8,0},{16,8},{24,16},{9,1},{17,9},{25,17},{10,2},{18,10},{26,18},{... | collective-permute-start | bytes 393224 | tf_op jit(solution)/shard_map/ppermute | solution.py:107
  289.1 5.0 %collective-permute-start.27 = (f32[4,32,1,128]{3,2,1,0:T(1,128)}, f32[4,32,1,128]{3,2,1,0:T(1,128)S(1)}, u32[]{:S(2)}, u32[]{:S(2)}) collective-permute-start(f32[4,32,1,128]{3,2,1,0:T(1,128)} %get-tuple-element.62), channel_id=1, source_target_pairs={{0,2},{2,4},{4,6},{1,3},{3,5},{5,7},{8,10},{10,12},{12,14},{9,11},... | collective-permute-start | bytes 196616 | tf_op jit(solution)/shard_map/ppermute | solution.py:107
  291.9 6.4 %collective-permute-start.28 = (f32[4,32,1,128]{3,2,1,0:T(1,128)}, f32[4,32,1,128]{3,2,1,0:T(1,128)S(1)}, u32[]{:S(2)}, u32[]{:S(2)}) collective-permute-start(f32[4,32,1,128]{3,2,1,0:T(1,128)} %get-tuple-element.63), channel_id=1, source_target_pairs={{2,0},{4,2},{6,4},{3,1},{5,3},{7,5},{10,8},{12,10},{14,12},{11,9},... | collective-permute-start | bytes 196616 | tf_op jit(solution)/shard_map/ppermute | solution.py:107
  327.8 12.9 %collective-permute-start.34 = (f32[4,32,64]{2,1,0:T(8,128)S(1)}, f32[4,32,64]{2,1,0:T(8,128)S(1)}, u32[]{:S(2)}, u32[]{:S(2)}) collective-permute-start(f32[4,32,64]{2,1,0:T(8,128)S(1)} %broadcast_select_fusion.6), channel_id=1, source_target_pairs={{0,1},{1,0},{2,3},{3,2},{4,5},{5,4},{6,7},{7,6},{8,9},{9,8},{10,11... | collective-permute-start | bytes 98312 | tf_op jit(solution)/shard_map/ppermute | solution.py:102
  329.7 15.9 %collective-permute-start.30 = (f32[4,64,128]{2,1,0:T(8,128)S(1)}, f32[4,64,128]{2,1,0:T(8,128)S(1)}, u32[]{:S(2)}, u32[]{:S(2)}) collective-permute-start(f32[4,64,128]{2,1,0:T(8,128)S(1)} %copy-done.125), channel_id=1, source_target_pairs={{0,8},{8,16},{16,24},{1,9},{9,17},{17,25},{2,10},{10,18},{18,26},{... | collective-permute-start | bytes 393224 | tf_op jit(solution)/shard_map/ppermute | solution.py:107
  334.6 11.0 %collective-permute-start.31 = (f32[4,64,128]{2,1,0:T(8,128)S(1)}, f32[4,64,128]{2,1,0:T(8,128)S(1)}, u32[]{:S(2)}, u32[]{:S(2)}) collective-permute-start(f32[4,64,128]{2,1,0:T(8,128)S(1)} %copy-done.124), channel_id=1, source_target_pairs={{8,0},{16,8},{24,16},{9,1},{17,9},{25,17},{10,2},{18,10},{26,18},{... | collective-permute-start | bytes 393224 | tf_op jit(solution)/shard_map/ppermute | solution.py:107
  335.9 5.5 %collective-permute-start.32 = (f32[4,32,1,128]{3,2,1,0:T(1,128)S(1)}, f32[4,32,1,128]{3,2,1,0:T(1,128)S(1)}, u32[]{:S(2)}, u32[]{:S(2)}) collective-permute-start(f32[4,32,1,128]{3,2,1,0:T(1,128)S(1)} %copy-done.129), channel_id=1, source_target_pairs={{0,2},{2,4},{4,6},{1,3},{3,5},{5,7},{8,10},{10,12},{12,14},{9,11},... | collective-permute-start | bytes 196616 | tf_op jit(solution)/shard_map/ppermute | solution.py:107
  339.4 6.2 %collective-permute-start.33 = (f32[4,32,1,128]{3,2,1,0:T(1,128)S(1)}, f32[4,32,1,128]{3,2,1,0:T(1,128)S(1)}, u32[]{:S(2)}, u32[]{:S(2)}) collective-permute-start(f32[4,32,1,128]{3,2,1,0:T(1,128)S(1)} %copy-done.128), channel_id=1, source_target_pairs={{2,0},{4,2},{6,4},{3,1},{5,3},{7,5},{10,8},{12,10},{14,12},{11,9},... | collective-permute-start | bytes 196616 | tf_op jit(solution)/shard_map/ppermute | solution.py:107
  (120 other events, 772.6 us)

commit v8 on v5

--- a/solution.py
+++ b/solution.py
@@ -151,9 +151,11 @@
     zf_hi[0] = flipped[half:half + nx, :]
 
 
-def sweep_kernel(first, second, final, d_ref, r_ref, p_ref, fxp, fxm, fyp, fym, fzp, fzm, dg_ref, inv_ref,
+def sweep_kernel(final, coef_ref, d_ref, r_ref, p_ref, fxp, fxm, fyp, fym, fzp, fzm, dg_ref, inv_ref,
                  xlo, xhi, ylo, yhi, zlo, zhi, r_out, d_out, p_out, *face_out):
     snapshot = pl.program_id(0)
+    first = coef_ref[0]
+    second = coef_ref[1]
     nx, ny, nz = d_ref.shape[1], d_ref.shape[2], d_ref.shape[3]
     row = lax.broadcasted_iota(jnp.int32, (ny, nz), 0)
     lane = lax.broadcasted_iota(jnp.int32, (ny, nz), 1)
@@ -187,7 +189,7 @@
             p_out[0, x] = p_ref[0, x] + step_dir
         return write_faces(x, step_dir, carry, *face_out)
 
-    columns = lax.fori_loop(0, nx, body, jnp.zeros((ny, nz), jnp.float32), unroll=2)
+    columns = lax.fori_loop(0, nx, body, jnp.zeros((ny, nz), jnp.float32), unroll=4)
     finish_faces(columns, *face_out)
 
 
@@ -250,14 +252,14 @@
         out_spec, out_shape = full, shape
     size = step_dir.size
     outs = pl.pallas_call(
-        functools.partial(sweep_kernel, first, second, final),
+        functools.partial(sweep_kernel, final),
         grid=(steps,),
-        in_specs=[full, full, full] + [fixed] * 8 + [x_face, x_face, y_face, y_face, face_specs[4], face_specs[4]],
+        in_specs=[pl.BlockSpec(memory_space=pltpu.SMEM), full, full, full] + [fixed] * 8 + [x_face, x_face, y_face, y_face, face_specs[4], face_specs[4]],
         out_specs=[full, full, out_spec] + face_specs,
         out_shape=[shape, shape, out_shape] + face_shapes,
         cost_estimate=pl.CostEstimate(flops=30 * size, transcendentals=0, bytes_accessed=4 * 7 * size + 4 * 7 * size // steps),
         name="chebyshev_sweep",
-    )(step_dir, residual, potential, *faces, diagonal, inverse, *halos)
+    )(jnp.array([first, second], jnp.float32), step_dir, residual, potential, *faces, diagonal, inverse, *halos)
     return outs[0], outs[1], outs[2], outs[3:]
 
 

time: 374 us -> 366 us (0.979)
  Pallas kernels: 101 us -> 94.3 us
    pallas_call x3, Pallas kernels: 87.1 us -> 80 us  [run_sweep(): pl.pallas_call(functools.partial(sweep_kernel, final), grid=(steps,), in_...]
where the time goes in v8:
time: 366 us; the launch traced here: 363 us
  Pallas kernels  94.3 us (26%)
  starting transfers between devices  90.6 us (25%)
  other arithmetic  72.7 us (20%)
  local copies, waits for them, and re-layouts  65.8 us (18%)
  waiting for transfers between devices  36.2 us (10%)
    pallas_call x3, Pallas kernels, run_sweep(): pl.pallas_call(functools.partial(sweep_kernel, final), grid=(steps,), in_...  80 us
    ppermute x14, starting transfers between devices, exchange(): lax.ppermute(top, axis, forward)  58.4 us
    all_to_all x1, waiting for transfers between devices, local(): lax.all_to_all(send_values.reshape(STEPS, devices, capacity, row_len), ('...  21.9 us
    ppermute x14, starting transfers between devices, exchange(): lax.ppermute(bottom, axis, backward)  18.1 us
    gather x2, local copies, waits for them, and re-layouts, local(): jnp.take(received, row_slot, axis=1)  17.7 us
    add x4, other arithmetic, membrane(): steady + (gate_state - steady) * jnp.exp(-DT_HEART / time_const)  16.1 us
    pallas_call x1, Pallas kernels, run_initial(): pl.pallas_call(functools.partial(initial_kernel, mid), grid=(source.shape...  14.3 us
    ppermute x14, waiting for transfers between devices, exchange(): lax.ppermute(bottom, axis, backward)  12.3 us
  transfers between devices with their start and end apart: 37, of which 8 were waited for; matrix products, arithmetic and copies ran while one was open for 18% of the time, Pallas kernels for 0%

profile of v8, /device:TPU:0, one launch (start us, length us, event | category | flops | bytes accessed | tf_op | source)
XLA Modules:
  0.0 362.5 jit_solution(2319277023448152451)
XLA Ops:
  0.6 1.8 fusion.118
  2.4 4.5 %select_add_fusion.1 = (f32[32,64,128]{2,1,0:T(8,128)S(1)}, pred[32,64,128]{2,1,0:T(8,128)(4,1)S(1)}, pred[32,64,128]{2,1,0:T(8,128)(4,1)S(1)}, pred[32,64,128]{2,1,0:T(8,128)(4,1)S(1)}, pred[32,64,128]{2,1,0:T(8,128)(4,1)S(1)}) fusion(f32[]{:T(128)} %bitcast.29, f32[]{:T(128)} %bitcast.28, f32[]{:T(128)} %bitcast.27, f32[]{:T(128)} %bitcast.26, ...), kind=kLoop, calls=%fused_computation.33 | loop fusion | flops 2883584 | bytes 3145744 | tf_op jit(solution)/shard_map/add | solution.py:310
  6.9 5.9 %select_add_fusion.2 = (f32[32,64,128]{2,1,0:T(8,128)S(1)}, f32[32,64,128]{2,1,0:T(8,128)S(1)}) fusion(pred[32,64,128]{2,1,0:T(8,128)(4,1)S(1)} %get-tuple-element.85, pred[32,64,128]{2,1,0:T(8,128)(4,1)S(1)} %get-tuple-element.84, pred[32,64,128]{2,1,0:T(8,128)(4,1)S(1)} %get-tuple-element.83, pred[32,64,128]{2,1,0:T(8,128)(4,1)S(1)} %get-tuple-element.82, ...), kind=kLoop, calls=%fused_computation.34 | loop fusion | flops 3670016 | bytes 3145760 | tf_op jit(solution)/shard_map/add | solution.py:310
  12.9 1.8 fusion.98
  17.1 5.5 %collective-permute-start.3 = (f32[5120]{0:T(1024)}, f32[5120]{0:T(1024)S(1)}, u32[]{:S(2)}, u32[]{:S(2)}) collective-permute-start(f32[5120]{0:T(1024)} %pad_maximum_fusion.5), channel_id=1, source_target_pairs={{0,2},{2,4},{4,6},{1,3},{3,5},{5,7},{8,10},{10,12},{12,14},{9,11},... | collective-permute-start | bytes 61448 | tf_op jit(solution)/shard_map/ppermute | solution.py:107
  23.4 3.8 %collective-permute-start.1 = (f32[12288]{0:T(1024)S(1)}, f32[12288]{0:T(1024)S(1)}, u32[]{:S(2)}, u32[]{:S(2)}) collective-permute-start(f32[12288]{0:T(1024)S(1)} %pad_maximum_fusion.3), channel_id=1, source_target_pairs={{0,8},{8,16},{16,24},{1,9},{9,17},{17,25},{2,10},{10,18},{18,26},{... | collective-permute-start | bytes 147464 | tf_op jit(solution)/shard_map/ppermute | solution.py:107
  34.6 1.3 reduce.66
  36.0 5.0 %gather_fusion = s32[768]{0:T(1024)S(1)} fusion(s32[256]{0:T(256)S(1)} %reshape.1868, s32[1024]{0:T(1024)S(1)} %pad_clamp_fusion), kind=kCustom, calls=%fused_computation | custom fusion | bytes 9216 | tf_op jit(solution)/shard_map/gather | solution.py:298
  41.7 6.1 %all-to-all-start = ((s32[32,1,24]{2,1,0:T(1,128)}), s32[32,1,24]{2,1,0:T(1,128)S(1)}, u32[]{:S(2)}, u32[]{:S(2)}) async-start(s32[32,1,24]{2,1,0:T(1,128)} %bitcast.116), calls=%async_computation | async-start | bytes 32768 | tf_op jit(solution)/shard_map/all_to_all | solution.py:299
  47.8 1.5 fusion.100
  49.3 1.6 fusion.101
  50.9 1.7 fusion.99
  55.1 1.5 multiply_add_fusion.3
  59.4 2.8 iota_reduce_fusion
  66.5 1.8 slice.567
  68.3 1.9 slice.568
  75.0 1.4 fusion.18
  76.5 2.8 multiply_add_fusion.2
  81.5 4.5 %collective-permute-start.6 = (f32[32,128]{1,0:T(8,128)S(1)}, f32[32,128]{1,0:T(8,128)S(1)}, u32[]{:S(2)}, u32[]{:S(2)}) collective-permute-start(f32[32,128]{1,0:T(8,128)S(1)} %get-tuple-element.152), channel_id=1, source_target_pairs={{0,8},{8,16},{16,24},{1,9},{9,17},{17,25},{2,10},{10,18},{18,26},{... | collective-permute-start | bytes 49160 | tf_op jit(solution)/shard_map/ppermute | solution.py:107
  87.3 4.5 %collective-permute-start.8 = (f32[8,128]{1,0:T(8,128)S(1)}, f32[8,128]{1,0:T(8,128)S(1)}, u32[]{:S(2)}, u32[]{:S(2)}) collective-permute-start(f32[8,128]{1,0:T(8,128)S(1)} %bitcast.357), channel_id=1, source_target_pairs={{0,2},{2,4},{4,6},{1,3},{3,5},{5,7},{8,10},{10,12},{12,14},{9,11},... | collective-permute-start | bytes 12296 | tf_op jit(solution)/shard_map/ppermute | solution.py:107
  100.4 1.4 fusion.33
  101.9 4.2 %multiply_add_fusion.1 = f32[18,8,32,128]{3,2,1,0:T(8,128)S(1)} fusion(f32[8,32,128]{2,1,0:T(8,128)S(1)} %bitcast.299, f32[18]{0:T(128)S(1)} %copy-done.84, f32[18]{0:T(128)S(1)} %copy-done.87, f32[18]{0:T(128)S(1)} %copy-done.90, f32[8,32,128]{2,1,0:T(8,128)S(1)} %bitcast.291, f32[19,8,32,128]{3,2,1,0:T(8,128)S(1)} %copy-done.4, ...), kind=kLoop, calls=%fused_computation.9 | loop fusion | flops 19464192 | bytes 5112024 | tf_op jit(solution)/shard_map/add | solution.py:59
  109.3 5.1 %collective-permute-start.11 = (f32[32,128]{1,0:T(8,128)S(1)}, f32[32,128]{1,0:T(8,128)S(1)}, u32[]{:S(2)}, u32[]{:S(2)}) collective-permute-start(f32[32,128]{1,0:T(8,128)S(1)} %get-tuple-element.136), channel_id=1, source_target_pairs={{0,8},{8,16},{16,24},{1,9},{9,17},{17,25},{2,10},{10,18},{18,26},{... | collective-permute-start | bytes 49160 | tf_op jit(solution)/shard_map/ppermute | solution.py:107
  115.7 4.8 %collective-permute-start.13 = (f32[8,128]{1,0:T(8,128)S(1)}, f32[8,128]{1,0:T(8,128)S(1)}, u32[]{:S(2)}, u32[]{:S(2)}) collective-permute-start(f32[8,128]{1,0:T(8,128)S(1)} %bitcast.359), channel_id=1, source_target_pairs={{0,2},{2,4},{4,6},{1,3},{3,5},{5,7},{8,10},{10,12},{12,14},{9,11},... | collective-permute-start | bytes 12296 | tf_op jit(solution)/shard_map/ppermute | solution.py:107
  126.8 5.4 %collective-permute-start.16 = (f32[32,128]{1,0:T(8,128)S(1)}, f32[32,128]{1,0:T(8,128)S(1)}, u32[]{:S(2)}, u32[]{:S(2)}) collective-permute-start(f32[32,128]{1,0:T(8,128)S(1)} %get-tuple-element.120), channel_id=1, source_target_pairs={{0,8},{8,16},{16,24},{1,9},{9,17},{17,25},{2,10},{10,18},{18,26},{... | collective-permute-start | bytes 49160 | tf_op jit(solution)/shard_map/ppermute | solution.py:107
  133.5 4.8 %collective-permute-start.18 = (f32[8,128]{1,0:T(8,128)S(1)}, f32[8,128]{1,0:T(8,128)S(1)}, u32[]{:S(2)}, u32[]{:S(2)}) collective-permute-start(f32[8,128]{1,0:T(8,128)S(1)} %bitcast.360), channel_id=1, source_target_pairs={{0,2},{2,4},{4,6},{1,3},{3,5},{5,7},{8,10},{10,12},{12,14},{9,11},... | collective-permute-start | bytes 12296 | tf_op jit(solution)/shard_map/ppermute | solution.py:107
  141.9 3.0 gather_fusion.1
  144.8 4.9 %select_select_fusion.1 = f32[4,32,24,128]{3,0,2,1:T(4,128)} fusion(f32[4,32,24,128]{3,0,2,1:T(4,128)S(1)} %bitcast.285, pred[32,24]{1,0:T(8,128)(4,1)} %broadcast_in_dim.362, pred[32,24]{1,0:T(8,128)(4,1)} %broadcast_in_dim.360), kind=kLoop, calls=%fused_computation.12 | loop fusion | flops 786432 | bytes 3147264 | tf_op jit(solution)/shard_map/jit(_where)/select_n | solution.py:328
  149.8 7.4 %all-to-all-start.1 = ((f32[4,32,24,128]{3,0,2,1:T(4,128)}), f32[4,32,24,128]{3,0,2,1:T(4,128)S(1)}, u32[]{:S(2)}, u32[]{:S(2)}) async-start(f32[4,32,24,128]{3,0,2,1:T(4,128)} %select_select_fusion.1), calls=%async_computation.1 | async-start | bytes 3145728 | tf_op jit(solution)/shard_map/all_to_all | solution.py:329
  157.2 7.1 %broadcast_divide_fusion = (f32[32,64,128]{2,1,0:T(8,128)}, f32[32,64,128]{2,1,0:T(8,128)}, f32[32,64,128]{2,1,0:T(8,128)}, f32[32,64,128]{2,1,0:T(8,128)}, f32[...) fusion(f32[32,64,128]{2,1,0:T(8,128)} %copy-done.1, ...), kind=kLoop, calls=%fused_computation.40 | loop fusion | flops 6553600 | bytes 17825792 | tf_op jit(solution)/shard_map/div | solution.py:349
  166.6 7.5 %multiply_add_fusion = f32[18,8,32,128]{3,2,1,0:T(8,128)} fusion(f32[8,32,128]{2,1,0:T(8,128)S(1)} %bitcast.302, f32[18]{0:T(128)} %param.18, f32[18]{0:T(128)} %param.16, f32[18]{0:T(128)} %copy-done.88, f32[8,32,128]{2,1,0:T(8,128)S(1)} %bitcast.301, f32[8,32,128]{2,1,0:T(8,128)S(1)} %bitcast.292, f32[19,8,32,128]{3,2,1,0:T(8,128)} %param.14, ...), kind=kLoop, calls=%fused_computation.8 | loop fusion | flops 25952256 | bytes 5243096 | tf_op jit(solution)/shard_map/add | solution.py:59
  174.1 21.9 %all-to-all-done.1 = f32[4,32,24,128]{3,0,2,1:T(4,128)S(1)} async-done(((f32[4,32,24,128]{3,0,2,1:T(4,128)}), f32[4,32,24,128]{3,0,2,1:T(4,128)S(1)}, u32[]{:S(2)}, u32[]{:S(2)}) %all-to-all-start.1) | async-done | bytes 1572896 | tf_op jit(solution)/shard_map/all_to_all | solution.py:329
  196.0 15.2 %gather_fusion.2 = f32[2048,4,128]{2,1,0:T(4,128)} fusion(f32[4,768,128]{2,0,1:T(4,128)S(1)} %bitcast.282, s32[2048]{0:T(1024)S(1)} %copy-done.58), kind=kCustom, calls=%fused_computation.2 | custom fusion | bytes 8396800 | tf_op jit(solution)/shard_map/jit(_take)/gather | solution.py:336
  211.3 2.5 copy.1555
  213.8 2.8 select_select_fusion.r_ref
  216.6 14.3 %chebyshev_start.1 = (f32[4,32,64,128]{3,2,1,0:T(8,128)}, f32[4,64,128]{2,1,0:T(8,128)}, f32[4,64,128]{2,1,0:T(8,128)}, f32[4,32,1,128]{3,2,1,0:T(1,128)}, f32[4...) custom-call(f32[4,32,64,128]{3,2,1,0:T(8,128)} %select_select_fusion.r_ref, ...), custom_call_target="tpu_custom_call" | custom-call | flops 2097152 | bytes 9437184 | tf_op jit(solution)/shard_map/chebyshev_start/pallas_call | solution.py:231
  232.7 2.7 collective-permute-start.20
  240.2 4.0 %collective-permute-done.23.yhi = f32[4,32,1,128]{3,2,1,0:T(1,128)S(1)} collective-permute-done((f32[4,32,1,128]{3,2,1,0:T(1,128)S(1)}, f32[4,32,1,128]{3,2,1,0:T(1,128)S(1)}, u32[]{:S(2)}, u32[]{:S(2)}) %collective-permute-start.23) | collective-permute-done | bytes 65568 | tf_op jit(solution)/shard_map/ppermute | solution.py:107
  244.9 25.7 %chebyshev_sweep.3 = (f32[4,32,64,128]{3,2,1,0:T(8,128)}, f32[4,32,64,128]{3,2,1,0:T(8,128)}, f32[4,32,64,128]{3,2,1,0:T(8,128)}, f32[4,64,128]{2,1,0:T(8,128)},...) custom-call(f32[2]{0:T(128)} %constant.119.clone.coef_ref, ...), custom_call_target="tpu_custom_call" | custom-call | flops 31457280 | bytes 36700160 | tf_op jit(solution)/shard_map/chebyshev_sweep/pallas_call | solution.py:254
  272.8 4.6 %collective-permute-start.25 = (f32[4,64,128]{2,1,0:T(8,128)}, f32[4,64,128]{2,1,0:T(8,128)S(1)}, u32[]{:S(2)}, u32[]{:S(2)}) collective-permute-start(f32[4,64,128]{2,1,0:T(8,128)} %get-tuple-element.42), channel_id=1, source_target_pairs={{0,8},{8,16},{16,24},{1,9},{9,17},{17,25},{2,10},{10,18},{18,26},{... | collective-permute-start | bytes 393224 | tf_op jit(solution)/shard_map/ppermute | solution.py:107
  278.7 2.8 collective-permute-start.27
  283.7 4.2 %collective-permute-done.28.yhi = f32[4,32,1,128]{3,2,1,0:T(1,128)S(1)} collective-permute-done((f32[4,32,1,128]{3,2,1,0:T(1,128)}, f32[4,32,1,128]{3,2,1,0:T(1,128)S(1)}, u32[]{:S(2)}, u32[]{:S(2)}) %collective-permute-start.28) | collective-permute-done | bytes 65568 | tf_op jit(solution)/shard_map/ppermute | solution.py:107
  288.5 25.6 %chebyshev_sweep.4 = (f32[4,32,64,128]{3,2,1,0:T(8,128)}, f32[4,32,64,128]{3,2,1,0:T(8,128)}, f32[4,32,64,128]{3,2,1,0:T(8,128)}, f32[4,64,128]{2,1,0:T(8,128)},...) custom-call(f32[2]{0:T(128)} %constant.120.clone.coef_ref, ...), custom_call_target="tpu_custom_call" | custom-call | flops 31457280 | bytes 36700160 | tf_op jit(solution)/shard_map/chebyshev_sweep/pallas_call | solution.py:254
  315.1 1.8 pad_maximum_fusion
  316.9 4.9 %collective-permute-start.30 = (f32[4,64,128]{2,1,0:T(8,128)S(1)}, f32[4,64,128]{2,1,0:T(8,128)S(1)}, u32[]{:S(2)}, u32[]{:S(2)}) collective-permute-start(f32[4,64,128]{2,1,0:T(8,128)S(1)} %copy-done.93), channel_id=1, source_target_pairs={{0,8},{8,16},{16,24},{1,9},{9,17},{17,25},{2,10},{10,18},{18,26},{... | collective-permute-start | bytes 393224 | tf_op jit(solution)/shard_map/ppermute | solution.py:107
  323.1 3.6 collective-permute-start.32
  328.7 4.2 %collective-permute-done.33.yhi = f32[4,32,1,128]{3,2,1,0:T(1,128)S(1)} collective-permute-done((f32[4,32,1,128]{3,2,1,0:T(1,128)S(1)}, f32[4,32,1,128]{3,2,1,0:T(1,128)S(1)}, u32[]{:S(2)}, u32[]{:S(2)}) %collective-permute-start.33) | collective-permute-done | bytes 65568 | tf_op jit(solution)/shard_map/ppermute | solution.py:107
  333.6 28.7 %chebyshev_sweep.5 = (f32[4,32,64,128]{3,2,1,0:T(8,128)}, f32[4,32,64,128]{3,2,1,0:T(8,128)}, f32[32,64,4,128]{3,2,1,0:T(4,128)}, f32[4,64,128]{2,1,0:T(8,128)},...) custom-call(f32[2]{0:T(128)} %constant.121.clone.coef_ref, ...), custom_call_target="tpu_custom_call" | custom-call | flops 31457280 | bytes 36700160 | tf_op jit(solution)/shard_map/chebyshev_sweep/pallas_call | solution.py:254
  (378 shorter events, 73.0 us)
Async XLA Ops:
  12.8 35.0 %copy-start = (f32[32,64,128]{2,1,0:T(8,128)}, f32[32,64,128]{2,1,0:T(8,128)S(1)}, u32[]{:S(2)}) copy-start(f32[32,64,128]{2,1,0:T(8,128)S(1)} %get-tuple-element.102) | copy-start | bytes 3145732
  12.8 36.5 %copy-start.1 = (f32[32,64,128]{2,1,0:T(8,128)}, f32[32,64,128]{2,1,0:T(8,128)S(1)}, u32[]{:S(2)}) copy-start(f32[32,64,128]{2,1,0:T(8,128)S(1)} %get-tuple-element.103) | copy-start | bytes 3145732
  15.2 55.3 %collective-permute-start.2 = (f32[5120]{0:T(1024)}, f32[5120]{0:T(1024)S(1)}, u32[]{:S(2)}, u32[]{:S(2)}) collective-permute-start(f32[5120]{0:T(1024)} %pad_maximum_fusion.4), channel_id=1, source_target_pairs={{2,0},{4,2},{6,4},{3,1},{5,3},{7,5},{10,8},{12,10},{14,12},{11,9},... | collective-permute-start | bytes 61448 | tf_op jit(solution)/shard_map/ppermute | solution.py:107
  17.1 53.4 %collective-permute-start.3 = (f32[5120]{0:T(1024)}, f32[5120]{0:T(1024)S(1)}, u32[]{:S(2)}, u32[]{:S(2)}) collective-permute-start(f32[5120]{0:T(1024)} %pad_maximum_fusion.5), channel_id=1, source_target_pairs={{0,2},{2,4},{4,6},{1,3},{3,5},{5,7},{8,10},{10,12},{12,14},{9,11},... | collective-permute-start | bytes 61448 | tf_op jit(solution)/shard_map/ppermute | solution.py:107
  23.4 47.7 %collective-permute-start.1 = (f32[12288]{0:T(1024)S(1)}, f32[12288]{0:T(1024)S(1)}, u32[]{:S(2)}, u32[]{:S(2)}) collective-permute-start(f32[12288]{0:T(1024)S(1)} %pad_maximum_fusion.3), channel_id=1, source_target_pairs={{0,8},{8,16},{16,24},{1,9},{9,17},{17,25},{2,10},{10,18},{18,26},{... | collective-permute-start | bytes 147464 | tf_op jit(solution)/shard_map/ppermute | solution.py:107
  27.9 43.3 %collective-permute-start = (f32[12288]{0:T(1024)}, f32[12288]{0:T(1024)S(1)}, u32[]{:S(2)}, u32[]{:S(2)}) collective-permute-start(f32[12288]{0:T(1024)} %pad_maximum_fusion.2), channel_id=1, source_target_pairs={{8,0},{16,8},{24,16},{9,1},{17,9},{25,17},{10,2},{18,10},{26,18},{... | collective-permute-start | bytes 147464 | tf_op jit(solution)/shard_map/ppermute | solution.py:107
  31.2 33.7 %collective-permute-start.4 = (f32[2304]{0:T(1024)}, f32[2304]{0:T(1024)}, u32[]{:S(2)}, u32[]{:S(2)}) collective-permute-start(f32[2304]{0:T(1024)} %maximum_select_fusion), channel_id=1, source_target_pairs={{0,1},{1,0},{2,3},{3,2},{4,5},{5,4},{6,7},{7,6},{8,9},{9,8},{10,11... | collective-permute-start | bytes 27656 | tf_op jit(solution)/shard_map/ppermute | solution.py:102
  41.7 16.9 %all-to-all-start = ((s32[32,1,24]{2,1,0:T(1,128)}), s32[32,1,24]{2,1,0:T(1,128)S(1)}, u32[]{:S(2)}, u32[]{:S(2)}) async-start(s32[32,1,24]{2,1,0:T(1,128)} %bitcast.116), calls=%async_computation | async-start | bytes 32768 | tf_op jit(solution)/shard_map/all_to_all | solution.py:299
  55.0 51.0 %copy-start.8 = (pred[8,32,128]{2,1,0:T(8,128)(4,1)}, pred[8,32,128]{2,1,0:T(8,128)(4,1)S(1)}, u32[]{:S(2)}) copy-start(pred[8,32,128]{2,1,0:T(8,128)(4,1)S(1)} %get-tuple-element.162) | copy-start | bytes 98308
  55.0 51.0 %copy-start.10 = (pred[8,32,128]{2,1,0:T(8,128)(4,1)}, pred[8,32,128]{2,1,0:T(8,128)(4,1)S(1)}, u32[]{:S(2)}) copy-start(pred[8,32,128]{2,1,0:T(8,128)(4,1)S(1)} %get-tuple-element.163) | copy-start | bytes 98308
  55.0 51.0 %copy-start.12 = (pred[8,32,128]{2,1,0:T(8,128)(4,1)}, pred[8,32,128]{2,1,0:T(8,128)(4,1)S(1)}, u32[]{:S(2)}) copy-start(pred[8,32,128]{2,1,0:T(8,128)(4,1)S(1)} %get-tuple-element.164) | copy-start | bytes 98308
  79.9 13.3 %collective-permute-start.9 = (f32[8,32]{1,0:T(8,128)S(1)}, f32[8,32]{1,0:T(8,128)S(1)}, u32[]{:S(2)}, u32[]{:S(2)}) collective-permute-start(f32[8,32]{1,0:T(8,128)S(1)} %fusion.10), channel_id=1, source_target_pairs={{0,1},{1,0},{2,3},{3,2},{4,5},{5,4},{6,7},{7,6},{8,9},{9,8},{10,11... | collective-permute-start | bytes 3080 | tf_op jit(solution)/shard_map/ppermute | solution.py:102
  80.2 16.4 %collective-permute-start.5 = (f32[32,128]{1,0:T(8,128)S(1)}, f32[32,128]{1,0:T(8,128)S(1)}, u32[]{:S(2)}, u32[]{:S(2)}) collective-permute-start(f32[32,128]{1,0:T(8,128)S(1)} %get-tuple-element.153), channel_id=1, source_target_pairs={{8,0},{16,8},{24,16},{9,1},{17,9},{25,17},{10,2},{18,10},{26,18},{... | collective-permute-start | bytes 49160 | tf_op jit(solution)/shard_map/ppermute | solution.py:107
  81.5 15.1 %collective-permute-start.6 = (f32[32,128]{1,0:T(8,128)S(1)}, f32[32,128]{1,0:T(8,128)S(1)}, u32[]{:S(2)}, u32[]{:S(2)}) collective-permute-start(f32[32,128]{1,0:T(8,128)S(1)} %get-tuple-element.152), channel_id=1, source_target_pairs={{0,8},{8,16},{16,24},{1,9},{9,17},{17,25},{2,10},{10,18},{18,26},{... | collective-permute-start | bytes 49160 | tf_op jit(solution)/shard_map/ppermute | solution.py:107
  86.0 10.5 %collective-permute-start.7 = (f32[8,128]{1,0:T(8,128)S(1)}, f32[8,128]{1,0:T(8,128)S(1)}, u32[]{:S(2)}, u32[]{:S(2)}) collective-permute-start(f32[8,128]{1,0:T(8,128)S(1)} %bitcast.358), channel_id=1, source_target_pairs={{2,0},{4,2},{6,4},{3,1},{5,3},{7,5},{10,8},{12,10},{14,12},{11,9},... | collective-permute-start | bytes 12296 | tf_op jit(solution)/shard_map/ppermute | solution.py:107
  87.3 9.2 %collective-permute-start.8 = (f32[8,128]{1,0:T(8,128)S(1)}, f32[8,128]{1,0:T(8,128)S(1)}, u32[]{:S(2)}, u32[]{:S(2)}) collective-permute-start(f32[8,128]{1,0:T(8,128)S(1)} %bitcast.357), channel_id=1, source_target_pairs={{0,2},{2,4},{4,6},{1,3},{3,5},{5,7},{8,10},{10,12},{12,14},{9,11},... | collective-permute-start | bytes 12296 | tf_op jit(solution)/shard_map/ppermute | solution.py:107
  106.6 13.9 %collective-permute-start.14 = (f32[8,32]{1,0:T(8,128)S(1)}, f32[8,32]{1,0:T(8,128)S(1)}, u32[]{:S(2)}, u32[]{:S(2)}) collective-permute-start(f32[8,32]{1,0:T(8,128)S(1)} %fusion.9), channel_id=1, source_target_pairs={{0,1},{1,0},{2,3},{3,2},{4,5},{5,4},{6,7},{7,6},{8,9},{9,8},{10,11... | collective-permute-start | bytes 3080 | tf_op jit(solution)/shard_map/ppermute | solution.py:102
  108.0 13.6 %collective-permute-start.10 = (f32[32,128]{1,0:T(8,128)S(1)}, f32[32,128]{1,0:T(8,128)S(1)}, u32[]{:S(2)}, u32[]{:S(2)}) collective-permute-start(f32[32,128]{1,0:T(8,128)S(1)} %get-tuple-element.137), channel_id=1, source_target_pairs={{8,0},{16,8},{24,16},{9,1},{17,9},{25,17},{10,2},{18,10},{26,18},{... | collective-permute-start | bytes 49160 | tf_op jit(solution)/shard_map/ppermute | solution.py:107
  109.3 12.3 %collective-permute-start.11 = (f32[32,128]{1,0:T(8,128)S(1)}, f32[32,128]{1,0:T(8,128)S(1)}, u32[]{:S(2)}, u32[]{:S(2)}) collective-permute-start(f32[32,128]{1,0:T(8,128)S(1)} %get-tuple-element.136), channel_id=1, source_target_pairs={{0,8},{8,16},{16,24},{1,9},{9,17},{17,25},{2,10},{10,18},{18,26},{... | collective-permute-start | bytes 49160 | tf_op jit(solution)/shard_map/ppermute | solution.py:107
  114.4 6.7 %collective-permute-start.12 = (f32[8,128]{1,0:T(8,128)S(1)}, f32[8,128]{1,0:T(8,128)S(1)}, u32[]{:S(2)}, u32[]{:S(2)}) collective-permute-start(f32[8,128]{1,0:T(8,128)S(1)} %bitcast.361), channel_id=1, source_target_pairs={{2,0},{4,2},{6,4},{3,1},{5,3},{7,5},{10,8},{12,10},{14,12},{11,9},... | collective-permute-start | bytes 12296 | tf_op jit(solution)/shard_map/ppermute | solution.py:107
  115.7 5.9 %collective-permute-start.13 = (f32[8,128]{1,0:T(8,128)S(1)}, f32[8,128]{1,0:T(8,128)S(1)}, u32[]{:S(2)}, u32[]{:S(2)}) collective-permute-start(f32[8,128]{1,0:T(8,128)S(1)} %bitcast.359), channel_id=1, source_target_pairs={{0,2},{2,4},{4,6},{1,3},{3,5},{5,7},{8,10},{10,12},{12,14},{9,11},... | collective-permute-start | bytes 12296 | tf_op jit(solution)/shard_map/ppermute | solution.py:107
  125.4 13.0 %collective-permute-start.19 = (f32[8,32]{1,0:T(8,128)S(1)}, f32[8,32]{1,0:T(8,128)S(1)}, u32[]{:S(2)}, u32[]{:S(2)}) collective-permute-start(f32[8,32]{1,0:T(8,128)S(1)} %fusion.8), channel_id=1, source_target_pairs={{0,1},{1,0},{2,3},{3,2},{4,5},{5,4},{6,7},{7,6},{8,9},{9,8},{10,11... | collective-permute-start | bytes 3080 | tf_op jit(solution)/shard_map/ppermute | solution.py:102
  125.5 14.2 %collective-permute-start.15 = (f32[32,128]{1,0:T(8,128)S(1)}, f32[32,128]{1,0:T(8,128)S(1)}, u32[]{:S(2)}, u32[]{:S(2)}) collective-permute-start(f32[32,128]{1,0:T(8,128)S(1)} %get-tuple-element.121), channel_id=1, source_target_pairs={{8,0},{16,8},{24,16},{9,1},{17,9},{25,17},{10,2},{18,10},{26,18},{... | collective-permute-start | bytes 49160 | tf_op jit(solution)/shard_map/ppermute | solution.py:107
  126.8 12.9 %collective-permute-start.16 = (f32[32,128]{1,0:T(8,128)S(1)}, f32[32,128]{1,0:T(8,128)S(1)}, u32[]{:S(2)}, u32[]{:S(2)}) collective-permute-start(f32[32,128]{1,0:T(8,128)S(1)} %get-tuple-element.120), channel_id=1, source_target_pairs={{0,8},{8,16},{16,24},{1,9},{9,17},{17,25},{2,10},{10,18},{18,26},{... | collective-permute-start | bytes 49160 | tf_op jit(solution)/shard_map/ppermute | solution.py:107
  132.2 6.4 %collective-permute-start.17 = (f32[8,128]{1,0:T(8,128)S(1)}, f32[8,128]{1,0:T(8,128)S(1)}, u32[]{:S(2)}, u32[]{:S(2)}) collective-permute-start(f32[8,128]{1,0:T(8,128)S(1)} %bitcast.362), channel_id=1, source_target_pairs={{2,0},{4,2},{6,4},{3,1},{5,3},{7,5},{10,8},{12,10},{14,12},{11,9},... | collective-permute-start | bytes 12296 | tf_op jit(solution)/shard_map/ppermute | solution.py:107
  133.5 6.1 %collective-permute-start.18 = (f32[8,128]{1,0:T(8,128)S(1)}, f32[8,128]{1,0:T(8,128)S(1)}, u32[]{:S(2)}, u32[]{:S(2)}) collective-permute-start(f32[8,128]{1,0:T(8,128)S(1)} %bitcast.360), channel_id=1, source_target_pairs={{0,2},{2,4},{4,6},{1,3},{3,5},{5,7},{8,10},{10,12},{12,14},{9,11},... | collective-permute-start | bytes 12296 | tf_op jit(solution)/shard_map/ppermute | solution.py:107
  149.8 46.2 %all-to-all-start.1 = ((f32[4,32,24,128]{3,0,2,1:T(4,128)}), f32[4,32,24,128]{3,0,2,1:T(4,128)S(1)}, u32[]{:S(2)}, u32[]{:S(2)}) async-start(f32[4,32,24,128]{3,0,2,1:T(4,128)} %select_select_fusion.1), calls=%async_computation.1 | async-start | bytes 3145728 | tf_op jit(solution)/shard_map/all_to_all | solution.py:329
  166.6 29.5 %copy-start.58 = (s32[2048]{0:T(1024)S(1)}, s32[2048]{0:T(1024)}, u32[]{:S(2)}) copy-start(s32[2048]{0:T(1024)} %fusion.84) | copy-start | bytes 24580
  231.8 7.5 %collective-permute-start.24 = (f32[4,32,64]{2,1,0:T(8,128)S(1)}, f32[4,32,64]{2,1,0:T(8,128)S(1)}, u32[]{:S(2)}, u32[]{:S(2)}) collective-permute-start(f32[4,32,64]{2,1,0:T(8,128)S(1)} %broadcast_select_fusion.8), channel_id=1, source_target_pairs={{0,1},{1,0},{2,3},{3,2},{4,5},{5,4},{6,7},{7,6},{8,9},{9,8},{10,11... | collective-permute-start | bytes 98312 | tf_op jit(solution)/shard_map/ppermute | solution.py:102
  232.7 11.5 %collective-permute-start.20 = (f32[4,64,128]{2,1,0:T(8,128)}, f32[4,64,128]{2,1,0:T(8,128)S(1)}, u32[]{:S(2)}, u32[]{:S(2)}) collective-permute-start(f32[4,64,128]{2,1,0:T(8,128)} %get-tuple-element.33), channel_id=1, source_target_pairs={{0,8},{8,16},{16,24},{1,9},{9,17},{17,25},{2,10},{10,18},{18,26},{... | collective-permute-start | bytes 393224 | tf_op jit(solution)/shard_map/ppermute | solution.py:107
  235.4 8.8 %collective-permute-start.21 = (f32[4,64,128]{2,1,0:T(8,128)}, f32[4,64,128]{2,1,0:T(8,128)S(1)}, u32[]{:S(2)}, u32[]{:S(2)}) collective-permute-start(f32[4,64,128]{2,1,0:T(8,128)} %get-tuple-element.34), channel_id=1, source_target_pairs={{8,0},{16,8},{24,16},{9,1},{17,9},{25,17},{10,2},{18,10},{26,18},{... | collective-permute-start | bytes 393224 | tf_op jit(solution)/shard_map/ppermute | solution.py:107
  236.7 3.5 collective-permute-start.22
  238.0 6.2 %collective-permute-start.23 = (f32[4,32,1,128]{3,2,1,0:T(1,128)S(1)}, f32[4,32,1,128]{3,2,1,0:T(1,128)S(1)}, u32[]{:S(2)}, u32[]{:S(2)}) collective-permute-start(f32[4,32,1,128]{3,2,1,0:T(1,128)S(1)} %copy-done.96), channel_id=1, source_target_pairs={{2,0},{4,2},{6,4},{3,1},{5,3},{7,5},{10,8},{12,10},{14,12},{11,9},... | collective-permute-start | bytes 196616 | tf_op jit(solution)/shard_map/ppermute | solution.py:107
  244.9 26.7 %copy-start.23 = (f32[1,8,32,127]{3,2,1,0:T(8,128)S(1)}, f32[1,8,32,127]{3,2,1,0:T(8,128)}, u32[]{:S(2)}) copy-start(f32[1,8,32,127]{3,2,1,0:T(8,128)} %get-tuple-element.115) | copy-start | bytes 390148
  244.9 26.7 %copy-start.43 = (f32[32,128]{1,0:T(8,128)S(1)}, f32[32,128]{1,0:T(8,128)}, u32[]{:S(2)}) copy-start(f32[32,128]{1,0:T(8,128)} %copy-done.42) | copy-start | bytes 49156
  244.9 26.7 %copy-start.45 = (f32[32,128]{1,0:T(8,128)S(1)}, f32[32,128]{1,0:T(8,128)}, u32[]{:S(2)}) copy-start(f32[32,128]{1,0:T(8,128)} %copy-done.44) | copy-start | bytes 49156
  244.9 26.7 %copy-start.65 = (f32[8,128]{1,0:T(8,128)S(1)}, f32[8,128]{1,0:T(8,128)}, u32[]{:S(2)}) copy-start(f32[8,128]{1,0:T(8,128)} %copy-done.64) | copy-start | bytes 12292
  244.9 26.7 %copy-start.67 = (f32[8,128]{1,0:T(8,128)S(1)}, f32[8,128]{1,0:T(8,128)}, u32[]{:S(2)}) copy-start(f32[8,128]{1,0:T(8,128)} %copy-done.66) | copy-start | bytes 12292
  271.5 11.3 %collective-permute-start.29 = (f32[4,32,64]{2,1,0:T(8,128)S(1)}, f32[4,32,64]{2,1,0:T(8,128)S(1)}, u32[]{:S(2)}, u32[]{:S(2)}) collective-permute-start(f32[4,32,64]{2,1,0:T(8,128)S(1)} %broadcast_select_fusion.7), channel_id=1, source_target_pairs={{0,1},{1,0},{2,3},{3,2},{4,5},{5,4},{6,7},{7,6},{8,9},{9,8},{10,11... | collective-permute-start | bytes 98312 | tf_op jit(solution)/shard_map/ppermute | solution.py:102
  272.8 15.0 %collective-permute-start.25 = (f32[4,64,128]{2,1,0:T(8,128)}, f32[4,64,128]{2,1,0:T(8,128)S(1)}, u32[]{:S(2)}, u32[]{:S(2)}) collective-permute-start(f32[4,64,128]{2,1,0:T(8,128)} %get-tuple-element.42), channel_id=1, source_target_pairs={{0,8},{8,16},{16,24},{1,9},{9,17},{17,25},{2,10},{10,18},{18,26},{... | collective-permute-start | bytes 393224 | tf_op jit(solution)/shard_map/ppermute | solution.py:107
  277.4 10.4 %collective-permute-start.26 = (f32[4,64,128]{2,1,0:T(8,128)}, f32[4,64,128]{2,1,0:T(8,128)S(1)}, u32[]{:S(2)}, u32[]{:S(2)}) collective-permute-start(f32[4,64,128]{2,1,0:T(8,128)} %get-tuple-element.43), channel_id=1, source_target_pairs={{8,0},{16,8},{24,16},{9,1},{17,9},{25,17},{10,2},{18,10},{26,18},{... | collective-permute-start | bytes 393224 | tf_op jit(solution)/shard_map/ppermute | solution.py:107
  278.7 5.0 %collective-permute-start.27 = (f32[4,32,1,128]{3,2,1,0:T(1,128)}, f32[4,32,1,128]{3,2,1,0:T(1,128)S(1)}, u32[]{:S(2)}, u32[]{:S(2)}) collective-permute-start(f32[4,32,1,128]{3,2,1,0:T(1,128)} %get-tuple-element.44), channel_id=1, source_target_pairs={{0,2},{2,4},{4,6},{1,3},{3,5},{5,7},{8,10},{10,12},{12,14},{9,11},... | collective-permute-start | bytes 196616 | tf_op jit(solution)/shard_map/ppermute | solution.py:107
  281.5 6.4 %collective-permute-start.28 = (f32[4,32,1,128]{3,2,1,0:T(1,128)}, f32[4,32,1,128]{3,2,1,0:T(1,128)S(1)}, u32[]{:S(2)}, u32[]{:S(2)}) collective-permute-start(f32[4,32,1,128]{3,2,1,0:T(1,128)} %get-tuple-element.45), channel_id=1, source_target_pairs={{2,0},{4,2},{6,4},{3,1},{5,3},{7,5},{10,8},{12,10},{14,12},{11,9},... | collective-permute-start | bytes 196616 | tf_op jit(solution)/shard_map/ppermute | solution.py:107
  315.1 12.9 %collective-permute-start.34 = (f32[4,32,64]{2,1,0:T(8,128)S(1)}, f32[4,32,64]{2,1,0:T(8,128)S(1)}, u32[]{:S(2)}, u32[]{:S(2)}) collective-permute-start(f32[4,32,64]{2,1,0:T(8,128)S(1)} %broadcast_select_fusion.6), channel_id=1, source_target_pairs={{0,1},{1,0},{2,3},{3,2},{4,5},{5,4},{6,7},{7,6},{8,9},{9,8},{10,11... | collective-permute-start | bytes 98312 | tf_op jit(solution)/shard_map/ppermute | solution.py:102
  316.9 16.0 %collective-permute-start.30 = (f32[4,64,128]{2,1,0:T(8,128)S(1)}, f32[4,64,128]{2,1,0:T(8,128)S(1)}, u32[]{:S(2)}, u32[]{:S(2)}) collective-permute-start(f32[4,64,128]{2,1,0:T(8,128)S(1)} %copy-done.93), channel_id=1, source_target_pairs={{0,8},{8,16},{16,24},{1,9},{9,17},{17,25},{2,10},{10,18},{18,26},{... | collective-permute-start | bytes 393224 | tf_op jit(solution)/shard_map/ppermute | solution.py:107
  321.8 11.1 %collective-permute-start.31 = (f32[4,64,128]{2,1,0:T(8,128)S(1)}, f32[4,64,128]{2,1,0:T(8,128)S(1)}, u32[]{:S(2)}, u32[]{:S(2)}) collective-permute-start(f32[4,64,128]{2,1,0:T(8,128)S(1)} %copy-done.92), channel_id=1, source_target_pairs={{8,0},{16,8},{24,16},{9,1},{17,9},{25,17},{10,2},{18,10},{26,18},{... | collective-permute-start | bytes 393224 | tf_op jit(solution)/shard_map/ppermute | solution.py:107
  323.1 5.6 %collective-permute-start.32 = (f32[4,32,1,128]{3,2,1,0:T(1,128)S(1)}, f32[4,32,1,128]{3,2,1,0:T(1,128)S(1)}, u32[]{:S(2)}, u32[]{:S(2)}) collective-permute-start(f32[4,32,1,128]{3,2,1,0:T(1,128)S(1)} %copy-done.95), channel_id=1, source_target_pairs={{0,2},{2,4},{4,6},{1,3},{3,5},{5,7},{8,10},{10,12},{12,14},{9,11},... | collective-permute-start | bytes 196616 | tf_op jit(solution)/shard_map/ppermute | solution.py:107
  326.7 6.2 %collective-permute-start.33 = (f32[4,32,1,128]{3,2,1,0:T(1,128)S(1)}, f32[4,32,1,128]{3,2,1,0:T(1,128)S(1)}, u32[]{:S(2)}, u32[]{:S(2)}) collective-permute-start(f32[4,32,1,128]{3,2,1,0:T(1,128)S(1)} %copy-done.94), channel_id=1, source_target_pairs={{2,0},{4,2},{6,4},{3,1},{5,3},{7,5},{10,8},{12,10},{14,12},{11,9},... | collective-permute-start | bytes 196616 | tf_op jit(solution)/shard_map/ppermute | solution.py:107
  (89 other events, 515.7 us)

commit v9 on v8

--- a/solution.py
+++ b/solution.py
@@ -189,7 +189,7 @@
             p_out[0, x] = p_ref[0, x] + step_dir
         return write_faces(x, step_dir, carry, *face_out)
 
-    columns = lax.fori_loop(0, nx, body, jnp.zeros((ny, nz), jnp.float32), unroll=4)
+    columns = lax.fori_loop(0, nx, body, jnp.zeros((ny, nz), jnp.float32), unroll=8)
     finish_faces(columns, *face_out)
 
 
@@ -201,7 +201,7 @@
         d_out[0, x] = step_dir
         return write_faces(x, step_dir, carry, *face_out)
 
-    columns = lax.fori_loop(0, nx, body, jnp.zeros((ny, nz), jnp.float32), unroll=2)
+    columns = lax.fori_loop(0, nx, body, jnp.zeros((ny, nz), jnp.float32), unroll=4)
     finish_faces(columns, *face_out)
 
 

time: 366 us -> 363 us (level)
  Pallas kernels: 94.3 us -> 90.5 us
where the time goes in v9:
time: 363 us; the launch traced here: 359 us
  starting transfers between devices  90.5 us (25%)
  Pallas kernels  90.5 us (25%)
  other arithmetic  72.7 us (20%)
  local copies, waits for them, and re-layouts  65.8 us (18%)
  waiting for transfers between devices  36.2 us (10%)
    pallas_call x3, Pallas kernels, run_sweep(): pl.pallas_call(functools.partial(sweep_kernel, final), grid=(steps,), in_...  76.4 us
    ppermute x14, starting transfers between devices, exchange(): lax.ppermute(top, axis, forward)  58.3 us
    all_to_all x1, waiting for transfers between devices, local(): lax.all_to_all(send_values.reshape(STEPS, devices, capacity, row_len), ('...  21.9 us
    ppermute x14, starting transfers between devices, exchange(): lax.ppermute(bottom, axis, backward)  18.1 us
    gather x2, local copies, waits for them, and re-layouts, local(): jnp.take(received, row_slot, axis=1)  17.7 us
    add x4, other arithmetic, membrane(): steady + (gate_state - steady) * jnp.exp(-DT_HEART / time_const)  16.1 us
    pallas_call x1, Pallas kernels, run_initial(): pl.pallas_call(functools.partial(initial_kernel, mid), grid=(source.shape...  14.1 us
    ppermute x14, waiting for transfers between devices, exchange(): lax.ppermute(bottom, axis, backward)  12.3 us
  transfers between devices with their start and end apart: 37, of which 8 were waited for; matrix products, arithmetic and copies ran while one was open for 18% of the time, Pallas kernels for 0%

profile of v9, /device:TPU:0, one launch (start us, length us, event | category | flops | bytes accessed | tf_op | source)
XLA Modules:
  0.0 358.7 jit_solution(4740543650634735733)
XLA Ops:
  0.6 1.8 fusion.118
  2.4 4.5 %select_add_fusion.1 = (f32[32,64,128]{2,1,0:T(8,128)S(1)}, pred[32,64,128]{2,1,0:T(8,128)(4,1)S(1)}, pred[32,64,128]{2,1,0:T(8,128)(4,1)S(1)}, pred[32,64,128]{2,1,0:T(8,128)(4,1)S(1)}, pred[32,64,128]{2,1,0:T(8,128)(4,1)S(1)}) fusion(f32[]{:T(128)} %bitcast.29, f32[]{:T(128)} %bitcast.28, f32[]{:T(128)} %bitcast.27, f32[]{:T(128)} %bitcast.26, ...), kind=kLoop, calls=%fused_computation.33 | loop fusion | flops 2883584 | bytes 3145744 | tf_op jit(solution)/shard_map/add | solution.py:310
  6.9 5.9 %select_add_fusion.2 = (f32[32,64,128]{2,1,0:T(8,128)S(1)}, f32[32,64,128]{2,1,0:T(8,128)S(1)}) fusion(pred[32,64,128]{2,1,0:T(8,128)(4,1)S(1)} %get-tuple-element.85, pred[32,64,128]{2,1,0:T(8,128)(4,1)S(1)} %get-tuple-element.84, pred[32,64,128]{2,1,0:T(8,128)(4,1)S(1)} %get-tuple-element.83, pred[32,64,128]{2,1,0:T(8,128)(4,1)S(1)} %get-tuple-element.82, ...), kind=kLoop, calls=%fused_computation.34 | loop fusion | flops 3670016 | bytes 3145760 | tf_op jit(solution)/shard_map/add | solution.py:310
  12.9 1.8 fusion.98
  17.1 5.5 %collective-permute-start.3 = (f32[5120]{0:T(1024)}, f32[5120]{0:T(1024)S(1)}, u32[]{:S(2)}, u32[]{:S(2)}) collective-permute-start(f32[5120]{0:T(1024)} %pad_maximum_fusion.5), channel_id=1, source_target_pairs={{0,2},{2,4},{4,6},{1,3},{3,5},{5,7},{8,10},{10,12},{12,14},{9,11},... | collective-permute-start | bytes 61448 | tf_op jit(solution)/shard_map/ppermute | solution.py:107
  23.4 3.8 %collective-permute-start.1 = (f32[12288]{0:T(1024)S(1)}, f32[12288]{0:T(1024)S(1)}, u32[]{:S(2)}, u32[]{:S(2)}) collective-permute-start(f32[12288]{0:T(1024)S(1)} %pad_maximum_fusion.3), channel_id=1, source_target_pairs={{0,8},{8,16},{16,24},{1,9},{9,17},{17,25},{2,10},{10,18},{18,26},{... | collective-permute-start | bytes 147464 | tf_op jit(solution)/shard_map/ppermute | solution.py:107
  34.6 1.3 reduce.66
  36.0 5.0 %gather_fusion = s32[768]{0:T(1024)S(1)} fusion(s32[256]{0:T(256)S(1)} %reshape.1868, s32[1024]{0:T(1024)S(1)} %pad_clamp_fusion), kind=kCustom, calls=%fused_computation | custom fusion | bytes 9216 | tf_op jit(solution)/shard_map/gather | solution.py:298
  41.7 6.1 %all-to-all-start = ((s32[32,1,24]{2,1,0:T(1,128)}), s32[32,1,24]{2,1,0:T(1,128)S(1)}, u32[]{:S(2)}, u32[]{:S(2)}) async-start(s32[32,1,24]{2,1,0:T(1,128)} %bitcast.116), calls=%async_computation | async-start | bytes 32768 | tf_op jit(solution)/shard_map/all_to_all | solution.py:299
  47.8 1.5 fusion.100
  49.3 1.6 fusion.101
  50.9 1.7 fusion.99
  55.1 1.5 multiply_add_fusion.3
  59.4 2.8 iota_reduce_fusion
  66.5 1.8 slice.567
  68.3 1.9 slice.568
  75.0 1.4 fusion.18
  76.5 2.8 multiply_add_fusion.2
  81.5 4.5 %collective-permute-start.6 = (f32[32,128]{1,0:T(8,128)S(1)}, f32[32,128]{1,0:T(8,128)S(1)}, u32[]{:S(2)}, u32[]{:S(2)}) collective-permute-start(f32[32,128]{1,0:T(8,128)S(1)} %get-tuple-element.152), channel_id=1, source_target_pairs={{0,8},{8,16},{16,24},{1,9},{9,17},{17,25},{2,10},{10,18},{18,26},{... | collective-permute-start | bytes 49160 | tf_op jit(solution)/shard_map/ppermute | solution.py:107
  87.3 4.5 %collective-permute-start.8 = (f32[8,128]{1,0:T(8,128)S(1)}, f32[8,128]{1,0:T(8,128)S(1)}, u32[]{:S(2)}, u32[]{:S(2)}) collective-permute-start(f32[8,128]{1,0:T(8,128)S(1)} %bitcast.357), channel_id=1, source_target_pairs={{0,2},{2,4},{4,6},{1,3},{3,5},{5,7},{8,10},{10,12},{12,14},{9,11},... | collective-permute-start | bytes 12296 | tf_op jit(solution)/shard_map/ppermute | solution.py:107
  100.4 1.4 fusion.33
  101.9 4.2 %multiply_add_fusion.1 = f32[18,8,32,128]{3,2,1,0:T(8,128)S(1)} fusion(f32[8,32,128]{2,1,0:T(8,128)S(1)} %bitcast.299, f32[18]{0:T(128)S(1)} %copy-done.84, f32[18]{0:T(128)S(1)} %copy-done.87, f32[18]{0:T(128)S(1)} %copy-done.90, f32[8,32,128]{2,1,0:T(8,128)S(1)} %bitcast.291, f32[19,8,32,128]{3,2,1,0:T(8,128)S(1)} %copy-done.4, ...), kind=kLoop, calls=%fused_computation.9 | loop fusion | flops 19464192 | bytes 5112024 | tf_op jit(solution)/shard_map/add | solution.py:59
  109.3 5.1 %collective-permute-start.11 = (f32[32,128]{1,0:T(8,128)S(1)}, f32[32,128]{1,0:T(8,128)S(1)}, u32[]{:S(2)}, u32[]{:S(2)}) collective-permute-start(f32[32,128]{1,0:T(8,128)S(1)} %get-tuple-element.136), channel_id=1, source_target_pairs={{0,8},{8,16},{16,24},{1,9},{9,17},{17,25},{2,10},{10,18},{18,26},{... | collective-permute-start | bytes 49160 | tf_op jit(solution)/shard_map/ppermute | solution.py:107
  115.7 4.8 %collective-permute-start.13 = (f32[8,128]{1,0:T(8,128)S(1)}, f32[8,128]{1,0:T(8,128)S(1)}, u32[]{:S(2)}, u32[]{:S(2)}) collective-permute-start(f32[8,128]{1,0:T(8,128)S(1)} %bitcast.359), channel_id=1, source_target_pairs={{0,2},{2,4},{4,6},{1,3},{3,5},{5,7},{8,10},{10,12},{12,14},{9,11},... | collective-permute-start | bytes 12296 | tf_op jit(solution)/shard_map/ppermute | solution.py:107
  126.8 5.4 %collective-permute-start.16 = (f32[32,128]{1,0:T(8,128)S(1)}, f32[32,128]{1,0:T(8,128)S(1)}, u32[]{:S(2)}, u32[]{:S(2)}) collective-permute-start(f32[32,128]{1,0:T(8,128)S(1)} %get-tuple-element.120), channel_id=1, source_target_pairs={{0,8},{8,16},{16,24},{1,9},{9,17},{17,25},{2,10},{10,18},{18,26},{... | collective-permute-start | bytes 49160 | tf_op jit(solution)/shard_map/ppermute | solution.py:107
  133.5 4.8 %collective-permute-start.18 = (f32[8,128]{1,0:T(8,128)S(1)}, f32[8,128]{1,0:T(8,128)S(1)}, u32[]{:S(2)}, u32[]{:S(2)}) collective-permute-start(f32[8,128]{1,0:T(8,128)S(1)} %bitcast.360), channel_id=1, source_target_pairs={{0,2},{2,4},{4,6},{1,3},{3,5},{5,7},{8,10},{10,12},{12,14},{9,11},... | collective-permute-start | bytes 12296 | tf_op jit(solution)/shard_map/ppermute | solution.py:107
  141.9 3.0 gather_fusion.1
  144.8 4.9 %select_select_fusion.1 = f32[4,32,24,128]{3,0,2,1:T(4,128)} fusion(f32[4,32,24,128]{3,0,2,1:T(4,128)S(1)} %bitcast.285, pred[32,24]{1,0:T(8,128)(4,1)} %broadcast_in_dim.362, pred[32,24]{1,0:T(8,128)(4,1)} %broadcast_in_dim.360), kind=kLoop, calls=%fused_computation.12 | loop fusion | flops 786432 | bytes 3147264 | tf_op jit(solution)/shard_map/jit(_where)/select_n | solution.py:328
  149.8 7.4 %all-to-all-start.1 = ((f32[4,32,24,128]{3,0,2,1:T(4,128)}), f32[4,32,24,128]{3,0,2,1:T(4,128)S(1)}, u32[]{:S(2)}, u32[]{:S(2)}) async-start(f32[4,32,24,128]{3,0,2,1:T(4,128)} %select_select_fusion.1), calls=%async_computation.1 | async-start | bytes 3145728 | tf_op jit(solution)/shard_map/all_to_all | solution.py:329
  157.2 7.1 %broadcast_divide_fusion = (f32[32,64,128]{2,1,0:T(8,128)}, f32[32,64,128]{2,1,0:T(8,128)}, f32[32,64,128]{2,1,0:T(8,128)}, f32[32,64,128]{2,1,0:T(8,128)}, f32[...) fusion(f32[32,64,128]{2,1,0:T(8,128)} %copy-done.1, ...), kind=kLoop, calls=%fused_computation.40 | loop fusion | flops 6553600 | bytes 17825792 | tf_op jit(solution)/shard_map/div | solution.py:349
  166.6 7.5 %multiply_add_fusion = f32[18,8,32,128]{3,2,1,0:T(8,128)} fusion(f32[8,32,128]{2,1,0:T(8,128)S(1)} %bitcast.302, f32[18]{0:T(128)} %param.18, f32[18]{0:T(128)} %param.16, f32[18]{0:T(128)} %copy-done.88, f32[8,32,128]{2,1,0:T(8,128)S(1)} %bitcast.301, f32[8,32,128]{2,1,0:T(8,128)S(1)} %bitcast.292, f32[19,8,32,128]{3,2,1,0:T(8,128)} %param.14, ...), kind=kLoop, calls=%fused_computation.8 | loop fusion | flops 25952256 | bytes 5243096 | tf_op jit(solution)/shard_map/add | solution.py:59
  174.1 21.9 %all-to-all-done.1 = f32[4,32,24,128]{3,0,2,1:T(4,128)S(1)} async-done(((f32[4,32,24,128]{3,0,2,1:T(4,128)}), f32[4,32,24,128]{3,0,2,1:T(4,128)S(1)}, u32[]{:S(2)}, u32[]{:S(2)}) %all-to-all-start.1) | async-done | bytes 1572896 | tf_op jit(solution)/shard_map/all_to_all | solution.py:329
  196.0 15.2 %gather_fusion.2 = f32[2048,4,128]{2,1,0:T(4,128)} fusion(f32[4,768,128]{2,0,1:T(4,128)S(1)} %bitcast.282, s32[2048]{0:T(1024)S(1)} %copy-done.58), kind=kCustom, calls=%fused_computation.2 | custom fusion | bytes 8396800 | tf_op jit(solution)/shard_map/jit(_take)/gather | solution.py:336
  211.3 2.5 copy.1555
  213.8 2.8 select_select_fusion.r_ref
  216.6 14.1 %chebyshev_start.1 = (f32[4,32,64,128]{3,2,1,0:T(8,128)}, f32[4,64,128]{2,1,0:T(8,128)}, f32[4,64,128]{2,1,0:T(8,128)}, f32[4,32,1,128]{3,2,1,0:T(1,128)}, f32[4...) custom-call(f32[4,32,64,128]{3,2,1,0:T(8,128)} %select_select_fusion.r_ref, ...), custom_call_target="tpu_custom_call" | custom-call | flops 2097152 | bytes 9437184 | tf_op jit(solution)/shard_map/chebyshev_start/pallas_call | solution.py:231
  232.5 2.7 collective-permute-start.20
  240.0 4.0 %collective-permute-done.23.yhi = f32[4,32,1,128]{3,2,1,0:T(1,128)S(1)} collective-permute-done((f32[4,32,1,128]{3,2,1,0:T(1,128)S(1)}, f32[4,32,1,128]{3,2,1,0:T(1,128)S(1)}, u32[]{:S(2)}, u32[]{:S(2)}) %collective-permute-start.23) | collective-permute-done | bytes 65568 | tf_op jit(solution)/shard_map/ppermute | solution.py:107
  244.7 24.5 %chebyshev_sweep.3 = (f32[4,32,64,128]{3,2,1,0:T(8,128)}, f32[4,32,64,128]{3,2,1,0:T(8,128)}, f32[4,32,64,128]{3,2,1,0:T(8,128)}, f32[4,64,128]{2,1,0:T(8,128)},...) custom-call(f32[2]{0:T(128)} %constant.119.clone.coef_ref, ...), custom_call_target="tpu_custom_call" | custom-call | flops 31457280 | bytes 36700160 | tf_op jit(solution)/shard_map/chebyshev_sweep/pallas_call | solution.py:254
  271.4 4.6 %collective-permute-start.25 = (f32[4,64,128]{2,1,0:T(8,128)}, f32[4,64,128]{2,1,0:T(8,128)S(1)}, u32[]{:S(2)}, u32[]{:S(2)}) collective-permute-start(f32[4,64,128]{2,1,0:T(8,128)} %get-tuple-element.42), channel_id=1, source_target_pairs={{0,8},{8,16},{16,24},{1,9},{9,17},{17,25},{2,10},{10,18},{18,26},{... | collective-permute-start | bytes 393224 | tf_op jit(solution)/shard_map/ppermute | solution.py:107
  277.3 2.7 collective-permute-start.27
  282.2 4.2 %collective-permute-done.28.yhi = f32[4,32,1,128]{3,2,1,0:T(1,128)S(1)} collective-permute-done((f32[4,32,1,128]{3,2,1,0:T(1,128)}, f32[4,32,1,128]{3,2,1,0:T(1,128)S(1)}, u32[]{:S(2)}, u32[]{:S(2)}) %collective-permute-start.28) | collective-permute-done | bytes 65568 | tf_op jit(solution)/shard_map/ppermute | solution.py:107
  287.1 24.4 %chebyshev_sweep.4 = (f32[4,32,64,128]{3,2,1,0:T(8,128)}, f32[4,32,64,128]{3,2,1,0:T(8,128)}, f32[4,32,64,128]{3,2,1,0:T(8,128)}, f32[4,64,128]{2,1,0:T(8,128)},...) custom-call(f32[2]{0:T(128)} %constant.120.clone.coef_ref, ...), custom_call_target="tpu_custom_call" | custom-call | flops 31457280 | bytes 36700160 | tf_op jit(solution)/shard_map/chebyshev_sweep/pallas_call | solution.py:254
  312.5 1.8 pad_maximum_fusion
  314.3 4.9 %collective-permute-start.30 = (f32[4,64,128]{2,1,0:T(8,128)S(1)}, f32[4,64,128]{2,1,0:T(8,128)S(1)}, u32[]{:S(2)}, u32[]{:S(2)}) collective-permute-start(f32[4,64,128]{2,1,0:T(8,128)S(1)} %copy-done.93), channel_id=1, source_target_pairs={{0,8},{8,16},{16,24},{1,9},{9,17},{17,25},{2,10},{10,18},{18,26},{... | collective-permute-start | bytes 393224 | tf_op jit(solution)/shard_map/ppermute | solution.py:107
  320.5 3.5 collective-permute-start.32
  326.0 4.2 %collective-permute-done.33.yhi = f32[4,32,1,128]{3,2,1,0:T(1,128)S(1)} collective-permute-done((f32[4,32,1,128]{3,2,1,0:T(1,128)S(1)}, f32[4,32,1,128]{3,2,1,0:T(1,128)S(1)}, u32[]{:S(2)}, u32[]{:S(2)}) %collective-permute-start.33) | collective-permute-done | bytes 65568 | tf_op jit(solution)/shard_map/ppermute | solution.py:107
  330.9 27.5 %chebyshev_sweep.5 = (f32[4,32,64,128]{3,2,1,0:T(8,128)}, f32[4,32,64,128]{3,2,1,0:T(8,128)}, f32[32,64,4,128]{3,2,1,0:T(4,128)}, f32[4,64,128]{2,1,0:T(8,128)},...) custom-call(f32[2]{0:T(128)} %constant.121.clone.coef_ref, ...), custom_call_target="tpu_custom_call" | custom-call | flops 31457280 | bytes 36700160 | tf_op jit(solution)/shard_map/chebyshev_sweep/pallas_call | solution.py:254
  (378 shorter events, 73.0 us)
Async XLA Ops:
  12.8 35.0 %copy-start = (f32[32,64,128]{2,1,0:T(8,128)}, f32[32,64,128]{2,1,0:T(8,128)S(1)}, u32[]{:S(2)}) copy-start(f32[32,64,128]{2,1,0:T(8,128)S(1)} %get-tuple-element.102) | copy-start | bytes 3145732
  12.8 36.5 %copy-start.1 = (f32[32,64,128]{2,1,0:T(8,128)}, f32[32,64,128]{2,1,0:T(8,128)S(1)}, u32[]{:S(2)}) copy-start(f32[32,64,128]{2,1,0:T(8,128)S(1)} %get-tuple-element.103) | copy-start | bytes 3145732
  15.2 55.3 %collective-permute-start.2 = (f32[5120]{0:T(1024)}, f32[5120]{0:T(1024)S(1)}, u32[]{:S(2)}, u32[]{:S(2)}) collective-permute-start(f32[5120]{0:T(1024)} %pad_maximum_fusion.4), channel_id=1, source_target_pairs={{2,0},{4,2},{6,4},{3,1},{5,3},{7,5},{10,8},{12,10},{14,12},{11,9},... | collective-permute-start | bytes 61448 | tf_op jit(solution)/shard_map/ppermute | solution.py:107
  17.1 53.4 %collective-permute-start.3 = (f32[5120]{0:T(1024)}, f32[5120]{0:T(1024)S(1)}, u32[]{:S(2)}, u32[]{:S(2)}) collective-permute-start(f32[5120]{0:T(1024)} %pad_maximum_fusion.5), channel_id=1, source_target_pairs={{0,2},{2,4},{4,6},{1,3},{3,5},{5,7},{8,10},{10,12},{12,14},{9,11},... | collective-permute-start | bytes 61448 | tf_op jit(solution)/shard_map/ppermute | solution.py:107
  23.4 47.7 %collective-permute-start.1 = (f32[12288]{0:T(1024)S(1)}, f32[12288]{0:T(1024)S(1)}, u32[]{:S(2)}, u32[]{:S(2)}) collective-permute-start(f32[12288]{0:T(1024)S(1)} %pad_maximum_fusion.3), channel_id=1, source_target_pairs={{0,8},{8,16},{16,24},{1,9},{9,17},{17,25},{2,10},{10,18},{18,26},{... | collective-permute-start | bytes 147464 | tf_op jit(solution)/shard_map/ppermute | solution.py:107
  27.9 43.3 %collective-permute-start = (f32[12288]{0:T(1024)}, f32[12288]{0:T(1024)S(1)}, u32[]{:S(2)}, u32[]{:S(2)}) collective-permute-start(f32[12288]{0:T(1024)} %pad_maximum_fusion.2), channel_id=1, source_target_pairs={{8,0},{16,8},{24,16},{9,1},{17,9},{25,17},{10,2},{18,10},{26,18},{... | collective-permute-start | bytes 147464 | tf_op jit(solution)/shard_map/ppermute | solution.py:107
  31.2 33.7 %collective-permute-start.4 = (f32[2304]{0:T(1024)}, f32[2304]{0:T(1024)}, u32[]{:S(2)}, u32[]{:S(2)}) collective-permute-start(f32[2304]{0:T(1024)} %maximum_select_fusion), channel_id=1, source_target_pairs={{0,1},{1,0},{2,3},{3,2},{4,5},{5,4},{6,7},{7,6},{8,9},{9,8},{10,11... | collective-permute-start | bytes 27656 | tf_op jit(solution)/shard_map/ppermute | solution.py:102
  41.7 16.9 %all-to-all-start = ((s32[32,1,24]{2,1,0:T(1,128)}), s32[32,1,24]{2,1,0:T(1,128)S(1)}, u32[]{:S(2)}, u32[]{:S(2)}) async-start(s32[32,1,24]{2,1,0:T(1,128)} %bitcast.116), calls=%async_computation | async-start | bytes 32768 | tf_op jit(solution)/shard_map/all_to_all | solution.py:299
  55.0 51.0 %copy-start.8 = (pred[8,32,128]{2,1,0:T(8,128)(4,1)}, pred[8,32,128]{2,1,0:T(8,128)(4,1)S(1)}, u32[]{:S(2)}) copy-start(pred[8,32,128]{2,1,0:T(8,128)(4,1)S(1)} %get-tuple-element.162) | copy-start | bytes 98308
  55.0 51.0 %copy-start.10 = (pred[8,32,128]{2,1,0:T(8,128)(4,1)}, pred[8,32,128]{2,1,0:T(8,128)(4,1)S(1)}, u32[]{:S(2)}) copy-start(pred[8,32,128]{2,1,0:T(8,128)(4,1)S(1)} %get-tuple-element.163) | copy-start | bytes 98308
  55.0 51.0 %copy-start.12 = (pred[8,32,128]{2,1,0:T(8,128)(4,1)}, pred[8,32,128]{2,1,0:T(8,128)(4,1)S(1)}, u32[]{:S(2)}) copy-start(pred[8,32,128]{2,1,0:T(8,128)(4,1)S(1)} %get-tuple-element.164) | copy-start | bytes 98308
  79.9 13.3 %collective-permute-start.9 = (f32[8,32]{1,0:T(8,128)S(1)}, f32[8,32]{1,0:T(8,128)S(1)}, u32[]{:S(2)}, u32[]{:S(2)}) collective-permute-start(f32[8,32]{1,0:T(8,128)S(1)} %fusion.10), channel_id=1, source_target_pairs={{0,1},{1,0},{2,3},{3,2},{4,5},{5,4},{6,7},{7,6},{8,9},{9,8},{10,11... | collective-permute-start | bytes 3080 | tf_op jit(solution)/shard_map/ppermute | solution.py:102
  80.2 16.4 %collective-permute-start.5 = (f32[32,128]{1,0:T(8,128)S(1)}, f32[32,128]{1,0:T(8,128)S(1)}, u32[]{:S(2)}, u32[]{:S(2)}) collective-permute-start(f32[32,128]{1,0:T(8,128)S(1)} %get-tuple-element.153), channel_id=1, source_target_pairs={{8,0},{16,8},{24,16},{9,1},{17,9},{25,17},{10,2},{18,10},{26,18},{... | collective-permute-start | bytes 49160 | tf_op jit(solution)/shard_map/ppermute | solution.py:107
  81.5 15.1 %collective-permute-start.6 = (f32[32,128]{1,0:T(8,128)S(1)}, f32[32,128]{1,0:T(8,128)S(1)}, u32[]{:S(2)}, u32[]{:S(2)}) collective-permute-start(f32[32,128]{1,0:T(8,128)S(1)} %get-tuple-element.152), channel_id=1, source_target_pairs={{0,8},{8,16},{16,24},{1,9},{9,17},{17,25},{2,10},{10,18},{18,26},{... | collective-permute-start | bytes 49160 | tf_op jit(solution)/shard_map/ppermute | solution.py:107
  86.0 10.5 %collective-permute-start.7 = (f32[8,128]{1,0:T(8,128)S(1)}, f32[8,128]{1,0:T(8,128)S(1)}, u32[]{:S(2)}, u32[]{:S(2)}) collective-permute-start(f32[8,128]{1,0:T(8,128)S(1)} %bitcast.358), channel_id=1, source_target_pairs={{2,0},{4,2},{6,4},{3,1},{5,3},{7,5},{10,8},{12,10},{14,12},{11,9},... | collective-permute-start | bytes 12296 | tf_op jit(solution)/shard_map/ppermute | solution.py:107
  87.3 9.2 %collective-permute-start.8 = (f32[8,128]{1,0:T(8,128)S(1)}, f32[8,128]{1,0:T(8,128)S(1)}, u32[]{:S(2)}, u32[]{:S(2)}) collective-permute-start(f32[8,128]{1,0:T(8,128)S(1)} %bitcast.357), channel_id=1, source_target_pairs={{0,2},{2,4},{4,6},{1,3},{3,5},{5,7},{8,10},{10,12},{12,14},{9,11},... | collective-permute-start | bytes 12296 | tf_op jit(solution)/shard_map/ppermute | solution.py:107
  106.6 13.9 %collective-permute-start.14 = (f32[8,32]{1,0:T(8,128)S(1)}, f32[8,32]{1,0:T(8,128)S(1)}, u32[]{:S(2)}, u32[]{:S(2)}) collective-permute-start(f32[8,32]{1,0:T(8,128)S(1)} %fusion.9), channel_id=1, source_target_pairs={{0,1},{1,0},{2,3},{3,2},{4,5},{5,4},{6,7},{7,6},{8,9},{9,8},{10,11... | collective-permute-start | bytes 3080 | tf_op jit(solution)/shard_map/ppermute | solution.py:102
  108.0 13.6 %collective-permute-start.10 = (f32[32,128]{1,0:T(8,128)S(1)}, f32[32,128]{1,0:T(8,128)S(1)}, u32[]{:S(2)}, u32[]{:S(2)}) collective-permute-start(f32[32,128]{1,0:T(8,128)S(1)} %get-tuple-element.137), channel_id=1, source_target_pairs={{8,0},{16,8},{24,16},{9,1},{17,9},{25,17},{10,2},{18,10},{26,18},{... | collective-permute-start | bytes 49160 | tf_op jit(solution)/shard_map/ppermute | solution.py:107
  109.3 12.3 %collective-permute-start.11 = (f32[32,128]{1,0:T(8,128)S(1)}, f32[32,128]{1,0:T(8,128)S(1)}, u32[]{:S(2)}, u32[]{:S(2)}) collective-permute-start(f32[32,128]{1,0:T(8,128)S(1)} %get-tuple-element.136), channel_id=1, source_target_pairs={{0,8},{8,16},{16,24},{1,9},{9,17},{17,25},{2,10},{10,18},{18,26},{... | collective-permute-start | bytes 49160 | tf_op jit(solution)/shard_map/ppermute | solution.py:107
  114.4 6.7 %collective-permute-start.12 = (f32[8,128]{1,0:T(8,128)S(1)}, f32[8,128]{1,0:T(8,128)S(1)}, u32[]{:S(2)}, u32[]{:S(2)}) collective-permute-start(f32[8,128]{1,0:T(8,128)S(1)} %bitcast.361), channel_id=1, source_target_pairs={{2,0},{4,2},{6,4},{3,1},{5,3},{7,5},{10,8},{12,10},{14,12},{11,9},... | collective-permute-start | bytes 12296 | tf_op jit(solution)/shard_map/ppermute | solution.py:107
  115.7 5.9 %collective-permute-start.13 = (f32[8,128]{1,0:T(8,128)S(1)}, f32[8,128]{1,0:T(8,128)S(1)}, u32[]{:S(2)}, u32[]{:S(2)}) collective-permute-start(f32[8,128]{1,0:T(8,128)S(1)} %bitcast.359), channel_id=1, source_target_pairs={{0,2},{2,4},{4,6},{1,3},{3,5},{5,7},{8,10},{10,12},{12,14},{9,11},... | collective-permute-start | bytes 12296 | tf_op jit(solution)/shard_map/ppermute | solution.py:107
  125.4 13.0 %collective-permute-start.19 = (f32[8,32]{1,0:T(8,128)S(1)}, f32[8,32]{1,0:T(8,128)S(1)}, u32[]{:S(2)}, u32[]{:S(2)}) collective-permute-start(f32[8,32]{1,0:T(8,128)S(1)} %fusion.8), channel_id=1, source_target_pairs={{0,1},{1,0},{2,3},{3,2},{4,5},{5,4},{6,7},{7,6},{8,9},{9,8},{10,11... | collective-permute-start | bytes 3080 | tf_op jit(solution)/shard_map/ppermute | solution.py:102
  125.5 14.2 %collective-permute-start.15 = (f32[32,128]{1,0:T(8,128)S(1)}, f32[32,128]{1,0:T(8,128)S(1)}, u32[]{:S(2)}, u32[]{:S(2)}) collective-permute-start(f32[32,128]{1,0:T(8,128)S(1)} %get-tuple-element.121), channel_id=1, source_target_pairs={{8,0},{16,8},{24,16},{9,1},{17,9},{25,17},{10,2},{18,10},{26,18},{... | collective-permute-start | bytes 49160 | tf_op jit(solution)/shard_map/ppermute | solution.py:107
  126.8 12.9 %collective-permute-start.16 = (f32[32,128]{1,0:T(8,128)S(1)}, f32[32,128]{1,0:T(8,128)S(1)}, u32[]{:S(2)}, u32[]{:S(2)}) collective-permute-start(f32[32,128]{1,0:T(8,128)S(1)} %get-tuple-element.120), channel_id=1, source_target_pairs={{0,8},{8,16},{16,24},{1,9},{9,17},{17,25},{2,10},{10,18},{18,26},{... | collective-permute-start | bytes 49160 | tf_op jit(solution)/shard_map/ppermute | solution.py:107
  132.2 6.4 %collective-permute-start.17 = (f32[8,128]{1,0:T(8,128)S(1)}, f32[8,128]{1,0:T(8,128)S(1)}, u32[]{:S(2)}, u32[]{:S(2)}) collective-permute-start(f32[8,128]{1,0:T(8,128)S(1)} %bitcast.362), channel_id=1, source_target_pairs={{2,0},{4,2},{6,4},{3,1},{5,3},{7,5},{10,8},{12,10},{14,12},{11,9},... | collective-permute-start | bytes 12296 | tf_op jit(solution)/shard_map/ppermute | solution.py:107
  133.5 6.1 %collective-permute-start.18 = (f32[8,128]{1,0:T(8,128)S(1)}, f32[8,128]{1,0:T(8,128)S(1)}, u32[]{:S(2)}, u32[]{:S(2)}) collective-permute-start(f32[8,128]{1,0:T(8,128)S(1)} %bitcast.360), channel_id=1, source_target_pairs={{0,2},{2,4},{4,6},{1,3},{3,5},{5,7},{8,10},{10,12},{12,14},{9,11},... | collective-permute-start | bytes 12296 | tf_op jit(solution)/shard_map/ppermute | solution.py:107
  149.8 46.2 %all-to-all-start.1 = ((f32[4,32,24,128]{3,0,2,1:T(4,128)}), f32[4,32,24,128]{3,0,2,1:T(4,128)S(1)}, u32[]{:S(2)}, u32[]{:S(2)}) async-start(f32[4,32,24,128]{3,0,2,1:T(4,128)} %select_select_fusion.1), calls=%async_computation.1 | async-start | bytes 3145728 | tf_op jit(solution)/shard_map/all_to_all | solution.py:329
  166.6 29.5 %copy-start.58 = (s32[2048]{0:T(1024)S(1)}, s32[2048]{0:T(1024)}, u32[]{:S(2)}) copy-start(s32[2048]{0:T(1024)} %fusion.84) | copy-start | bytes 24580
  231.6 7.6 %collective-permute-start.24 = (f32[4,32,64]{2,1,0:T(8,128)S(1)}, f32[4,32,64]{2,1,0:T(8,128)S(1)}, u32[]{:S(2)}, u32[]{:S(2)}) collective-permute-start(f32[4,32,64]{2,1,0:T(8,128)S(1)} %broadcast_select_fusion.8), channel_id=1, source_target_pairs={{0,1},{1,0},{2,3},{3,2},{4,5},{5,4},{6,7},{7,6},{8,9},{9,8},{10,11... | collective-permute-start | bytes 98312 | tf_op jit(solution)/shard_map/ppermute | solution.py:102
  232.5 11.5 %collective-permute-start.20 = (f32[4,64,128]{2,1,0:T(8,128)}, f32[4,64,128]{2,1,0:T(8,128)S(1)}, u32[]{:S(2)}, u32[]{:S(2)}) collective-permute-start(f32[4,64,128]{2,1,0:T(8,128)} %get-tuple-element.33), channel_id=1, source_target_pairs={{0,8},{8,16},{16,24},{1,9},{9,17},{17,25},{2,10},{10,18},{18,26},{... | collective-permute-start | bytes 393224 | tf_op jit(solution)/shard_map/ppermute | solution.py:107
  235.2 8.8 %collective-permute-start.21 = (f32[4,64,128]{2,1,0:T(8,128)}, f32[4,64,128]{2,1,0:T(8,128)S(1)}, u32[]{:S(2)}, u32[]{:S(2)}) collective-permute-start(f32[4,64,128]{2,1,0:T(8,128)} %get-tuple-element.34), channel_id=1, source_target_pairs={{8,0},{16,8},{24,16},{9,1},{17,9},{25,17},{10,2},{18,10},{26,18},{... | collective-permute-start | bytes 393224 | tf_op jit(solution)/shard_map/ppermute | solution.py:107
  236.5 3.5 collective-permute-start.22
  237.8 6.2 %collective-permute-start.23 = (f32[4,32,1,128]{3,2,1,0:T(1,128)S(1)}, f32[4,32,1,128]{3,2,1,0:T(1,128)S(1)}, u32[]{:S(2)}, u32[]{:S(2)}) collective-permute-start(f32[4,32,1,128]{3,2,1,0:T(1,128)S(1)} %copy-done.96), channel_id=1, source_target_pairs={{2,0},{4,2},{6,4},{3,1},{5,3},{7,5},{10,8},{12,10},{14,12},{11,9},... | collective-permute-start | bytes 196616 | tf_op jit(solution)/shard_map/ppermute | solution.py:107
  244.7 25.5 %copy-start.23 = (f32[1,8,32,127]{3,2,1,0:T(8,128)S(1)}, f32[1,8,32,127]{3,2,1,0:T(8,128)}, u32[]{:S(2)}) copy-start(f32[1,8,32,127]{3,2,1,0:T(8,128)} %get-tuple-element.115) | copy-start | bytes 390148
  244.7 25.5 %copy-start.43 = (f32[32,128]{1,0:T(8,128)S(1)}, f32[32,128]{1,0:T(8,128)}, u32[]{:S(2)}) copy-start(f32[32,128]{1,0:T(8,128)} %copy-done.42) | copy-start | bytes 49156
  244.7 25.5 %copy-start.45 = (f32[32,128]{1,0:T(8,128)S(1)}, f32[32,128]{1,0:T(8,128)}, u32[]{:S(2)}) copy-start(f32[32,128]{1,0:T(8,128)} %copy-done.44) | copy-start | bytes 49156
  244.7 25.5 %copy-start.65 = (f32[8,128]{1,0:T(8,128)S(1)}, f32[8,128]{1,0:T(8,128)}, u32[]{:S(2)}) copy-start(f32[8,128]{1,0:T(8,128)} %copy-done.64) | copy-start | bytes 12292
  244.7 25.5 %copy-start.67 = (f32[8,128]{1,0:T(8,128)S(1)}, f32[8,128]{1,0:T(8,128)}, u32[]{:S(2)}) copy-start(f32[8,128]{1,0:T(8,128)} %copy-done.66) | copy-start | bytes 12292
  270.1 11.2 %collective-permute-start.29 = (f32[4,32,64]{2,1,0:T(8,128)S(1)}, f32[4,32,64]{2,1,0:T(8,128)S(1)}, u32[]{:S(2)}, u32[]{:S(2)}) collective-permute-start(f32[4,32,64]{2,1,0:T(8,128)S(1)} %broadcast_select_fusion.7), channel_id=1, source_target_pairs={{0,1},{1,0},{2,3},{3,2},{4,5},{5,4},{6,7},{7,6},{8,9},{9,8},{10,11... | collective-permute-start | bytes 98312 | tf_op jit(solution)/shard_map/ppermute | solution.py:102
  271.4 15.0 %collective-permute-start.25 = (f32[4,64,128]{2,1,0:T(8,128)}, f32[4,64,128]{2,1,0:T(8,128)S(1)}, u32[]{:S(2)}, u32[]{:S(2)}) collective-permute-start(f32[4,64,128]{2,1,0:T(8,128)} %get-tuple-element.42), channel_id=1, source_target_pairs={{0,8},{8,16},{16,24},{1,9},{9,17},{17,25},{2,10},{10,18},{18,26},{... | collective-permute-start | bytes 393224 | tf_op jit(solution)/shard_map/ppermute | solution.py:107
  276.0 10.4 %collective-permute-start.26 = (f32[4,64,128]{2,1,0:T(8,128)}, f32[4,64,128]{2,1,0:T(8,128)S(1)}, u32[]{:S(2)}, u32[]{:S(2)}) collective-permute-start(f32[4,64,128]{2,1,0:T(8,128)} %get-tuple-element.43), channel_id=1, source_target_pairs={{8,0},{16,8},{24,16},{9,1},{17,9},{25,17},{10,2},{18,10},{26,18},{... | collective-permute-start | bytes 393224 | tf_op jit(solution)/shard_map/ppermute | solution.py:107
  277.3 4.9 %collective-permute-start.27 = (f32[4,32,1,128]{3,2,1,0:T(1,128)}, f32[4,32,1,128]{3,2,1,0:T(1,128)S(1)}, u32[]{:S(2)}, u32[]{:S(2)}) collective-permute-start(f32[4,32,1,128]{3,2,1,0:T(1,128)} %get-tuple-element.44), channel_id=1, source_target_pairs={{0,2},{2,4},{4,6},{1,3},{3,5},{5,7},{8,10},{10,12},{12,14},{9,11},... | collective-permute-start | bytes 196616 | tf_op jit(solution)/shard_map/ppermute | solution.py:107
  280.0 6.4 %collective-permute-start.28 = (f32[4,32,1,128]{3,2,1,0:T(1,128)}, f32[4,32,1,128]{3,2,1,0:T(1,128)S(1)}, u32[]{:S(2)}, u32[]{:S(2)}) collective-permute-start(f32[4,32,1,128]{3,2,1,0:T(1,128)} %get-tuple-element.45), channel_id=1, source_target_pairs={{2,0},{4,2},{6,4},{3,1},{5,3},{7,5},{10,8},{12,10},{14,12},{11,9},... | collective-permute-start | bytes 196616 | tf_op jit(solution)/shard_map/ppermute | solution.py:107
  312.4 12.9 %collective-permute-start.34 = (f32[4,32,64]{2,1,0:T(8,128)S(1)}, f32[4,32,64]{2,1,0:T(8,128)S(1)}, u32[]{:S(2)}, u32[]{:S(2)}) collective-permute-start(f32[4,32,64]{2,1,0:T(8,128)S(1)} %broadcast_select_fusion.6), channel_id=1, source_target_pairs={{0,1},{1,0},{2,3},{3,2},{4,5},{5,4},{6,7},{7,6},{8,9},{9,8},{10,11... | collective-permute-start | bytes 98312 | tf_op jit(solution)/shard_map/ppermute | solution.py:102
  314.3 15.9 %collective-permute-start.30 = (f32[4,64,128]{2,1,0:T(8,128)S(1)}, f32[4,64,128]{2,1,0:T(8,128)S(1)}, u32[]{:S(2)}, u32[]{:S(2)}) collective-permute-start(f32[4,64,128]{2,1,0:T(8,128)S(1)} %copy-done.93), channel_id=1, source_target_pairs={{0,8},{8,16},{16,24},{1,9},{9,17},{17,25},{2,10},{10,18},{18,26},{... | collective-permute-start | bytes 393224 | tf_op jit(solution)/shard_map/ppermute | solution.py:107
  319.2 11.0 %collective-permute-start.31 = (f32[4,64,128]{2,1,0:T(8,128)S(1)}, f32[4,64,128]{2,1,0:T(8,128)S(1)}, u32[]{:S(2)}, u32[]{:S(2)}) collective-permute-start(f32[4,64,128]{2,1,0:T(8,128)S(1)} %copy-done.92), channel_id=1, source_target_pairs={{8,0},{16,8},{24,16},{9,1},{17,9},{25,17},{10,2},{18,10},{26,18},{... | collective-permute-start | bytes 393224 | tf_op jit(solution)/shard_map/ppermute | solution.py:107
  320.5 5.5 %collective-permute-start.32 = (f32[4,32,1,128]{3,2,1,0:T(1,128)S(1)}, f32[4,32,1,128]{3,2,1,0:T(1,128)S(1)}, u32[]{:S(2)}, u32[]{:S(2)}) collective-permute-start(f32[4,32,1,128]{3,2,1,0:T(1,128)S(1)} %copy-done.95), channel_id=1, source_target_pairs={{0,2},{2,4},{4,6},{1,3},{3,5},{5,7},{8,10},{10,12},{12,14},{9,11},... | collective-permute-start | bytes 196616 | tf_op jit(solution)/shard_map/ppermute | solution.py:107
  324.0 6.2 %collective-permute-start.33 = (f32[4,32,1,128]{3,2,1,0:T(1,128)S(1)}, f32[4,32,1,128]{3,2,1,0:T(1,128)S(1)}, u32[]{:S(2)}, u32[]{:S(2)}) collective-permute-start(f32[4,32,1,128]{3,2,1,0:T(1,128)S(1)} %copy-done.94), channel_id=1, source_target_pairs={{2,0},{4,2},{6,4},{3,1},{5,3},{7,5},{10,8},{12,10},{14,12},{11,9},... | collective-permute-start | bytes 196616 | tf_op jit(solution)/shard_map/ppermute | solution.py:107
  (89 other events, 511.5 us)

commit v10 on v9

--- a/solution.py
+++ b/solution.py
@@ -138,8 +138,8 @@
 
     yf_lo[0, x] = value[0:1, :]
     yf_hi[0, x] = value[ny - 1:ny, :]
-    columns = jnp.where(lane == x, jnp.broadcast_to(value[:, 0:1], (ny, nz)), columns)
-    columns = jnp.where(lane == half + x, jnp.broadcast_to(value[:, nz - 1:nz], (ny, nz)), columns)
+    columns = jnp.where(lane == x, pltpu.roll(value, x, 1), columns)
+    columns = jnp.where(lane == half + x, pltpu.roll(value, lax.rem(half + x + 1, nz), 1), columns)
     return columns
 
 

time: 363 us -> 361 us (level)
  no operation moved by 1% of the time
where the time goes in v10:
time: 361 us; the launch traced here: 357 us
  starting transfers between devices  90.5 us (25%)
  Pallas kernels  88.6 us (25%)
  other arithmetic  72.7 us (20%)
  local copies, waits for them, and re-layouts  65.8 us (18%)
  waiting for transfers between devices  36.2 us (10%)
    pallas_call x3, Pallas kernels, run_sweep(): pl.pallas_call(functools.partial(sweep_kernel, final), grid=(steps,), in_...  74.6 us
    ppermute x14, starting transfers between devices, exchange(): lax.ppermute(top, axis, forward)  58.4 us
    all_to_all x1, waiting for transfers between devices, local(): lax.all_to_all(send_values.reshape(STEPS, devices, capacity, row_len), ('...  21.9 us
    ppermute x14, starting transfers between devices, exchange(): lax.ppermute(bottom, axis, backward)  18.1 us
    gather x2, local copies, waits for them, and re-layouts, local(): jnp.take(received, row_slot, axis=1)  17.7 us
    add x4, other arithmetic, membrane(): steady + (gate_state - steady) * jnp.exp(-DT_HEART / time_const)  16.1 us
    pallas_call x1, Pallas kernels, run_initial(): pl.pallas_call(functools.partial(initial_kernel, mid), grid=(source.shape...  14 us
    ppermute x14, waiting for transfers between devices, exchange(): lax.ppermute(bottom, axis, backward)  12.3 us
  transfers between devices with their start and end apart: 37, of which 8 were waited for; matrix products, arithmetic and copies ran while one was open for 18% of the time, Pallas kernels for 0%

profile of v10, /device:TPU:0, one launch (start us, length us, event | category | flops | bytes accessed | tf_op | source)
XLA Modules:
  0.0 356.8 jit_solution(12317218652180232768)
XLA Ops:
  0.6 1.8 fusion.118
  2.4 4.5 %select_add_fusion.1 = (f32[32,64,128]{2,1,0:T(8,128)S(1)}, pred[32,64,128]{2,1,0:T(8,128)(4,1)S(1)}, pred[32,64,128]{2,1,0:T(8,128)(4,1)S(1)}, pred[32,64,128]{2,1,0:T(8,128)(4,1)S(1)}, pred[32,64,128]{2,1,0:T(8,128)(4,1)S(1)}) fusion(f32[]{:T(128)} %bitcast.29, f32[]{:T(128)} %bitcast.28, f32[]{:T(128)} %bitcast.27, f32[]{:T(128)} %bitcast.26, ...), kind=kLoop, calls=%fused_computation.33 | loop fusion | flops 2883584 | bytes 3145744 | tf_op jit(solution)/shard_map/add | solution.py:310
  6.9 5.9 %select_add_fusion.2 = (f32[32,64,128]{2,1,0:T(8,128)S(1)}, f32[32,64,128]{2,1,0:T(8,128)S(1)}) fusion(pred[32,64,128]{2,1,0:T(8,128)(4,1)S(1)} %get-tuple-element.85, pred[32,64,128]{2,1,0:T(8,128)(4,1)S(1)} %get-tuple-element.84, pred[32,64,128]{2,1,0:T(8,128)(4,1)S(1)} %get-tuple-element.83, pred[32,64,128]{2,1,0:T(8,128)(4,1)S(1)} %get-tuple-element.82, ...), kind=kLoop, calls=%fused_computation.34 | loop fusion | flops 3670016 | bytes 3145760 | tf_op jit(solution)/shard_map/add | solution.py:310
  12.9 1.8 fusion.98
  17.1 5.5 %collective-permute-start.3 = (f32[5120]{0:T(1024)}, f32[5120]{0:T(1024)S(1)}, u32[]{:S(2)}, u32[]{:S(2)}) collective-permute-start(f32[5120]{0:T(1024)} %pad_maximum_fusion.5), channel_id=1, source_target_pairs={{0,2},{2,4},{4,6},{1,3},{3,5},{5,7},{8,10},{10,12},{12,14},{9,11},... | collective-permute-start | bytes 61448 | tf_op jit(solution)/shard_map/ppermute | solution.py:107
  23.4 3.8 %collective-permute-start.1 = (f32[12288]{0:T(1024)S(1)}, f32[12288]{0:T(1024)S(1)}, u32[]{:S(2)}, u32[]{:S(2)}) collective-permute-start(f32[12288]{0:T(1024)S(1)} %pad_maximum_fusion.3), channel_id=1, source_target_pairs={{0,8},{8,16},{16,24},{1,9},{9,17},{17,25},{2,10},{10,18},{18,26},{... | collective-permute-start | bytes 147464 | tf_op jit(solution)/shard_map/ppermute | solution.py:107
  34.6 1.3 reduce.66
  36.0 5.0 %gather_fusion = s32[768]{0:T(1024)S(1)} fusion(s32[256]{0:T(256)S(1)} %reshape.1868, s32[1024]{0:T(1024)S(1)} %pad_clamp_fusion), kind=kCustom, calls=%fused_computation | custom fusion | bytes 9216 | tf_op jit(solution)/shard_map/gather | solution.py:298
  41.7 6.1 %all-to-all-start = ((s32[32,1,24]{2,1,0:T(1,128)}), s32[32,1,24]{2,1,0:T(1,128)S(1)}, u32[]{:S(2)}, u32[]{:S(2)}) async-start(s32[32,1,24]{2,1,0:T(1,128)} %bitcast.116), calls=%async_computation | async-start | bytes 32768 | tf_op jit(solution)/shard_map/all_to_all | solution.py:299
  47.8 1.5 fusion.100
  49.3 1.6 fusion.101
  50.9 1.7 fusion.99
  55.1 1.5 multiply_add_fusion.3
  59.4 2.8 iota_reduce_fusion
  66.5 1.8 slice.567
  68.3 1.9 slice.568
  75.0 1.4 fusion.18
  76.5 2.8 multiply_add_fusion.2
  81.5 4.5 %collective-permute-start.6 = (f32[32,128]{1,0:T(8,128)S(1)}, f32[32,128]{1,0:T(8,128)S(1)}, u32[]{:S(2)}, u32[]{:S(2)}) collective-permute-start(f32[32,128]{1,0:T(8,128)S(1)} %get-tuple-element.152), channel_id=1, source_target_pairs={{0,8},{8,16},{16,24},{1,9},{9,17},{17,25},{2,10},{10,18},{18,26},{... | collective-permute-start | bytes 49160 | tf_op jit(solution)/shard_map/ppermute | solution.py:107
  87.3 4.5 %collective-permute-start.8 = (f32[8,128]{1,0:T(8,128)S(1)}, f32[8,128]{1,0:T(8,128)S(1)}, u32[]{:S(2)}, u32[]{:S(2)}) collective-permute-start(f32[8,128]{1,0:T(8,128)S(1)} %bitcast.357), channel_id=1, source_target_pairs={{0,2},{2,4},{4,6},{1,3},{3,5},{5,7},{8,10},{10,12},{12,14},{9,11},... | collective-permute-start | bytes 12296 | tf_op jit(solution)/shard_map/ppermute | solution.py:107
  100.4 1.4 fusion.33
  101.9 4.2 %multiply_add_fusion.1 = f32[18,8,32,128]{3,2,1,0:T(8,128)S(1)} fusion(f32[8,32,128]{2,1,0:T(8,128)S(1)} %bitcast.299, f32[18]{0:T(128)S(1)} %copy-done.84, f32[18]{0:T(128)S(1)} %copy-done.87, f32[18]{0:T(128)S(1)} %copy-done.90, f32[8,32,128]{2,1,0:T(8,128)S(1)} %bitcast.291, f32[19,8,32,128]{3,2,1,0:T(8,128)S(1)} %copy-done.4, ...), kind=kLoop, calls=%fused_computation.9 | loop fusion | flops 19464192 | bytes 5112024 | tf_op jit(solution)/shard_map/add | solution.py:59
  109.3 5.1 %collective-permute-start.11 = (f32[32,128]{1,0:T(8,128)S(1)}, f32[32,128]{1,0:T(8,128)S(1)}, u32[]{:S(2)}, u32[]{:S(2)}) collective-permute-start(f32[32,128]{1,0:T(8,128)S(1)} %get-tuple-element.136), channel_id=1, source_target_pairs={{0,8},{8,16},{16,24},{1,9},{9,17},{17,25},{2,10},{10,18},{18,26},{... | collective-permute-start | bytes 49160 | tf_op jit(solution)/shard_map/ppermute | solution.py:107
  115.7 4.8 %collective-permute-start.13 = (f32[8,128]{1,0:T(8,128)S(1)}, f32[8,128]{1,0:T(8,128)S(1)}, u32[]{:S(2)}, u32[]{:S(2)}) collective-permute-start(f32[8,128]{1,0:T(8,128)S(1)} %bitcast.359), channel_id=1, source_target_pairs={{0,2},{2,4},{4,6},{1,3},{3,5},{5,7},{8,10},{10,12},{12,14},{9,11},... | collective-permute-start | bytes 12296 | tf_op jit(solution)/shard_map/ppermute | solution.py:107
  126.8 5.4 %collective-permute-start.16 = (f32[32,128]{1,0:T(8,128)S(1)}, f32[32,128]{1,0:T(8,128)S(1)}, u32[]{:S(2)}, u32[]{:S(2)}) collective-permute-start(f32[32,128]{1,0:T(8,128)S(1)} %get-tuple-element.120), channel_id=1, source_target_pairs={{0,8},{8,16},{16,24},{1,9},{9,17},{17,25},{2,10},{10,18},{18,26},{... | collective-permute-start | bytes 49160 | tf_op jit(solution)/shard_map/ppermute | solution.py:107
  133.5 4.8 %collective-permute-start.18 = (f32[8,128]{1,0:T(8,128)S(1)}, f32[8,128]{1,0:T(8,128)S(1)}, u32[]{:S(2)}, u32[]{:S(2)}) collective-permute-start(f32[8,128]{1,0:T(8,128)S(1)} %bitcast.360), channel_id=1, source_target_pairs={{0,2},{2,4},{4,6},{1,3},{3,5},{5,7},{8,10},{10,12},{12,14},{9,11},... | collective-permute-start | bytes 12296 | tf_op jit(solution)/shard_map/ppermute | solution.py:107
  141.9 3.0 gather_fusion.1
  144.8 4.9 %select_select_fusion.1 = f32[4,32,24,128]{3,0,2,1:T(4,128)} fusion(f32[4,32,24,128]{3,0,2,1:T(4,128)S(1)} %bitcast.285, pred[32,24]{1,0:T(8,128)(4,1)} %broadcast_in_dim.362, pred[32,24]{1,0:T(8,128)(4,1)} %broadcast_in_dim.360), kind=kLoop, calls=%fused_computation.12 | loop fusion | flops 786432 | bytes 3147264 | tf_op jit(solution)/shard_map/jit(_where)/select_n | solution.py:328
  149.8 7.4 %all-to-all-start.1 = ((f32[4,32,24,128]{3,0,2,1:T(4,128)}), f32[4,32,24,128]{3,0,2,1:T(4,128)S(1)}, u32[]{:S(2)}, u32[]{:S(2)}) async-start(f32[4,32,24,128]{3,0,2,1:T(4,128)} %select_select_fusion.1), calls=%async_computation.1 | async-start | bytes 3145728 | tf_op jit(solution)/shard_map/all_to_all | solution.py:329
  157.2 7.1 %broadcast_divide_fusion = (f32[32,64,128]{2,1,0:T(8,128)}, f32[32,64,128]{2,1,0:T(8,128)}, f32[32,64,128]{2,1,0:T(8,128)}, f32[32,64,128]{2,1,0:T(8,128)}, f32[...) fusion(f32[32,64,128]{2,1,0:T(8,128)} %copy-done.1, ...), kind=kLoop, calls=%fused_computation.40 | loop fusion | flops 6553600 | bytes 17825792 | tf_op jit(solution)/shard_map/div | solution.py:349
  166.6 7.5 %multiply_add_fusion = f32[18,8,32,128]{3,2,1,0:T(8,128)} fusion(f32[8,32,128]{2,1,0:T(8,128)S(1)} %bitcast.302, f32[18]{0:T(128)} %param.18, f32[18]{0:T(128)} %param.16, f32[18]{0:T(128)} %copy-done.88, f32[8,32,128]{2,1,0:T(8,128)S(1)} %bitcast.301, f32[8,32,128]{2,1,0:T(8,128)S(1)} %bitcast.292, f32[19,8,32,128]{3,2,1,0:T(8,128)} %param.14, ...), kind=kLoop, calls=%fused_computation.8 | loop fusion | flops 25952256 | bytes 5243096 | tf_op jit(solution)/shard_map/add | solution.py:59
  174.1 21.9 %all-to-all-done.1 = f32[4,32,24,128]{3,0,2,1:T(4,128)S(1)} async-done(((f32[4,32,24,128]{3,0,2,1:T(4,128)}), f32[4,32,24,128]{3,0,2,1:T(4,128)S(1)}, u32[]{:S(2)}, u32[]{:S(2)}) %all-to-all-start.1) | async-done | bytes 1572896 | tf_op jit(solution)/shard_map/all_to_all | solution.py:329
  196.0 15.2 %gather_fusion.2 = f32[2048,4,128]{2,1,0:T(4,128)} fusion(f32[4,768,128]{2,0,1:T(4,128)S(1)} %bitcast.282, s32[2048]{0:T(1024)S(1)} %copy-done.58), kind=kCustom, calls=%fused_computation.2 | custom fusion | bytes 8396800 | tf_op jit(solution)/shard_map/jit(_take)/gather | solution.py:336
  211.3 2.5 copy.1555
  213.8 2.8 select_select_fusion.r_ref
  216.6 14.0 %chebyshev_start.1 = (f32[4,32,64,128]{3,2,1,0:T(8,128)}, f32[4,64,128]{2,1,0:T(8,128)}, f32[4,64,128]{2,1,0:T(8,128)}, f32[4,32,1,128]{3,2,1,0:T(1,128)}, f32[4...) custom-call(f32[4,32,64,128]{3,2,1,0:T(8,128)} %select_select_fusion.r_ref, ...), custom_call_target="tpu_custom_call" | custom-call | flops 2097152 | bytes 9437184 | tf_op jit(solution)/shard_map/chebyshev_start/pallas_call | solution.py:231
  232.4 2.7 collective-permute-start.20
  239.9 4.0 %collective-permute-done.23.yhi = f32[4,32,1,128]{3,2,1,0:T(1,128)S(1)} collective-permute-done((f32[4,32,1,128]{3,2,1,0:T(1,128)S(1)}, f32[4,32,1,128]{3,2,1,0:T(1,128)S(1)}, u32[]{:S(2)}, u32[]{:S(2)}) %collective-permute-start.23) | collective-permute-done | bytes 65568 | tf_op jit(solution)/shard_map/ppermute | solution.py:107
  244.7 23.9 %chebyshev_sweep.3 = (f32[4,32,64,128]{3,2,1,0:T(8,128)}, f32[4,32,64,128]{3,2,1,0:T(8,128)}, f32[4,32,64,128]{3,2,1,0:T(8,128)}, f32[4,64,128]{2,1,0:T(8,128)},...) custom-call(f32[2]{0:T(128)} %constant.119.clone.coef_ref, ...), custom_call_target="tpu_custom_call" | custom-call | flops 31457280 | bytes 36700160 | tf_op jit(solution)/shard_map/chebyshev_sweep/pallas_call | solution.py:254
  270.8 4.6 %collective-permute-start.25 = (f32[4,64,128]{2,1,0:T(8,128)}, f32[4,64,128]{2,1,0:T(8,128)S(1)}, u32[]{:S(2)}, u32[]{:S(2)}) collective-permute-start(f32[4,64,128]{2,1,0:T(8,128)} %get-tuple-element.42), channel_id=1, source_target_pairs={{0,8},{8,16},{16,24},{1,9},{9,17},{17,25},{2,10},{10,18},{18,26},{... | collective-permute-start | bytes 393224 | tf_op jit(solution)/shard_map/ppermute | solution.py:107
  276.6 2.7 collective-permute-start.27
  281.6 4.2 %collective-permute-done.28.yhi = f32[4,32,1,128]{3,2,1,0:T(1,128)S(1)} collective-permute-done((f32[4,32,1,128]{3,2,1,0:T(1,128)}, f32[4,32,1,128]{3,2,1,0:T(1,128)S(1)}, u32[]{:S(2)}, u32[]{:S(2)}) %collective-permute-start.28) | collective-permute-done | bytes 65568 | tf_op jit(solution)/shard_map/ppermute | solution.py:107
  286.5 23.8 %chebyshev_sweep.4 = (f32[4,32,64,128]{3,2,1,0:T(8,128)}, f32[4,32,64,128]{3,2,1,0:T(8,128)}, f32[4,32,64,128]{3,2,1,0:T(8,128)}, f32[4,64,128]{2,1,0:T(8,128)},...) custom-call(f32[2]{0:T(128)} %constant.120.clone.coef_ref, ...), custom_call_target="tpu_custom_call" | custom-call | flops 31457280 | bytes 36700160 | tf_op jit(solution)/shard_map/chebyshev_sweep/pallas_call | solution.py:254
  311.3 1.8 pad_maximum_fusion
  313.1 4.9 %collective-permute-start.30 = (f32[4,64,128]{2,1,0:T(8,128)S(1)}, f32[4,64,128]{2,1,0:T(8,128)S(1)}, u32[]{:S(2)}, u32[]{:S(2)}) collective-permute-start(f32[4,64,128]{2,1,0:T(8,128)S(1)} %copy-done.93), channel_id=1, source_target_pairs={{0,8},{8,16},{16,24},{1,9},{9,17},{17,25},{2,10},{10,18},{18,26},{... | collective-permute-start | bytes 393224 | tf_op jit(solution)/shard_map/ppermute | solution.py:107
  319.3 3.5 collective-permute-start.32
  324.8 4.2 %collective-permute-done.33.yhi = f32[4,32,1,128]{3,2,1,0:T(1,128)S(1)} collective-permute-done((f32[4,32,1,128]{3,2,1,0:T(1,128)S(1)}, f32[4,32,1,128]{3,2,1,0:T(1,128)S(1)}, u32[]{:S(2)}, u32[]{:S(2)}) %collective-permute-start.33) | collective-permute-done | bytes 65568 | tf_op jit(solution)/shard_map/ppermute | solution.py:107
  329.7 26.8 %chebyshev_sweep.5 = (f32[4,32,64,128]{3,2,1,0:T(8,128)}, f32[4,32,64,128]{3,2,1,0:T(8,128)}, f32[32,64,4,128]{3,2,1,0:T(4,128)}, f32[4,64,128]{2,1,0:T(8,128)},...) custom-call(f32[2]{0:T(128)} %constant.121.clone.coef_ref, ...), custom_call_target="tpu_custom_call" | custom-call | flops 31457280 | bytes 36700160 | tf_op jit(solution)/shard_map/chebyshev_sweep/pallas_call | solution.py:254
  (378 shorter events, 73.0 us)
Async XLA Ops:
  12.8 35.0 %copy-start = (f32[32,64,128]{2,1,0:T(8,128)}, f32[32,64,128]{2,1,0:T(8,128)S(1)}, u32[]{:S(2)}) copy-start(f32[32,64,128]{2,1,0:T(8,128)S(1)} %get-tuple-element.102) | copy-start | bytes 3145732
  12.8 36.5 %copy-start.1 = (f32[32,64,128]{2,1,0:T(8,128)}, f32[32,64,128]{2,1,0:T(8,128)S(1)}, u32[]{:S(2)}) copy-start(f32[32,64,128]{2,1,0:T(8,128)S(1)} %get-tuple-element.103) | copy-start | bytes 3145732
  15.2 55.3 %collective-permute-start.2 = (f32[5120]{0:T(1024)}, f32[5120]{0:T(1024)S(1)}, u32[]{:S(2)}, u32[]{:S(2)}) collective-permute-start(f32[5120]{0:T(1024)} %pad_maximum_fusion.4), channel_id=1, source_target_pairs={{2,0},{4,2},{6,4},{3,1},{5,3},{7,5},{10,8},{12,10},{14,12},{11,9},... | collective-permute-start | bytes 61448 | tf_op jit(solution)/shard_map/ppermute | solution.py:107
  17.1 53.4 %collective-permute-start.3 = (f32[5120]{0:T(1024)}, f32[5120]{0:T(1024)S(1)}, u32[]{:S(2)}, u32[]{:S(2)}) collective-permute-start(f32[5120]{0:T(1024)} %pad_maximum_fusion.5), channel_id=1, source_target_pairs={{0,2},{2,4},{4,6},{1,3},{3,5},{5,7},{8,10},{10,12},{12,14},{9,11},... | collective-permute-start | bytes 61448 | tf_op jit(solution)/shard_map/ppermute | solution.py:107
  23.4 47.7 %collective-permute-start.1 = (f32[12288]{0:T(1024)S(1)}, f32[12288]{0:T(1024)S(1)}, u32[]{:S(2)}, u32[]{:S(2)}) collective-permute-start(f32[12288]{0:T(1024)S(1)} %pad_maximum_fusion.3), channel_id=1, source_target_pairs={{0,8},{8,16},{16,24},{1,9},{9,17},{17,25},{2,10},{10,18},{18,26},{... | collective-permute-start | bytes 147464 | tf_op jit(solution)/shard_map/ppermute | solution.py:107
  27.9 43.3 %collective-permute-start = (f32[12288]{0:T(1024)}, f32[12288]{0:T(1024)S(1)}, u32[]{:S(2)}, u32[]{:S(2)}) collective-permute-start(f32[12288]{0:T(1024)} %pad_maximum_fusion.2), channel_id=1, source_target_pairs={{8,0},{16,8},{24,16},{9,1},{17,9},{25,17},{10,2},{18,10},{26,18},{... | collective-permute-start | bytes 147464 | tf_op jit(solution)/shard_map/ppermute | solution.py:107
  31.2 33.7 %collective-permute-start.4 = (f32[2304]{0:T(1024)}, f32[2304]{0:T(1024)}, u32[]{:S(2)}, u32[]{:S(2)}) collective-permute-start(f32[2304]{0:T(1024)} %maximum_select_fusion), channel_id=1, source_target_pairs={{0,1},{1,0},{2,3},{3,2},{4,5},{5,4},{6,7},{7,6},{8,9},{9,8},{10,11... | collective-permute-start | bytes 27656 | tf_op jit(solution)/shard_map/ppermute | solution.py:102
  41.7 16.9 %all-to-all-start = ((s32[32,1,24]{2,1,0:T(1,128)}), s32[32,1,24]{2,1,0:T(1,128)S(1)}, u32[]{:S(2)}, u32[]{:S(2)}) async-start(s32[32,1,24]{2,1,0:T(1,128)} %bitcast.116), calls=%async_computation | async-start | bytes 32768 | tf_op jit(solution)/shard_map/all_to_all | solution.py:299
  55.0 51.0 %copy-start.8 = (pred[8,32,128]{2,1,0:T(8,128)(4,1)}, pred[8,32,128]{2,1,0:T(8,128)(4,1)S(1)}, u32[]{:S(2)}) copy-start(pred[8,32,128]{2,1,0:T(8,128)(4,1)S(1)} %get-tuple-element.162) | copy-start | bytes 98308
  55.0 51.0 %copy-start.10 = (pred[8,32,128]{2,1,0:T(8,128)(4,1)}, pred[8,32,128]{2,1,0:T(8,128)(4,1)S(1)}, u32[]{:S(2)}) copy-start(pred[8,32,128]{2,1,0:T(8,128)(4,1)S(1)} %get-tuple-element.163) | copy-start | bytes 98308
  55.0 51.0 %copy-start.12 = (pred[8,32,128]{2,1,0:T(8,128)(4,1)}, pred[8,32,128]{2,1,0:T(8,128)(4,1)S(1)}, u32[]{:S(2)}) copy-start(pred[8,32,128]{2,1,0:T(8,128)(4,1)S(1)} %get-tuple-element.164) | copy-start | bytes 98308
  79.9 13.3 %collective-permute-start.9 = (f32[8,32]{1,0:T(8,128)S(1)}, f32[8,32]{1,0:T(8,128)S(1)}, u32[]{:S(2)}, u32[]{:S(2)}) collective-permute-start(f32[8,32]{1,0:T(8,128)S(1)} %fusion.10), channel_id=1, source_target_pairs={{0,1},{1,0},{2,3},{3,2},{4,5},{5,4},{6,7},{7,6},{8,9},{9,8},{10,11... | collective-permute-start | bytes 3080 | tf_op jit(solution)/shard_map/ppermute | solution.py:102
  80.2 16.4 %collective-permute-start.5 = (f32[32,128]{1,0:T(8,128)S(1)}, f32[32,128]{1,0:T(8,128)S(1)}, u32[]{:S(2)}, u32[]{:S(2)}) collective-permute-start(f32[32,128]{1,0:T(8,128)S(1)} %get-tuple-element.153), channel_id=1, source_target_pairs={{8,0},{16,8},{24,16},{9,1},{17,9},{25,17},{10,2},{18,10},{26,18},{... | collective-permute-start | bytes 49160 | tf_op jit(solution)/shard_map/ppermute | solution.py:107
  81.5 15.1 %collective-permute-start.6 = (f32[32,128]{1,0:T(8,128)S(1)}, f32[32,128]{1,0:T(8,128)S(1)}, u32[]{:S(2)}, u32[]{:S(2)}) collective-permute-start(f32[32,128]{1,0:T(8,128)S(1)} %get-tuple-element.152), channel_id=1, source_target_pairs={{0,8},{8,16},{16,24},{1,9},{9,17},{17,25},{2,10},{10,18},{18,26},{... | collective-permute-start | bytes 49160 | tf_op jit(solution)/shard_map/ppermute | solution.py:107
  86.0 10.5 %collective-permute-start.7 = (f32[8,128]{1,0:T(8,128)S(1)}, f32[8,128]{1,0:T(8,128)S(1)}, u32[]{:S(2)}, u32[]{:S(2)}) collective-permute-start(f32[8,128]{1,0:T(8,128)S(1)} %bitcast.358), channel_id=1, source_target_pairs={{2,0},{4,2},{6,4},{3,1},{5,3},{7,5},{10,8},{12,10},{14,12},{11,9},... | collective-permute-start | bytes 12296 | tf_op jit(solution)/shard_map/ppermute | solution.py:107
  87.3 9.2 %collective-permute-start.8 = (f32[8,128]{1,0:T(8,128)S(1)}, f32[8,128]{1,0:T(8,128)S(1)}, u32[]{:S(2)}, u32[]{:S(2)}) collective-permute-start(f32[8,128]{1,0:T(8,128)S(1)} %bitcast.357), channel_id=1, source_target_pairs={{0,2},{2,4},{4,6},{1,3},{3,5},{5,7},{8,10},{10,12},{12,14},{9,11},... | collective-permute-start | bytes 12296 | tf_op jit(solution)/shard_map/ppermute | solution.py:107
  106.6 13.9 %collective-permute-start.14 = (f32[8,32]{1,0:T(8,128)S(1)}, f32[8,32]{1,0:T(8,128)S(1)}, u32[]{:S(2)}, u32[]{:S(2)}) collective-permute-start(f32[8,32]{1,0:T(8,128)S(1)} %fusion.9), channel_id=1, source_target_pairs={{0,1},{1,0},{2,3},{3,2},{4,5},{5,4},{6,7},{7,6},{8,9},{9,8},{10,11... | collective-permute-start | bytes 3080 | tf_op jit(solution)/shard_map/ppermute | solution.py:102
  108.0 13.6 %collective-permute-start.10 = (f32[32,128]{1,0:T(8,128)S(1)}, f32[32,128]{1,0:T(8,128)S(1)}, u32[]{:S(2)}, u32[]{:S(2)}) collective-permute-start(f32[32,128]{1,0:T(8,128)S(1)} %get-tuple-element.137), channel_id=1, source_target_pairs={{8,0},{16,8},{24,16},{9,1},{17,9},{25,17},{10,2},{18,10},{26,18},{... | collective-permute-start | bytes 49160 | tf_op jit(solution)/shard_map/ppermute | solution.py:107
  109.3 12.3 %collective-permute-start.11 = (f32[32,128]{1,0:T(8,128)S(1)}, f32[32,128]{1,0:T(8,128)S(1)}, u32[]{:S(2)}, u32[]{:S(2)}) collective-permute-start(f32[32,128]{1,0:T(8,128)S(1)} %get-tuple-element.136), channel_id=1, source_target_pairs={{0,8},{8,16},{16,24},{1,9},{9,17},{17,25},{2,10},{10,18},{18,26},{... | collective-permute-start | bytes 49160 | tf_op jit(solution)/shard_map/ppermute | solution.py:107
  114.4 6.7 %collective-permute-start.12 = (f32[8,128]{1,0:T(8,128)S(1)}, f32[8,128]{1,0:T(8,128)S(1)}, u32[]{:S(2)}, u32[]{:S(2)}) collective-permute-start(f32[8,128]{1,0:T(8,128)S(1)} %bitcast.361), channel_id=1, source_target_pairs={{2,0},{4,2},{6,4},{3,1},{5,3},{7,5},{10,8},{12,10},{14,12},{11,9},... | collective-permute-start | bytes 12296 | tf_op jit(solution)/shard_map/ppermute | solution.py:107
  115.7 5.9 %collective-permute-start.13 = (f32[8,128]{1,0:T(8,128)S(1)}, f32[8,128]{1,0:T(8,128)S(1)}, u32[]{:S(2)}, u32[]{:S(2)}) collective-permute-start(f32[8,128]{1,0:T(8,128)S(1)} %bitcast.359), channel_id=1, source_target_pairs={{0,2},{2,4},{4,6},{1,3},{3,5},{5,7},{8,10},{10,12},{12,14},{9,11},... | collective-permute-start | bytes 12296 | tf_op jit(solution)/shard_map/ppermute | solution.py:107
  125.4 13.0 %collective-permute-start.19 = (f32[8,32]{1,0:T(8,128)S(1)}, f32[8,32]{1,0:T(8,128)S(1)}, u32[]{:S(2)}, u32[]{:S(2)}) collective-permute-start(f32[8,32]{1,0:T(8,128)S(1)} %fusion.8), channel_id=1, source_target_pairs={{0,1},{1,0},{2,3},{3,2},{4,5},{5,4},{6,7},{7,6},{8,9},{9,8},{10,11... | collective-permute-start | bytes 3080 | tf_op jit(solution)/shard_map/ppermute | solution.py:102
  125.5 14.2 %collective-permute-start.15 = (f32[32,128]{1,0:T(8,128)S(1)}, f32[32,128]{1,0:T(8,128)S(1)}, u32[]{:S(2)}, u32[]{:S(2)}) collective-permute-start(f32[32,128]{1,0:T(8,128)S(1)} %get-tuple-element.121), channel_id=1, source_target_pairs={{8,0},{16,8},{24,16},{9,1},{17,9},{25,17},{10,2},{18,10},{26,18},{... | collective-permute-start | bytes 49160 | tf_op jit(solution)/shard_map/ppermute | solution.py:107
  126.8 12.9 %collective-permute-start.16 = (f32[32,128]{1,0:T(8,128)S(1)}, f32[32,128]{1,0:T(8,128)S(1)}, u32[]{:S(2)}, u32[]{:S(2)}) collective-permute-start(f32[32,128]{1,0:T(8,128)S(1)} %get-tuple-element.120), channel_id=1, source_target_pairs={{0,8},{8,16},{16,24},{1,9},{9,17},{17,25},{2,10},{10,18},{18,26},{... | collective-permute-start | bytes 49160 | tf_op jit(solution)/shard_map/ppermute | solution.py:107
  132.2 6.4 %collective-permute-start.17 = (f32[8,128]{1,0:T(8,128)S(1)}, f32[8,128]{1,0:T(8,128)S(1)}, u32[]{:S(2)}, u32[]{:S(2)}) collective-permute-start(f32[8,128]{1,0:T(8,128)S(1)} %bitcast.362), channel_id=1, source_target_pairs={{2,0},{4,2},{6,4},{3,1},{5,3},{7,5},{10,8},{12,10},{14,12},{11,9},... | collective-permute-start | bytes 12296 | tf_op jit(solution)/shard_map/ppermute | solution.py:107
  133.5 6.1 %collective-permute-start.18 = (f32[8,128]{1,0:T(8,128)S(1)}, f32[8,128]{1,0:T(8,128)S(1)}, u32[]{:S(2)}, u32[]{:S(2)}) collective-permute-start(f32[8,128]{1,0:T(8,128)S(1)} %bitcast.360), channel_id=1, source_target_pairs={{0,2},{2,4},{4,6},{1,3},{3,5},{5,7},{8,10},{10,12},{12,14},{9,11},... | collective-permute-start | bytes 12296 | tf_op jit(solution)/shard_map/ppermute | solution.py:107
  149.8 46.2 %all-to-all-start.1 = ((f32[4,32,24,128]{3,0,2,1:T(4,128)}), f32[4,32,24,128]{3,0,2,1:T(4,128)S(1)}, u32[]{:S(2)}, u32[]{:S(2)}) async-start(f32[4,32,24,128]{3,0,2,1:T(4,128)} %select_select_fusion.1), calls=%async_computation.1 | async-start | bytes 3145728 | tf_op jit(solution)/shard_map/all_to_all | solution.py:329
  166.6 29.5 %copy-start.58 = (s32[2048]{0:T(1024)S(1)}, s32[2048]{0:T(1024)}, u32[]{:S(2)}) copy-start(s32[2048]{0:T(1024)} %fusion.84) | copy-start | bytes 24580
  231.5 7.5 %collective-permute-start.24 = (f32[4,32,64]{2,1,0:T(8,128)S(1)}, f32[4,32,64]{2,1,0:T(8,128)S(1)}, u32[]{:S(2)}, u32[]{:S(2)}) collective-permute-start(f32[4,32,64]{2,1,0:T(8,128)S(1)} %broadcast_select_fusion.8), channel_id=1, source_target_pairs={{0,1},{1,0},{2,3},{3,2},{4,5},{5,4},{6,7},{7,6},{8,9},{9,8},{10,11... | collective-permute-start | bytes 98312 | tf_op jit(solution)/shard_map/ppermute | solution.py:102
  232.4 11.5 %collective-permute-start.20 = (f32[4,64,128]{2,1,0:T(8,128)}, f32[4,64,128]{2,1,0:T(8,128)S(1)}, u32[]{:S(2)}, u32[]{:S(2)}) collective-permute-start(f32[4,64,128]{2,1,0:T(8,128)} %get-tuple-element.33), channel_id=1, source_target_pairs={{0,8},{8,16},{16,24},{1,9},{9,17},{17,25},{2,10},{10,18},{18,26},{... | collective-permute-start | bytes 393224 | tf_op jit(solution)/shard_map/ppermute | solution.py:107
  235.1 8.8 %collective-permute-start.21 = (f32[4,64,128]{2,1,0:T(8,128)}, f32[4,64,128]{2,1,0:T(8,128)S(1)}, u32[]{:S(2)}, u32[]{:S(2)}) collective-permute-start(f32[4,64,128]{2,1,0:T(8,128)} %get-tuple-element.34), channel_id=1, source_target_pairs={{8,0},{16,8},{24,16},{9,1},{17,9},{25,17},{10,2},{18,10},{26,18},{... | collective-permute-start | bytes 393224 | tf_op jit(solution)/shard_map/ppermute | solution.py:107
  236.4 3.5 collective-permute-start.22
  237.8 6.2 %collective-permute-start.23 = (f32[4,32,1,128]{3,2,1,0:T(1,128)S(1)}, f32[4,32,1,128]{3,2,1,0:T(1,128)S(1)}, u32[]{:S(2)}, u32[]{:S(2)}) collective-permute-start(f32[4,32,1,128]{3,2,1,0:T(1,128)S(1)} %copy-done.96), channel_id=1, source_target_pairs={{2,0},{4,2},{6,4},{3,1},{5,3},{7,5},{10,8},{12,10},{14,12},{11,9},... | collective-permute-start | bytes 196616 | tf_op jit(solution)/shard_map/ppermute | solution.py:107
  244.6 24.9 %copy-start.23 = (f32[1,8,32,127]{3,2,1,0:T(8,128)S(1)}, f32[1,8,32,127]{3,2,1,0:T(8,128)}, u32[]{:S(2)}) copy-start(f32[1,8,32,127]{3,2,1,0:T(8,128)} %get-tuple-element.115) | copy-start | bytes 390148
  244.6 24.9 %copy-start.43 = (f32[32,128]{1,0:T(8,128)S(1)}, f32[32,128]{1,0:T(8,128)}, u32[]{:S(2)}) copy-start(f32[32,128]{1,0:T(8,128)} %copy-done.42) | copy-start | bytes 49156
  244.6 24.9 %copy-start.45 = (f32[32,128]{1,0:T(8,128)S(1)}, f32[32,128]{1,0:T(8,128)}, u32[]{:S(2)}) copy-start(f32[32,128]{1,0:T(8,128)} %copy-done.44) | copy-start | bytes 49156
  244.7 24.9 %copy-start.65 = (f32[8,128]{1,0:T(8,128)S(1)}, f32[8,128]{1,0:T(8,128)}, u32[]{:S(2)}) copy-start(f32[8,128]{1,0:T(8,128)} %copy-done.64) | copy-start | bytes 12292
  244.7 24.9 %copy-start.67 = (f32[8,128]{1,0:T(8,128)S(1)}, f32[8,128]{1,0:T(8,128)}, u32[]{:S(2)}) copy-start(f32[8,128]{1,0:T(8,128)} %copy-done.66) | copy-start | bytes 12292
  269.5 11.2 %collective-permute-start.29 = (f32[4,32,64]{2,1,0:T(8,128)S(1)}, f32[4,32,64]{2,1,0:T(8,128)S(1)}, u32[]{:S(2)}, u32[]{:S(2)}) collective-permute-start(f32[4,32,64]{2,1,0:T(8,128)S(1)} %broadcast_select_fusion.7), channel_id=1, source_target_pairs={{0,1},{1,0},{2,3},{3,2},{4,5},{5,4},{6,7},{7,6},{8,9},{9,8},{10,11... | collective-permute-start | bytes 98312 | tf_op jit(solution)/shard_map/ppermute | solution.py:102
  270.8 15.0 %collective-permute-start.25 = (f32[4,64,128]{2,1,0:T(8,128)}, f32[4,64,128]{2,1,0:T(8,128)S(1)}, u32[]{:S(2)}, u32[]{:S(2)}) collective-permute-start(f32[4,64,128]{2,1,0:T(8,128)} %get-tuple-element.42), channel_id=1, source_target_pairs={{0,8},{8,16},{16,24},{1,9},{9,17},{17,25},{2,10},{10,18},{18,26},{... | collective-permute-start | bytes 393224 | tf_op jit(solution)/shard_map/ppermute | solution.py:107
  275.3 10.4 %collective-permute-start.26 = (f32[4,64,128]{2,1,0:T(8,128)}, f32[4,64,128]{2,1,0:T(8,128)S(1)}, u32[]{:S(2)}, u32[]{:S(2)}) collective-permute-start(f32[4,64,128]{2,1,0:T(8,128)} %get-tuple-element.43), channel_id=1, source_target_pairs={{8,0},{16,8},{24,16},{9,1},{17,9},{25,17},{10,2},{18,10},{26,18},{... | collective-permute-start | bytes 393224 | tf_op jit(solution)/shard_map/ppermute | solution.py:107
  276.6 5.0 %collective-permute-start.27 = (f32[4,32,1,128]{3,2,1,0:T(1,128)}, f32[4,32,1,128]{3,2,1,0:T(1,128)S(1)}, u32[]{:S(2)}, u32[]{:S(2)}) collective-permute-start(f32[4,32,1,128]{3,2,1,0:T(1,128)} %get-tuple-element.44), channel_id=1, source_target_pairs={{0,2},{2,4},{4,6},{1,3},{3,5},{5,7},{8,10},{10,12},{12,14},{9,11},... | collective-permute-start | bytes 196616 | tf_op jit(solution)/shard_map/ppermute | solution.py:107
  279.4 6.4 %collective-permute-start.28 = (f32[4,32,1,128]{3,2,1,0:T(1,128)}, f32[4,32,1,128]{3,2,1,0:T(1,128)S(1)}, u32[]{:S(2)}, u32[]{:S(2)}) collective-permute-start(f32[4,32,1,128]{3,2,1,0:T(1,128)} %get-tuple-element.45), channel_id=1, source_target_pairs={{2,0},{4,2},{6,4},{3,1},{5,3},{7,5},{10,8},{12,10},{14,12},{11,9},... | collective-permute-start | bytes 196616 | tf_op jit(solution)/shard_map/ppermute | solution.py:107
  311.2 12.9 %collective-permute-start.34 = (f32[4,32,64]{2,1,0:T(8,128)S(1)}, f32[4,32,64]{2,1,0:T(8,128)S(1)}, u32[]{:S(2)}, u32[]{:S(2)}) collective-permute-start(f32[4,32,64]{2,1,0:T(8,128)S(1)} %broadcast_select_fusion.6), channel_id=1, source_target_pairs={{0,1},{1,0},{2,3},{3,2},{4,5},{5,4},{6,7},{7,6},{8,9},{9,8},{10,11... | collective-permute-start | bytes 98312 | tf_op jit(solution)/shard_map/ppermute | solution.py:102
  313.1 15.9 %collective-permute-start.30 = (f32[4,64,128]{2,1,0:T(8,128)S(1)}, f32[4,64,128]{2,1,0:T(8,128)S(1)}, u32[]{:S(2)}, u32[]{:S(2)}) collective-permute-start(f32[4,64,128]{2,1,0:T(8,128)S(1)} %copy-done.93), channel_id=1, source_target_pairs={{0,8},{8,16},{16,24},{1,9},{9,17},{17,25},{2,10},{10,18},{18,26},{... | collective-permute-start | bytes 393224 | tf_op jit(solution)/shard_map/ppermute | solution.py:107
  318.0 11.0 %collective-permute-start.31 = (f32[4,64,128]{2,1,0:T(8,128)S(1)}, f32[4,64,128]{2,1,0:T(8,128)S(1)}, u32[]{:S(2)}, u32[]{:S(2)}) collective-permute-start(f32[4,64,128]{2,1,0:T(8,128)S(1)} %copy-done.92), channel_id=1, source_target_pairs={{8,0},{16,8},{24,16},{9,1},{17,9},{25,17},{10,2},{18,10},{26,18},{... | collective-permute-start | bytes 393224 | tf_op jit(solution)/shard_map/ppermute | solution.py:107
  319.3 5.5 %collective-permute-start.32 = (f32[4,32,1,128]{3,2,1,0:T(1,128)S(1)}, f32[4,32,1,128]{3,2,1,0:T(1,128)S(1)}, u32[]{:S(2)}, u32[]{:S(2)}) collective-permute-start(f32[4,32,1,128]{3,2,1,0:T(1,128)S(1)} %copy-done.95), channel_id=1, source_target_pairs={{0,2},{2,4},{4,6},{1,3},{3,5},{5,7},{8,10},{10,12},{12,14},{9,11},... | collective-permute-start | bytes 196616 | tf_op jit(solution)/shard_map/ppermute | solution.py:107
  322.9 6.2 %collective-permute-start.33 = (f32[4,32,1,128]{3,2,1,0:T(1,128)S(1)}, f32[4,32,1,128]{3,2,1,0:T(1,128)S(1)}, u32[]{:S(2)}, u32[]{:S(2)}) collective-permute-start(f32[4,32,1,128]{3,2,1,0:T(1,128)S(1)} %copy-done.94), channel_id=1, source_target_pairs={{2,0},{4,2},{6,4},{3,1},{5,3},{7,5},{10,8},{12,10},{14,12},{11,9},... | collective-permute-start | bytes 196616 | tf_op jit(solution)/shard_map/ppermute | solution.py:107
  (89 other events, 509.9 us)

commit v11 on v10

--- a/solution.py
+++ b/solution.py
@@ -189,7 +189,7 @@
             p_out[0, x] = p_ref[0, x] + step_dir
         return write_faces(x, step_dir, carry, *face_out)
 
-    columns = lax.fori_loop(0, nx, body, jnp.zeros((ny, nz), jnp.float32), unroll=8)
+    columns = lax.fori_loop(0, nx, body, jnp.zeros((ny, nz), jnp.float32), unroll=16)
     finish_faces(columns, *face_out)
 
 

time: 361 us -> 359 us (level)
  transfers between devices with their start and end apart: 37 -> 37, of which waited for: 8 -> 7; matrix products, arithmetic and copies ran while one was open for 18% -> 18% of each run, Pallas kernels for 0% -> 0%
where the time goes in v11:
time: 359 us; the launch traced here: 355 us
  starting transfers between devices  90.8 us (25%)
  Pallas kernels  86.7 us (24%)
  other arithmetic  72.7 us (20%)
  local copies, waits for them, and re-layouts  65.8 us (18%)
  waiting for transfers between devices  36 us (10%)
    pallas_call x3, Pallas kernels, run_sweep(): pl.pallas_call(functools.partial(sweep_kernel, final), grid=(steps,), in_...  72.7 us
    ppermute x14, starting transfers between devices, exchange(): lax.ppermute(top, axis, forward)  58.4 us
    all_to_all x1, waiting for transfers between devices, local(): lax.all_to_all(send_values.reshape(STEPS, devices, capacity, row_len), ('...  21.9 us
    ppermute x14, starting transfers between devices, exchange(): lax.ppermute(bottom, axis, backward)  18.3 us
    gather x2, local copies, waits for them, and re-layouts, local(): jnp.take(received, row_slot, axis=1)  17.7 us
    add x4, other arithmetic, membrane(): steady + (gate_state - steady) * jnp.exp(-DT_HEART / time_const)  16.1 us
    pallas_call x1, Pallas kernels, run_initial(): pl.pallas_call(functools.partial(initial_kernel, mid), grid=(source.shape...  14 us
    ppermute x14, waiting for transfers between devices, exchange(): lax.ppermute(bottom, axis, backward)  12.3 us
  transfers between devices with their start and end apart: 37, of which 7 were waited for; matrix products, arithmetic and copies ran while one was open for 18% of the time, Pallas kernels for 0%

profile of v11, /device:TPU:0, one launch (start us, length us, event | category | flops | bytes accessed | tf_op | source)
XLA Modules:
  0.0 354.9 jit_solution(8333656347773462116)
XLA Ops:
  0.6 1.8 fusion.118
  2.4 4.5 %select_add_fusion.1 = (f32[32,64,128]{2,1,0:T(8,128)S(1)}, pred[32,64,128]{2,1,0:T(8,128)(4,1)S(1)}, pred[32,64,128]{2,1,0:T(8,128)(4,1)S(1)}, pred[32,64,128]{2,1,0:T(8,128)(4,1)S(1)}, pred[32,64,128]{2,1,0:T(8,128)(4,1)S(1)}) fusion(f32[]{:T(128)} %bitcast.29, f32[]{:T(128)} %bitcast.28, f32[]{:T(128)} %bitcast.27, f32[]{:T(128)} %bitcast.26, ...), kind=kLoop, calls=%fused_computation.33 | loop fusion | flops 2883584 | bytes 3145744 | tf_op jit(solution)/shard_map/add | solution.py:310
  6.9 5.9 %select_add_fusion.2 = (f32[32,64,128]{2,1,0:T(8,128)S(1)}, f32[32,64,128]{2,1,0:T(8,128)S(1)}) fusion(pred[32,64,128]{2,1,0:T(8,128)(4,1)S(1)} %get-tuple-element.85, pred[32,64,128]{2,1,0:T(8,128)(4,1)S(1)} %get-tuple-element.84, pred[32,64,128]{2,1,0:T(8,128)(4,1)S(1)} %get-tuple-element.83, pred[32,64,128]{2,1,0:T(8,128)(4,1)S(1)} %get-tuple-element.82, ...), kind=kLoop, calls=%fused_computation.34 | loop fusion | flops 3670016 | bytes 3145760 | tf_op jit(solution)/shard_map/add | solution.py:310
  12.9 1.8 fusion.98
  17.1 5.5 %collective-permute-start.3 = (f32[5120]{0:T(1024)}, f32[5120]{0:T(1024)S(1)}, u32[]{:S(2)}, u32[]{:S(2)}) collective-permute-start(f32[5120]{0:T(1024)} %pad_maximum_fusion.5), channel_id=1, source_target_pairs={{0,2},{2,4},{4,6},{1,3},{3,5},{5,7},{8,10},{10,12},{12,14},{9,11},... | collective-permute-start | bytes 61448 | tf_op jit(solution)/shard_map/ppermute | solution.py:107
  23.4 3.8 %collective-permute-start.1 = (f32[12288]{0:T(1024)S(1)}, f32[12288]{0:T(1024)S(1)}, u32[]{:S(2)}, u32[]{:S(2)}) collective-permute-start(f32[12288]{0:T(1024)S(1)} %pad_maximum_fusion.3), channel_id=1, source_target_pairs={{0,8},{8,16},{16,24},{1,9},{9,17},{17,25},{2,10},{10,18},{18,26},{... | collective-permute-start | bytes 147464 | tf_op jit(solution)/shard_map/ppermute | solution.py:107
  36.0 5.0 %gather_fusion = s32[768]{0:T(1024)S(1)} fusion(s32[256]{0:T(256)S(1)} %reshape.1868, s32[1024]{0:T(1024)S(1)} %pad_clamp_fusion), kind=kCustom, calls=%fused_computation | custom fusion | bytes 9216 | tf_op jit(solution)/shard_map/gather | solution.py:298
  41.7 6.1 %all-to-all-start = ((s32[32,1,24]{2,1,0:T(1,128)}), s32[32,1,24]{2,1,0:T(1,128)S(1)}, u32[]{:S(2)}, u32[]{:S(2)}) async-start(s32[32,1,24]{2,1,0:T(1,128)} %bitcast.116), calls=%async_computation | async-start | bytes 32768 | tf_op jit(solution)/shard_map/all_to_all | solution.py:299
  47.8 1.5 fusion.100
  49.3 1.6 fusion.101
  50.9 1.7 fusion.99
  55.1 1.5 multiply_add_fusion.3
  59.4 2.8 iota_reduce_fusion
  66.5 1.8 slice.567
  68.3 1.9 slice.568
  75.0 1.4 fusion.18
  76.5 2.8 multiply_add_fusion.2
  81.5 4.5 %collective-permute-start.6 = (f32[32,128]{1,0:T(8,128)S(1)}, f32[32,128]{1,0:T(8,128)S(1)}, u32[]{:S(2)}, u32[]{:S(2)}) collective-permute-start(f32[32,128]{1,0:T(8,128)S(1)} %get-tuple-element.152), channel_id=1, source_target_pairs={{0,8},{8,16},{16,24},{1,9},{9,17},{17,25},{2,10},{10,18},{18,26},{... | collective-permute-start | bytes 49160 | tf_op jit(solution)/shard_map/ppermute | solution.py:107
  87.3 4.5 %collective-permute-start.8 = (f32[8,128]{1,0:T(8,128)S(1)}, f32[8,128]{1,0:T(8,128)S(1)}, u32[]{:S(2)}, u32[]{:S(2)}) collective-permute-start(f32[8,128]{1,0:T(8,128)S(1)} %bitcast.357), channel_id=1, source_target_pairs={{0,2},{2,4},{4,6},{1,3},{3,5},{5,7},{8,10},{10,12},{12,14},{9,11},... | collective-permute-start | bytes 12296 | tf_op jit(solution)/shard_map/ppermute | solution.py:107
  100.4 1.4 fusion.33
  101.9 4.2 %multiply_add_fusion.1 = f32[18,8,32,128]{3,2,1,0:T(8,128)S(1)} fusion(f32[8,32,128]{2,1,0:T(8,128)S(1)} %bitcast.299, f32[18]{0:T(128)S(1)} %copy-done.84, f32[18]{0:T(128)S(1)} %copy-done.87, f32[18]{0:T(128)S(1)} %copy-done.90, f32[8,32,128]{2,1,0:T(8,128)S(1)} %bitcast.291, f32[19,8,32,128]{3,2,1,0:T(8,128)S(1)} %copy-done.4, ...), kind=kLoop, calls=%fused_computation.9 | loop fusion | flops 19464192 | bytes 5112024 | tf_op jit(solution)/shard_map/add | solution.py:59
  109.3 5.1 %collective-permute-start.11 = (f32[32,128]{1,0:T(8,128)S(1)}, f32[32,128]{1,0:T(8,128)S(1)}, u32[]{:S(2)}, u32[]{:S(2)}) collective-permute-start(f32[32,128]{1,0:T(8,128)S(1)} %get-tuple-element.136), channel_id=1, source_target_pairs={{0,8},{8,16},{16,24},{1,9},{9,17},{17,25},{2,10},{10,18},{18,26},{... | collective-permute-start | bytes 49160 | tf_op jit(solution)/shard_map/ppermute | solution.py:107
  115.7 4.8 %collective-permute-start.13 = (f32[8,128]{1,0:T(8,128)S(1)}, f32[8,128]{1,0:T(8,128)S(1)}, u32[]{:S(2)}, u32[]{:S(2)}) collective-permute-start(f32[8,128]{1,0:T(8,128)S(1)} %bitcast.359), channel_id=1, source_target_pairs={{0,2},{2,4},{4,6},{1,3},{3,5},{5,7},{8,10},{10,12},{12,14},{9,11},... | collective-permute-start | bytes 12296 | tf_op jit(solution)/shard_map/ppermute | solution.py:107
  126.8 5.4 %collective-permute-start.16 = (f32[32,128]{1,0:T(8,128)S(1)}, f32[32,128]{1,0:T(8,128)S(1)}, u32[]{:S(2)}, u32[]{:S(2)}) collective-permute-start(f32[32,128]{1,0:T(8,128)S(1)} %get-tuple-element.120), channel_id=1, source_target_pairs={{0,8},{8,16},{16,24},{1,9},{9,17},{17,25},{2,10},{10,18},{18,26},{... | collective-permute-start | bytes 49160 | tf_op jit(solution)/shard_map/ppermute | solution.py:107
  133.5 4.8 %collective-permute-start.18 = (f32[8,128]{1,0:T(8,128)S(1)}, f32[8,128]{1,0:T(8,128)S(1)}, u32[]{:S(2)}, u32[]{:S(2)}) collective-permute-start(f32[8,128]{1,0:T(8,128)S(1)} %bitcast.360), channel_id=1, source_target_pairs={{0,2},{2,4},{4,6},{1,3},{3,5},{5,7},{8,10},{10,12},{12,14},{9,11},... | collective-permute-start | bytes 12296 | tf_op jit(solution)/shard_map/ppermute | solution.py:107
  141.9 3.0 gather_fusion.1
  144.8 4.9 %select_select_fusion.1 = f32[4,32,24,128]{3,0,2,1:T(4,128)} fusion(f32[4,32,24,128]{3,0,2,1:T(4,128)S(1)} %bitcast.285, pred[32,24]{1,0:T(8,128)(4,1)} %broadcast_in_dim.362, pred[32,24]{1,0:T(8,128)(4,1)} %broadcast_in_dim.360), kind=kLoop, calls=%fused_computation.12 | loop fusion | flops 786432 | bytes 3147264 | tf_op jit(solution)/shard_map/jit(_where)/select_n | solution.py:328
  149.8 7.4 %all-to-all-start.1 = ((f32[4,32,24,128]{3,0,2,1:T(4,128)}), f32[4,32,24,128]{3,0,2,1:T(4,128)S(1)}, u32[]{:S(2)}, u32[]{:S(2)}) async-start(f32[4,32,24,128]{3,0,2,1:T(4,128)} %select_select_fusion.1), calls=%async_computation.1 | async-start | bytes 3145728 | tf_op jit(solution)/shard_map/all_to_all | solution.py:329
  157.2 7.1 %broadcast_divide_fusion = (f32[32,64,128]{2,1,0:T(8,128)}, f32[32,64,128]{2,1,0:T(8,128)}, f32[32,64,128]{2,1,0:T(8,128)}, f32[32,64,128]{2,1,0:T(8,128)}, f32[...) fusion(f32[32,64,128]{2,1,0:T(8,128)} %copy-done.1, ...), kind=kLoop, calls=%fused_computation.40 | loop fusion | flops 6553600 | bytes 17825792 | tf_op jit(solution)/shard_map/div | solution.py:349
  166.6 7.5 %multiply_add_fusion = f32[18,8,32,128]{3,2,1,0:T(8,128)} fusion(f32[8,32,128]{2,1,0:T(8,128)S(1)} %bitcast.302, f32[18]{0:T(128)} %param.18, f32[18]{0:T(128)} %param.16, f32[18]{0:T(128)} %copy-done.88, f32[8,32,128]{2,1,0:T(8,128)S(1)} %bitcast.301, f32[8,32,128]{2,1,0:T(8,128)S(1)} %bitcast.292, f32[19,8,32,128]{3,2,1,0:T(8,128)} %param.14, ...), kind=kLoop, calls=%fused_computation.8 | loop fusion | flops 25952256 | bytes 5243096 | tf_op jit(solution)/shard_map/add | solution.py:59
  174.1 21.9 %all-to-all-done.1 = f32[4,32,24,128]{3,0,2,1:T(4,128)S(1)} async-done(((f32[4,32,24,128]{3,0,2,1:T(4,128)}), f32[4,32,24,128]{3,0,2,1:T(4,128)S(1)}, u32[]{:S(2)}, u32[]{:S(2)}) %all-to-all-start.1) | async-done | bytes 1572896 | tf_op jit(solution)/shard_map/all_to_all | solution.py:329
  196.0 15.2 %gather_fusion.2 = f32[2048,4,128]{2,1,0:T(4,128)} fusion(f32[4,768,128]{2,0,1:T(4,128)S(1)} %bitcast.282, s32[2048]{0:T(1024)S(1)} %copy-done.58), kind=kCustom, calls=%fused_computation.2 | custom fusion | bytes 8396800 | tf_op jit(solution)/shard_map/jit(_take)/gather | solution.py:336
  211.3 2.5 copy.1555
  213.8 2.8 select_select_fusion.r_ref
  216.6 14.0 %chebyshev_start.1 = (f32[4,32,64,128]{3,2,1,0:T(8,128)}, f32[4,64,128]{2,1,0:T(8,128)}, f32[4,64,128]{2,1,0:T(8,128)}, f32[4,32,1,128]{3,2,1,0:T(1,128)}, f32[4...) custom-call(f32[4,32,64,128]{3,2,1,0:T(8,128)} %select_select_fusion.r_ref, ...), custom_call_target="tpu_custom_call" | custom-call | flops 2097152 | bytes 9437184 | tf_op jit(solution)/shard_map/chebyshev_start/pallas_call | solution.py:231
  232.4 2.7 collective-permute-start.20
  239.9 4.0 %collective-permute-done.23.yhi = f32[4,32,1,128]{3,2,1,0:T(1,128)S(1)} collective-permute-done((f32[4,32,1,128]{3,2,1,0:T(1,128)S(1)}, f32[4,32,1,128]{3,2,1,0:T(1,128)S(1)}, u32[]{:S(2)}, u32[]{:S(2)}) %collective-permute-start.23) | collective-permute-done | bytes 65568 | tf_op jit(solution)/shard_map/ppermute | solution.py:107
  244.7 23.2 %chebyshev_sweep.3 = (f32[4,32,64,128]{3,2,1,0:T(8,128)}, f32[4,32,64,128]{3,2,1,0:T(8,128)}, f32[4,32,64,128]{3,2,1,0:T(8,128)}, f32[4,64,128]{2,1,0:T(8,128)},...) custom-call(f32[2]{0:T(128)} %constant.119.clone.coef_ref, ...), custom_call_target="tpu_custom_call" | custom-call | flops 31457280 | bytes 36700160 | tf_op jit(solution)/shard_map/chebyshev_sweep/pallas_call | solution.py:254
  270.1 4.6 %collective-permute-start.25 = (f32[4,64,128]{2,1,0:T(8,128)}, f32[4,64,128]{2,1,0:T(8,128)S(1)}, u32[]{:S(2)}, u32[]{:S(2)}) collective-permute-start(f32[4,64,128]{2,1,0:T(8,128)} %get-tuple-element.42), channel_id=1, source_target_pairs={{0,8},{8,16},{16,24},{1,9},{9,17},{17,25},{2,10},{10,18},{18,26},{... | collective-permute-start | bytes 393224 | tf_op jit(solution)/shard_map/ppermute | solution.py:107
  276.0 2.8 collective-permute-start.27
  278.7 1.6 collective-permute-start.28
  281.0 4.1 %collective-permute-done.28.yhi = f32[4,32,1,128]{3,2,1,0:T(1,128)S(1)} collective-permute-done((f32[4,32,1,128]{3,2,1,0:T(1,128)}, f32[4,32,1,128]{3,2,1,0:T(1,128)S(1)}, u32[]{:S(2)}, u32[]{:S(2)}) %collective-permute-start.28) | collective-permute-done | bytes 65568 | tf_op jit(solution)/shard_map/ppermute | solution.py:107
  285.8 23.2 %chebyshev_sweep.4 = (f32[4,32,64,128]{3,2,1,0:T(8,128)}, f32[4,32,64,128]{3,2,1,0:T(8,128)}, f32[4,32,64,128]{3,2,1,0:T(8,128)}, f32[4,64,128]{2,1,0:T(8,128)},...) custom-call(f32[2]{0:T(128)} %constant.120.clone.coef_ref, ...), custom_call_target="tpu_custom_call" | custom-call | flops 31457280 | bytes 36700160 | tf_op jit(solution)/shard_map/chebyshev_sweep/pallas_call | solution.py:254
  310.0 1.8 pad_maximum_fusion
  311.8 4.9 %collective-permute-start.30 = (f32[4,64,128]{2,1,0:T(8,128)S(1)}, f32[4,64,128]{2,1,0:T(8,128)S(1)}, u32[]{:S(2)}, u32[]{:S(2)}) collective-permute-start(f32[4,64,128]{2,1,0:T(8,128)S(1)} %copy-done.93), channel_id=1, source_target_pairs={{0,8},{8,16},{16,24},{1,9},{9,17},{17,25},{2,10},{10,18},{18,26},{... | collective-permute-start | bytes 393224 | tf_op jit(solution)/shard_map/ppermute | solution.py:107
  318.0 3.5 collective-permute-start.32
  323.5 4.2 %collective-permute-done.33.yhi = f32[4,32,1,128]{3,2,1,0:T(1,128)S(1)} collective-permute-done((f32[4,32,1,128]{3,2,1,0:T(1,128)S(1)}, f32[4,32,1,128]{3,2,1,0:T(1,128)S(1)}, u32[]{:S(2)}, u32[]{:S(2)}) %collective-permute-start.33) | collective-permute-done | bytes 65568 | tf_op jit(solution)/shard_map/ppermute | solution.py:107
  328.4 26.2 %chebyshev_sweep.5 = (f32[4,32,64,128]{3,2,1,0:T(8,128)}, f32[4,32,64,128]{3,2,1,0:T(8,128)}, f32[32,64,4,128]{3,2,1,0:T(4,128)}, f32[4,64,128]{2,1,0:T(8,128)},...) custom-call(f32[2]{0:T(128)} %constant.121.clone.coef_ref, ...), custom_call_target="tpu_custom_call" | custom-call | flops 31457280 | bytes 36700160 | tf_op jit(solution)/shard_map/chebyshev_sweep/pallas_call | solution.py:254
  (378 shorter events, 72.8 us)
Async XLA Ops:
  12.8 35.0 %copy-start = (f32[32,64,128]{2,1,0:T(8,128)}, f32[32,64,128]{2,1,0:T(8,128)S(1)}, u32[]{:S(2)}) copy-start(f32[32,64,128]{2,1,0:T(8,128)S(1)} %get-tuple-element.102) | copy-start | bytes 3145732
  12.8 36.5 %copy-start.1 = (f32[32,64,128]{2,1,0:T(8,128)}, f32[32,64,128]{2,1,0:T(8,128)S(1)}, u32[]{:S(2)}) copy-start(f32[32,64,128]{2,1,0:T(8,128)S(1)} %get-tuple-element.103) | copy-start | bytes 3145732
  15.2 55.3 %collective-permute-start.2 = (f32[5120]{0:T(1024)}, f32[5120]{0:T(1024)S(1)}, u32[]{:S(2)}, u32[]{:S(2)}) collective-permute-start(f32[5120]{0:T(1024)} %pad_maximum_fusion.4), channel_id=1, source_target_pairs={{2,0},{4,2},{6,4},{3,1},{5,3},{7,5},{10,8},{12,10},{14,12},{11,9},... | collective-permute-start | bytes 61448 | tf_op jit(solution)/shard_map/ppermute | solution.py:107
  17.1 53.4 %collective-permute-start.3 = (f32[5120]{0:T(1024)}, f32[5120]{0:T(1024)S(1)}, u32[]{:S(2)}, u32[]{:S(2)}) collective-permute-start(f32[5120]{0:T(1024)} %pad_maximum_fusion.5), channel_id=1, source_target_pairs={{0,2},{2,4},{4,6},{1,3},{3,5},{5,7},{8,10},{10,12},{12,14},{9,11},... | collective-permute-start | bytes 61448 | tf_op jit(solution)/shard_map/ppermute | solution.py:107
  23.4 47.7 %collective-permute-start.1 = (f32[12288]{0:T(1024)S(1)}, f32[12288]{0:T(1024)S(1)}, u32[]{:S(2)}, u32[]{:S(2)}) collective-permute-start(f32[12288]{0:T(1024)S(1)} %pad_maximum_fusion.3), channel_id=1, source_target_pairs={{0,8},{8,16},{16,24},{1,9},{9,17},{17,25},{2,10},{10,18},{18,26},{... | collective-permute-start | bytes 147464 | tf_op jit(solution)/shard_map/ppermute | solution.py:107
  27.9 43.3 %collective-permute-start = (f32[12288]{0:T(1024)}, f32[12288]{0:T(1024)S(1)}, u32[]{:S(2)}, u32[]{:S(2)}) collective-permute-start(f32[12288]{0:T(1024)} %pad_maximum_fusion.2), channel_id=1, source_target_pairs={{8,0},{16,8},{24,16},{9,1},{17,9},{25,17},{10,2},{18,10},{26,18},{... | collective-permute-start | bytes 147464 | tf_op jit(solution)/shard_map/ppermute | solution.py:107
  31.2 33.7 %collective-permute-start.4 = (f32[2304]{0:T(1024)}, f32[2304]{0:T(1024)}, u32[]{:S(2)}, u32[]{:S(2)}) collective-permute-start(f32[2304]{0:T(1024)} %maximum_select_fusion), channel_id=1, source_target_pairs={{0,1},{1,0},{2,3},{3,2},{4,5},{5,4},{6,7},{7,6},{8,9},{9,8},{10,11... | collective-permute-start | bytes 27656 | tf_op jit(solution)/shard_map/ppermute | solution.py:102
  41.7 16.9 %all-to-all-start = ((s32[32,1,24]{2,1,0:T(1,128)}), s32[32,1,24]{2,1,0:T(1,128)S(1)}, u32[]{:S(2)}, u32[]{:S(2)}) async-start(s32[32,1,24]{2,1,0:T(1,128)} %bitcast.116), calls=%async_computation | async-start | bytes 32768 | tf_op jit(solution)/shard_map/all_to_all | solution.py:299
  55.0 51.0 %copy-start.8 = (pred[8,32,128]{2,1,0:T(8,128)(4,1)}, pred[8,32,128]{2,1,0:T(8,128)(4,1)S(1)}, u32[]{:S(2)}) copy-start(pred[8,32,128]{2,1,0:T(8,128)(4,1)S(1)} %get-tuple-element.162) | copy-start | bytes 98308
  55.0 51.0 %copy-start.10 = (pred[8,32,128]{2,1,0:T(8,128)(4,1)}, pred[8,32,128]{2,1,0:T(8,128)(4,1)S(1)}, u32[]{:S(2)}) copy-start(pred[8,32,128]{2,1,0:T(8,128)(4,1)S(1)} %get-tuple-element.163) | copy-start | bytes 98308
  55.0 51.0 %copy-start.12 = (pred[8,32,128]{2,1,0:T(8,128)(4,1)}, pred[8,32,128]{2,1,0:T(8,128)(4,1)S(1)}, u32[]{:S(2)}) copy-start(pred[8,32,128]{2,1,0:T(8,128)(4,1)S(1)} %get-tuple-element.164) | copy-start | bytes 98308
  79.9 13.3 %collective-permute-start.9 = (f32[8,32]{1,0:T(8,128)S(1)}, f32[8,32]{1,0:T(8,128)S(1)}, u32[]{:S(2)}, u32[]{:S(2)}) collective-permute-start(f32[8,32]{1,0:T(8,128)S(1)} %fusion.10), channel_id=1, source_target_pairs={{0,1},{1,0},{2,3},{3,2},{4,5},{5,4},{6,7},{7,6},{8,9},{9,8},{10,11... | collective-permute-start | bytes 3080 | tf_op jit(solution)/shard_map/ppermute | solution.py:102
  80.2 16.4 %collective-permute-start.5 = (f32[32,128]{1,0:T(8,128)S(1)}, f32[32,128]{1,0:T(8,128)S(1)}, u32[]{:S(2)}, u32[]{:S(2)}) collective-permute-start(f32[32,128]{1,0:T(8,128)S(1)} %get-tuple-element.153), channel_id=1, source_target_pairs={{8,0},{16,8},{24,16},{9,1},{17,9},{25,17},{10,2},{18,10},{26,18},{... | collective-permute-start | bytes 49160 | tf_op jit(solution)/shard_map/ppermute | solution.py:107
  81.5 15.1 %collective-permute-start.6 = (f32[32,128]{1,0:T(8,128)S(1)}, f32[32,128]{1,0:T(8,128)S(1)}, u32[]{:S(2)}, u32[]{:S(2)}) collective-permute-start(f32[32,128]{1,0:T(8,128)S(1)} %get-tuple-element.152), channel_id=1, source_target_pairs={{0,8},{8,16},{16,24},{1,9},{9,17},{17,25},{2,10},{10,18},{18,26},{... | collective-permute-start | bytes 49160 | tf_op jit(solution)/shard_map/ppermute | solution.py:107
  86.0 10.5 %collective-permute-start.7 = (f32[8,128]{1,0:T(8,128)S(1)}, f32[8,128]{1,0:T(8,128)S(1)}, u32[]{:S(2)}, u32[]{:S(2)}) collective-permute-start(f32[8,128]{1,0:T(8,128)S(1)} %bitcast.358), channel_id=1, source_target_pairs={{2,0},{4,2},{6,4},{3,1},{5,3},{7,5},{10,8},{12,10},{14,12},{11,9},... | collective-permute-start | bytes 12296 | tf_op jit(solution)/shard_map/ppermute | solution.py:107
  87.3 9.2 %collective-permute-start.8 = (f32[8,128]{1,0:T(8,128)S(1)}, f32[8,128]{1,0:T(8,128)S(1)}, u32[]{:S(2)}, u32[]{:S(2)}) collective-permute-start(f32[8,128]{1,0:T(8,128)S(1)} %bitcast.357), channel_id=1, source_target_pairs={{0,2},{2,4},{4,6},{1,3},{3,5},{5,7},{8,10},{10,12},{12,14},{9,11},... | collective-permute-start | bytes 12296 | tf_op jit(solution)/shard_map/ppermute | solution.py:107
  106.6 13.9 %collective-permute-start.14 = (f32[8,32]{1,0:T(8,128)S(1)}, f32[8,32]{1,0:T(8,128)S(1)}, u32[]{:S(2)}, u32[]{:S(2)}) collective-permute-start(f32[8,32]{1,0:T(8,128)S(1)} %fusion.9), channel_id=1, source_target_pairs={{0,1},{1,0},{2,3},{3,2},{4,5},{5,4},{6,7},{7,6},{8,9},{9,8},{10,11... | collective-permute-start | bytes 3080 | tf_op jit(solution)/shard_map/ppermute | solution.py:102
  108.0 13.6 %collective-permute-start.10 = (f32[32,128]{1,0:T(8,128)S(1)}, f32[32,128]{1,0:T(8,128)S(1)}, u32[]{:S(2)}, u32[]{:S(2)}) collective-permute-start(f32[32,128]{1,0:T(8,128)S(1)} %get-tuple-element.137), channel_id=1, source_target_pairs={{8,0},{16,8},{24,16},{9,1},{17,9},{25,17},{10,2},{18,10},{26,18},{... | collective-permute-start | bytes 49160 | tf_op jit(solution)/shard_map/ppermute | solution.py:107
  109.3 12.3 %collective-permute-start.11 = (f32[32,128]{1,0:T(8,128)S(1)}, f32[32,128]{1,0:T(8,128)S(1)}, u32[]{:S(2)}, u32[]{:S(2)}) collective-permute-start(f32[32,128]{1,0:T(8,128)S(1)} %get-tuple-element.136), channel_id=1, source_target_pairs={{0,8},{8,16},{16,24},{1,9},{9,17},{17,25},{2,10},{10,18},{18,26},{... | collective-permute-start | bytes 49160 | tf_op jit(solution)/shard_map/ppermute | solution.py:107
  114.4 6.7 %collective-permute-start.12 = (f32[8,128]{1,0:T(8,128)S(1)}, f32[8,128]{1,0:T(8,128)S(1)}, u32[]{:S(2)}, u32[]{:S(2)}) collective-permute-start(f32[8,128]{1,0:T(8,128)S(1)} %bitcast.361), channel_id=1, source_target_pairs={{2,0},{4,2},{6,4},{3,1},{5,3},{7,5},{10,8},{12,10},{14,12},{11,9},... | collective-permute-start | bytes 12296 | tf_op jit(solution)/shard_map/ppermute | solution.py:107
  115.7 5.9 %collective-permute-start.13 = (f32[8,128]{1,0:T(8,128)S(1)}, f32[8,128]{1,0:T(8,128)S(1)}, u32[]{:S(2)}, u32[]{:S(2)}) collective-permute-start(f32[8,128]{1,0:T(8,128)S(1)} %bitcast.359), channel_id=1, source_target_pairs={{0,2},{2,4},{4,6},{1,3},{3,5},{5,7},{8,10},{10,12},{12,14},{9,11},... | collective-permute-start | bytes 12296 | tf_op jit(solution)/shard_map/ppermute | solution.py:107
  125.4 13.0 %collective-permute-start.19 = (f32[8,32]{1,0:T(8,128)S(1)}, f32[8,32]{1,0:T(8,128)S(1)}, u32[]{:S(2)}, u32[]{:S(2)}) collective-permute-start(f32[8,32]{1,0:T(8,128)S(1)} %fusion.8), channel_id=1, source_target_pairs={{0,1},{1,0},{2,3},{3,2},{4,5},{5,4},{6,7},{7,6},{8,9},{9,8},{10,11... | collective-permute-start | bytes 3080 | tf_op jit(solution)/shard_map/ppermute | solution.py:102
  125.5 14.2 %collective-permute-start.15 = (f32[32,128]{1,0:T(8,128)S(1)}, f32[32,128]{1,0:T(8,128)S(1)}, u32[]{:S(2)}, u32[]{:S(2)}) collective-permute-start(f32[32,128]{1,0:T(8,128)S(1)} %get-tuple-element.121), channel_id=1, source_target_pairs={{8,0},{16,8},{24,16},{9,1},{17,9},{25,17},{10,2},{18,10},{26,18},{... | collective-permute-start | bytes 49160 | tf_op jit(solution)/shard_map/ppermute | solution.py:107
  126.8 12.9 %collective-permute-start.16 = (f32[32,128]{1,0:T(8,128)S(1)}, f32[32,128]{1,0:T(8,128)S(1)}, u32[]{:S(2)}, u32[]{:S(2)}) collective-permute-start(f32[32,128]{1,0:T(8,128)S(1)} %get-tuple-element.120), channel_id=1, source_target_pairs={{0,8},{8,16},{16,24},{1,9},{9,17},{17,25},{2,10},{10,18},{18,26},{... | collective-permute-start | bytes 49160 | tf_op jit(solution)/shard_map/ppermute | solution.py:107
  132.2 6.4 %collective-permute-start.17 = (f32[8,128]{1,0:T(8,128)S(1)}, f32[8,128]{1,0:T(8,128)S(1)}, u32[]{:S(2)}, u32[]{:S(2)}) collective-permute-start(f32[8,128]{1,0:T(8,128)S(1)} %bitcast.362), channel_id=1, source_target_pairs={{2,0},{4,2},{6,4},{3,1},{5,3},{7,5},{10,8},{12,10},{14,12},{11,9},... | collective-permute-start | bytes 12296 | tf_op jit(solution)/shard_map/ppermute | solution.py:107
  133.5 6.1 %collective-permute-start.18 = (f32[8,128]{1,0:T(8,128)S(1)}, f32[8,128]{1,0:T(8,128)S(1)}, u32[]{:S(2)}, u32[]{:S(2)}) collective-permute-start(f32[8,128]{1,0:T(8,128)S(1)} %bitcast.360), channel_id=1, source_target_pairs={{0,2},{2,4},{4,6},{1,3},{3,5},{5,7},{8,10},{10,12},{12,14},{9,11},... | collective-permute-start | bytes 12296 | tf_op jit(solution)/shard_map/ppermute | solution.py:107
  149.8 46.2 %all-to-all-start.1 = ((f32[4,32,24,128]{3,0,2,1:T(4,128)}), f32[4,32,24,128]{3,0,2,1:T(4,128)S(1)}, u32[]{:S(2)}, u32[]{:S(2)}) async-start(f32[4,32,24,128]{3,0,2,1:T(4,128)} %select_select_fusion.1), calls=%async_computation.1 | async-start | bytes 3145728 | tf_op jit(solution)/shard_map/all_to_all | solution.py:329
  166.6 29.5 %copy-start.58 = (s32[2048]{0:T(1024)S(1)}, s32[2048]{0:T(1024)}, u32[]{:S(2)}) copy-start(s32[2048]{0:T(1024)} %fusion.84) | copy-start | bytes 24580
  231.5 7.5 %collective-permute-start.24 = (f32[4,32,64]{2,1,0:T(8,128)S(1)}, f32[4,32,64]{2,1,0:T(8,128)S(1)}, u32[]{:S(2)}, u32[]{:S(2)}) collective-permute-start(f32[4,32,64]{2,1,0:T(8,128)S(1)} %broadcast_select_fusion.8), channel_id=1, source_target_pairs={{0,1},{1,0},{2,3},{3,2},{4,5},{5,4},{6,7},{7,6},{8,9},{9,8},{10,11... | collective-permute-start | bytes 98312 | tf_op jit(solution)/shard_map/ppermute | solution.py:102
  232.4 11.5 %collective-permute-start.20 = (f32[4,64,128]{2,1,0:T(8,128)}, f32[4,64,128]{2,1,0:T(8,128)S(1)}, u32[]{:S(2)}, u32[]{:S(2)}) collective-permute-start(f32[4,64,128]{2,1,0:T(8,128)} %get-tuple-element.33), channel_id=1, source_target_pairs={{0,8},{8,16},{16,24},{1,9},{9,17},{17,25},{2,10},{10,18},{18,26},{... | collective-permute-start | bytes 393224 | tf_op jit(solution)/shard_map/ppermute | solution.py:107
  235.1 8.8 %collective-permute-start.21 = (f32[4,64,128]{2,1,0:T(8,128)}, f32[4,64,128]{2,1,0:T(8,128)S(1)}, u32[]{:S(2)}, u32[]{:S(2)}) collective-permute-start(f32[4,64,128]{2,1,0:T(8,128)} %get-tuple-element.34), channel_id=1, source_target_pairs={{8,0},{16,8},{24,16},{9,1},{17,9},{25,17},{10,2},{18,10},{26,18},{... | collective-permute-start | bytes 393224 | tf_op jit(solution)/shard_map/ppermute | solution.py:107
  236.4 3.5 collective-permute-start.22
  237.8 6.2 %collective-permute-start.23 = (f32[4,32,1,128]{3,2,1,0:T(1,128)S(1)}, f32[4,32,1,128]{3,2,1,0:T(1,128)S(1)}, u32[]{:S(2)}, u32[]{:S(2)}) collective-permute-start(f32[4,32,1,128]{3,2,1,0:T(1,128)S(1)} %copy-done.96), channel_id=1, source_target_pairs={{2,0},{4,2},{6,4},{3,1},{5,3},{7,5},{10,8},{12,10},{14,12},{11,9},... | collective-permute-start | bytes 196616 | tf_op jit(solution)/shard_map/ppermute | solution.py:107
  244.6 24.3 %copy-start.23 = (f32[1,8,32,127]{3,2,1,0:T(8,128)S(1)}, f32[1,8,32,127]{3,2,1,0:T(8,128)}, u32[]{:S(2)}) copy-start(f32[1,8,32,127]{3,2,1,0:T(8,128)} %get-tuple-element.115) | copy-start | bytes 390148
  244.6 24.3 %copy-start.43 = (f32[32,128]{1,0:T(8,128)S(1)}, f32[32,128]{1,0:T(8,128)}, u32[]{:S(2)}) copy-start(f32[32,128]{1,0:T(8,128)} %copy-done.42) | copy-start | bytes 49156
  244.6 24.3 %copy-start.45 = (f32[32,128]{1,0:T(8,128)S(1)}, f32[32,128]{1,0:T(8,128)}, u32[]{:S(2)}) copy-start(f32[32,128]{1,0:T(8,128)} %copy-done.44) | copy-start | bytes 49156
  244.7 24.3 %copy-start.65 = (f32[8,128]{1,0:T(8,128)S(1)}, f32[8,128]{1,0:T(8,128)}, u32[]{:S(2)}) copy-start(f32[8,128]{1,0:T(8,128)} %copy-done.64) | copy-start | bytes 12292
  244.7 24.3 %copy-start.67 = (f32[8,128]{1,0:T(8,128)S(1)}, f32[8,128]{1,0:T(8,128)}, u32[]{:S(2)}) copy-start(f32[8,128]{1,0:T(8,128)} %copy-done.66) | copy-start | bytes 12292
  268.8 11.5 %collective-permute-start.29 = (f32[4,32,64]{2,1,0:T(8,128)S(1)}, f32[4,32,64]{2,1,0:T(8,128)S(1)}, u32[]{:S(2)}, u32[]{:S(2)}) collective-permute-start(f32[4,32,64]{2,1,0:T(8,128)S(1)} %broadcast_select_fusion.7), channel_id=1, source_target_pairs={{0,1},{1,0},{2,3},{3,2},{4,5},{5,4},{6,7},{7,6},{8,9},{9,8},{10,11... | collective-permute-start | bytes 98312 | tf_op jit(solution)/shard_map/ppermute | solution.py:102
  270.1 15.0 %collective-permute-start.25 = (f32[4,64,128]{2,1,0:T(8,128)}, f32[4,64,128]{2,1,0:T(8,128)S(1)}, u32[]{:S(2)}, u32[]{:S(2)}) collective-permute-start(f32[4,64,128]{2,1,0:T(8,128)} %get-tuple-element.42), channel_id=1, source_target_pairs={{0,8},{8,16},{16,24},{1,9},{9,17},{17,25},{2,10},{10,18},{18,26},{... | collective-permute-start | bytes 393224 | tf_op jit(solution)/shard_map/ppermute | solution.py:107
  274.7 10.4 %collective-permute-start.26 = (f32[4,64,128]{2,1,0:T(8,128)}, f32[4,64,128]{2,1,0:T(8,128)S(1)}, u32[]{:S(2)}, u32[]{:S(2)}) collective-permute-start(f32[4,64,128]{2,1,0:T(8,128)} %get-tuple-element.43), channel_id=1, source_target_pairs={{8,0},{16,8},{24,16},{9,1},{17,9},{25,17},{10,2},{18,10},{26,18},{... | collective-permute-start | bytes 393224 | tf_op jit(solution)/shard_map/ppermute | solution.py:107
  276.0 5.0 %collective-permute-start.27 = (f32[4,32,1,128]{3,2,1,0:T(1,128)}, f32[4,32,1,128]{3,2,1,0:T(1,128)S(1)}, u32[]{:S(2)}, u32[]{:S(2)}) collective-permute-start(f32[4,32,1,128]{3,2,1,0:T(1,128)} %get-tuple-element.44), channel_id=1, source_target_pairs={{0,2},{2,4},{4,6},{1,3},{3,5},{5,7},{8,10},{10,12},{12,14},{9,11},... | collective-permute-start | bytes 196616 | tf_op jit(solution)/shard_map/ppermute | solution.py:107
  278.7 6.4 %collective-permute-start.28 = (f32[4,32,1,128]{3,2,1,0:T(1,128)}, f32[4,32,1,128]{3,2,1,0:T(1,128)S(1)}, u32[]{:S(2)}, u32[]{:S(2)}) collective-permute-start(f32[4,32,1,128]{3,2,1,0:T(1,128)} %get-tuple-element.45), channel_id=1, source_target_pairs={{2,0},{4,2},{6,4},{3,1},{5,3},{7,5},{10,8},{12,10},{14,12},{11,9},... | collective-permute-start | bytes 196616 | tf_op jit(solution)/shard_map/ppermute | solution.py:107
  309.9 12.9 %collective-permute-start.34 = (f32[4,32,64]{2,1,0:T(8,128)S(1)}, f32[4,32,64]{2,1,0:T(8,128)S(1)}, u32[]{:S(2)}, u32[]{:S(2)}) collective-permute-start(f32[4,32,64]{2,1,0:T(8,128)S(1)} %broadcast_select_fusion.6), channel_id=1, source_target_pairs={{0,1},{1,0},{2,3},{3,2},{4,5},{5,4},{6,7},{7,6},{8,9},{9,8},{10,11... | collective-permute-start | bytes 98312 | tf_op jit(solution)/shard_map/ppermute | solution.py:102
  311.8 15.9 %collective-permute-start.30 = (f32[4,64,128]{2,1,0:T(8,128)S(1)}, f32[4,64,128]{2,1,0:T(8,128)S(1)}, u32[]{:S(2)}, u32[]{:S(2)}) collective-permute-start(f32[4,64,128]{2,1,0:T(8,128)S(1)} %copy-done.93), channel_id=1, source_target_pairs={{0,8},{8,16},{16,24},{1,9},{9,17},{17,25},{2,10},{10,18},{18,26},{... | collective-permute-start | bytes 393224 | tf_op jit(solution)/shard_map/ppermute | solution.py:107
  316.7 11.0 %collective-permute-start.31 = (f32[4,64,128]{2,1,0:T(8,128)S(1)}, f32[4,64,128]{2,1,0:T(8,128)S(1)}, u32[]{:S(2)}, u32[]{:S(2)}) collective-permute-start(f32[4,64,128]{2,1,0:T(8,128)S(1)} %copy-done.92), channel_id=1, source_target_pairs={{8,0},{16,8},{24,16},{9,1},{17,9},{25,17},{10,2},{18,10},{26,18},{... | collective-permute-start | bytes 393224 | tf_op jit(solution)/shard_map/ppermute | solution.py:107
  318.0 5.5 %collective-permute-start.32 = (f32[4,32,1,128]{3,2,1,0:T(1,128)S(1)}, f32[4,32,1,128]{3,2,1,0:T(1,128)S(1)}, u32[]{:S(2)}, u32[]{:S(2)}) collective-permute-start(f32[4,32,1,128]{3,2,1,0:T(1,128)S(1)} %copy-done.95), channel_id=1, source_target_pairs={{0,2},{2,4},{4,6},{1,3},{3,5},{5,7},{8,10},{10,12},{12,14},{9,11},... | collective-permute-start | bytes 196616 | tf_op jit(solution)/shard_map/ppermute | solution.py:107
  321.5 6.2 %collective-permute-start.33 = (f32[4,32,1,128]{3,2,1,0:T(1,128)S(1)}, f32[4,32,1,128]{3,2,1,0:T(1,128)S(1)}, u32[]{:S(2)}, u32[]{:S(2)}) collective-permute-start(f32[4,32,1,128]{3,2,1,0:T(1,128)S(1)} %copy-done.94), channel_id=1, source_target_pairs={{2,0},{4,2},{6,4},{3,1},{5,3},{7,5},{10,8},{12,10},{14,12},{11,9},... | collective-permute-start | bytes 196616 | tf_op jit(solution)/shard_map/ppermute | solution.py:107
  (89 other events, 508.5 us)

commit v12 on v11

--- a/solution.py
+++ b/solution.py
@@ -128,14 +128,6 @@
     half = nz // 2
     lane = lax.broadcasted_iota(jnp.int32, (ny, nz), 1)
 
-    @pl.when(x == 0)
-    def _():
-        xf_lo[0] = value
-
-    @pl.when(x == nx - 1)
-    def _():
-        xf_hi[0] = value
-
     yf_lo[0, x] = value[0:1, :]
     yf_hi[0, x] = value[ny - 1:ny, :]
     columns = jnp.where(lane == x, pltpu.roll(value, x, 1), columns)
@@ -143,8 +135,10 @@
     return columns
 
 
-def finish_faces(columns, xf_lo, xf_hi, yf_lo, yf_hi, zf_lo, zf_hi):
+def finish_faces(d_out, columns, xf_lo, xf_hi, yf_lo, yf_hi, zf_lo, zf_hi):
     nx = yf_lo.shape[1]
+    xf_lo[0] = d_out[0, 0]
+    xf_hi[0] = d_out[0, nx - 1]
     half = columns.shape[1] // 2
     flipped = columns.T
     zf_lo[0] = flipped[0:nx, :]
@@ -190,7 +184,7 @@
         return write_faces(x, step_dir, carry, *face_out)
 
     columns = lax.fori_loop(0, nx, body, jnp.zeros((ny, nz), jnp.float32), unroll=16)
-    finish_faces(columns, *face_out)
+    finish_faces(d_out, columns, *face_out)
 
 
 def initial_kernel(mid, r_ref, inv_ref, d_out, *face_out):
@@ -202,7 +196,7 @@
         return write_faces(x, step_dir, carry, *face_out)
 
     columns = lax.fori_loop(0, nx, body, jnp.zeros((ny, nz), jnp.float32), unroll=4)
-    finish_faces(columns, *face_out)
+    finish_faces(d_out, columns, *face_out)
 
 
 def specs(shape):

time: 359 us -> 349 us (0.972)
  Pallas kernels: 86.7 us -> 76.8 us
    pallas_call x1, Pallas kernels: 14 us -> 7.94 us  [run_initial(): pl.pallas_call(functools.partial(initial_kernel, mid), grid=(source.shape...]
    pallas_call x3, Pallas kernels: 72.7 us -> 68.9 us  [run_sweep(): pl.pallas_call(functools.partial(sweep_kernel, final), grid=(steps,), in_...]
  transfers between devices with their start and end apart: 37 -> 37, of which waited for: 7 -> 7; matrix products, arithmetic and copies ran while one was open for 18% -> 19% of each run, Pallas kernels for 0% -> 0%
where the time goes in v12:
time: 349 us; the launch traced here: 345 us
  starting transfers between devices  90.8 us (26%)
  Pallas kernels  76.8 us (22%)
  other arithmetic  72.7 us (21%)
  local copies, waits for them, and re-layouts  65.8 us (19%)
  waiting for transfers between devices  36 us (10%)
    pallas_call x3, Pallas kernels, run_sweep(): pl.pallas_call(functools.partial(sweep_kernel, final), grid=(steps,), in_...  68.9 us
    ppermute x14, starting transfers between devices, exchange(): lax.ppermute(top, axis, forward)  58.4 us
    all_to_all x1, waiting for transfers between devices, local(): lax.all_to_all(send_values.reshape(STEPS, devices, capacity, row_len), ('...  21.9 us
    ppermute x14, starting transfers between devices, exchange(): lax.ppermute(bottom, axis, backward)  18.3 us
    gather x2, local copies, waits for them, and re-layouts, local(): jnp.take(received, row_slot, axis=1)  17.7 us
    add x4, other arithmetic, membrane(): steady + (gate_state - steady) * jnp.exp(-DT_HEART / time_const)  16.1 us
    ppermute x14, waiting for transfers between devices, exchange(): lax.ppermute(bottom, axis, backward)  12.3 us
    add x2, other arithmetic, local(): value + jnp.where(tissue == tissue_kind, tissue_sigma[tissue_kind, dim_in...  10.3 us
  transfers between devices with their start and end apart: 37, of which 7 were waited for; matrix products, arithmetic and copies ran while one was open for 19% of the time, Pallas kernels for 0%

profile of v12, /device:TPU:0, one launch (start us, length us, event | category | flops | bytes accessed | tf_op | source)
XLA Modules:
  0.0 345.0 jit_solution(12201496176825001977)
XLA Ops:
  0.6 1.8 fusion.118
  2.4 4.5 %select_add_fusion.1 = (f32[32,64,128]{2,1,0:T(8,128)S(1)}, pred[32,64,128]{2,1,0:T(8,128)(4,1)S(1)}, pred[32,64,128]{2,1,0:T(8,128)(4,1)S(1)}, pred[32,64,128]{2,1,0:T(8,128)(4,1)S(1)}, pred[32,64,128]{2,1,0:T(8,128)(4,1)S(1)}) fusion(f32[]{:T(128)} %bitcast.29, f32[]{:T(128)} %bitcast.28, f32[]{:T(128)} %bitcast.27, f32[]{:T(128)} %bitcast.26, ...), kind=kLoop, calls=%fused_computation.33 | loop fusion | flops 2883584 | bytes 3145744 | tf_op jit(solution)/shard_map/add | solution.py:304
  6.9 5.9 %select_add_fusion.2 = (f32[32,64,128]{2,1,0:T(8,128)S(1)}, f32[32,64,128]{2,1,0:T(8,128)S(1)}) fusion(pred[32,64,128]{2,1,0:T(8,128)(4,1)S(1)} %get-tuple-element.85, pred[32,64,128]{2,1,0:T(8,128)(4,1)S(1)} %get-tuple-element.84, pred[32,64,128]{2,1,0:T(8,128)(4,1)S(1)} %get-tuple-element.83, pred[32,64,128]{2,1,0:T(8,128)(4,1)S(1)} %get-tuple-element.82, ...), kind=kLoop, calls=%fused_computation.34 | loop fusion | flops 3670016 | bytes 3145760 | tf_op jit(solution)/shard_map/add | solution.py:304
  12.9 1.8 fusion.98
  17.1 5.5 %collective-permute-start.3 = (f32[5120]{0:T(1024)}, f32[5120]{0:T(1024)S(1)}, u32[]{:S(2)}, u32[]{:S(2)}) collective-permute-start(f32[5120]{0:T(1024)} %pad_maximum_fusion.5), channel_id=1, source_target_pairs={{0,2},{2,4},{4,6},{1,3},{3,5},{5,7},{8,10},{10,12},{12,14},{9,11},... | collective-permute-start | bytes 61448 | tf_op jit(solution)/shard_map/ppermute | solution.py:107
  23.4 3.8 %collective-permute-start.1 = (f32[12288]{0:T(1024)S(1)}, f32[12288]{0:T(1024)S(1)}, u32[]{:S(2)}, u32[]{:S(2)}) collective-permute-start(f32[12288]{0:T(1024)S(1)} %pad_maximum_fusion.3), channel_id=1, source_target_pairs={{0,8},{8,16},{16,24},{1,9},{9,17},{17,25},{2,10},{10,18},{18,26},{... | collective-permute-start | bytes 147464 | tf_op jit(solution)/shard_map/ppermute | solution.py:107
  36.0 5.0 %gather_fusion = s32[768]{0:T(1024)S(1)} fusion(s32[256]{0:T(256)S(1)} %reshape.1868, s32[1024]{0:T(1024)S(1)} %pad_clamp_fusion), kind=kCustom, calls=%fused_computation | custom fusion | bytes 9216 | tf_op jit(solution)/shard_map/gather | solution.py:292
  41.7 6.1 %all-to-all-start = ((s32[32,1,24]{2,1,0:T(1,128)}), s32[32,1,24]{2,1,0:T(1,128)S(1)}, u32[]{:S(2)}, u32[]{:S(2)}) async-start(s32[32,1,24]{2,1,0:T(1,128)} %bitcast.116), calls=%async_computation | async-start | bytes 32768 | tf_op jit(solution)/shard_map/all_to_all | solution.py:293
  47.8 1.5 fusion.100
  49.3 1.6 fusion.101
  50.9 1.7 fusion.99
  55.1 1.5 multiply_add_fusion.3
  59.4 2.8 iota_reduce_fusion
  66.5 1.8 slice.567
  68.3 1.9 slice.568
  75.0 1.4 fusion.18
  76.5 2.8 multiply_add_fusion.2
  81.5 4.5 %collective-permute-start.6 = (f32[32,128]{1,0:T(8,128)S(1)}, f32[32,128]{1,0:T(8,128)S(1)}, u32[]{:S(2)}, u32[]{:S(2)}) collective-permute-start(f32[32,128]{1,0:T(8,128)S(1)} %get-tuple-element.152), channel_id=1, source_target_pairs={{0,8},{8,16},{16,24},{1,9},{9,17},{17,25},{2,10},{10,18},{18,26},{... | collective-permute-start | bytes 49160 | tf_op jit(solution)/shard_map/ppermute | solution.py:107
  87.3 4.5 %collective-permute-start.8 = (f32[8,128]{1,0:T(8,128)S(1)}, f32[8,128]{1,0:T(8,128)S(1)}, u32[]{:S(2)}, u32[]{:S(2)}) collective-permute-start(f32[8,128]{1,0:T(8,128)S(1)} %bitcast.357), channel_id=1, source_target_pairs={{0,2},{2,4},{4,6},{1,3},{3,5},{5,7},{8,10},{10,12},{12,14},{9,11},... | collective-permute-start | bytes 12296 | tf_op jit(solution)/shard_map/ppermute | solution.py:107
  100.4 1.4 fusion.33
  101.9 4.2 %multiply_add_fusion.1 = f32[18,8,32,128]{3,2,1,0:T(8,128)S(1)} fusion(f32[8,32,128]{2,1,0:T(8,128)S(1)} %bitcast.299, f32[18]{0:T(128)S(1)} %copy-done.84, f32[18]{0:T(128)S(1)} %copy-done.87, f32[18]{0:T(128)S(1)} %copy-done.90, f32[8,32,128]{2,1,0:T(8,128)S(1)} %bitcast.291, f32[19,8,32,128]{3,2,1,0:T(8,128)S(1)} %copy-done.4, ...), kind=kLoop, calls=%fused_computation.9 | loop fusion | flops 19464192 | bytes 5112024 | tf_op jit(solution)/shard_map/add | solution.py:59
  109.3 5.1 %collective-permute-start.11 = (f32[32,128]{1,0:T(8,128)S(1)}, f32[32,128]{1,0:T(8,128)S(1)}, u32[]{:S(2)}, u32[]{:S(2)}) collective-permute-start(f32[32,128]{1,0:T(8,128)S(1)} %get-tuple-element.136), channel_id=1, source_target_pairs={{0,8},{8,16},{16,24},{1,9},{9,17},{17,25},{2,10},{10,18},{18,26},{... | collective-permute-start | bytes 49160 | tf_op jit(solution)/shard_map/ppermute | solution.py:107
  115.7 4.8 %collective-permute-start.13 = (f32[8,128]{1,0:T(8,128)S(1)}, f32[8,128]{1,0:T(8,128)S(1)}, u32[]{:S(2)}, u32[]{:S(2)}) collective-permute-start(f32[8,128]{1,0:T(8,128)S(1)} %bitcast.359), channel_id=1, source_target_pairs={{0,2},{2,4},{4,6},{1,3},{3,5},{5,7},{8,10},{10,12},{12,14},{9,11},... | collective-permute-start | bytes 12296 | tf_op jit(solution)/shard_map/ppermute | solution.py:107
  126.8 5.4 %collective-permute-start.16 = (f32[32,128]{1,0:T(8,128)S(1)}, f32[32,128]{1,0:T(8,128)S(1)}, u32[]{:S(2)}, u32[]{:S(2)}) collective-permute-start(f32[32,128]{1,0:T(8,128)S(1)} %get-tuple-element.120), channel_id=1, source_target_pairs={{0,8},{8,16},{16,24},{1,9},{9,17},{17,25},{2,10},{10,18},{18,26},{... | collective-permute-start | bytes 49160 | tf_op jit(solution)/shard_map/ppermute | solution.py:107
  133.5 4.8 %collective-permute-start.18 = (f32[8,128]{1,0:T(8,128)S(1)}, f32[8,128]{1,0:T(8,128)S(1)}, u32[]{:S(2)}, u32[]{:S(2)}) collective-permute-start(f32[8,128]{1,0:T(8,128)S(1)} %bitcast.360), channel_id=1, source_target_pairs={{0,2},{2,4},{4,6},{1,3},{3,5},{5,7},{8,10},{10,12},{12,14},{9,11},... | collective-permute-start | bytes 12296 | tf_op jit(solution)/shard_map/ppermute | solution.py:107
  141.9 3.0 gather_fusion.1
  144.8 4.9 %select_select_fusion.1 = f32[4,32,24,128]{3,0,2,1:T(4,128)} fusion(f32[4,32,24,128]{3,0,2,1:T(4,128)S(1)} %bitcast.285, pred[32,24]{1,0:T(8,128)(4,1)} %broadcast_in_dim.362, pred[32,24]{1,0:T(8,128)(4,1)} %broadcast_in_dim.360), kind=kLoop, calls=%fused_computation.12 | loop fusion | flops 786432 | bytes 3147264 | tf_op jit(solution)/shard_map/jit(_where)/select_n | solution.py:322
  149.8 7.4 %all-to-all-start.1 = ((f32[4,32,24,128]{3,0,2,1:T(4,128)}), f32[4,32,24,128]{3,0,2,1:T(4,128)S(1)}, u32[]{:S(2)}, u32[]{:S(2)}) async-start(f32[4,32,24,128]{3,0,2,1:T(4,128)} %select_select_fusion.1), calls=%async_computation.1 | async-start | bytes 3145728 | tf_op jit(solution)/shard_map/all_to_all | solution.py:323
  157.2 7.1 %broadcast_divide_fusion = (f32[32,64,128]{2,1,0:T(8,128)}, f32[32,64,128]{2,1,0:T(8,128)}, f32[32,64,128]{2,1,0:T(8,128)}, f32[32,64,128]{2,1,0:T(8,128)}, f32[...) fusion(f32[32,64,128]{2,1,0:T(8,128)} %copy-done.1, ...), kind=kLoop, calls=%fused_computation.40 | loop fusion | flops 6553600 | bytes 17825792 | tf_op jit(solution)/shard_map/div | solution.py:343
  166.6 7.5 %multiply_add_fusion = f32[18,8,32,128]{3,2,1,0:T(8,128)} fusion(f32[8,32,128]{2,1,0:T(8,128)S(1)} %bitcast.302, f32[18]{0:T(128)} %param.18, f32[18]{0:T(128)} %param.16, f32[18]{0:T(128)} %copy-done.88, f32[8,32,128]{2,1,0:T(8,128)S(1)} %bitcast.301, f32[8,32,128]{2,1,0:T(8,128)S(1)} %bitcast.292, f32[19,8,32,128]{3,2,1,0:T(8,128)} %param.14, ...), kind=kLoop, calls=%fused_computation.8 | loop fusion | flops 25952256 | bytes 5243096 | tf_op jit(solution)/shard_map/add | solution.py:59
  174.1 21.9 %all-to-all-done.1 = f32[4,32,24,128]{3,0,2,1:T(4,128)S(1)} async-done(((f32[4,32,24,128]{3,0,2,1:T(4,128)}), f32[4,32,24,128]{3,0,2,1:T(4,128)S(1)}, u32[]{:S(2)}, u32[]{:S(2)}) %all-to-all-start.1) | async-done | bytes 1572896 | tf_op jit(solution)/shard_map/all_to_all | solution.py:323
  196.0 15.2 %gather_fusion.2 = f32[2048,4,128]{2,1,0:T(4,128)} fusion(f32[4,768,128]{2,0,1:T(4,128)S(1)} %bitcast.282, s32[2048]{0:T(1024)S(1)} %copy-done.58), kind=kCustom, calls=%fused_computation.2 | custom fusion | bytes 8396800 | tf_op jit(solution)/shard_map/jit(_take)/gather | solution.py:330
  211.3 2.5 copy.1555
  213.8 2.8 select_select_fusion.r_ref
  216.6 7.9 %chebyshev_start.1 = (f32[4,32,64,128]{3,2,1,0:T(8,128)}, f32[4,64,128]{2,1,0:T(8,128)}, f32[4,64,128]{2,1,0:T(8,128)}, f32[4,32,1,128]{3,2,1,0:T(1,128)}, f32[4...) custom-call(f32[4,32,64,128]{3,2,1,0:T(8,128)} %select_select_fusion.r_ref, ...), custom_call_target="tpu_custom_call" | custom-call | flops 2097152 | bytes 9437184 | tf_op jit(solution)/shard_map/chebyshev_start/pallas_call | solution.py:225
  226.4 2.7 collective-permute-start.20
  233.9 4.0 %collective-permute-done.23.yhi = f32[4,32,1,128]{3,2,1,0:T(1,128)S(1)} collective-permute-done((f32[4,32,1,128]{3,2,1,0:T(1,128)S(1)}, f32[4,32,1,128]{3,2,1,0:T(1,128)S(1)}, u32[]{:S(2)}, u32[]{:S(2)}) %collective-permute-start.23) | collective-permute-done | bytes 65568 | tf_op jit(solution)/shard_map/ppermute | solution.py:107
  238.6 22.4 %chebyshev_sweep.3 = (f32[4,32,64,128]{3,2,1,0:T(8,128)}, f32[4,32,64,128]{3,2,1,0:T(8,128)}, f32[4,32,64,128]{3,2,1,0:T(8,128)}, f32[4,64,128]{2,1,0:T(8,128)},...) custom-call(f32[2]{0:T(128)} %constant.119.clone.coef_ref, ...), custom_call_target="tpu_custom_call" | custom-call | flops 31457280 | bytes 36700160 | tf_op jit(solution)/shard_map/chebyshev_sweep/pallas_call | solution.py:248
  263.2 4.6 %collective-permute-start.25 = (f32[4,64,128]{2,1,0:T(8,128)}, f32[4,64,128]{2,1,0:T(8,128)S(1)}, u32[]{:S(2)}, u32[]{:S(2)}) collective-permute-start(f32[4,64,128]{2,1,0:T(8,128)} %get-tuple-element.42), channel_id=1, source_target_pairs={{0,8},{8,16},{16,24},{1,9},{9,17},{17,25},{2,10},{10,18},{18,26},{... | collective-permute-start | bytes 393224 | tf_op jit(solution)/shard_map/ppermute | solution.py:107
  269.0 2.8 collective-permute-start.27
  271.8 1.6 collective-permute-start.28
  274.0 4.1 %collective-permute-done.28.yhi = f32[4,32,1,128]{3,2,1,0:T(1,128)S(1)} collective-permute-done((f32[4,32,1,128]{3,2,1,0:T(1,128)}, f32[4,32,1,128]{3,2,1,0:T(1,128)S(1)}, u32[]{:S(2)}, u32[]{:S(2)}) %collective-permute-start.28) | collective-permute-done | bytes 65568 | tf_op jit(solution)/shard_map/ppermute | solution.py:107
  278.9 22.3 %chebyshev_sweep.4 = (f32[4,32,64,128]{3,2,1,0:T(8,128)}, f32[4,32,64,128]{3,2,1,0:T(8,128)}, f32[4,32,64,128]{3,2,1,0:T(8,128)}, f32[4,64,128]{2,1,0:T(8,128)},...) custom-call(f32[2]{0:T(128)} %constant.120.clone.coef_ref, ...), custom_call_target="tpu_custom_call" | custom-call | flops 31457280 | bytes 36700160 | tf_op jit(solution)/shard_map/chebyshev_sweep/pallas_call | solution.py:248
  302.1 1.8 pad_maximum_fusion
  303.9 4.9 %collective-permute-start.30 = (f32[4,64,128]{2,1,0:T(8,128)S(1)}, f32[4,64,128]{2,1,0:T(8,128)S(1)}, u32[]{:S(2)}, u32[]{:S(2)}) collective-permute-start(f32[4,64,128]{2,1,0:T(8,128)S(1)} %copy-done.93), channel_id=1, source_target_pairs={{0,8},{8,16},{16,24},{1,9},{9,17},{17,25},{2,10},{10,18},{18,26},{... | collective-permute-start | bytes 393224 | tf_op jit(solution)/shard_map/ppermute | solution.py:107
  310.1 3.5 %collective-permute-start.32 = (f32[4,32,1,128]{3,2,1,0:T(1,128)S(1)}, f32[4,32,1,128]{3,2,1,0:T(1,128)S(1)}, u32[]{:S(2)}, u32[]{:S(2)}) collective-permute-start(f32[4,32,1,128]{3,2,1,0:T(1,128)S(1)} %copy-done.95), channel_id=1, source_target_pairs={{0,2},{2,4},{4,6},{1,3},{3,5},{5,7},{8,10},{10,12},{12,14},{9,11},... | collective-permute-start | bytes 196616 | tf_op jit(solution)/shard_map/ppermute | solution.py:107
  315.7 4.2 %collective-permute-done.33.yhi = f32[4,32,1,128]{3,2,1,0:T(1,128)S(1)} collective-permute-done((f32[4,32,1,128]{3,2,1,0:T(1,128)S(1)}, f32[4,32,1,128]{3,2,1,0:T(1,128)S(1)}, u32[]{:S(2)}, u32[]{:S(2)}) %collective-permute-start.33) | collective-permute-done | bytes 65568 | tf_op jit(solution)/shard_map/ppermute | solution.py:107
  320.6 24.3 %chebyshev_sweep.5 = (f32[4,32,64,128]{3,2,1,0:T(8,128)}, f32[4,32,64,128]{3,2,1,0:T(8,128)}, f32[32,64,4,128]{3,2,1,0:T(4,128)}, f32[4,64,128]{2,1,0:T(8,128)},...) custom-call(f32[2]{0:T(128)} %constant.121.clone.coef_ref, ...), custom_call_target="tpu_custom_call" | custom-call | flops 31457280 | bytes 36700160 | tf_op jit(solution)/shard_map/chebyshev_sweep/pallas_call | solution.py:248
  (378 shorter events, 72.8 us)
Async XLA Ops:
  12.8 35.0 %copy-start = (f32[32,64,128]{2,1,0:T(8,128)}, f32[32,64,128]{2,1,0:T(8,128)S(1)}, u32[]{:S(2)}) copy-start(f32[32,64,128]{2,1,0:T(8,128)S(1)} %get-tuple-element.102) | copy-start | bytes 3145732
  12.8 36.5 %copy-start.1 = (f32[32,64,128]{2,1,0:T(8,128)}, f32[32,64,128]{2,1,0:T(8,128)S(1)}, u32[]{:S(2)}) copy-start(f32[32,64,128]{2,1,0:T(8,128)S(1)} %get-tuple-element.103) | copy-start | bytes 3145732
  15.2 55.3 %collective-permute-start.2 = (f32[5120]{0:T(1024)}, f32[5120]{0:T(1024)S(1)}, u32[]{:S(2)}, u32[]{:S(2)}) collective-permute-start(f32[5120]{0:T(1024)} %pad_maximum_fusion.4), channel_id=1, source_target_pairs={{2,0},{4,2},{6,4},{3,1},{5,3},{7,5},{10,8},{12,10},{14,12},{11,9},... | collective-permute-start | bytes 61448 | tf_op jit(solution)/shard_map/ppermute | solution.py:107
  17.1 53.4 %collective-permute-start.3 = (f32[5120]{0:T(1024)}, f32[5120]{0:T(1024)S(1)}, u32[]{:S(2)}, u32[]{:S(2)}) collective-permute-start(f32[5120]{0:T(1024)} %pad_maximum_fusion.5), channel_id=1, source_target_pairs={{0,2},{2,4},{4,6},{1,3},{3,5},{5,7},{8,10},{10,12},{12,14},{9,11},... | collective-permute-start | bytes 61448 | tf_op jit(solution)/shard_map/ppermute | solution.py:107
  23.4 47.7 %collective-permute-start.1 = (f32[12288]{0:T(1024)S(1)}, f32[12288]{0:T(1024)S(1)}, u32[]{:S(2)}, u32[]{:S(2)}) collective-permute-start(f32[12288]{0:T(1024)S(1)} %pad_maximum_fusion.3), channel_id=1, source_target_pairs={{0,8},{8,16},{16,24},{1,9},{9,17},{17,25},{2,10},{10,18},{18,26},{... | collective-permute-start | bytes 147464 | tf_op jit(solution)/shard_map/ppermute | solution.py:107
  27.9 43.3 %collective-permute-start = (f32[12288]{0:T(1024)}, f32[12288]{0:T(1024)S(1)}, u32[]{:S(2)}, u32[]{:S(2)}) collective-permute-start(f32[12288]{0:T(1024)} %pad_maximum_fusion.2), channel_id=1, source_target_pairs={{8,0},{16,8},{24,16},{9,1},{17,9},{25,17},{10,2},{18,10},{26,18},{... | collective-permute-start | bytes 147464 | tf_op jit(solution)/shard_map/ppermute | solution.py:107
  31.2 33.7 %collective-permute-start.4 = (f32[2304]{0:T(1024)}, f32[2304]{0:T(1024)}, u32[]{:S(2)}, u32[]{:S(2)}) collective-permute-start(f32[2304]{0:T(1024)} %maximum_select_fusion), channel_id=1, source_target_pairs={{0,1},{1,0},{2,3},{3,2},{4,5},{5,4},{6,7},{7,6},{8,9},{9,8},{10,11... | collective-permute-start | bytes 27656 | tf_op jit(solution)/shard_map/ppermute | solution.py:102
  41.7 16.9 %all-to-all-start = ((s32[32,1,24]{2,1,0:T(1,128)}), s32[32,1,24]{2,1,0:T(1,128)S(1)}, u32[]{:S(2)}, u32[]{:S(2)}) async-start(s32[32,1,24]{2,1,0:T(1,128)} %bitcast.116), calls=%async_computation | async-start | bytes 32768 | tf_op jit(solution)/shard_map/all_to_all | solution.py:293
  55.0 51.0 %copy-start.8 = (pred[8,32,128]{2,1,0:T(8,128)(4,1)}, pred[8,32,128]{2,1,0:T(8,128)(4,1)S(1)}, u32[]{:S(2)}) copy-start(pred[8,32,128]{2,1,0:T(8,128)(4,1)S(1)} %get-tuple-element.162) | copy-start | bytes 98308
  55.0 51.0 %copy-start.10 = (pred[8,32,128]{2,1,0:T(8,128)(4,1)}, pred[8,32,128]{2,1,0:T(8,128)(4,1)S(1)}, u32[]{:S(2)}) copy-start(pred[8,32,128]{2,1,0:T(8,128)(4,1)S(1)} %get-tuple-element.163) | copy-start | bytes 98308
  55.0 51.0 %copy-start.12 = (pred[8,32,128]{2,1,0:T(8,128)(4,1)}, pred[8,32,128]{2,1,0:T(8,128)(4,1)S(1)}, u32[]{:S(2)}) copy-start(pred[8,32,128]{2,1,0:T(8,128)(4,1)S(1)} %get-tuple-element.164) | copy-start | bytes 98308
  79.9 13.3 %collective-permute-start.9 = (f32[8,32]{1,0:T(8,128)S(1)}, f32[8,32]{1,0:T(8,128)S(1)}, u32[]{:S(2)}, u32[]{:S(2)}) collective-permute-start(f32[8,32]{1,0:T(8,128)S(1)} %fusion.10), channel_id=1, source_target_pairs={{0,1},{1,0},{2,3},{3,2},{4,5},{5,4},{6,7},{7,6},{8,9},{9,8},{10,11... | collective-permute-start | bytes 3080 | tf_op jit(solution)/shard_map/ppermute | solution.py:102
  80.2 16.4 %collective-permute-start.5 = (f32[32,128]{1,0:T(8,128)S(1)}, f32[32,128]{1,0:T(8,128)S(1)}, u32[]{:S(2)}, u32[]{:S(2)}) collective-permute-start(f32[32,128]{1,0:T(8,128)S(1)} %get-tuple-element.153), channel_id=1, source_target_pairs={{8,0},{16,8},{24,16},{9,1},{17,9},{25,17},{10,2},{18,10},{26,18},{... | collective-permute-start | bytes 49160 | tf_op jit(solution)/shard_map/ppermute | solution.py:107
  81.5 15.1 %collective-permute-start.6 = (f32[32,128]{1,0:T(8,128)S(1)}, f32[32,128]{1,0:T(8,128)S(1)}, u32[]{:S(2)}, u32[]{:S(2)}) collective-permute-start(f32[32,128]{1,0:T(8,128)S(1)} %get-tuple-element.152), channel_id=1, source_target_pairs={{0,8},{8,16},{16,24},{1,9},{9,17},{17,25},{2,10},{10,18},{18,26},{... | collective-permute-start | bytes 49160 | tf_op jit(solution)/shard_map/ppermute | solution.py:107
  86.0 10.5 %collective-permute-start.7 = (f32[8,128]{1,0:T(8,128)S(1)}, f32[8,128]{1,0:T(8,128)S(1)}, u32[]{:S(2)}, u32[]{:S(2)}) collective-permute-start(f32[8,128]{1,0:T(8,128)S(1)} %bitcast.358), channel_id=1, source_target_pairs={{2,0},{4,2},{6,4},{3,1},{5,3},{7,5},{10,8},{12,10},{14,12},{11,9},... | collective-permute-start | bytes 12296 | tf_op jit(solution)/shard_map/ppermute | solution.py:107
  87.3 9.2 %collective-permute-start.8 = (f32[8,128]{1,0:T(8,128)S(1)}, f32[8,128]{1,0:T(8,128)S(1)}, u32[]{:S(2)}, u32[]{:S(2)}) collective-permute-start(f32[8,128]{1,0:T(8,128)S(1)} %bitcast.357), channel_id=1, source_target_pairs={{0,2},{2,4},{4,6},{1,3},{3,5},{5,7},{8,10},{10,12},{12,14},{9,11},... | collective-permute-start | bytes 12296 | tf_op jit(solution)/shard_map/ppermute | solution.py:107
  106.6 13.9 %collective-permute-start.14 = (f32[8,32]{1,0:T(8,128)S(1)}, f32[8,32]{1,0:T(8,128)S(1)}, u32[]{:S(2)}, u32[]{:S(2)}) collective-permute-start(f32[8,32]{1,0:T(8,128)S(1)} %fusion.9), channel_id=1, source_target_pairs={{0,1},{1,0},{2,3},{3,2},{4,5},{5,4},{6,7},{7,6},{8,9},{9,8},{10,11... | collective-permute-start | bytes 3080 | tf_op jit(solution)/shard_map/ppermute | solution.py:102
  108.0 13.6 %collective-permute-start.10 = (f32[32,128]{1,0:T(8,128)S(1)}, f32[32,128]{1,0:T(8,128)S(1)}, u32[]{:S(2)}, u32[]{:S(2)}) collective-permute-start(f32[32,128]{1,0:T(8,128)S(1)} %get-tuple-element.137), channel_id=1, source_target_pairs={{8,0},{16,8},{24,16},{9,1},{17,9},{25,17},{10,2},{18,10},{26,18},{... | collective-permute-start | bytes 49160 | tf_op jit(solution)/shard_map/ppermute | solution.py:107
  109.3 12.3 %collective-permute-start.11 = (f32[32,128]{1,0:T(8,128)S(1)}, f32[32,128]{1,0:T(8,128)S(1)}, u32[]{:S(2)}, u32[]{:S(2)}) collective-permute-start(f32[32,128]{1,0:T(8,128)S(1)} %get-tuple-element.136), channel_id=1, source_target_pairs={{0,8},{8,16},{16,24},{1,9},{9,17},{17,25},{2,10},{10,18},{18,26},{... | collective-permute-start | bytes 49160 | tf_op jit(solution)/shard_map/ppermute | solution.py:107
  114.4 6.7 %collective-permute-start.12 = (f32[8,128]{1,0:T(8,128)S(1)}, f32[8,128]{1,0:T(8,128)S(1)}, u32[]{:S(2)}, u32[]{:S(2)}) collective-permute-start(f32[8,128]{1,0:T(8,128)S(1)} %bitcast.361), channel_id=1, source_target_pairs={{2,0},{4,2},{6,4},{3,1},{5,3},{7,5},{10,8},{12,10},{14,12},{11,9},... | collective-permute-start | bytes 12296 | tf_op jit(solution)/shard_map/ppermute | solution.py:107
  115.7 5.9 %collective-permute-start.13 = (f32[8,128]{1,0:T(8,128)S(1)}, f32[8,128]{1,0:T(8,128)S(1)}, u32[]{:S(2)}, u32[]{:S(2)}) collective-permute-start(f32[8,128]{1,0:T(8,128)S(1)} %bitcast.359), channel_id=1, source_target_pairs={{0,2},{2,4},{4,6},{1,3},{3,5},{5,7},{8,10},{10,12},{12,14},{9,11},... | collective-permute-start | bytes 12296 | tf_op jit(solution)/shard_map/ppermute | solution.py:107
  125.4 13.0 %collective-permute-start.19 = (f32[8,32]{1,0:T(8,128)S(1)}, f32[8,32]{1,0:T(8,128)S(1)}, u32[]{:S(2)}, u32[]{:S(2)}) collective-permute-start(f32[8,32]{1,0:T(8,128)S(1)} %fusion.8), channel_id=1, source_target_pairs={{0,1},{1,0},{2,3},{3,2},{4,5},{5,4},{6,7},{7,6},{8,9},{9,8},{10,11... | collective-permute-start | bytes 3080 | tf_op jit(solution)/shard_map/ppermute | solution.py:102
  125.5 14.2 %collective-permute-start.15 = (f32[32,128]{1,0:T(8,128)S(1)}, f32[32,128]{1,0:T(8,128)S(1)}, u32[]{:S(2)}, u32[]{:S(2)}) collective-permute-start(f32[32,128]{1,0:T(8,128)S(1)} %get-tuple-element.121), channel_id=1, source_target_pairs={{8,0},{16,8},{24,16},{9,1},{17,9},{25,17},{10,2},{18,10},{26,18},{... | collective-permute-start | bytes 49160 | tf_op jit(solution)/shard_map/ppermute | solution.py:107
  126.8 12.9 %collective-permute-start.16 = (f32[32,128]{1,0:T(8,128)S(1)}, f32[32,128]{1,0:T(8,128)S(1)}, u32[]{:S(2)}, u32[]{:S(2)}) collective-permute-start(f32[32,128]{1,0:T(8,128)S(1)} %get-tuple-element.120), channel_id=1, source_target_pairs={{0,8},{8,16},{16,24},{1,9},{9,17},{17,25},{2,10},{10,18},{18,26},{... | collective-permute-start | bytes 49160 | tf_op jit(solution)/shard_map/ppermute | solution.py:107
  132.2 6.4 %collective-permute-start.17 = (f32[8,128]{1,0:T(8,128)S(1)}, f32[8,128]{1,0:T(8,128)S(1)}, u32[]{:S(2)}, u32[]{:S(2)}) collective-permute-start(f32[8,128]{1,0:T(8,128)S(1)} %bitcast.362), channel_id=1, source_target_pairs={{2,0},{4,2},{6,4},{3,1},{5,3},{7,5},{10,8},{12,10},{14,12},{11,9},... | collective-permute-start | bytes 12296 | tf_op jit(solution)/shard_map/ppermute | solution.py:107
  133.5 6.1 %collective-permute-start.18 = (f32[8,128]{1,0:T(8,128)S(1)}, f32[8,128]{1,0:T(8,128)S(1)}, u32[]{:S(2)}, u32[]{:S(2)}) collective-permute-start(f32[8,128]{1,0:T(8,128)S(1)} %bitcast.360), channel_id=1, source_target_pairs={{0,2},{2,4},{4,6},{1,3},{3,5},{5,7},{8,10},{10,12},{12,14},{9,11},... | collective-permute-start | bytes 12296 | tf_op jit(solution)/shard_map/ppermute | solution.py:107
  149.8 46.2 %all-to-all-start.1 = ((f32[4,32,24,128]{3,0,2,1:T(4,128)}), f32[4,32,24,128]{3,0,2,1:T(4,128)S(1)}, u32[]{:S(2)}, u32[]{:S(2)}) async-start(f32[4,32,24,128]{3,0,2,1:T(4,128)} %select_select_fusion.1), calls=%async_computation.1 | async-start | bytes 3145728 | tf_op jit(solution)/shard_map/all_to_all | solution.py:323
  166.6 29.5 %copy-start.58 = (s32[2048]{0:T(1024)S(1)}, s32[2048]{0:T(1024)}, u32[]{:S(2)}) copy-start(s32[2048]{0:T(1024)} %fusion.84) | copy-start | bytes 24580
  225.5 7.5 %collective-permute-start.24 = (f32[4,32,64]{2,1,0:T(8,128)S(1)}, f32[4,32,64]{2,1,0:T(8,128)S(1)}, u32[]{:S(2)}, u32[]{:S(2)}) collective-permute-start(f32[4,32,64]{2,1,0:T(8,128)S(1)} %broadcast_select_fusion.8), channel_id=1, source_target_pairs={{0,1},{1,0},{2,3},{3,2},{4,5},{5,4},{6,7},{7,6},{8,9},{9,8},{10,11... | collective-permute-start | bytes 98312 | tf_op jit(solution)/shard_map/ppermute | solution.py:102
  226.4 11.5 %collective-permute-start.20 = (f32[4,64,128]{2,1,0:T(8,128)}, f32[4,64,128]{2,1,0:T(8,128)S(1)}, u32[]{:S(2)}, u32[]{:S(2)}) collective-permute-start(f32[4,64,128]{2,1,0:T(8,128)} %get-tuple-element.33), channel_id=1, source_target_pairs={{0,8},{8,16},{16,24},{1,9},{9,17},{17,25},{2,10},{10,18},{18,26},{... | collective-permute-start | bytes 393224 | tf_op jit(solution)/shard_map/ppermute | solution.py:107
  229.1 8.8 %collective-permute-start.21 = (f32[4,64,128]{2,1,0:T(8,128)}, f32[4,64,128]{2,1,0:T(8,128)S(1)}, u32[]{:S(2)}, u32[]{:S(2)}) collective-permute-start(f32[4,64,128]{2,1,0:T(8,128)} %get-tuple-element.34), channel_id=1, source_target_pairs={{8,0},{16,8},{24,16},{9,1},{17,9},{25,17},{10,2},{18,10},{26,18},{... | collective-permute-start | bytes 393224 | tf_op jit(solution)/shard_map/ppermute | solution.py:107
  230.4 3.5 %collective-permute-start.22 = (f32[4,32,1,128]{3,2,1,0:T(1,128)}, f32[4,32,1,128]{3,2,1,0:T(1,128)S(1)}, u32[]{:S(2)}, u32[]{:S(2)}) collective-permute-start(f32[4,32,1,128]{3,2,1,0:T(1,128)} %get-tuple-element.35), channel_id=1, source_target_pairs={{0,2},{2,4},{4,6},{1,3},{3,5},{5,7},{8,10},{10,12},{12,14},{9,11},... | collective-permute-start | bytes 196616 | tf_op jit(solution)/shard_map/ppermute | solution.py:107
  231.7 6.2 %collective-permute-start.23 = (f32[4,32,1,128]{3,2,1,0:T(1,128)S(1)}, f32[4,32,1,128]{3,2,1,0:T(1,128)S(1)}, u32[]{:S(2)}, u32[]{:S(2)}) collective-permute-start(f32[4,32,1,128]{3,2,1,0:T(1,128)S(1)} %copy-done.96), channel_id=1, source_target_pairs={{2,0},{4,2},{6,4},{3,1},{5,3},{7,5},{10,8},{12,10},{14,12},{11,9},... | collective-permute-start | bytes 196616 | tf_op jit(solution)/shard_map/ppermute | solution.py:107
  238.6 23.4 %copy-start.23 = (f32[1,8,32,127]{3,2,1,0:T(8,128)S(1)}, f32[1,8,32,127]{3,2,1,0:T(8,128)}, u32[]{:S(2)}) copy-start(f32[1,8,32,127]{3,2,1,0:T(8,128)} %get-tuple-element.115) | copy-start | bytes 390148
  238.6 23.4 %copy-start.43 = (f32[32,128]{1,0:T(8,128)S(1)}, f32[32,128]{1,0:T(8,128)}, u32[]{:S(2)}) copy-start(f32[32,128]{1,0:T(8,128)} %copy-done.42) | copy-start | bytes 49156
  238.6 23.4 %copy-start.45 = (f32[32,128]{1,0:T(8,128)S(1)}, f32[32,128]{1,0:T(8,128)}, u32[]{:S(2)}) copy-start(f32[32,128]{1,0:T(8,128)} %copy-done.44) | copy-start | bytes 49156
  238.6 23.4 %copy-start.65 = (f32[8,128]{1,0:T(8,128)S(1)}, f32[8,128]{1,0:T(8,128)}, u32[]{:S(2)}) copy-start(f32[8,128]{1,0:T(8,128)} %copy-done.64) | copy-start | bytes 12292
  238.6 23.4 %copy-start.67 = (f32[8,128]{1,0:T(8,128)S(1)}, f32[8,128]{1,0:T(8,128)}, u32[]{:S(2)}) copy-start(f32[8,128]{1,0:T(8,128)} %copy-done.66) | copy-start | bytes 12292
  261.8 11.5 %collective-permute-start.29 = (f32[4,32,64]{2,1,0:T(8,128)S(1)}, f32[4,32,64]{2,1,0:T(8,128)S(1)}, u32[]{:S(2)}, u32[]{:S(2)}) collective-permute-start(f32[4,32,64]{2,1,0:T(8,128)S(1)} %broadcast_select_fusion.7), channel_id=1, source_target_pairs={{0,1},{1,0},{2,3},{3,2},{4,5},{5,4},{6,7},{7,6},{8,9},{9,8},{10,11... | collective-permute-start | bytes 98312 | tf_op jit(solution)/shard_map/ppermute | solution.py:102
  263.2 15.0 %collective-permute-start.25 = (f32[4,64,128]{2,1,0:T(8,128)}, f32[4,64,128]{2,1,0:T(8,128)S(1)}, u32[]{:S(2)}, u32[]{:S(2)}) collective-permute-start(f32[4,64,128]{2,1,0:T(8,128)} %get-tuple-element.42), channel_id=1, source_target_pairs={{0,8},{8,16},{16,24},{1,9},{9,17},{17,25},{2,10},{10,18},{18,26},{... | collective-permute-start | bytes 393224 | tf_op jit(solution)/shard_map/ppermute | solution.py:107
  267.7 10.4 %collective-permute-start.26 = (f32[4,64,128]{2,1,0:T(8,128)}, f32[4,64,128]{2,1,0:T(8,128)S(1)}, u32[]{:S(2)}, u32[]{:S(2)}) collective-permute-start(f32[4,64,128]{2,1,0:T(8,128)} %get-tuple-element.43), channel_id=1, source_target_pairs={{8,0},{16,8},{24,16},{9,1},{17,9},{25,17},{10,2},{18,10},{26,18},{... | collective-permute-start | bytes 393224 | tf_op jit(solution)/shard_map/ppermute | solution.py:107
  269.0 5.0 %collective-permute-start.27 = (f32[4,32,1,128]{3,2,1,0:T(1,128)}, f32[4,32,1,128]{3,2,1,0:T(1,128)S(1)}, u32[]{:S(2)}, u32[]{:S(2)}) collective-permute-start(f32[4,32,1,128]{3,2,1,0:T(1,128)} %get-tuple-element.44), channel_id=1, source_target_pairs={{0,2},{2,4},{4,6},{1,3},{3,5},{5,7},{8,10},{10,12},{12,14},{9,11},... | collective-permute-start | bytes 196616 | tf_op jit(solution)/shard_map/ppermute | solution.py:107
  271.8 6.4 %collective-permute-start.28 = (f32[4,32,1,128]{3,2,1,0:T(1,128)}, f32[4,32,1,128]{3,2,1,0:T(1,128)S(1)}, u32[]{:S(2)}, u32[]{:S(2)}) collective-permute-start(f32[4,32,1,128]{3,2,1,0:T(1,128)} %get-tuple-element.45), channel_id=1, source_target_pairs={{2,0},{4,2},{6,4},{3,1},{5,3},{7,5},{10,8},{12,10},{14,12},{11,9},... | collective-permute-start | bytes 196616 | tf_op jit(solution)/shard_map/ppermute | solution.py:107
  302.1 12.9 %collective-permute-start.34 = (f32[4,32,64]{2,1,0:T(8,128)S(1)}, f32[4,32,64]{2,1,0:T(8,128)S(1)}, u32[]{:S(2)}, u32[]{:S(2)}) collective-permute-start(f32[4,32,64]{2,1,0:T(8,128)S(1)} %broadcast_select_fusion.6), channel_id=1, source_target_pairs={{0,1},{1,0},{2,3},{3,2},{4,5},{5,4},{6,7},{7,6},{8,9},{9,8},{10,11... | collective-permute-start | bytes 98312 | tf_op jit(solution)/shard_map/ppermute | solution.py:102
  303.9 15.9 %collective-permute-start.30 = (f32[4,64,128]{2,1,0:T(8,128)S(1)}, f32[4,64,128]{2,1,0:T(8,128)S(1)}, u32[]{:S(2)}, u32[]{:S(2)}) collective-permute-start(f32[4,64,128]{2,1,0:T(8,128)S(1)} %copy-done.93), channel_id=1, source_target_pairs={{0,8},{8,16},{16,24},{1,9},{9,17},{17,25},{2,10},{10,18},{18,26},{... | collective-permute-start | bytes 393224 | tf_op jit(solution)/shard_map/ppermute | solution.py:107
  308.8 11.0 %collective-permute-start.31 = (f32[4,64,128]{2,1,0:T(8,128)S(1)}, f32[4,64,128]{2,1,0:T(8,128)S(1)}, u32[]{:S(2)}, u32[]{:S(2)}) collective-permute-start(f32[4,64,128]{2,1,0:T(8,128)S(1)} %copy-done.92), channel_id=1, source_target_pairs={{8,0},{16,8},{24,16},{9,1},{17,9},{25,17},{10,2},{18,10},{26,18},{... | collective-permute-start | bytes 393224 | tf_op jit(solution)/shard_map/ppermute | solution.py:107
  310.1 5.5 %collective-permute-start.32 = (f32[4,32,1,128]{3,2,1,0:T(1,128)S(1)}, f32[4,32,1,128]{3,2,1,0:T(1,128)S(1)}, u32[]{:S(2)}, u32[]{:S(2)}) collective-permute-start(f32[4,32,1,128]{3,2,1,0:T(1,128)S(1)} %copy-done.95), channel_id=1, source_target_pairs={{0,2},{2,4},{4,6},{1,3},{3,5},{5,7},{8,10},{10,12},{12,14},{9,11},... | collective-permute-start | bytes 196616 | tf_op jit(solution)/shard_map/ppermute | solution.py:107
  313.7 6.2 %collective-permute-start.33 = (f32[4,32,1,128]{3,2,1,0:T(1,128)S(1)}, f32[4,32,1,128]{3,2,1,0:T(1,128)S(1)}, u32[]{:S(2)}, u32[]{:S(2)}) collective-permute-start(f32[4,32,1,128]{3,2,1,0:T(1,128)S(1)} %copy-done.94), channel_id=1, source_target_pairs={{2,0},{4,2},{6,4},{3,1},{5,3},{7,5},{10,8},{12,10},{14,12},{11,9},... | collective-permute-start | bytes 196616 | tf_op jit(solution)/shard_map/ppermute | solution.py:107
  (89 other events, 458.3 us)

commit v13 on v12

--- a/solution.py
+++ b/solution.py
@@ -195,7 +195,7 @@
         d_out[0, x] = step_dir
         return write_faces(x, step_dir, carry, *face_out)
 
-    columns = lax.fori_loop(0, nx, body, jnp.zeros((ny, nz), jnp.float32), unroll=4)
+    columns = lax.fori_loop(0, nx, body, jnp.zeros((ny, nz), jnp.float32), unroll=16)
     finish_faces(d_out, columns, *face_out)
 
 

time: 349 us -> 348 us (level)
  no operation moved by 1% of the time
where the time goes in v13:
time: 348 us; the launch traced here: 344 us
  starting transfers between devices  90.8 us (26%)
  Pallas kernels  75.5 us (22%)
  other arithmetic  72.7 us (21%)
  local copies, waits for them, and re-layouts  65.8 us (19%)
  waiting for transfers between devices  36 us (10%)
    pallas_call x3, Pallas kernels, run_sweep(): pl.pallas_call(functools.partial(sweep_kernel, final), grid=(steps,), in_...  68.9 us
    ppermute x14, starting transfers between devices, exchange(): lax.ppermute(top, axis, forward)  58.3 us
    all_to_all x1, waiting for transfers between devices, local(): lax.all_to_all(send_values.reshape(STEPS, devices, capacity, row_len), ('...  21.9 us
    ppermute x14, starting transfers between devices, exchange(): lax.ppermute(bottom, axis, backward)  18.3 us
    gather x2, local copies, waits for them, and re-layouts, local(): jnp.take(received, row_slot, axis=1)  17.7 us
    add x4, other arithmetic, membrane(): steady + (gate_state - steady) * jnp.exp(-DT_HEART / time_const)  16.1 us
    ppermute x14, waiting for transfers between devices, exchange(): lax.ppermute(bottom, axis, backward)  12.3 us
    add x2, other arithmetic, local(): value + jnp.where(tissue == tissue_kind, tissue_sigma[tissue_kind, dim_in...  10.3 us
  transfers between devices with their start and end apart: 37, of which 7 were waited for; matrix products, arithmetic and copies ran while one was open for 19% of the time, Pallas kernels for 0%

profile of v13, /device:TPU:0, one launch (start us, length us, event | category | flops | bytes accessed | tf_op | source)
XLA Modules:
  0.0 343.8 jit_solution(8679330273745317966)
XLA Ops:
  0.6 1.8 fusion.118
  2.4 4.5 %select_add_fusion.1 = (f32[32,64,128]{2,1,0:T(8,128)S(1)}, pred[32,64,128]{2,1,0:T(8,128)(4,1)S(1)}, pred[32,64,128]{2,1,0:T(8,128)(4,1)S(1)}, pred[32,64,128]{2,1,0:T(8,128)(4,1)S(1)}, pred[32,64,128]{2,1,0:T(8,128)(4,1)S(1)}) fusion(f32[]{:T(128)} %bitcast.29, f32[]{:T(128)} %bitcast.28, f32[]{:T(128)} %bitcast.27, f32[]{:T(128)} %bitcast.26, ...), kind=kLoop, calls=%fused_computation.33 | loop fusion | flops 2883584 | bytes 3145744 | tf_op jit(solution)/shard_map/add | solution.py:304
  6.9 5.9 %select_add_fusion.2 = (f32[32,64,128]{2,1,0:T(8,128)S(1)}, f32[32,64,128]{2,1,0:T(8,128)S(1)}) fusion(pred[32,64,128]{2,1,0:T(8,128)(4,1)S(1)} %get-tuple-element.85, pred[32,64,128]{2,1,0:T(8,128)(4,1)S(1)} %get-tuple-element.84, pred[32,64,128]{2,1,0:T(8,128)(4,1)S(1)} %get-tuple-element.83, pred[32,64,128]{2,1,0:T(8,128)(4,1)S(1)} %get-tuple-element.82, ...), kind=kLoop, calls=%fused_computation.34 | loop fusion | flops 3670016 | bytes 3145760 | tf_op jit(solution)/shard_map/add | solution.py:304
  12.9 1.8 fusion.98
  17.1 5.5 %collective-permute-start.3 = (f32[5120]{0:T(1024)}, f32[5120]{0:T(1024)S(1)}, u32[]{:S(2)}, u32[]{:S(2)}) collective-permute-start(f32[5120]{0:T(1024)} %pad_maximum_fusion.5), channel_id=1, source_target_pairs={{0,2},{2,4},{4,6},{1,3},{3,5},{5,7},{8,10},{10,12},{12,14},{9,11},... | collective-permute-start | bytes 61448 | tf_op jit(solution)/shard_map/ppermute | solution.py:107
  23.4 3.8 %collective-permute-start.1 = (f32[12288]{0:T(1024)S(1)}, f32[12288]{0:T(1024)S(1)}, u32[]{:S(2)}, u32[]{:S(2)}) collective-permute-start(f32[12288]{0:T(1024)S(1)} %pad_maximum_fusion.3), channel_id=1, source_target_pairs={{0,8},{8,16},{16,24},{1,9},{9,17},{17,25},{2,10},{10,18},{18,26},{... | collective-permute-start | bytes 147464 | tf_op jit(solution)/shard_map/ppermute | solution.py:107
  36.0 5.0 %gather_fusion = s32[768]{0:T(1024)S(1)} fusion(s32[256]{0:T(256)S(1)} %reshape.1868, s32[1024]{0:T(1024)S(1)} %pad_clamp_fusion), kind=kCustom, calls=%fused_computation | custom fusion | bytes 9216 | tf_op jit(solution)/shard_map/gather | solution.py:292
  41.7 6.1 %all-to-all-start = ((s32[32,1,24]{2,1,0:T(1,128)}), s32[32,1,24]{2,1,0:T(1,128)S(1)}, u32[]{:S(2)}, u32[]{:S(2)}) async-start(s32[32,1,24]{2,1,0:T(1,128)} %bitcast.116), calls=%async_computation | async-start | bytes 32768 | tf_op jit(solution)/shard_map/all_to_all | solution.py:293
  47.8 1.5 fusion.100
  49.3 1.6 fusion.101
  50.9 1.7 fusion.99
  55.1 1.5 multiply_add_fusion.3
  59.4 2.8 iota_reduce_fusion
  66.5 1.8 slice.567
  68.3 1.9 slice.568
  75.0 1.4 fusion.18
  76.5 2.8 multiply_add_fusion.2
  81.5 4.5 %collective-permute-start.6 = (f32[32,128]{1,0:T(8,128)S(1)}, f32[32,128]{1,0:T(8,128)S(1)}, u32[]{:S(2)}, u32[]{:S(2)}) collective-permute-start(f32[32,128]{1,0:T(8,128)S(1)} %get-tuple-element.152), channel_id=1, source_target_pairs={{0,8},{8,16},{16,24},{1,9},{9,17},{17,25},{2,10},{10,18},{18,26},{... | collective-permute-start | bytes 49160 | tf_op jit(solution)/shard_map/ppermute | solution.py:107
  87.3 4.5 %collective-permute-start.8 = (f32[8,128]{1,0:T(8,128)S(1)}, f32[8,128]{1,0:T(8,128)S(1)}, u32[]{:S(2)}, u32[]{:S(2)}) collective-permute-start(f32[8,128]{1,0:T(8,128)S(1)} %bitcast.357), channel_id=1, source_target_pairs={{0,2},{2,4},{4,6},{1,3},{3,5},{5,7},{8,10},{10,12},{12,14},{9,11},... | collective-permute-start | bytes 12296 | tf_op jit(solution)/shard_map/ppermute | solution.py:107
  100.4 1.4 fusion.33
  101.9 4.2 %multiply_add_fusion.1 = f32[18,8,32,128]{3,2,1,0:T(8,128)S(1)} fusion(f32[8,32,128]{2,1,0:T(8,128)S(1)} %bitcast.299, f32[18]{0:T(128)S(1)} %copy-done.84, f32[18]{0:T(128)S(1)} %copy-done.87, f32[18]{0:T(128)S(1)} %copy-done.90, f32[8,32,128]{2,1,0:T(8,128)S(1)} %bitcast.291, f32[19,8,32,128]{3,2,1,0:T(8,128)S(1)} %copy-done.4, ...), kind=kLoop, calls=%fused_computation.9 | loop fusion | flops 19464192 | bytes 5112024 | tf_op jit(solution)/shard_map/add | solution.py:59
  109.3 5.1 %collective-permute-start.11 = (f32[32,128]{1,0:T(8,128)S(1)}, f32[32,128]{1,0:T(8,128)S(1)}, u32[]{:S(2)}, u32[]{:S(2)}) collective-permute-start(f32[32,128]{1,0:T(8,128)S(1)} %get-tuple-element.136), channel_id=1, source_target_pairs={{0,8},{8,16},{16,24},{1,9},{9,17},{17,25},{2,10},{10,18},{18,26},{... | collective-permute-start | bytes 49160 | tf_op jit(solution)/shard_map/ppermute | solution.py:107
  115.7 4.8 %collective-permute-start.13 = (f32[8,128]{1,0:T(8,128)S(1)}, f32[8,128]{1,0:T(8,128)S(1)}, u32[]{:S(2)}, u32[]{:S(2)}) collective-permute-start(f32[8,128]{1,0:T(8,128)S(1)} %bitcast.359), channel_id=1, source_target_pairs={{0,2},{2,4},{4,6},{1,3},{3,5},{5,7},{8,10},{10,12},{12,14},{9,11},... | collective-permute-start | bytes 12296 | tf_op jit(solution)/shard_map/ppermute | solution.py:107
  126.8 5.4 %collective-permute-start.16 = (f32[32,128]{1,0:T(8,128)S(1)}, f32[32,128]{1,0:T(8,128)S(1)}, u32[]{:S(2)}, u32[]{:S(2)}) collective-permute-start(f32[32,128]{1,0:T(8,128)S(1)} %get-tuple-element.120), channel_id=1, source_target_pairs={{0,8},{8,16},{16,24},{1,9},{9,17},{17,25},{2,10},{10,18},{18,26},{... | collective-permute-start | bytes 49160 | tf_op jit(solution)/shard_map/ppermute | solution.py:107
  133.5 4.8 %collective-permute-start.18 = (f32[8,128]{1,0:T(8,128)S(1)}, f32[8,128]{1,0:T(8,128)S(1)}, u32[]{:S(2)}, u32[]{:S(2)}) collective-permute-start(f32[8,128]{1,0:T(8,128)S(1)} %bitcast.360), channel_id=1, source_target_pairs={{0,2},{2,4},{4,6},{1,3},{3,5},{5,7},{8,10},{10,12},{12,14},{9,11},... | collective-permute-start | bytes 12296 | tf_op jit(solution)/shard_map/ppermute | solution.py:107
  141.9 3.0 gather_fusion.1
  144.8 4.9 %select_select_fusion.1 = f32[4,32,24,128]{3,0,2,1:T(4,128)} fusion(f32[4,32,24,128]{3,0,2,1:T(4,128)S(1)} %bitcast.285, pred[32,24]{1,0:T(8,128)(4,1)} %broadcast_in_dim.362, pred[32,24]{1,0:T(8,128)(4,1)} %broadcast_in_dim.360), kind=kLoop, calls=%fused_computation.12 | loop fusion | flops 786432 | bytes 3147264 | tf_op jit(solution)/shard_map/jit(_where)/select_n | solution.py:322
  149.8 7.4 %all-to-all-start.1 = ((f32[4,32,24,128]{3,0,2,1:T(4,128)}), f32[4,32,24,128]{3,0,2,1:T(4,128)S(1)}, u32[]{:S(2)}, u32[]{:S(2)}) async-start(f32[4,32,24,128]{3,0,2,1:T(4,128)} %select_select_fusion.1), calls=%async_computation.1 | async-start | bytes 3145728 | tf_op jit(solution)/shard_map/all_to_all | solution.py:323
  157.2 7.1 %broadcast_divide_fusion = (f32[32,64,128]{2,1,0:T(8,128)}, f32[32,64,128]{2,1,0:T(8,128)}, f32[32,64,128]{2,1,0:T(8,128)}, f32[32,64,128]{2,1,0:T(8,128)}, f32[...) fusion(f32[32,64,128]{2,1,0:T(8,128)} %copy-done.1, ...), kind=kLoop, calls=%fused_computation.40 | loop fusion | flops 6553600 | bytes 17825792 | tf_op jit(solution)/shard_map/div | solution.py:343
  166.6 7.5 %multiply_add_fusion = f32[18,8,32,128]{3,2,1,0:T(8,128)} fusion(f32[8,32,128]{2,1,0:T(8,128)S(1)} %bitcast.302, f32[18]{0:T(128)} %param.18, f32[18]{0:T(128)} %param.16, f32[18]{0:T(128)} %copy-done.88, f32[8,32,128]{2,1,0:T(8,128)S(1)} %bitcast.301, f32[8,32,128]{2,1,0:T(8,128)S(1)} %bitcast.292, f32[19,8,32,128]{3,2,1,0:T(8,128)} %param.14, ...), kind=kLoop, calls=%fused_computation.8 | loop fusion | flops 25952256 | bytes 5243096 | tf_op jit(solution)/shard_map/add | solution.py:59
  174.1 21.9 %all-to-all-done.1 = f32[4,32,24,128]{3,0,2,1:T(4,128)S(1)} async-done(((f32[4,32,24,128]{3,0,2,1:T(4,128)}), f32[4,32,24,128]{3,0,2,1:T(4,128)S(1)}, u32[]{:S(2)}, u32[]{:S(2)}) %all-to-all-start.1) | async-done | bytes 1572896 | tf_op jit(solution)/shard_map/all_to_all | solution.py:323
  196.0 15.3 %gather_fusion.2 = f32[2048,4,128]{2,1,0:T(4,128)} fusion(f32[4,768,128]{2,0,1:T(4,128)S(1)} %bitcast.282, s32[2048]{0:T(1024)S(1)} %copy-done.58), kind=kCustom, calls=%fused_computation.2 | custom fusion | bytes 8396800 | tf_op jit(solution)/shard_map/jit(_take)/gather | solution.py:330
  211.3 2.5 copy.1555
  213.8 2.8 select_select_fusion.r_ref
  216.6 6.7 %chebyshev_start.1 = (f32[4,32,64,128]{3,2,1,0:T(8,128)}, f32[4,64,128]{2,1,0:T(8,128)}, f32[4,64,128]{2,1,0:T(8,128)}, f32[4,32,1,128]{3,2,1,0:T(1,128)}, f32[4...) custom-call(f32[4,32,64,128]{3,2,1,0:T(8,128)} %select_select_fusion.r_ref, ...), custom_call_target="tpu_custom_call" | custom-call | flops 2097152 | bytes 9437184 | tf_op jit(solution)/shard_map/chebyshev_start/pallas_call | solution.py:225
  225.1 2.7 collective-permute-start.20
  232.6 4.0 %collective-permute-done.23.yhi = f32[4,32,1,128]{3,2,1,0:T(1,128)S(1)} collective-permute-done((f32[4,32,1,128]{3,2,1,0:T(1,128)S(1)}, f32[4,32,1,128]{3,2,1,0:T(1,128)S(1)}, u32[]{:S(2)}, u32[]{:S(2)}) %collective-permute-start.23) | collective-permute-done | bytes 65568 | tf_op jit(solution)/shard_map/ppermute | solution.py:107
  237.4 22.4 %chebyshev_sweep.3 = (f32[4,32,64,128]{3,2,1,0:T(8,128)}, f32[4,32,64,128]{3,2,1,0:T(8,128)}, f32[4,32,64,128]{3,2,1,0:T(8,128)}, f32[4,64,128]{2,1,0:T(8,128)},...) custom-call(f32[2]{0:T(128)} %constant.119.clone.coef_ref, ...), custom_call_target="tpu_custom_call" | custom-call | flops 31457280 | bytes 36700160 | tf_op jit(solution)/shard_map/chebyshev_sweep/pallas_call | solution.py:248
  261.9 4.6 %collective-permute-start.25 = (f32[4,64,128]{2,1,0:T(8,128)}, f32[4,64,128]{2,1,0:T(8,128)S(1)}, u32[]{:S(2)}, u32[]{:S(2)}) collective-permute-start(f32[4,64,128]{2,1,0:T(8,128)} %get-tuple-element.42), channel_id=1, source_target_pairs={{0,8},{8,16},{16,24},{1,9},{9,17},{17,25},{2,10},{10,18},{18,26},{... | collective-permute-start | bytes 393224 | tf_op jit(solution)/shard_map/ppermute | solution.py:107
  267.8 2.8 collective-permute-start.27
  270.5 1.6 collective-permute-start.28
  272.8 4.1 %collective-permute-done.28.yhi = f32[4,32,1,128]{3,2,1,0:T(1,128)S(1)} collective-permute-done((f32[4,32,1,128]{3,2,1,0:T(1,128)}, f32[4,32,1,128]{3,2,1,0:T(1,128)S(1)}, u32[]{:S(2)}, u32[]{:S(2)}) %collective-permute-start.28) | collective-permute-done | bytes 65568 | tf_op jit(solution)/shard_map/ppermute | solution.py:107
  277.6 22.3 %chebyshev_sweep.4 = (f32[4,32,64,128]{3,2,1,0:T(8,128)}, f32[4,32,64,128]{3,2,1,0:T(8,128)}, f32[4,32,64,128]{3,2,1,0:T(8,128)}, f32[4,64,128]{2,1,0:T(8,128)},...) custom-call(f32[2]{0:T(128)} %constant.120.clone.coef_ref, ...), custom_call_target="tpu_custom_call" | custom-call | flops 31457280 | bytes 36700160 | tf_op jit(solution)/shard_map/chebyshev_sweep/pallas_call | solution.py:248
  300.9 1.8 pad_maximum_fusion
  302.7 4.9 %collective-permute-start.30 = (f32[4,64,128]{2,1,0:T(8,128)S(1)}, f32[4,64,128]{2,1,0:T(8,128)S(1)}, u32[]{:S(2)}, u32[]{:S(2)}) collective-permute-start(f32[4,64,128]{2,1,0:T(8,128)S(1)} %copy-done.93), channel_id=1, source_target_pairs={{0,8},{8,16},{16,24},{1,9},{9,17},{17,25},{2,10},{10,18},{18,26},{... | collective-permute-start | bytes 393224 | tf_op jit(solution)/shard_map/ppermute | solution.py:107
  308.8 3.5 %collective-permute-start.32 = (f32[4,32,1,128]{3,2,1,0:T(1,128)S(1)}, f32[4,32,1,128]{3,2,1,0:T(1,128)S(1)}, u32[]{:S(2)}, u32[]{:S(2)}) collective-permute-start(f32[4,32,1,128]{3,2,1,0:T(1,128)S(1)} %copy-done.95), channel_id=1, source_target_pairs={{0,2},{2,4},{4,6},{1,3},{3,5},{5,7},{8,10},{10,12},{12,14},{9,11},... | collective-permute-start | bytes 196616 | tf_op jit(solution)/shard_map/ppermute | solution.py:107
  314.4 4.2 %collective-permute-done.33.yhi = f32[4,32,1,128]{3,2,1,0:T(1,128)S(1)} collective-permute-done((f32[4,32,1,128]{3,2,1,0:T(1,128)S(1)}, f32[4,32,1,128]{3,2,1,0:T(1,128)S(1)}, u32[]{:S(2)}, u32[]{:S(2)}) %collective-permute-start.33) | collective-permute-done | bytes 65568 | tf_op jit(solution)/shard_map/ppermute | solution.py:107
  319.3 24.3 %chebyshev_sweep.5 = (f32[4,32,64,128]{3,2,1,0:T(8,128)}, f32[4,32,64,128]{3,2,1,0:T(8,128)}, f32[32,64,4,128]{3,2,1,0:T(4,128)}, f32[4,64,128]{2,1,0:T(8,128)},...) custom-call(f32[2]{0:T(128)} %constant.121.clone.coef_ref, ...), custom_call_target="tpu_custom_call" | custom-call | flops 31457280 | bytes 36700160 | tf_op jit(solution)/shard_map/chebyshev_sweep/pallas_call | solution.py:248
  (378 shorter events, 72.8 us)
Async XLA Ops:
  12.8 35.0 %copy-start = (f32[32,64,128]{2,1,0:T(8,128)}, f32[32,64,128]{2,1,0:T(8,128)S(1)}, u32[]{:S(2)}) copy-start(f32[32,64,128]{2,1,0:T(8,128)S(1)} %get-tuple-element.102) | copy-start | bytes 3145732
  12.8 36.5 %copy-start.1 = (f32[32,64,128]{2,1,0:T(8,128)}, f32[32,64,128]{2,1,0:T(8,128)S(1)}, u32[]{:S(2)}) copy-start(f32[32,64,128]{2,1,0:T(8,128)S(1)} %get-tuple-element.103) | copy-start | bytes 3145732
  15.2 55.3 %collective-permute-start.2 = (f32[5120]{0:T(1024)}, f32[5120]{0:T(1024)S(1)}, u32[]{:S(2)}, u32[]{:S(2)}) collective-permute-start(f32[5120]{0:T(1024)} %pad_maximum_fusion.4), channel_id=1, source_target_pairs={{2,0},{4,2},{6,4},{3,1},{5,3},{7,5},{10,8},{12,10},{14,12},{11,9},... | collective-permute-start | bytes 61448 | tf_op jit(solution)/shard_map/ppermute | solution.py:107
  17.1 53.4 %collective-permute-start.3 = (f32[5120]{0:T(1024)}, f32[5120]{0:T(1024)S(1)}, u32[]{:S(2)}, u32[]{:S(2)}) collective-permute-start(f32[5120]{0:T(1024)} %pad_maximum_fusion.5), channel_id=1, source_target_pairs={{0,2},{2,4},{4,6},{1,3},{3,5},{5,7},{8,10},{10,12},{12,14},{9,11},... | collective-permute-start | bytes 61448 | tf_op jit(solution)/shard_map/ppermute | solution.py:107
  23.4 47.7 %collective-permute-start.1 = (f32[12288]{0:T(1024)S(1)}, f32[12288]{0:T(1024)S(1)}, u32[]{:S(2)}, u32[]{:S(2)}) collective-permute-start(f32[12288]{0:T(1024)S(1)} %pad_maximum_fusion.3), channel_id=1, source_target_pairs={{0,8},{8,16},{16,24},{1,9},{9,17},{17,25},{2,10},{10,18},{18,26},{... | collective-permute-start | bytes 147464 | tf_op jit(solution)/shard_map/ppermute | solution.py:107
  27.9 43.3 %collective-permute-start = (f32[12288]{0:T(1024)}, f32[12288]{0:T(1024)S(1)}, u32[]{:S(2)}, u32[]{:S(2)}) collective-permute-start(f32[12288]{0:T(1024)} %pad_maximum_fusion.2), channel_id=1, source_target_pairs={{8,0},{16,8},{24,16},{9,1},{17,9},{25,17},{10,2},{18,10},{26,18},{... | collective-permute-start | bytes 147464 | tf_op jit(solution)/shard_map/ppermute | solution.py:107
  31.2 33.7 %collective-permute-start.4 = (f32[2304]{0:T(1024)}, f32[2304]{0:T(1024)}, u32[]{:S(2)}, u32[]{:S(2)}) collective-permute-start(f32[2304]{0:T(1024)} %maximum_select_fusion), channel_id=1, source_target_pairs={{0,1},{1,0},{2,3},{3,2},{4,5},{5,4},{6,7},{7,6},{8,9},{9,8},{10,11... | collective-permute-start | bytes 27656 | tf_op jit(solution)/shard_map/ppermute | solution.py:102
  41.7 16.9 %all-to-all-start = ((s32[32,1,24]{2,1,0:T(1,128)}), s32[32,1,24]{2,1,0:T(1,128)S(1)}, u32[]{:S(2)}, u32[]{:S(2)}) async-start(s32[32,1,24]{2,1,0:T(1,128)} %bitcast.116), calls=%async_computation | async-start | bytes 32768 | tf_op jit(solution)/shard_map/all_to_all | solution.py:293
  55.0 51.0 %copy-start.8 = (pred[8,32,128]{2,1,0:T(8,128)(4,1)}, pred[8,32,128]{2,1,0:T(8,128)(4,1)S(1)}, u32[]{:S(2)}) copy-start(pred[8,32,128]{2,1,0:T(8,128)(4,1)S(1)} %get-tuple-element.162) | copy-start | bytes 98308
  55.0 51.0 %copy-start.10 = (pred[8,32,128]{2,1,0:T(8,128)(4,1)}, pred[8,32,128]{2,1,0:T(8,128)(4,1)S(1)}, u32[]{:S(2)}) copy-start(pred[8,32,128]{2,1,0:T(8,128)(4,1)S(1)} %get-tuple-element.163) | copy-start | bytes 98308
  55.0 51.0 %copy-start.12 = (pred[8,32,128]{2,1,0:T(8,128)(4,1)}, pred[8,32,128]{2,1,0:T(8,128)(4,1)S(1)}, u32[]{:S(2)}) copy-start(pred[8,32,128]{2,1,0:T(8,128)(4,1)S(1)} %get-tuple-element.164) | copy-start | bytes 98308
  79.9 13.3 %collective-permute-start.9 = (f32[8,32]{1,0:T(8,128)S(1)}, f32[8,32]{1,0:T(8,128)S(1)}, u32[]{:S(2)}, u32[]{:S(2)}) collective-permute-start(f32[8,32]{1,0:T(8,128)S(1)} %fusion.10), channel_id=1, source_target_pairs={{0,1},{1,0},{2,3},{3,2},{4,5},{5,4},{6,7},{7,6},{8,9},{9,8},{10,11... | collective-permute-start | bytes 3080 | tf_op jit(solution)/shard_map/ppermute | solution.py:102
  80.2 16.4 %collective-permute-start.5 = (f32[32,128]{1,0:T(8,128)S(1)}, f32[32,128]{1,0:T(8,128)S(1)}, u32[]{:S(2)}, u32[]{:S(2)}) collective-permute-start(f32[32,128]{1,0:T(8,128)S(1)} %get-tuple-element.153), channel_id=1, source_target_pairs={{8,0},{16,8},{24,16},{9,1},{17,9},{25,17},{10,2},{18,10},{26,18},{... | collective-permute-start | bytes 49160 | tf_op jit(solution)/shard_map/ppermute | solution.py:107
  81.5 15.1 %collective-permute-start.6 = (f32[32,128]{1,0:T(8,128)S(1)}, f32[32,128]{1,0:T(8,128)S(1)}, u32[]{:S(2)}, u32[]{:S(2)}) collective-permute-start(f32[32,128]{1,0:T(8,128)S(1)} %get-tuple-element.152), channel_id=1, source_target_pairs={{0,8},{8,16},{16,24},{1,9},{9,17},{17,25},{2,10},{10,18},{18,26},{... | collective-permute-start | bytes 49160 | tf_op jit(solution)/shard_map/ppermute | solution.py:107
  86.0 10.5 %collective-permute-start.7 = (f32[8,128]{1,0:T(8,128)S(1)}, f32[8,128]{1,0:T(8,128)S(1)}, u32[]{:S(2)}, u32[]{:S(2)}) collective-permute-start(f32[8,128]{1,0:T(8,128)S(1)} %bitcast.358), channel_id=1, source_target_pairs={{2,0},{4,2},{6,4},{3,1},{5,3},{7,5},{10,8},{12,10},{14,12},{11,9},... | collective-permute-start | bytes 12296 | tf_op jit(solution)/shard_map/ppermute | solution.py:107
  87.3 9.2 %collective-permute-start.8 = (f32[8,128]{1,0:T(8,128)S(1)}, f32[8,128]{1,0:T(8,128)S(1)}, u32[]{:S(2)}, u32[]{:S(2)}) collective-permute-start(f32[8,128]{1,0:T(8,128)S(1)} %bitcast.357), channel_id=1, source_target_pairs={{0,2},{2,4},{4,6},{1,3},{3,5},{5,7},{8,10},{10,12},{12,14},{9,11},... | collective-permute-start | bytes 12296 | tf_op jit(solution)/shard_map/ppermute | solution.py:107
  106.6 13.9 %collective-permute-start.14 = (f32[8,32]{1,0:T(8,128)S(1)}, f32[8,32]{1,0:T(8,128)S(1)}, u32[]{:S(2)}, u32[]{:S(2)}) collective-permute-start(f32[8,32]{1,0:T(8,128)S(1)} %fusion.9), channel_id=1, source_target_pairs={{0,1},{1,0},{2,3},{3,2},{4,5},{5,4},{6,7},{7,6},{8,9},{9,8},{10,11... | collective-permute-start | bytes 3080 | tf_op jit(solution)/shard_map/ppermute | solution.py:102
  108.0 13.6 %collective-permute-start.10 = (f32[32,128]{1,0:T(8,128)S(1)}, f32[32,128]{1,0:T(8,128)S(1)}, u32[]{:S(2)}, u32[]{:S(2)}) collective-permute-start(f32[32,128]{1,0:T(8,128)S(1)} %get-tuple-element.137), channel_id=1, source_target_pairs={{8,0},{16,8},{24,16},{9,1},{17,9},{25,17},{10,2},{18,10},{26,18},{... | collective-permute-start | bytes 49160 | tf_op jit(solution)/shard_map/ppermute | solution.py:107
  109.3 12.3 %collective-permute-start.11 = (f32[32,128]{1,0:T(8,128)S(1)}, f32[32,128]{1,0:T(8,128)S(1)}, u32[]{:S(2)}, u32[]{:S(2)}) collective-permute-start(f32[32,128]{1,0:T(8,128)S(1)} %get-tuple-element.136), channel_id=1, source_target_pairs={{0,8},{8,16},{16,24},{1,9},{9,17},{17,25},{2,10},{10,18},{18,26},{... | collective-permute-start | bytes 49160 | tf_op jit(solution)/shard_map/ppermute | solution.py:107
  114.4 6.7 %collective-permute-start.12 = (f32[8,128]{1,0:T(8,128)S(1)}, f32[8,128]{1,0:T(8,128)S(1)}, u32[]{:S(2)}, u32[]{:S(2)}) collective-permute-start(f32[8,128]{1,0:T(8,128)S(1)} %bitcast.361), channel_id=1, source_target_pairs={{2,0},{4,2},{6,4},{3,1},{5,3},{7,5},{10,8},{12,10},{14,12},{11,9},... | collective-permute-start | bytes 12296 | tf_op jit(solution)/shard_map/ppermute | solution.py:107
  115.7 5.9 %collective-permute-start.13 = (f32[8,128]{1,0:T(8,128)S(1)}, f32[8,128]{1,0:T(8,128)S(1)}, u32[]{:S(2)}, u32[]{:S(2)}) collective-permute-start(f32[8,128]{1,0:T(8,128)S(1)} %bitcast.359), channel_id=1, source_target_pairs={{0,2},{2,4},{4,6},{1,3},{3,5},{5,7},{8,10},{10,12},{12,14},{9,11},... | collective-permute-start | bytes 12296 | tf_op jit(solution)/shard_map/ppermute | solution.py:107
  125.4 13.0 %collective-permute-start.19 = (f32[8,32]{1,0:T(8,128)S(1)}, f32[8,32]{1,0:T(8,128)S(1)}, u32[]{:S(2)}, u32[]{:S(2)}) collective-permute-start(f32[8,32]{1,0:T(8,128)S(1)} %fusion.8), channel_id=1, source_target_pairs={{0,1},{1,0},{2,3},{3,2},{4,5},{5,4},{6,7},{7,6},{8,9},{9,8},{10,11... | collective-permute-start | bytes 3080 | tf_op jit(solution)/shard_map/ppermute | solution.py:102
  125.5 14.2 %collective-permute-start.15 = (f32[32,128]{1,0:T(8,128)S(1)}, f32[32,128]{1,0:T(8,128)S(1)}, u32[]{:S(2)}, u32[]{:S(2)}) collective-permute-start(f32[32,128]{1,0:T(8,128)S(1)} %get-tuple-element.121), channel_id=1, source_target_pairs={{8,0},{16,8},{24,16},{9,1},{17,9},{25,17},{10,2},{18,10},{26,18},{... | collective-permute-start | bytes 49160 | tf_op jit(solution)/shard_map/ppermute | solution.py:107
  126.8 12.9 %collective-permute-start.16 = (f32[32,128]{1,0:T(8,128)S(1)}, f32[32,128]{1,0:T(8,128)S(1)}, u32[]{:S(2)}, u32[]{:S(2)}) collective-permute-start(f32[32,128]{1,0:T(8,128)S(1)} %get-tuple-element.120), channel_id=1, source_target_pairs={{0,8},{8,16},{16,24},{1,9},{9,17},{17,25},{2,10},{10,18},{18,26},{... | collective-permute-start | bytes 49160 | tf_op jit(solution)/shard_map/ppermute | solution.py:107
  132.2 6.4 %collective-permute-start.17 = (f32[8,128]{1,0:T(8,128)S(1)}, f32[8,128]{1,0:T(8,128)S(1)}, u32[]{:S(2)}, u32[]{:S(2)}) collective-permute-start(f32[8,128]{1,0:T(8,128)S(1)} %bitcast.362), channel_id=1, source_target_pairs={{2,0},{4,2},{6,4},{3,1},{5,3},{7,5},{10,8},{12,10},{14,12},{11,9},... | collective-permute-start | bytes 12296 | tf_op jit(solution)/shard_map/ppermute | solution.py:107
  133.5 6.1 %collective-permute-start.18 = (f32[8,128]{1,0:T(8,128)S(1)}, f32[8,128]{1,0:T(8,128)S(1)}, u32[]{:S(2)}, u32[]{:S(2)}) collective-permute-start(f32[8,128]{1,0:T(8,128)S(1)} %bitcast.360), channel_id=1, source_target_pairs={{0,2},{2,4},{4,6},{1,3},{3,5},{5,7},{8,10},{10,12},{12,14},{9,11},... | collective-permute-start | bytes 12296 | tf_op jit(solution)/shard_map/ppermute | solution.py:107
  149.8 46.2 %all-to-all-start.1 = ((f32[4,32,24,128]{3,0,2,1:T(4,128)}), f32[4,32,24,128]{3,0,2,1:T(4,128)S(1)}, u32[]{:S(2)}, u32[]{:S(2)}) async-start(f32[4,32,24,128]{3,0,2,1:T(4,128)} %select_select_fusion.1), calls=%async_computation.1 | async-start | bytes 3145728 | tf_op jit(solution)/shard_map/all_to_all | solution.py:323
  166.6 29.5 %copy-start.58 = (s32[2048]{0:T(1024)S(1)}, s32[2048]{0:T(1024)}, u32[]{:S(2)}) copy-start(s32[2048]{0:T(1024)} %fusion.84) | copy-start | bytes 24580
  224.2 7.5 %collective-permute-start.24 = (f32[4,32,64]{2,1,0:T(8,128)S(1)}, f32[4,32,64]{2,1,0:T(8,128)S(1)}, u32[]{:S(2)}, u32[]{:S(2)}) collective-permute-start(f32[4,32,64]{2,1,0:T(8,128)S(1)} %broadcast_select_fusion.8), channel_id=1, source_target_pairs={{0,1},{1,0},{2,3},{3,2},{4,5},{5,4},{6,7},{7,6},{8,9},{9,8},{10,11... | collective-permute-start | bytes 98312 | tf_op jit(solution)/shard_map/ppermute | solution.py:102
  225.1 11.5 %collective-permute-start.20 = (f32[4,64,128]{2,1,0:T(8,128)}, f32[4,64,128]{2,1,0:T(8,128)S(1)}, u32[]{:S(2)}, u32[]{:S(2)}) collective-permute-start(f32[4,64,128]{2,1,0:T(8,128)} %get-tuple-element.33), channel_id=1, source_target_pairs={{0,8},{8,16},{16,24},{1,9},{9,17},{17,25},{2,10},{10,18},{18,26},{... | collective-permute-start | bytes 393224 | tf_op jit(solution)/shard_map/ppermute | solution.py:107
  227.8 8.8 %collective-permute-start.21 = (f32[4,64,128]{2,1,0:T(8,128)}, f32[4,64,128]{2,1,0:T(8,128)S(1)}, u32[]{:S(2)}, u32[]{:S(2)}) collective-permute-start(f32[4,64,128]{2,1,0:T(8,128)} %get-tuple-element.34), channel_id=1, source_target_pairs={{8,0},{16,8},{24,16},{9,1},{17,9},{25,17},{10,2},{18,10},{26,18},{... | collective-permute-start | bytes 393224 | tf_op jit(solution)/shard_map/ppermute | solution.py:107
  229.1 3.5 %collective-permute-start.22 = (f32[4,32,1,128]{3,2,1,0:T(1,128)}, f32[4,32,1,128]{3,2,1,0:T(1,128)S(1)}, u32[]{:S(2)}, u32[]{:S(2)}) collective-permute-start(f32[4,32,1,128]{3,2,1,0:T(1,128)} %get-tuple-element.35), channel_id=1, source_target_pairs={{0,2},{2,4},{4,6},{1,3},{3,5},{5,7},{8,10},{10,12},{12,14},{9,11},... | collective-permute-start | bytes 196616 | tf_op jit(solution)/shard_map/ppermute | solution.py:107
  230.4 6.2 %collective-permute-start.23 = (f32[4,32,1,128]{3,2,1,0:T(1,128)S(1)}, f32[4,32,1,128]{3,2,1,0:T(1,128)S(1)}, u32[]{:S(2)}, u32[]{:S(2)}) collective-permute-start(f32[4,32,1,128]{3,2,1,0:T(1,128)S(1)} %copy-done.96), channel_id=1, source_target_pairs={{2,0},{4,2},{6,4},{3,1},{5,3},{7,5},{10,8},{12,10},{14,12},{11,9},... | collective-permute-start | bytes 196616 | tf_op jit(solution)/shard_map/ppermute | solution.py:107
  237.3 23.4 %copy-start.23 = (f32[1,8,32,127]{3,2,1,0:T(8,128)S(1)}, f32[1,8,32,127]{3,2,1,0:T(8,128)}, u32[]{:S(2)}) copy-start(f32[1,8,32,127]{3,2,1,0:T(8,128)} %get-tuple-element.115) | copy-start | bytes 390148
  237.3 23.4 %copy-start.43 = (f32[32,128]{1,0:T(8,128)S(1)}, f32[32,128]{1,0:T(8,128)}, u32[]{:S(2)}) copy-start(f32[32,128]{1,0:T(8,128)} %copy-done.42) | copy-start | bytes 49156
  237.3 23.4 %copy-start.45 = (f32[32,128]{1,0:T(8,128)S(1)}, f32[32,128]{1,0:T(8,128)}, u32[]{:S(2)}) copy-start(f32[32,128]{1,0:T(8,128)} %copy-done.44) | copy-start | bytes 49156
  237.3 23.4 %copy-start.65 = (f32[8,128]{1,0:T(8,128)S(1)}, f32[8,128]{1,0:T(8,128)}, u32[]{:S(2)}) copy-start(f32[8,128]{1,0:T(8,128)} %copy-done.64) | copy-start | bytes 12292
  237.3 23.4 %copy-start.67 = (f32[8,128]{1,0:T(8,128)S(1)}, f32[8,128]{1,0:T(8,128)}, u32[]{:S(2)}) copy-start(f32[8,128]{1,0:T(8,128)} %copy-done.66) | copy-start | bytes 12292
  260.6 11.5 %collective-permute-start.29 = (f32[4,32,64]{2,1,0:T(8,128)S(1)}, f32[4,32,64]{2,1,0:T(8,128)S(1)}, u32[]{:S(2)}, u32[]{:S(2)}) collective-permute-start(f32[4,32,64]{2,1,0:T(8,128)S(1)} %broadcast_select_fusion.7), channel_id=1, source_target_pairs={{0,1},{1,0},{2,3},{3,2},{4,5},{5,4},{6,7},{7,6},{8,9},{9,8},{10,11... | collective-permute-start | bytes 98312 | tf_op jit(solution)/shard_map/ppermute | solution.py:102
  261.9 15.0 %collective-permute-start.25 = (f32[4,64,128]{2,1,0:T(8,128)}, f32[4,64,128]{2,1,0:T(8,128)S(1)}, u32[]{:S(2)}, u32[]{:S(2)}) collective-permute-start(f32[4,64,128]{2,1,0:T(8,128)} %get-tuple-element.42), channel_id=1, source_target_pairs={{0,8},{8,16},{16,24},{1,9},{9,17},{17,25},{2,10},{10,18},{18,26},{... | collective-permute-start | bytes 393224 | tf_op jit(solution)/shard_map/ppermute | solution.py:107
  266.5 10.4 %collective-permute-start.26 = (f32[4,64,128]{2,1,0:T(8,128)}, f32[4,64,128]{2,1,0:T(8,128)S(1)}, u32[]{:S(2)}, u32[]{:S(2)}) collective-permute-start(f32[4,64,128]{2,1,0:T(8,128)} %get-tuple-element.43), channel_id=1, source_target_pairs={{8,0},{16,8},{24,16},{9,1},{17,9},{25,17},{10,2},{18,10},{26,18},{... | collective-permute-start | bytes 393224 | tf_op jit(solution)/shard_map/ppermute | solution.py:107
  267.8 5.0 %collective-permute-start.27 = (f32[4,32,1,128]{3,2,1,0:T(1,128)}, f32[4,32,1,128]{3,2,1,0:T(1,128)S(1)}, u32[]{:S(2)}, u32[]{:S(2)}) collective-permute-start(f32[4,32,1,128]{3,2,1,0:T(1,128)} %get-tuple-element.44), channel_id=1, source_target_pairs={{0,2},{2,4},{4,6},{1,3},{3,5},{5,7},{8,10},{10,12},{12,14},{9,11},... | collective-permute-start | bytes 196616 | tf_op jit(solution)/shard_map/ppermute | solution.py:107
  270.5 6.4 %collective-permute-start.28 = (f32[4,32,1,128]{3,2,1,0:T(1,128)}, f32[4,32,1,128]{3,2,1,0:T(1,128)S(1)}, u32[]{:S(2)}, u32[]{:S(2)}) collective-permute-start(f32[4,32,1,128]{3,2,1,0:T(1,128)} %get-tuple-element.45), channel_id=1, source_target_pairs={{2,0},{4,2},{6,4},{3,1},{5,3},{7,5},{10,8},{12,10},{14,12},{11,9},... | collective-permute-start | bytes 196616 | tf_op jit(solution)/shard_map/ppermute | solution.py:107
  300.8 12.9 %collective-permute-start.34 = (f32[4,32,64]{2,1,0:T(8,128)S(1)}, f32[4,32,64]{2,1,0:T(8,128)S(1)}, u32[]{:S(2)}, u32[]{:S(2)}) collective-permute-start(f32[4,32,64]{2,1,0:T(8,128)S(1)} %broadcast_select_fusion.6), channel_id=1, source_target_pairs={{0,1},{1,0},{2,3},{3,2},{4,5},{5,4},{6,7},{7,6},{8,9},{9,8},{10,11... | collective-permute-start | bytes 98312 | tf_op jit(solution)/shard_map/ppermute | solution.py:102
  302.7 15.9 %collective-permute-start.30 = (f32[4,64,128]{2,1,0:T(8,128)S(1)}, f32[4,64,128]{2,1,0:T(8,128)S(1)}, u32[]{:S(2)}, u32[]{:S(2)}) collective-permute-start(f32[4,64,128]{2,1,0:T(8,128)S(1)} %copy-done.93), channel_id=1, source_target_pairs={{0,8},{8,16},{16,24},{1,9},{9,17},{17,25},{2,10},{10,18},{18,26},{... | collective-permute-start | bytes 393224 | tf_op jit(solution)/shard_map/ppermute | solution.py:107
  307.5 11.0 %collective-permute-start.31 = (f32[4,64,128]{2,1,0:T(8,128)S(1)}, f32[4,64,128]{2,1,0:T(8,128)S(1)}, u32[]{:S(2)}, u32[]{:S(2)}) collective-permute-start(f32[4,64,128]{2,1,0:T(8,128)S(1)} %copy-done.92), channel_id=1, source_target_pairs={{8,0},{16,8},{24,16},{9,1},{17,9},{25,17},{10,2},{18,10},{26,18},{... | collective-permute-start | bytes 393224 | tf_op jit(solution)/shard_map/ppermute | solution.py:107
  308.8 5.5 %collective-permute-start.32 = (f32[4,32,1,128]{3,2,1,0:T(1,128)S(1)}, f32[4,32,1,128]{3,2,1,0:T(1,128)S(1)}, u32[]{:S(2)}, u32[]{:S(2)}) collective-permute-start(f32[4,32,1,128]{3,2,1,0:T(1,128)S(1)} %copy-done.95), channel_id=1, source_target_pairs={{0,2},{2,4},{4,6},{1,3},{3,5},{5,7},{8,10},{10,12},{12,14},{9,11},... | collective-permute-start | bytes 196616 | tf_op jit(solution)/shard_map/ppermute | solution.py:107
  312.4 6.2 %collective-permute-start.33 = (f32[4,32,1,128]{3,2,1,0:T(1,128)S(1)}, f32[4,32,1,128]{3,2,1,0:T(1,128)S(1)}, u32[]{:S(2)}, u32[]{:S(2)}) collective-permute-start(f32[4,32,1,128]{3,2,1,0:T(1,128)S(1)} %copy-done.94), channel_id=1, source_target_pairs={{2,0},{4,2},{6,4},{3,1},{5,3},{7,5},{10,8},{12,10},{14,12},{11,9},... | collective-permute-start | bytes 196616 | tf_op jit(solution)/shard_map/ppermute | solution.py:107
  (89 other events, 448.0 us)
